TPU v7x, 512 devices: a whole 4x8x8 slice. The times are simulated.
512 devices in a mesh: section: 2 (over core), req: 64 (over y, z), head: 4 (over x).
Axes of the slice: x: 4, y: 8, z: 8, core: 2. Of those that a mesh axis runs over, the one named last changes fastest.
Arguments:
- embedding_per_slot: bfloat16 [512, 4, 1024], P('req', None, 'head'), may hold values from -6 to 6
- tally_per_slot: int32 [512], P('req'), may hold values from 1 to 4
- slot_requests: int32 [512], replicated, may hold values from 0 to 511, as said below
- memory_per_request: float32 [2, 512, 16, 64, 64], P('section', 'req', 'head'), may hold values from -4 to 4
- previous_step_feature: bfloat16 [2, 512, 1024], P('section', 'req', 'head'), may hold values from -6 to 6
- lag_interpolants: bfloat16 [2, 5, 1024], P('section'), may hold values from 0 to 1
- acceptor_projection: bfloat16 [2, 1024, 1024], P('section', None, 'head'), may hold values from -0.1875 to 0.1875
- address_projection: bfloat16 [2, 1024, 1024], P('section', None, 'head'), may hold values from -0.1875 to 0.1875
- content_projection: bfloat16 [2, 1024, 1024], P('section', None, 'head'), may hold values from -0.1875 to 0.1875
- readout_projection: bfloat16 [2, 1024, 1024], P('section', 'head'), may hold values from -0.1875 to 0.1875
- fading_first_lowrank: bfloat16 [2, 1024, 96], P('section', 'head'), may hold values from -0.1875 to 0.1875
- fading_second_lowrank: bfloat16 [2, 96, 1024], P('section', None, 'head'), may hold values from -0.625 to 0.625
- adapt_first_lowrank: bfloat16 [2, 1024, 96], P('section', 'head'), may hold values from -0.1875 to 0.1875
- adapt_second_lowrank: bfloat16 [2, 96, 1024], P('section', None, 'head'), may hold values from -0.625 to 0.625
- fading_baseline: float32 [2, 1024], P('section', 'head'), may hold values from -4 to 1
- adapt_baseline: float32 [2, 1024], P('section', 'head'), may hold values from -3 to 3
- erasing_address_gains: float32 [2, 1024], P('section', 'head'), may hold values from 0.5 to 1.5
- address_rate_coupling: float32 [2, 1024], P('section', 'head'), may hold values from 0 to 1
- present_extra_gain: float32 [2, 1024], P('section', 'head'), may hold values from -3 to 3
- section_standard_gains: float32 [2, 1024], P('section', 'head'), may hold values from 0.1 to 1.9
- section_standard_shift_terms: float32 [2, 1024], P('section', 'head'), may hold values from -2 to 2
Outputs:
- layer_out: bfloat16 [2, 512, 4, 1024], P('section', 'req', None, 'head')
Inputs may be any that keep to these rules, and one draw needn't show every extreme that they name: `slot_requests`: every request appears once. Of one group's 8 arrival slots at most 1 hold requests stored in any one group, and each group holds exactly 1 from some group.
All inputs are finite; a program needn't handle non-finite values.
Results may differ from a plain program's by a relative error of at most 0.02.
Values may be sent and summed in bfloat16 or wider, within the bound.
No kernel may reach another device: no remote copies, remote signals or barrier semaphores. Data moves between devices by JAX's collectives and lax.ppermute only.
A program may use at most 64 MiB of HBM per device.

v0:
```python
import jax
import jax.numpy as jnp
from jax import lax
from jax.sharding import PartitionSpec as P

highest = lax.Precision.HIGHEST


def from_behind(block, axis, distance):
    devices = range(lax.axis_size(axis))
    route = [(i - distance, i) for i in devices if i - distance in devices]
    return lax.ppermute(block, axis, route)


def sequence_recurrence(
    acceptor_entries,
    address_entries,
    content_entries,
    latent_response,
    adapt_latent,
    starting_memory,
    fading_second_lowrank,
    adapt_second_lowrank,
    fading_baseline,
    adapt_baseline,
    erasing_address_gains,
    address_rate_coupling,
    present_extra_gain,
    section_standard_gains,
    section_standard_shift_terms,
):
    batch_rows = starting_memory.shape[0]
    stored_memory_parts = starting_memory.shape[1]
    subspace_span = starting_memory.shape[2]

    def to_heads(array_in):
        return array_in.reshape(batch_rows, -1, stored_memory_parts, subspace_span)

    log_rate = (
        -jax.nn.softplus(
            -(
                fading_baseline
                + jnp.dot(
                    latent_response, fading_second_lowrank, preferred_element_type=jnp.float32
                )
            )
        )
        - 0.5
    )
    decays = to_heads(jnp.exp(-jnp.exp(log_rate)))
    learning = jax.nn.sigmoid(
        adapt_baseline
        + jnp.dot(adapt_latent, adapt_second_lowrank, preferred_element_type=jnp.float32)
    )
    learn_heads = to_heads(learning)
    scaled = to_heads(address_entries * erasing_address_gains)
    normed = scaled / jnp.sqrt(jnp.sum(scaled * scaled, axis=-1, keepdims=True) + 1e-06)
    erasing_address = to_heads(address_entries * (1.0 + (learning - 1.0) * address_rate_coupling))
    acceptor_parts = to_heads(acceptor_entries)
    content_part_lines = to_heads(content_entries)
    states = starting_memory
    readout = []
    for position in range(acceptor_parts.shape[1]):
        pulled = jnp.einsum("rhij,rhj->rhi", states, normed[:, position], precision=highest)
        states = (
            states * decays[:, position][:, :, None, :]
            - jnp.einsum(
                "rhi,rhj->rhij",
                pulled,
                normed[:, position] * learn_heads[:, position],
                precision=highest,
            )
            + jnp.einsum(
                "rhi,rhj->rhij",
                content_part_lines[:, position],
                erasing_address[:, position],
                precision=highest,
            )
        )
        readout.append(
            jnp.einsum("rhij,rhj->rhi", states, acceptor_parts[:, position], precision=highest)
        )
    read_all = jnp.stack(readout, axis=1)
    center = read_all - jnp.mean(read_all, axis=-1, keepdims=True)
    variance = jnp.mean(center * center, axis=-1, keepdims=True)
    gain_heads = section_standard_gains.reshape(stored_memory_parts, subspace_span)
    bias_heads = section_standard_shift_terms.reshape(stored_memory_parts, subspace_span)
    standardized_parts = center / jnp.sqrt(variance + 0.00064) * gain_heads + bias_heads
    present_extra_term = (
        jnp.sum(
            acceptor_parts
            * erasing_address
            * present_extra_gain.reshape(stored_memory_parts, subspace_span),
            axis=-1,
            keepdims=True,
        )
        * content_part_lines
    )
    return (
        (standardized_parts + present_extra_term)
        .astype(jnp.bfloat16)
        .reshape(-1, stored_memory_parts * subspace_span)
    )


def run_sublevel(lowrank_latent, earlier_entry, starting_memory, params):
    (
        lag_interpolants,
        acceptor_projection,
        address_projection,
        content_projection,
        readout_projection,
        fading_first_lowrank,
        fading_second_lowrank,
        adapt_first_lowrank,
        adapt_second_lowrank,
        fading_baseline,
        adapt_baseline,
        erasing_address_gains,
        address_rate_coupling,
        present_extra_gain,
        section_standard_gains,
        section_standard_shift_terms,
    ) = params
    batch_rows, steps_count, shard_width = lowrank_latent.shape
    previous = jnp.concatenate([earlier_entry[:, None, :], lowrank_latent[:, :-1, :]], axis=1)
    piece_now = lax.all_gather(lowrank_latent, "head", axis=2, tiled=True)
    piece_prev = lax.all_gather(previous, "head", axis=2, tiled=True)
    span_width = piece_now.shape[2]
    coef_rows = lag_interpolants.astype(jnp.float32)
    current_piece = piece_now.astype(jnp.float32)
    spread_piece = piece_prev.astype(jnp.float32) - current_piece
    updated = []
    for slot_num, which_mix, weight_all in (
        (0, 0, acceptor_projection),
        (1, 2, address_projection),
        (2, 3, content_projection),
    ):
        blend = (
            (current_piece + spread_piece * coef_rows[which_mix])
            .astype(jnp.bfloat16)
            .reshape(-1, span_width)
        )
        updated.append(jnp.dot(blend, weight_all, preferred_element_type=jnp.float32))
    acceptor_entries = updated[0]
    address_entries = updated[1]
    content_entries = updated[2]
    current = lowrank_latent.astype(jnp.float32)
    spread = previous.astype(jnp.float32) - current
    column_start = lax.axis_index("head") * shard_width
    decay_mix = lax.dynamic_slice_in_dim(lag_interpolants[1], column_start, shard_width, 0).astype(
        jnp.float32
    )
    learn_mix = lax.dynamic_slice_in_dim(lag_interpolants[4], column_start, shard_width, 0).astype(
        jnp.float32
    )
    decay_input = (current + spread * decay_mix).astype(jnp.bfloat16).reshape(-1, shard_width)
    learn_input = (current + spread * learn_mix).astype(jnp.bfloat16).reshape(-1, shard_width)
    partial_rank = jnp.dot(decay_input, fading_first_lowrank, preferred_element_type=jnp.float32)
    partial_learn = jnp.dot(learn_input, adapt_first_lowrank, preferred_element_type=jnp.float32)
    decay_total, learn_total = lax.psum((partial_rank, partial_learn), "head")
    latent_response = jnp.tanh(decay_total).astype(jnp.bfloat16)
    adapt_latent = learn_total.astype(jnp.bfloat16)
    lagged_features = sequence_recurrence(
        acceptor_entries,
        address_entries,
        content_entries,
        latent_response,
        adapt_latent,
        starting_memory,
        fading_second_lowrank,
        adapt_second_lowrank,
        fading_baseline,
        adapt_baseline,
        erasing_address_gains,
        address_rate_coupling,
        present_extra_gain,
        section_standard_gains,
        section_standard_shift_terms,
    )
    own_rows = lax.psum_scatter(
        lax.dot_general(
            readout_projection,
            lagged_features,
            (((0,), (1,)), ((), ())),
            preferred_element_type=jnp.float32,
        ),
        "head",
        scatter_dimension=0,
        tiled=True,
    )
    projected = own_rows.T.reshape(batch_rows, steps_count, shard_width)
    return (current + projected).astype(jnp.bfloat16)


def run_sections(inputs, states_use, last_use, params):
    section_num = lax.axis_index("section")
    section_count = lax.axis_size("section")
    block_count = 1
    block_rows = inputs.shape[0] // block_count
    result = jnp.zeros_like(inputs)
    incoming = jnp.zeros((block_rows,) + inputs.shape[1:], jnp.bfloat16)
    tick_total = block_count + section_count - 1
    for tick_num in range(tick_total):
        lag = tick_num - section_num
        entering = jnp.where(section_num == 0, inputs, incoming)
        produced = run_sublevel(entering, last_use, states_use, params)
        is_valid = (lag >= 0) & (lag < block_count)
        result = jnp.where(is_valid, produced, result)
        if tick_num + 1 < tick_total:
            incoming = from_behind(produced, "section", 1)
    return result


def body(
    embedding_per_slot,
    tally_per_slot,
    slot_requests,
    memory_per_request,
    previous_step_feature,
    lag_interpolants,
    acceptor_projection,
    address_projection,
    content_projection,
    readout_projection,
    fading_first_lowrank,
    fading_second_lowrank,
    adapt_first_lowrank,
    adapt_second_lowrank,
    fading_baseline,
    adapt_baseline,
    erasing_address_gains,
    address_rate_coupling,
    present_extra_gain,
    section_standard_gains,
    section_standard_shift_terms,
):
    local_rows = embedding_per_slot.shape[0]
    groups = lax.axis_size("req")
    capacity = (local_rows + groups - 1) // groups
    my_group = lax.axis_index("req")
    slot_ids = jnp.arange(local_rows, dtype=jnp.int32)
    table = slot_requests.reshape(groups, local_rows)
    my_arrivals = lax.dynamic_index_in_dim(table, my_group, 0, keepdims=False)
    home_group = my_arrivals // local_rows
    earlier = slot_ids[None, :] < slot_ids[:, None]
    arrival_rank = jnp.sum(
        ((home_group[:, None] == home_group[None, :]) & earlier).astype(jnp.int32), axis=1
    )
    arrival_slot = home_group * capacity + arrival_rank
    requests = my_group * local_rows + slot_ids
    total_rows = slot_requests.shape[0]
    found = slot_requests[None, :] == requests[:, None]
    positions = jnp.sum(
        jnp.where(found, jnp.arange(total_rows, dtype=jnp.int32)[None, :], 0), axis=1
    )
    source = positions // local_rows
    within = positions % local_rows
    source_homes = jnp.take(table, source, axis=0) // local_rows
    home_rank = jnp.sum(
        ((source_homes == my_group) & (slot_ids[None, :] < within[:, None])).astype(jnp.int32),
        axis=1,
    )
    home_slot = source * capacity + home_rank
    buffer_rows = groups * capacity
    params = (
        lag_interpolants[0],
        acceptor_projection[0],
        address_projection[0],
        content_projection[0],
        readout_projection[0],
        fading_first_lowrank[0],
        fading_second_lowrank[0],
        adapt_first_lowrank[0],
        adapt_second_lowrank[0],
        fading_baseline[0],
        adapt_baseline[0],
        erasing_address_gains[0],
        address_rate_coupling[0],
        present_extra_gain[0],
        section_standard_gains[0],
        section_standard_shift_terms[0],
    )
    states_local = memory_per_request[0]
    last_local = previous_step_feature[0]
    outgoing = (
        jnp.zeros((buffer_rows,) + embedding_per_slot.shape[1:], jnp.bfloat16)
        .at[arrival_slot]
        .set(embedding_per_slot)
    )
    arrived = lax.all_to_all(outgoing, "req", split_axis=0, concat_axis=0, tiled=True)
    inputs = jnp.take(arrived, home_slot, axis=0)
    result = run_sections(inputs, states_local, last_local, params)
    going_back = (
        jnp.zeros((buffer_rows,) + result.shape[1:], jnp.bfloat16).at[home_slot].set(result)
    )
    returned = lax.all_to_all(going_back, "req", split_axis=0, concat_axis=0, tiled=True)
    result = jnp.take(returned, arrival_slot, axis=0)
    live_mask = (
        jnp.arange(embedding_per_slot.shape[1], dtype=jnp.int32)[None, :] < tally_per_slot[:, None]
    )
    return jnp.where(live_mask[:, :, None], result, jnp.zeros_like(result))[None]


def solution(mesh):
    return jax.shard_map(
        body,
        mesh=mesh,
        in_specs=(
            P("req", None, "head"),
            P("req"),
            P(),
            P("section", "req", "head", None, None),
            P("section", "req", "head"),
            P("section", None, None),
            P("section", None, "head"),
            P("section", None, "head"),
            P("section", None, "head"),
            P("section", "head", None),
            P("section", "head", None),
            P("section", None, "head"),
            P("section", "head", None),
            P("section", None, "head"),
            P("section", "head"),
            P("section", "head"),
            P("section", "head"),
            P("section", "head"),
            P("section", "head"),
            P("section", "head"),
            P("section", "head"),
        ),
        out_specs=P("section", "req", None, "head"),
        check_vma=False,
    )
```

profile of v0, /device:TPU:6, one launch (start us, length us, event | category | flops | bytes accessed | tf_op | source)
XLA Modules:
  0.0 272.9 jit_solution(2103046319629629872)
XLA Ops:
  8.4 2.0 scatter_fusion
  10.3 16.6 %all-to-all-start = ((bf16[64,4,256]{2,1,0:T(4,128)(2,1)}), bf16[64,4,256]{2,1,0:T(4,128)(2,1)S(1)}, u32[]{:S(2)}, u32[]{:S(2)}) async-start(bf16[64,4,256]{2,1,0:T(4,128)(2,1)} %scatter_fusion), calls=%async_computation | async-start | bytes 262144 | tf_op jit(solution)/shard_map/all_to_all | solution.py:291
  36.4 3.2 %all-to-all-done = bf16[64,4,256]{2,1,0:T(4,128)(2,1)S(1)} async-done(((bf16[64,4,256]{2,1,0:T(4,128)(2,1)}), bf16[64,4,256]{2,1,0:T(4,128)(2,1)S(1)}, u32[]{:S(2)}, u32[]{:S(2)}) %all-to-all-start) | async-done | bytes 131104 | tf_op jit(solution)/shard_map/all_to_all | solution.py:291
  40.3 12.1 %all_gather.12 = bf16[8,4,1024]{2,0,1:T(8,128)(2,1)S(1)} all-gather(bf16[8,4,256]{2,0,1:T(8,128)(2,1)S(1)} %broadcast_select_fusion.1), channel_id=1, replica_groups=mesh['section'=2,'req'=64,'head'=4] {'head'}, dimensions={2}, use_global_device_ids=true | all-gather | bytes 81920 | tf_op jit(solution)/shard_map/all_gather | solution.py:127
  52.4 11.8 %all_gather.13 = bf16[8,4,1024]{2,0,1:T(8,128)(2,1)S(1)} all-gather(bf16[8,4,256]{2,0,1:T(8,128)(2,1)S(1)} %pad_maximum_fusion.3), channel_id=1, replica_groups=mesh['section'=2,'req'=64,'head'=4] {'head'}, dimensions={2}, use_global_device_ids=true | all-gather | bytes 81920 | tf_op jit(solution)/shard_map/all_gather | solution.py:128
  66.2 14.1 %all-reduce.1 = (bf16[32,96]{1,0:T(8,128)(2,1)S(1)}, f32[32,96]{1,0:T(8,128)S(1)}) all-reduce(f32[32,96]{1,0:T(8,128)S(1)} %fusion.86, f32[32,96]{1,0:T(8,128)S(1)} %fusion.92), channel_id=1, replica_groups=mesh['section'=2,'req'=64,'head'=4] {'head'}, use_global_device_ids=true, to_apply=%region_6.8 | all-reduce | flops 6144 | bytes 43008 | tf_op jit(solution)/shard_map/psum | solution.py:161
  90.3 1.7 fusion.20
  92.1 2.1 fusion.137
  94.9 2.1 fusion.160
  97.7 3.2 %fusion.55 = f32[8,4,1,64]{3,2,1,0:T(1,128)S(1)} fusion(f32[8,4,64]{2,1,0:T(4,128)S(1)} %copy-done.15, f32[8,4,64]{2,1,0:T(4,128)S(1)} %copy.164, f32[8,4,64]{2,1,0:T(4,128)S(1)} %copy-done.9, f32[8,4,64]{2,1,0:T(4,128)S(1)} %bitcast.461, f32[8,4,64]{2,1,0:T(4,128)S(1)} %get-tuple-element.50, f32[8,4,64,1]{2,0,1,3:T(8,128)S(1)} %copy-done.31, ...), kind=kOutput, calls=%fused_computation.72 | convolution fusion | flops 2883584 | bytes 622592 | tf_op jit(solution)/shard_map/rhij,rhj->rhi/dot_general | solution.py:81
  101.7 2.8 %fusion.54 = f32[8,4,1,64]{3,2,1,0:T(1,128)S(1)} fusion(f32[8,4,64,1]{2,3,1,0:T(1,128)S(1)} %bitcast.471, f32[8,4,64]{2,1,0:T(4,128)S(1)} %copy-done.15, f32[8,4,64]{2,1,0:T(4,128)S(1)} %copy.164, f32[8,4,64]{2,1,0:T(4,128)S(1)} %copy-done.9, f32[8,4,64]{2,1,0:T(4,128)S(1)} %bitcast.462, f32[8,4,64]{2,1,0:T(4,128)S(1)} %get-tuple-element.50, ...), kind=kOutput, calls=%fused_computation.71 | convolution fusion | flops 2883584 | bytes 622592 | tf_op jit(solution)/shard_map/rhij,rhj->rhi/dot_general | solution.py:64
  105.2 2.0 multiply_add_fusion.2
  107.2 1.7 fusion.134
  109.7 1.7 fusion.168
  112.2 2.1 fusion.32
  116.6 23.6 %reduce-scatter.3.cloned.1.call-done = f32[256,32]{0,1:T(8,128)} async-done(((f32[1024,32]{0,1:T(8,128)}), f32[256,32]{0,1:T(8,128)}) %reduce-scatter.3.cloned.1.call-update) | async-done | bytes 32784 | tf_op jit(solution)/shard_map/reduce_scatter | solution.py:181
  143.2 12.0 %all_gather.14 = bf16[8,4,1024]{2,0,1:T(8,128)(2,1)S(1)} all-gather(bf16[8,4,256]{2,0,1:T(8,128)(2,1)S(1)} %broadcast_select_fusion), channel_id=1, replica_groups=mesh['section'=2,'req'=64,'head'=4] {'head'}, dimensions={2}, use_global_device_ids=true | all-gather | bytes 81920 | tf_op jit(solution)/shard_map/all_gather | solution.py:127
  155.2 11.9 %all_gather.15 = bf16[8,4,1024]{2,0,1:T(8,128)(2,1)S(1)} all-gather(bf16[8,4,256]{2,0,1:T(8,128)(2,1)S(1)} %pad_maximum_fusion.2), channel_id=1, replica_groups=mesh['section'=2,'req'=64,'head'=4] {'head'}, dimensions={2}, use_global_device_ids=true | all-gather | bytes 81920 | tf_op jit(solution)/shard_map/all_gather | solution.py:128
  170.7 14.8 %all-reduce = (bf16[32,96]{1,0:T(8,128)(2,1)S(1)}, f32[32,96]{1,0:T(8,128)S(1)}) all-reduce(f32[32,96]{1,0:T(8,128)S(1)} %fusion.84, f32[32,96]{1,0:T(8,128)S(1)} %fusion.90), channel_id=1, replica_groups=mesh['section'=2,'req'=64,'head'=4] {'head'}, use_global_device_ids=true, to_apply=%region_13.15 | all-reduce | flops 6144 | bytes 43008 | tf_op jit(solution)/shard_map/psum | solution.py:161
  187.6 1.7 fusion.18
  190.6 2.1 fusion.131
  192.7 2.1 fusion.155
  194.7 3.2 %fusion.57 = f32[8,4,1,64]{3,2,1,0:T(1,128)S(1)} fusion(f32[8,4,64]{2,1,0:T(4,128)S(1)} %get-tuple-element.42, f32[8,4,64]{2,1,0:T(4,128)S(1)} %copy.178, f32[8,4,64]{2,1,0:T(4,128)S(1)} %get-tuple-element.18, f32[8,4,64]{2,1,0:T(4,128)S(1)} %bitcast.464, f32[8,4,64]{2,1,0:T(4,128)S(1)} %get-tuple-element.30, f32[8,4,64,1]{2,0,1,3:T(8,128)S(1)} %get-tuple-element.27, ...), kind=kOutput, calls=%fused_computation.74 | convolution fusion | flops 2883584 | bytes 622592 | tf_op jit(solution)/shard_map/rhij,rhj->rhi/dot_general | solution.py:81
  198.0 2.8 %fusion.56 = f32[8,4,1,64]{3,2,1,0:T(1,128)S(1)} fusion(f32[8,4,64,1]{2,3,1,0:T(1,128)S(1)} %bitcast.473, f32[8,4,64]{2,1,0:T(4,128)S(1)} %get-tuple-element.42, f32[8,4,64]{2,1,0:T(4,128)S(1)} %copy.178, f32[8,4,64]{2,1,0:T(4,128)S(1)} %get-tuple-element.18, f32[8,4,64]{2,1,0:T(4,128)S(1)} %bitcast.465, f32[8,4,64]{2,1,0:T(4,128)S(1)} %get-tuple-element.30, ...), kind=kOutput, calls=%fused_computation.73 | convolution fusion | flops 2883584 | bytes 622592 | tf_op jit(solution)/shard_map/rhij,rhj->rhi/dot_general | solution.py:64
  200.8 2.0 multiply_add_fusion
  202.8 1.7 fusion.128
  204.6 1.7 fusion.169
  206.3 2.1 fusion.26
  212.1 24.0 %reduce-scatter.5.cloned.1.call-done = f32[256,32]{0,1:T(8,128)} async-done(((f32[1024,32]{0,1:T(8,128)}), f32[256,32]{0,1:T(8,128)}) %reduce-scatter.5.cloned.1.call-update) | async-done | bytes 32784 | tf_op jit(solution)/shard_map/reduce_scatter | solution.py:181
  237.6 1.9 scatter_fusion.1
  239.5 12.6 %all-to-all-start.1 = ((bf16[64,4,256]{2,1,0:T(4,128)(2,1)}), bf16[64,4,256]{2,1,0:T(4,128)(2,1)S(1)}, u32[]{:S(2)}, u32[]{:S(2)}) async-start(bf16[64,4,256]{2,1,0:T(4,128)(2,1)} %scatter_fusion.1), calls=%async_computation.3 | async-start | bytes 262144 | tf_op jit(solution)/shard_map/all_to_all | solution.py:297
  252.8 12.0 %all-to-all-done.1 = bf16[64,4,256]{2,1,0:T(4,128)(2,1)S(1)} async-done(((bf16[64,4,256]{2,1,0:T(4,128)(2,1)}), bf16[64,4,256]{2,1,0:T(4,128)(2,1)S(1)}, u32[]{:S(2)}, u32[]{:S(2)}) %all-to-all-start.1) | async-done | bytes 131104 | tf_op jit(solution)/shard_map/all_to_all | solution.py:297
  (268 shorter events, 47.0 us)
Async XLA Ops:
  6.5 109.1 %copy-start = (bf16[1,256,1024]{2,1,0:T(8,128)(2,1)S(1)}, bf16[1,256,1024]{2,1,0:T(8,128)(2,1)}, u32[]{:S(2)}) copy-start(bf16[1,256,1024]{2,1,0:T(8,128)(2,1)} %param.32) | copy-start | bytes 1572868
  6.5 23.3 %copy-start.3 = (bf16[1,1024,256]{2,1,0:T(8,128)(2,1)S(1)}, bf16[1,1024,256]{2,1,0:T(8,128)(2,1)}, u32[]{:S(2)}) copy-start(bf16[1,1024,256]{2,1,0:T(8,128)(2,1)} %param.29) | copy-start | bytes 1572868
  7.4 21.0 %copy-start.8 = (s32[64,8]{1,0:T(8,128)}, s32[64,8]{1,0:T(8,128)S(1)}, u32[]{:S(2)}) copy-start(s32[64,8]{1,0:T(8,128)S(1)} %reshape.364) | copy-start | bytes 6148
  10.3 29.3 %all-to-all-start = ((bf16[64,4,256]{2,1,0:T(4,128)(2,1)}), bf16[64,4,256]{2,1,0:T(4,128)(2,1)S(1)}, u32[]{:S(2)}, u32[]{:S(2)}) async-start(bf16[64,4,256]{2,1,0:T(4,128)(2,1)} %scatter_fusion), calls=%async_computation | async-start | bytes 262144 | tf_op jit(solution)/shard_map/all_to_all | solution.py:291
  26.9 113.3 %reduce-scatter.3.cloned.1.call-start = ((), (), s32[]{:S(2)}) async-start(), calls=%async_computation.4 | async-start | bytes 163840 | tf_op jit(solution)/shard_map/reduce_scatter | solution.py:181
  28.9 0.8 copy-start.25
  29.7 34.6 %copy-start.33 = (pred[8]{0:T(512)(128)(4,1)}, pred[8]{0:T(512)(128)(4,1)S(1)}, u32[]{:S(2)}) copy-start(pred[8]{0:T(512)(128)(4,1)S(1)} %get-tuple-element.12) | copy-start | bytes 28
  29.8 34.6 %copy-start.35 = (f32[1,1,256]{2,1,0:T(1,128)}, f32[1,1,256]{2,1,0:T(1,128)S(1)}, u32[]{:S(2)}) copy-start(f32[1,1,256]{2,1,0:T(1,128)S(1)} %get-tuple-element.77) | copy-start | bytes 3076
  29.8 34.6 %copy-start.37 = (f32[1,1,256]{2,1,0:T(1,128)}, f32[1,1,256]{2,1,0:T(1,128)S(1)}, u32[]{:S(2)}) copy-start(f32[1,1,256]{2,1,0:T(1,128)S(1)} %get-tuple-element.78) | copy-start | bytes 3076
  29.8 1.0 copy-start.4
  36.4 27.8 %copy-start.23 = (f32[1,1,1024]{2,1,0:T(1,128)}, f32[1,1,1024]{2,1,0:T(1,128)S(1)}, u32[]{:S(2)}) copy-start(f32[1,1,1024]{2,1,0:T(1,128)S(1)} %get-tuple-element.73) | copy-start | bytes 12292
  36.4 47.4 %copy-start.21 = (f32[1,1,1024]{2,1,0:T(1,128)}, f32[1,1,1024]{2,1,0:T(1,128)S(1)}, u32[]{:S(2)}) copy-start(f32[1,1,1024]{2,1,0:T(1,128)S(1)} %get-tuple-element.72) | copy-start | bytes 12292
  40.3 12.1 %copy-start.17 = (bf16[1,8,256]{2,1,0:T(8,128)(2,1)S(1)}, bf16[1,8,256]{2,1,0:T(8,128)(2,1)}, u32[]{:S(2)}) copy-start(bf16[1,8,256]{2,1,0:T(8,128)(2,1)} %param.27) | copy-start | bytes 12292
  64.2 17.0 %copy-start.2 = (bf16[1,1024,256]{2,1,0:T(8,128)(2,1)S(1)}, bf16[1,1024,256]{2,1,0:T(8,128)(2,1)}, u32[]{:S(2)}) copy-start(bf16[1,1024,256]{2,1,0:T(8,128)(2,1)} %param.30) | copy-start | bytes 1572868
  64.5 0.8 copy-start.5
  65.3 0.8 copy-start.6
  66.1 14.2 %copy-start.55 = (bf16[1,96,256]{2,1,0:T(8,128)(2,1)S(1)}, bf16[1,96,256]{2,1,0:T(8,128)(2,1)}, u32[]{:S(2)}) copy-start(bf16[1,96,256]{2,1,0:T(8,128)(2,1)} %param.36) | copy-start | bytes 147460
  83.8 5.9 %copy-start.1 = (f32[1,8,4,64,64]{4,3,2,1,0:T(8,128)S(1)}, f32[1,8,4,64,64]{4,3,2,1,0:T(8,128)}, u32[]{:S(2)}) copy-start(f32[1,8,4,64,64]{4,3,2,1,0:T(8,128)} %param.26) | copy-start | bytes 1572868
  90.3 1.7 copy-start.10
  90.3 1.7 copy-start.16
  90.3 1.8 copy-start.32
  94.9 2.1 copy-start.31
  105.2 2.0 copy-start.12
  109.7 1.8 copy-start.28
  116.6 119.5 %reduce-scatter.5.cloned.1.call-start = ((), (), s32[]{:S(2)}) async-start(), calls=%async_computation.5 | async-start | bytes 163840 | tf_op jit(solution)/shard_map/reduce_scatter | solution.py:181
  141.1 2.1 collective-permute-start
  143.2 12.0 %copy-start.18 = (bf16[1,8,256]{2,1,0:T(8,128)(2,1)S(1)}, bf16[1,8,256]{2,1,0:T(8,128)(2,1)}, u32[]{:S(2)}) copy-start(bf16[1,8,256]{2,1,0:T(8,128)(2,1)} %param.27) | copy-start | bytes 12292
  155.2 11.9 %copy-start.22 = (f32[1,1,1024]{2,1,0:T(1,128)S(1)}, f32[1,1,1024]{2,1,0:T(1,128)}, u32[]{:S(2)}) copy-start(f32[1,1,1024]{2,1,0:T(1,128)} %copy-done.21) | copy-start | bytes 12292
  169.7 0.8 copy-start.7
  170.6 14.9 %copy-start.56 = (bf16[1,96,256]{2,1,0:T(8,128)(2,1)S(1)}, bf16[1,96,256]{2,1,0:T(8,128)(2,1)}, u32[]{:S(2)}) copy-start(bf16[1,96,256]{2,1,0:T(8,128)(2,1)} %param.36) | copy-start | bytes 147460
  189.4 0.8 copy-start.57
  239.5 25.2 %all-to-all-start.1 = ((bf16[64,4,256]{2,1,0:T(4,128)(2,1)}), bf16[64,4,256]{2,1,0:T(4,128)(2,1)S(1)}, u32[]{:S(2)}, u32[]{:S(2)}) async-start(bf16[64,4,256]{2,1,0:T(4,128)(2,1)} %scatter_fusion.1), calls=%async_computation.3 | async-start | bytes 262144 | tf_op jit(solution)/shard_map/all_to_all | solution.py:297
  (36 other events, 24.8 us)
Sparse Core Ops, SparseCore 0:
  116.7 23.4 reduce-scatter.2
  210.2 25.8 reduce-scatter.4
where the time goes:
time: 276 us; the launch traced here: 273 us
  blocking collectives  76.6 us (28%)
  waiting for transfers between devices  63.7 us (23%)
  matrix products  40.9 us (15%)
  local copies, waits for them, and re-layouts  35.8 us (13%)
  starting transfers between devices  30.6 us (11%)
  between operations  14.4 us (5%)
  other arithmetic  11 us (4%)
    reduce_scatter x2, waiting for transfers between devices, run_sublevel(): lax.psum_scatter(lax.dot_general(readout_projection, lagged_features, (((...  47.6 us
    psum x2, blocking collectives, run_sublevel(): decay_total, learn_total = lax.psum((partial_rank, partial_learn), 'head')  28.9 us
    all_gather x2, blocking collectives, run_sublevel(): piece_now = lax.all_gather(lowrank_latent, 'head', axis=2, tiled=True)  24 us
    all_gather x2, blocking collectives, run_sublevel(): piece_prev = lax.all_gather(previous, 'head', axis=2, tiled=True)  23.7 us
    unnamed x129, local copies, waits for them, and re-layouts  19.2 us
    dot_general x8, matrix products, sequence_recurrence(): jnp.einsum('rhij,rhj->rhi', states, acceptor_parts[:, position], precisio...  18.2 us
    dot_general x8, matrix products, sequence_recurrence(): jnp.einsum('rhij,rhj->rhi', states, normed[:, position], precision=highest)  16.7 us
    all_to_all x1, starting transfers between devices, body(): lax.all_to_all(outgoing, 'req', split_axis=0, concat_axis=0, tiled=True)  16.6 us
  transfers between devices with their start and end apart: 5, of which 5 were waited for; matrix products, arithmetic and copies ran while one was open for 3% of the time, Pallas kernels for 0%

commit v1 on v0

--- a/solution.py
+++ b/solution.py
@@ -4,12 +4,6 @@
 from jax.sharding import PartitionSpec as P
 
 highest = lax.Precision.HIGHEST
-
-
-def from_behind(block, axis, distance):
-    devices = range(lax.axis_size(axis))
-    route = [(i - distance, i) for i in devices if i - distance in devices]
-    return lax.ppermute(block, axis, route)
 
 
 def sequence_recurrence(
@@ -103,16 +97,55 @@
     )
 
 
-def run_sublevel(lowrank_latent, earlier_entry, starting_memory, params):
+def gather_heads(block, axis):
+    n = lax.axis_size("head")
+    me = lax.axis_index("head")
+    pieces = [block]
+    for k in range(1, n):
+        pieces.append(lax.ppermute(block, "head", [(i, (i + k) % n) for i in range(n)]))
+    stacked = jnp.stack(pieces[::-1], axis=0)
+    ordered = jnp.roll(stacked, me + 1, axis=0)
+    moved = jnp.moveaxis(ordered, 0, axis)
+    shape = list(block.shape)
+    shape[axis] = shape[axis] * n
+    return moved.reshape(shape)
+
+
+def scatter_heads(partial):
+    n = lax.axis_size("head")
+    me = lax.axis_index("head")
+    width = partial.shape[1] // n
+    total = lax.dynamic_slice_in_dim(partial, me * width, width, 1)
+    for k in range(1, n):
+        chunk = lax.dynamic_slice_in_dim(partial, ((me + k) % n) * width, width, 1)
+        total = total + lax.ppermute(chunk, "head", [(i, (i + k) % n) for i in range(n)])
+    return total
+
+
+def hand_over(block):
+    n = lax.axis_size("head")
+    me = lax.axis_index("head")
+    pieces = []
+    for k in range(n):
+        pieces.append(
+            lax.ppermute(block, ("section", "head"), [(i, n + (i + k) % n) for i in range(n)])
+        )
+    stacked = jnp.stack(pieces[::-1], axis=0)
+    ordered = jnp.roll(stacked, me + 1, axis=0)
+    moved = jnp.moveaxis(ordered, 0, 2)
+    return moved.reshape(block.shape[:2] + (block.shape[2] * n,)), pieces[0]
+
+
+def run_layer(full_now, full_prev_row, params):
     (
         lag_interpolants,
         acceptor_projection,
         address_projection,
         content_projection,
         readout_projection,
-        fading_first_lowrank,
+        fading_first_full,
         fading_second_lowrank,
-        adapt_first_lowrank,
+        adapt_first_full,
         adapt_second_lowrank,
         fading_baseline,
         adapt_baseline,
@@ -122,94 +155,54 @@
         section_standard_gains,
         section_standard_shift_terms,
     ) = params
-    batch_rows, steps_count, shard_width = lowrank_latent.shape
-    previous = jnp.concatenate([earlier_entry[:, None, :], lowrank_latent[:, :-1, :]], axis=1)
-    piece_now = lax.all_gather(lowrank_latent, "head", axis=2, tiled=True)
-    piece_prev = lax.all_gather(previous, "head", axis=2, tiled=True)
-    span_width = piece_now.shape[2]
+    batch_rows, steps_count, span_width = full_now.shape
+    previous = jnp.concatenate([full_prev_row[:, None, :], full_now[:, :-1, :]], axis=1)
     coef_rows = lag_interpolants.astype(jnp.float32)
-    current_piece = piece_now.astype(jnp.float32)
-    spread_piece = piece_prev.astype(jnp.float32) - current_piece
-    updated = []
-    for slot_num, which_mix, weight_all in (
-        (0, 0, acceptor_projection),
-        (1, 2, address_projection),
-        (2, 3, content_projection),
-    ):
-        blend = (
-            (current_piece + spread_piece * coef_rows[which_mix])
-            .astype(jnp.bfloat16)
-            .reshape(-1, span_width)
-        )
-        updated.append(jnp.dot(blend, weight_all, preferred_element_type=jnp.float32))
-    acceptor_entries = updated[0]
-    address_entries = updated[1]
-    content_entries = updated[2]
-    current = lowrank_latent.astype(jnp.float32)
-    spread = previous.astype(jnp.float32) - current
-    column_start = lax.axis_index("head") * shard_width
-    decay_mix = lax.dynamic_slice_in_dim(lag_interpolants[1], column_start, shard_width, 0).astype(
-        jnp.float32
-    )
-    learn_mix = lax.dynamic_slice_in_dim(lag_interpolants[4], column_start, shard_width, 0).astype(
-        jnp.float32
-    )
-    decay_input = (current + spread * decay_mix).astype(jnp.bfloat16).reshape(-1, shard_width)
-    learn_input = (current + spread * learn_mix).astype(jnp.bfloat16).reshape(-1, shard_width)
-    partial_rank = jnp.dot(decay_input, fading_first_lowrank, preferred_element_type=jnp.float32)
-    partial_learn = jnp.dot(learn_input, adapt_first_lowrank, preferred_element_type=jnp.float32)
-    decay_total, learn_total = lax.psum((partial_rank, partial_learn), "head")
-    latent_response = jnp.tanh(decay_total).astype(jnp.bfloat16)
-    adapt_latent = learn_total.astype(jnp.bfloat16)
+    current_piece = full_now.astype(jnp.float32)
+    spread_piece = previous.astype(jnp.float32) - current_piece
+    blends = [
+        (current_piece + spread_piece * coef_rows[which_mix])
+        .astype(jnp.bfloat16)
+        .reshape(-1, span_width)
+        for which_mix in range(5)
+    ]
+    acceptor_entries = jnp.dot(blends[0], acceptor_projection, preferred_element_type=jnp.float32)
+    address_entries = jnp.dot(blends[2], address_projection, preferred_element_type=jnp.float32)
+    content_entries = jnp.dot(blends[3], content_projection, preferred_element_type=jnp.float32)
+    latent_response = jnp.tanh(
+        jnp.dot(blends[1], fading_first_full, preferred_element_type=jnp.float32)
+    ).astype(jnp.bfloat16)
+    adapt_latent = jnp.dot(blends[4], adapt_first_full, preferred_element_type=jnp.float32).astype(
+        jnp.bfloat16
+    )
+    return acceptor_entries, address_entries, content_entries, latent_response, adapt_latent
+
+
+def layer_partial(full_now, full_prev_row, starting_memory, params):
+    entries = run_layer(full_now, full_prev_row, params)
     lagged_features = sequence_recurrence(
-        acceptor_entries,
-        address_entries,
-        content_entries,
-        latent_response,
-        adapt_latent,
+        *entries,
         starting_memory,
-        fading_second_lowrank,
-        adapt_second_lowrank,
-        fading_baseline,
-        adapt_baseline,
-        erasing_address_gains,
-        address_rate_coupling,
-        present_extra_gain,
-        section_standard_gains,
-        section_standard_shift_terms,
-    )
-    own_rows = lax.psum_scatter(
-        lax.dot_general(
-            readout_projection,
-            lagged_features,
-            (((0,), (1,)), ((), ())),
-            preferred_element_type=jnp.float32,
-        ),
-        "head",
-        scatter_dimension=0,
-        tiled=True,
-    )
-    projected = own_rows.T.reshape(batch_rows, steps_count, shard_width)
-    return (current + projected).astype(jnp.bfloat16)
+        params[6],
+        params[8],
+        *params[9:],
+    )
+    return jnp.dot(lagged_features, params[4], preferred_element_type=jnp.float32)
 
 
 def run_sections(inputs, states_use, last_use, params):
     section_num = lax.axis_index("section")
-    section_count = lax.axis_size("section")
-    block_count = 1
-    block_rows = inputs.shape[0] // block_count
-    result = jnp.zeros_like(inputs)
-    incoming = jnp.zeros((block_rows,) + inputs.shape[1:], jnp.bfloat16)
-    tick_total = block_count + section_count - 1
-    for tick_num in range(tick_total):
-        lag = tick_num - section_num
-        entering = jnp.where(section_num == 0, inputs, incoming)
-        produced = run_sublevel(entering, last_use, states_use, params)
-        is_valid = (lag >= 0) & (lag < block_count)
-        result = jnp.where(is_valid, produced, result)
-        if tick_num + 1 < tick_total:
-            incoming = from_behind(produced, "section", 1)
-    return result
+    batch_rows, steps_count, shard_width = inputs.shape
+    full_prev = gather_heads(last_use, 1)
+    full_first = gather_heads(inputs, 2)
+    partial_first = layer_partial(full_first, full_prev, states_use, params)
+    own_first = scatter_heads(partial_first).reshape(batch_rows, steps_count, shard_width)
+    first_out = (inputs.astype(jnp.float32) + own_first).astype(jnp.bfloat16)
+    full_second, second_in = hand_over(first_out)
+    partial_second = layer_partial(full_second, full_prev, states_use, params)
+    own_second = scatter_heads(partial_second).reshape(batch_rows, steps_count, shard_width)
+    second_out = (second_in.astype(jnp.float32) + own_second).astype(jnp.bfloat16)
+    return jnp.where(section_num == 0, first_out, second_out)
 
 
 def body(
@@ -269,9 +262,9 @@
         address_projection[0],
         content_projection[0],
         readout_projection[0],
-        fading_first_lowrank[0],
+        gather_heads(fading_first_lowrank[0], 0),
         fading_second_lowrank[0],
-        adapt_first_lowrank[0],
+        gather_heads(adapt_first_lowrank[0], 0),
         adapt_second_lowrank[0],
         fading_baseline[0],
         adapt_baseline[0],

time: 276 us -> 225 us (0.82)
  blocking collectives: 76.6 us -> 0 us
  starting transfers between devices: 30.6 us -> 92.2 us
  waiting for transfers between devices: 63.7 us -> 25.8 us
  between operations: 14.4 us -> 1.54 us
  local copies, waits for them, and re-layouts: 35.8 us -> 42.1 us
  other arithmetic: 11 us -> 16.4 us
  matrix products: 40.9 us -> 43.7 us
    ppermute x1 -> x22, starting transfers between devices: 1.28 us -> 65.9 us  [the longest x12 43.5 us: gather_heads(): lax.ppermute(block, 'head', [(i, (i + k) % n) for i in range(n)])]
    all_gather x4 -> x0, blocking collectives: 47.7 us -> none  [the longest x2 24 us: run_sublevel(): piece_now = lax.all_gather(lowrank_latent, 'head', axis=2, tiled=True)]
    reduce_scatter x2 -> x0, waiting for transfers between devices: 47.6 us -> none  [run_sublevel(): lax.psum_scatter(lax.dot_general(readout_projection, lagged_features, (((...]
    psum x2 -> x0, blocking collectives: 28.9 us -> none  [run_sublevel(): decay_total, learn_total = lax.psum((partial_rank, partial_learn), 'head')]
    ppermute x1 -> x22, waiting for transfers between devices: 0.82 us -> 13.7 us  [the longest x6 8.07 us: scatter_heads(): lax.ppermute(chunk, 'head', [(i, (i + k) % n) for i in range(n)])]
    all_to_all x1, waiting for transfers between devices: 3.24 us -> 0.01 us  [body(): lax.all_to_all(outgoing, 'req', split_axis=0, concat_axis=0, tiled=True)]
    all_to_all x1, starting transfers between devices: 16.6 us -> 13.6 us  [body(): lax.all_to_all(outgoing, 'req', split_axis=0, concat_axis=0, tiled=True)]
    unnamed x129 -> x166, local copies, waits for them, and re-layouts: 19.2 us -> 22.1 us
  transfers between devices with their start and end apart: 5 -> 24, of which waited for: 5 -> 8; matrix products, arithmetic and copies ran while one was open for 3% -> 6% of each run, Pallas kernels for 0% -> 0%
where the time goes in v1:
time: 225 us; the launch traced here: 222 us
  starting transfers between devices  92.2 us (41%)
  matrix products  43.7 us (19%)
  local copies, waits for them, and re-layouts  42.1 us (19%)
  waiting for transfers between devices  25.8 us (11%)
  other arithmetic  16.4 us (7%)
    ppermute x12, starting transfers between devices, gather_heads(): lax.ppermute(block, 'head', [(i, (i + k) % n) for i in range(n)])  43.5 us
    unnamed x166, local copies, waits for them, and re-layouts  22.1 us
    dot_general x8, matrix products, sequence_recurrence(): jnp.einsum('rhij,rhj->rhi', states, acceptor_parts[:, position], precisio...  18.2 us
    ppermute x6, starting transfers between devices, scatter_heads(): lax.ppermute(chunk, 'head', [(i, (i + k) % n) for i in range(n)])  17 us
    dot_general x8, matrix products, sequence_recurrence(): jnp.einsum('rhij,rhj->rhi', states, normed[:, position], precision=highest)  16.7 us
    all_to_all x1, starting transfers between devices, body(): lax.all_to_all(outgoing, 'req', split_axis=0, concat_axis=0, tiled=True)  13.6 us
    all_to_all x1, starting transfers between devices, body(): lax.all_to_all(going_back, 'req', split_axis=0, concat_axis=0, tiled=True)  12.7 us
    all_to_all x1, waiting for transfers between devices, body(): lax.all_to_all(going_back, 'req', split_axis=0, concat_axis=0, tiled=True)  12.1 us
  transfers between devices with their start and end apart: 24, of which 8 were waited for; matrix products, arithmetic and copies ran while one was open for 6% of the time, Pallas kernels for 0%

profile of v1, /device:TPU:6, one launch (start us, length us, event | category | flops | bytes accessed | tf_op | source)
XLA Modules:
  0.0 221.8 jit_solution(14026913865218481864)
XLA Ops:
  0.0 2.9 %collective-permute-start.3 = (bf16[8,256]{1,0:T(8,128)(2,1)}, bf16[8,256]{1,0:T(8,128)(2,1)S(1)}, u32[]{:S(2)}, u32[]{:S(2)}) collective-permute-start(bf16[8,256]{1,0:T(8,128)(2,1)} %bitcast.565), channel_id=1, source_target_pairs={{0,3},{1,0},{2,1},{3,2},{4,7},{5,4},{6,5},{7,6},{8,11},{9,8},{10,9... | collective-permute-start | bytes 12296 | tf_op jit(solution)/shard_map/ppermute | solution.py:105
  2.9 8.4 %collective-permute-start.4 = (bf16[8,256]{1,0:T(8,128)(2,1)}, bf16[8,256]{1,0:T(8,128)(2,1)S(1)}, u32[]{:S(2)}, u32[]{:S(2)}) collective-permute-start(bf16[8,256]{1,0:T(8,128)(2,1)} %bitcast.566), channel_id=1, source_target_pairs={{0,2},{1,3},{2,0},{3,1},{4,6},{5,7},{6,4},{7,5},{8,10},{9,11},{10,... | collective-permute-start | bytes 12296 | tf_op jit(solution)/shard_map/ppermute | solution.py:105
  13.2 3.9 %collective-permute-start.6 = (bf16[256,96]{0,1:T(8,128)(2,1)}, bf16[256,96]{0,1:T(8,128)(2,1)S(1)}, u32[]{:S(2)}, u32[]{:S(2)}) collective-permute-start(bf16[256,96]{0,1:T(8,128)(2,1)} %bitcast.543), channel_id=1, source_target_pairs={{0,3},{1,0},{2,1},{3,2},{4,7},{5,4},{6,5},{7,6},{8,11},{9,8},{10,9... | collective-permute-start | bytes 147464 | tf_op jit(solution)/shard_map/ppermute | solution.py:105
  22.8 13.6 %all-to-all-start = ((bf16[64,4,256]{2,1,0:T(4,128)(2,1)}), bf16[64,4,256]{2,1,0:T(4,128)(2,1)S(1)}, u32[]{:S(2)}, u32[]{:S(2)}) async-start(bf16[64,4,256]{2,1,0:T(4,128)(2,1)} %scatter_fusion), calls=%async_computation | async-start | bytes 262144 | tf_op jit(solution)/shard_map/all_to_all | solution.py:284
  45.4 4.3 %collective-permute-start.8 = (bf16[256,96]{0,1:T(8,128)(2,1)S(1)}, bf16[256,96]{0,1:T(8,128)(2,1)S(1)}, u32[]{:S(2)}, u32[]{:S(2)}) collective-permute-start(bf16[256,96]{0,1:T(8,128)(2,1)S(1)} %bitcast.545), channel_id=1, source_target_pairs={{0,1},{1,2},{2,3},{3,0},{4,5},{5,6},{6,7},{7,4},{8,9},{9,10},{10,1... | collective-permute-start | bytes 147464 | tf_op jit(solution)/shard_map/ppermute | solution.py:105
  51.7 3.4 %collective-permute-start.10 = (bf16[256,96]{0,1:T(8,128)(2,1)S(1)}, bf16[256,96]{0,1:T(8,128)(2,1)S(1)}, u32[]{:S(2)}, u32[]{:S(2)}) collective-permute-start(bf16[256,96]{0,1:T(8,128)(2,1)S(1)} %bitcast.541), channel_id=1, source_target_pairs={{0,2},{1,3},{2,0},{3,1},{4,6},{5,7},{6,4},{7,5},{8,10},{9,11},{10,... | collective-permute-start | bytes 147464 | tf_op jit(solution)/shard_map/ppermute | solution.py:105
  55.1 4.5 %collective-permute-start.11 = (bf16[256,96]{0,1:T(8,128)(2,1)S(1)}, bf16[256,96]{0,1:T(8,128)(2,1)S(1)}, u32[]{:S(2)}, u32[]{:S(2)}) collective-permute-start(bf16[256,96]{0,1:T(8,128)(2,1)S(1)} %bitcast.542), channel_id=1, source_target_pairs={{0,1},{1,2},{2,3},{3,0},{4,5},{5,6},{6,7},{7,4},{8,9},{9,10},{10,1... | collective-permute-start | bytes 147464 | tf_op jit(solution)/shard_map/ppermute | solution.py:105
  59.7 2.0 collective-permute-done.11
  62.9 3.9 %collective-permute-start = (bf16[8,4,256]{2,0,1:T(8,128)(2,1)S(1)}, bf16[8,4,256]{2,0,1:T(8,128)(2,1)S(1)}, u32[]{:S(2)}, u32[]{:S(2)}) collective-permute-start(bf16[8,4,256]{2,0,1:T(8,128)(2,1)S(1)} %copy_select_fusion), channel_id=1, source_target_pairs={{0,3},{1,0},{2,1},{3,2},{4,7},{5,4},{6,5},{7,6},{8,11},{9,8},{10,9... | collective-permute-start | bytes 49160 | tf_op jit(solution)/shard_map/ppermute | solution.py:105
  66.8 4.5 %collective-permute-start.1 = (bf16[8,4,256]{2,0,1:T(8,128)(2,1)S(1)}, bf16[8,4,256]{2,0,1:T(8,128)(2,1)S(1)}, u32[]{:S(2)}, u32[]{:S(2)}) collective-permute-start(bf16[8,4,256]{2,0,1:T(8,128)(2,1)S(1)} %copy_select_fusion), channel_id=1, source_target_pairs={{0,2},{1,3},{2,0},{3,1},{4,6},{5,7},{6,4},{7,5},{8,10},{9,11},{10,... | collective-permute-start | bytes 49160 | tf_op jit(solution)/shard_map/ppermute | solution.py:105
  74.0 3.0 %collective-permute-done.2 = bf16[8,4,256]{2,0,1:T(8,128)(2,1)S(1)} collective-permute-done((bf16[8,4,256]{2,0,1:T(8,128)(2,1)S(1)}, bf16[8,4,256]{2,0,1:T(8,128)(2,1)S(1)}, u32[]{:S(2)}, u32[]{:S(2)}) %collective-permute-start.2) | collective-permute-done | bytes 16416 | tf_op jit(solution)/shard_map/ppermute | solution.py:105
  92.2 2.1 fusion.142
  95.0 2.1 fusion.162
  97.9 3.2 %fusion.59 = f32[8,4,1,64]{3,2,1,0:T(1,128)S(1)} fusion(f32[8,4,64]{2,1,0:T(4,128)S(1)} %copy-done.24, f32[8,4,64]{2,1,0:T(4,128)S(1)} %copy.261, f32[8,4,64]{2,1,0:T(4,128)S(1)} %copy-done.18, f32[8,4,64]{2,1,0:T(4,128)S(1)} %bitcast.552, f32[8,4,64]{2,1,0:T(4,128)S(1)} %get-tuple-element.71, f32[8,4,64,1]{2,0,1,3:T(8,128)S(1)} %get-tuple-element.68, ...), kind=kOutput, calls=%fused_computation.94 | convolution fusion | flops 2883584 | bytes 622592 | tf_op jit(solution)/shard_map/rhij,rhj->rhi/dot_general | solution.py:75
  101.8 2.8 %fusion.58 = f32[8,4,1,64]{3,2,1,0:T(1,128)S(1)} fusion(f32[8,4,64,1]{2,3,1,0:T(1,128)S(1)} %bitcast.568, f32[8,4,64]{2,1,0:T(4,128)S(1)} %copy-done.24, f32[8,4,64]{2,1,0:T(4,128)S(1)} %copy.261, f32[8,4,64]{2,1,0:T(4,128)S(1)} %copy-done.18, f32[8,4,64]{2,1,0:T(4,128)S(1)} %bitcast.553, f32[8,4,64]{2,1,0:T(4,128)S(1)} %get-tuple-element.71, ...), kind=kOutput, calls=%fused_computation.93 | convolution fusion | flops 2883584 | bytes 622592 | tf_op jit(solution)/shard_map/rhij,rhj->rhi/dot_general | solution.py:58
  112.3 2.1 fusion.34
  120.0 3.2 %collective-permute-start.12 = (f32[32,256]{1,0:T(8,128)}, f32[32,256]{1,0:T(8,128)}, u32[]{:S(2)}, u32[]{:S(2)}) collective-permute-start(f32[32,256]{1,0:T(8,128)} %get-tuple-element.33), channel_id=1, source_target_pairs={{0,1},{1,2},{2,3},{3,0},{4,5},{5,6},{6,7},{7,4},{8,9},{9,10},{10,1... | collective-permute-start | bytes 98312 | tf_op jit(solution)/shard_map/ppermute | solution.py:121
  123.2 2.4 %collective-permute-start.13 = (f32[32,256]{1,0:T(8,128)}, f32[32,256]{1,0:T(8,128)}, u32[]{:S(2)}, u32[]{:S(2)}) collective-permute-start(f32[32,256]{1,0:T(8,128)} %get-tuple-element.35), channel_id=1, source_target_pairs={{0,2},{1,3},{2,0},{3,1},{4,6},{5,7},{6,4},{7,5},{8,10},{9,11},{10,... | collective-permute-start | bytes 98312 | tf_op jit(solution)/shard_map/ppermute | solution.py:121
  125.6 2.4 %collective-permute-start.14 = (f32[32,256]{1,0:T(8,128)}, f32[32,256]{1,0:T(8,128)}, u32[]{:S(2)}, u32[]{:S(2)}) collective-permute-start(f32[32,256]{1,0:T(8,128)} %get-tuple-element.34), channel_id=1, source_target_pairs={{0,3},{1,0},{2,1},{3,2},{4,7},{5,4},{6,5},{7,6},{8,11},{9,8},{10,9... | collective-permute-start | bytes 98312 | tf_op jit(solution)/shard_map/ppermute | solution.py:121
  128.1 2.7 %collective-permute-done.13 = f32[32,256]{1,0:T(8,128)} collective-permute-done((f32[32,256]{1,0:T(8,128)}, f32[32,256]{1,0:T(8,128)}, u32[]{:S(2)}, u32[]{:S(2)}) %collective-permute-start.13) | collective-permute-done | bytes 32800 | tf_op jit(solution)/shard_map/ppermute | solution.py:121
  130.8 2.1 collective-permute-done.14
  157.8 2.1 fusion.136
  159.9 2.1 fusion.157
  162.7 3.2 %fusion.61 = f32[8,4,1,64]{3,2,1,0:T(1,128)S(1)} fusion(f32[8,4,64]{2,1,0:T(4,128)S(1)} %get-tuple-element.63, f32[8,4,64]{2,1,0:T(4,128)S(1)} %copy.283, f32[8,4,64]{2,1,0:T(4,128)S(1)} %get-tuple-element.31, f32[8,4,64]{2,1,0:T(4,128)S(1)} %bitcast.555, f32[8,4,64]{2,1,0:T(4,128)S(1)} %copy-done.20, f32[8,4,64,1]{2,0,1,3:T(8,128)S(1)} %get-tuple-element.48, ...), kind=kOutput, calls=%fused_computation.96 | convolution fusion | flops 2883584 | bytes 622592 | tf_op jit(solution)/shard_map/rhij,rhj->rhi/dot_general | solution.py:75
  165.9 2.8 %fusion.60 = f32[8,4,1,64]{3,2,1,0:T(1,128)S(1)} fusion(f32[8,4,64,1]{2,3,1,0:T(1,128)S(1)} %bitcast.570, f32[8,4,64]{2,1,0:T(4,128)S(1)} %get-tuple-element.63, f32[8,4,64]{2,1,0:T(4,128)S(1)} %copy.283, f32[8,4,64]{2,1,0:T(4,128)S(1)} %get-tuple-element.31, f32[8,4,64]{2,1,0:T(4,128)S(1)} %bitcast.556, f32[8,4,64]{2,1,0:T(4,128)S(1)} %copy-done.20, ...), kind=kOutput, calls=%fused_computation.95 | convolution fusion | flops 2883584 | bytes 622592 | tf_op jit(solution)/shard_map/rhij,rhj->rhi/dot_general | solution.py:58
  168.7 2.0 multiply_add_fusion
  175.0 2.1 fusion.28
  178.7 3.6 %collective-permute-start.19 = (f32[32,256]{1,0:T(8,128)S(1)}, f32[32,256]{1,0:T(8,128)S(1)}, u32[]{:S(2)}, u32[]{:S(2)}) collective-permute-start(f32[32,256]{1,0:T(8,128)S(1)} %get-tuple-element.26), channel_id=1, source_target_pairs={{0,1},{1,2},{2,3},{3,0},{4,5},{5,6},{6,7},{7,4},{8,9},{9,10},{10,1... | collective-permute-start | bytes 98312 | tf_op jit(solution)/shard_map/ppermute | solution.py:121
  182.3 2.0 collective-permute-start.20
  184.4 3.3 %collective-permute-start.21 = (f32[32,256]{1,0:T(8,128)S(1)}, f32[32,256]{1,0:T(8,128)S(1)}, u32[]{:S(2)}, u32[]{:S(2)}) collective-permute-start(f32[32,256]{1,0:T(8,128)S(1)} %get-tuple-element.27), channel_id=1, source_target_pairs={{0,3},{1,0},{2,1},{3,2},{4,7},{5,4},{6,5},{7,6},{8,11},{9,8},{10,9... | collective-permute-start | bytes 98312 | tf_op jit(solution)/shard_map/ppermute | solution.py:121
  195.0 12.7 %all-to-all-start.1 = ((bf16[64,4,256]{2,1,0:T(4,128)(2,1)}), bf16[64,4,256]{2,1,0:T(4,128)(2,1)S(1)}, u32[]{:S(2)}, u32[]{:S(2)}) async-start(bf16[64,4,256]{2,1,0:T(4,128)(2,1)} %scatter_fusion.1), calls=%async_computation.1 | async-start | bytes 262144 | tf_op jit(solution)/shard_map/all_to_all | solution.py:290
  208.4 12.1 %all-to-all-done.1 = bf16[64,4,256]{2,1,0:T(4,128)(2,1)S(1)} async-done(((bf16[64,4,256]{2,1,0:T(4,128)(2,1)}), bf16[64,4,256]{2,1,0:T(4,128)(2,1)S(1)}, u32[]{:S(2)}, u32[]{:S(2)}) %all-to-all-start.1) | async-done | bytes 131104 | tf_op jit(solution)/shard_map/all_to_all | solution.py:290
  (336 shorter events, 92.6 us)
Async XLA Ops:
  0.0 117.8 %copy-start = (bf16[1,256,1024]{2,1,0:T(8,128)(2,1)S(1)}, bf16[1,256,1024]{2,1,0:T(8,128)(2,1)}, u32[]{:S(2)}) copy-start(bf16[1,256,1024]{2,1,0:T(8,128)(2,1)} %param.36) | copy-start | bytes 1572868
  0.0 39.4 %copy-start.3 = (bf16[1,1024,256]{2,1,0:T(8,128)(2,1)S(1)}, bf16[1,1024,256]{2,1,0:T(8,128)(2,1)}, u32[]{:S(2)}) copy-start(bf16[1,1024,256]{2,1,0:T(8,128)(2,1)} %param.35) | copy-start | bytes 1572868
  0.0 45.4 %collective-permute-start.3 = (bf16[8,256]{1,0:T(8,128)(2,1)}, bf16[8,256]{1,0:T(8,128)(2,1)S(1)}, u32[]{:S(2)}, u32[]{:S(2)}) collective-permute-start(bf16[8,256]{1,0:T(8,128)(2,1)} %bitcast.565), channel_id=1, source_target_pairs={{0,3},{1,0},{2,1},{3,2},{4,7},{5,4},{6,5},{7,6},{8,11},{9,8},{10,9... | collective-permute-start | bytes 12296 | tf_op jit(solution)/shard_map/ppermute | solution.py:105
  2.9 46.8 %collective-permute-start.4 = (bf16[8,256]{1,0:T(8,128)(2,1)}, bf16[8,256]{1,0:T(8,128)(2,1)S(1)}, u32[]{:S(2)}, u32[]{:S(2)}) collective-permute-start(bf16[8,256]{1,0:T(8,128)(2,1)} %bitcast.566), channel_id=1, source_target_pairs={{0,2},{1,3},{2,0},{3,1},{4,6},{5,7},{6,4},{7,5},{8,10},{9,11},{10,... | collective-permute-start | bytes 12296 | tf_op jit(solution)/shard_map/ppermute | solution.py:105
  11.3 40.4 %collective-permute-start.5 = (bf16[8,256]{1,0:T(8,128)(2,1)}, bf16[8,256]{1,0:T(8,128)(2,1)S(1)}, u32[]{:S(2)}, u32[]{:S(2)}) collective-permute-start(bf16[8,256]{1,0:T(8,128)(2,1)} %bitcast.567), channel_id=1, source_target_pairs={{0,1},{1,2},{2,3},{3,0},{4,5},{5,6},{6,7},{7,4},{8,9},{9,10},{10,1... | collective-permute-start | bytes 12296 | tf_op jit(solution)/shard_map/ppermute | solution.py:105
  13.2 41.9 %collective-permute-start.6 = (bf16[256,96]{0,1:T(8,128)(2,1)}, bf16[256,96]{0,1:T(8,128)(2,1)S(1)}, u32[]{:S(2)}, u32[]{:S(2)}) collective-permute-start(bf16[256,96]{0,1:T(8,128)(2,1)} %bitcast.543), channel_id=1, source_target_pairs={{0,3},{1,0},{2,1},{3,2},{4,7},{5,4},{6,5},{7,6},{8,11},{9,8},{10,9... | collective-permute-start | bytes 147464 | tf_op jit(solution)/shard_map/ppermute | solution.py:105
  17.1 42.5 %collective-permute-start.7 = (bf16[256,96]{0,1:T(8,128)(2,1)}, bf16[256,96]{0,1:T(8,128)(2,1)S(1)}, u32[]{:S(2)}, u32[]{:S(2)}) collective-permute-start(bf16[256,96]{0,1:T(8,128)(2,1)} %bitcast.544), channel_id=1, source_target_pairs={{0,2},{1,3},{2,0},{3,1},{4,6},{5,7},{6,4},{7,5},{8,10},{9,11},{10,... | collective-permute-start | bytes 147464 | tf_op jit(solution)/shard_map/ppermute | solution.py:105
  22.8 39.5 %all-to-all-start = ((bf16[64,4,256]{2,1,0:T(4,128)(2,1)}), bf16[64,4,256]{2,1,0:T(4,128)(2,1)S(1)}, u32[]{:S(2)}, u32[]{:S(2)}) async-start(bf16[64,4,256]{2,1,0:T(4,128)(2,1)} %scatter_fusion), calls=%async_computation | async-start | bytes 262144 | tf_op jit(solution)/shard_map/all_to_all | solution.py:284
  39.1 34.2 %copy-start.50 = (pred[8]{0:T(512)(128)(4,1)}, pred[8]{0:T(512)(128)(4,1)S(1)}, u32[]{:S(2)}) copy-start(pred[8]{0:T(512)(128)(4,1)S(1)} %get-tuple-element.17) | copy-start | bytes 28
  39.3 37.8 %copy-start.33 = (f32[4,256]{1,0:T(4,128)}, f32[4,256]{1,0:T(4,128)S(1)}, u32[]{:S(2)}) copy-start(f32[4,256]{1,0:T(4,128)S(1)} %mul.332) | copy-start | bytes 12292
  39.3 37.8 %copy-start.35 = (f32[4,256]{1,0:T(4,128)}, f32[4,256]{1,0:T(4,128)S(1)}, u32[]{:S(2)}) copy-start(f32[4,256]{1,0:T(4,128)S(1)} %mul.338) | copy-start | bytes 12292
  39.3 37.8 %copy-start.37 = (f32[4,256]{1,0:T(4,128)}, f32[4,256]{1,0:T(4,128)S(1)}, u32[]{:S(2)}) copy-start(f32[4,256]{1,0:T(4,128)S(1)} %mul.345) | copy-start | bytes 12292
  39.4 37.8 %copy-start.39 = (f32[4,256]{1,0:T(4,128)}, f32[4,256]{1,0:T(4,128)S(1)}, u32[]{:S(2)}) copy-start(f32[4,256]{1,0:T(4,128)S(1)} %mul.349) | copy-start | bytes 12292
  39.4 37.8 %copy-start.41 = (f32[4,256]{1,0:T(4,128)}, f32[4,256]{1,0:T(4,128)S(1)}, u32[]{:S(2)}) copy-start(f32[4,256]{1,0:T(4,128)S(1)} %mul.356) | copy-start | bytes 12292
  45.4 14.3 %collective-permute-start.8 = (bf16[256,96]{0,1:T(8,128)(2,1)S(1)}, bf16[256,96]{0,1:T(8,128)(2,1)S(1)}, u32[]{:S(2)}, u32[]{:S(2)}) collective-permute-start(bf16[256,96]{0,1:T(8,128)(2,1)S(1)} %bitcast.545), channel_id=1, source_target_pairs={{0,1},{1,2},{2,3},{3,0},{4,5},{5,6},{6,7},{7,4},{8,9},{9,10},{10,1... | collective-permute-start | bytes 147464 | tf_op jit(solution)/shard_map/ppermute | solution.py:105
  49.7 10.0 %collective-permute-start.9 = (bf16[256,96]{0,1:T(8,128)(2,1)S(1)}, bf16[256,96]{0,1:T(8,128)(2,1)S(1)}, u32[]{:S(2)}, u32[]{:S(2)}) collective-permute-start(bf16[256,96]{0,1:T(8,128)(2,1)S(1)} %bitcast.540), channel_id=1, source_target_pairs={{0,3},{1,0},{2,1},{3,2},{4,7},{5,4},{6,5},{7,6},{8,11},{9,8},{10,9... | collective-permute-start | bytes 147464 | tf_op jit(solution)/shard_map/ppermute | solution.py:105
  51.7 8.0 %collective-permute-start.10 = (bf16[256,96]{0,1:T(8,128)(2,1)S(1)}, bf16[256,96]{0,1:T(8,128)(2,1)S(1)}, u32[]{:S(2)}, u32[]{:S(2)}) collective-permute-start(bf16[256,96]{0,1:T(8,128)(2,1)S(1)} %bitcast.541), channel_id=1, source_target_pairs={{0,2},{1,3},{2,0},{3,1},{4,6},{5,7},{6,4},{7,5},{8,10},{9,11},{10,... | collective-permute-start | bytes 147464 | tf_op jit(solution)/shard_map/ppermute | solution.py:105
  55.1 6.6 %collective-permute-start.11 = (bf16[256,96]{0,1:T(8,128)(2,1)S(1)}, bf16[256,96]{0,1:T(8,128)(2,1)S(1)}, u32[]{:S(2)}, u32[]{:S(2)}) collective-permute-start(bf16[256,96]{0,1:T(8,128)(2,1)S(1)} %bitcast.542), channel_id=1, source_target_pairs={{0,1},{1,2},{2,3},{3,0},{4,5},{5,6},{6,7},{7,4},{8,9},{9,10},{10,1... | collective-permute-start | bytes 147464 | tf_op jit(solution)/shard_map/ppermute | solution.py:105
  62.9 10.5 %collective-permute-start = (bf16[8,4,256]{2,0,1:T(8,128)(2,1)S(1)}, bf16[8,4,256]{2,0,1:T(8,128)(2,1)S(1)}, u32[]{:S(2)}, u32[]{:S(2)}) collective-permute-start(bf16[8,4,256]{2,0,1:T(8,128)(2,1)S(1)} %copy_select_fusion), channel_id=1, source_target_pairs={{0,3},{1,0},{2,1},{3,2},{4,7},{5,4},{6,5},{7,6},{8,11},{9,8},{10,9... | collective-permute-start | bytes 49160 | tf_op jit(solution)/shard_map/ppermute | solution.py:105
  66.8 7.1 %collective-permute-start.1 = (bf16[8,4,256]{2,0,1:T(8,128)(2,1)S(1)}, bf16[8,4,256]{2,0,1:T(8,128)(2,1)S(1)}, u32[]{:S(2)}, u32[]{:S(2)}) collective-permute-start(bf16[8,4,256]{2,0,1:T(8,128)(2,1)S(1)} %copy_select_fusion), channel_id=1, source_target_pairs={{0,2},{1,3},{2,0},{3,1},{4,6},{5,7},{6,4},{7,5},{8,10},{9,11},{10,... | collective-permute-start | bytes 49160 | tf_op jit(solution)/shard_map/ppermute | solution.py:105
  71.4 5.6 %collective-permute-start.2 = (bf16[8,4,256]{2,0,1:T(8,128)(2,1)S(1)}, bf16[8,4,256]{2,0,1:T(8,128)(2,1)S(1)}, u32[]{:S(2)}, u32[]{:S(2)}) collective-permute-start(bf16[8,4,256]{2,0,1:T(8,128)(2,1)S(1)} %copy_select_fusion), channel_id=1, source_target_pairs={{0,1},{1,2},{2,3},{3,0},{4,5},{5,6},{6,7},{7,4},{8,9},{9,10},{10,1... | collective-permute-start | bytes 49160 | tf_op jit(solution)/shard_map/ppermute | solution.py:105
  120.0 8.1 %collective-permute-start.12 = (f32[32,256]{1,0:T(8,128)}, f32[32,256]{1,0:T(8,128)}, u32[]{:S(2)}, u32[]{:S(2)}) collective-permute-start(f32[32,256]{1,0:T(8,128)} %get-tuple-element.33), channel_id=1, source_target_pairs={{0,1},{1,2},{2,3},{3,0},{4,5},{5,6},{6,7},{7,4},{8,9},{9,10},{10,1... | collective-permute-start | bytes 98312 | tf_op jit(solution)/shard_map/ppermute | solution.py:121
  123.2 7.6 %collective-permute-start.13 = (f32[32,256]{1,0:T(8,128)}, f32[32,256]{1,0:T(8,128)}, u32[]{:S(2)}, u32[]{:S(2)}) collective-permute-start(f32[32,256]{1,0:T(8,128)} %get-tuple-element.35), channel_id=1, source_target_pairs={{0,2},{1,3},{2,0},{3,1},{4,6},{5,7},{6,4},{7,5},{8,10},{9,11},{10,... | collective-permute-start | bytes 98312 | tf_op jit(solution)/shard_map/ppermute | solution.py:121
  125.6 7.3 %collective-permute-start.14 = (f32[32,256]{1,0:T(8,128)}, f32[32,256]{1,0:T(8,128)}, u32[]{:S(2)}, u32[]{:S(2)}) collective-permute-start(f32[32,256]{1,0:T(8,128)} %get-tuple-element.34), channel_id=1, source_target_pairs={{0,3},{1,0},{2,1},{3,2},{4,7},{5,4},{6,5},{7,6},{8,11},{9,8},{10,9... | collective-permute-start | bytes 98312 | tf_op jit(solution)/shard_map/ppermute | solution.py:121
  136.6 6.0 %collective-permute-start.16 = (bf16[8,4,256]{2,0,1:T(8,128)(2,1)S(1)}, bf16[8,4,256]{2,0,1:T(8,128)(2,1)S(1)}, u32[]{:S(2)}, u32[]{:S(2)}) collective-permute-start(bf16[8,4,256]{2,0,1:T(8,128)(2,1)S(1)} %fusion.114), channel_id=1, source_target_pairs={{0,259},{1,256},{2,257},{3,258},{4,263},{5,260},{6,261},{7,262},{8... | collective-permute-start | bytes 49160 | tf_op jit(solution)/shard_map/ppermute | solution.py:131
  137.9 4.7 %collective-permute-start.17 = (bf16[8,4,256]{2,0,1:T(8,128)(2,1)S(1)}, bf16[8,4,256]{2,0,1:T(8,128)(2,1)S(1)}, u32[]{:S(2)}, u32[]{:S(2)}) collective-permute-start(bf16[8,4,256]{2,0,1:T(8,128)(2,1)S(1)} %fusion.114), channel_id=1, source_target_pairs={{0,258},{1,259},{2,256},{3,257},{4,262},{5,263},{6,260},{7,261},{8... | collective-permute-start | bytes 49160 | tf_op jit(solution)/shard_map/ppermute | solution.py:131
  139.2 3.4 %collective-permute-start.18 = (bf16[8,4,256]{2,0,1:T(8,128)(2,1)S(1)}, bf16[8,4,256]{2,0,1:T(8,128)(2,1)S(1)}, u32[]{:S(2)}, u32[]{:S(2)}) collective-permute-start(bf16[8,4,256]{2,0,1:T(8,128)(2,1)S(1)} %fusion.114), channel_id=1, source_target_pairs={{0,257},{1,258},{2,259},{3,256},{4,261},{5,262},{6,263},{7,260},{8... | collective-permute-start | bytes 49160 | tf_op jit(solution)/shard_map/ppermute | solution.py:131
  140.5 2.1 collective-permute-start.15
  178.7 9.7 %collective-permute-start.19 = (f32[32,256]{1,0:T(8,128)S(1)}, f32[32,256]{1,0:T(8,128)S(1)}, u32[]{:S(2)}, u32[]{:S(2)}) collective-permute-start(f32[32,256]{1,0:T(8,128)S(1)} %get-tuple-element.26), channel_id=1, source_target_pairs={{0,1},{1,2},{2,3},{3,0},{4,5},{5,6},{6,7},{7,4},{8,9},{9,10},{10,1... | collective-permute-start | bytes 98312 | tf_op jit(solution)/shard_map/ppermute | solution.py:121
  182.3 7.4 %collective-permute-start.20 = (f32[32,256]{1,0:T(8,128)S(1)}, f32[32,256]{1,0:T(8,128)S(1)}, u32[]{:S(2)}, u32[]{:S(2)}) collective-permute-start(f32[32,256]{1,0:T(8,128)S(1)} %get-tuple-element.28), channel_id=1, source_target_pairs={{0,2},{1,3},{2,0},{3,1},{4,6},{5,7},{6,4},{7,5},{8,10},{9,11},{10,... | collective-permute-start | bytes 98312 | tf_op jit(solution)/shard_map/ppermute | solution.py:121
  184.4 7.3 %collective-permute-start.21 = (f32[32,256]{1,0:T(8,128)S(1)}, f32[32,256]{1,0:T(8,128)S(1)}, u32[]{:S(2)}, u32[]{:S(2)}) collective-permute-start(f32[32,256]{1,0:T(8,128)S(1)} %get-tuple-element.27), channel_id=1, source_target_pairs={{0,3},{1,0},{2,1},{3,2},{4,7},{5,4},{6,5},{7,6},{8,11},{9,8},{10,9... | collective-permute-start | bytes 98312 | tf_op jit(solution)/shard_map/ppermute | solution.py:121
  195.0 25.5 %all-to-all-start.1 = ((bf16[64,4,256]{2,1,0:T(4,128)(2,1)}), bf16[64,4,256]{2,1,0:T(4,128)(2,1)S(1)}, u32[]{:S(2)}, u32[]{:S(2)}) async-start(bf16[64,4,256]{2,1,0:T(4,128)(2,1)} %scatter_fusion.1), calls=%async_computation.1 | async-start | bytes 262144 | tf_op jit(solution)/shard_map/all_to_all | solution.py:290
  (67 other events, 127.7 us)

commit v2 on v1

--- a/solution.py
+++ b/solution.py
@@ -1,9 +1,35 @@
 import jax
 import jax.numpy as jnp
 from jax import lax
+from jax.experimental import pallas as pl
+from jax.experimental.pallas import tpu as pltpu
 from jax.sharding import PartitionSpec as P
 
 highest = lax.Precision.HIGHEST
+
+
+def recurrence_kernel(memory_ref, vector_ref, content_ref, read_ref):
+    states = memory_ref[...]
+    for position in range(vector_ref.shape[0]):
+        decay = vector_ref[position, 0]
+        normed = vector_ref[position, 1]
+        normed_learn = vector_ref[position, 2]
+        erasing = vector_ref[position, 3]
+        acceptor = vector_ref[position, 4]
+        pulled = jnp.sum(states * normed, axis=-1, keepdims=True)
+        states = states * decay - pulled * normed_learn + content_ref[position] * erasing
+        read_ref[position] = jnp.sum(states * acceptor, axis=-1, keepdims=True)
+
+
+def run_recurrence(starting_memory, vectors, content):
+    steps = vectors.shape[0]
+    blocks, span, _ = starting_memory.shape
+    return pl.pallas_call(
+        recurrence_kernel,
+        out_shape=jax.ShapeDtypeStruct((steps, blocks, span, 1), jnp.float32),
+        in_specs=[pl.BlockSpec(memory_space=pltpu.VMEM)] * 3,
+        out_specs=pl.BlockSpec(memory_space=pltpu.VMEM),
+    )(starting_memory, vectors, content)
 
 
 def sequence_recurrence(
@@ -52,29 +78,34 @@
     erasing_address = to_heads(address_entries * (1.0 + (learning - 1.0) * address_rate_coupling))
     acceptor_parts = to_heads(acceptor_entries)
     content_part_lines = to_heads(content_entries)
-    states = starting_memory
-    readout = []
-    for position in range(acceptor_parts.shape[1]):
-        pulled = jnp.einsum("rhij,rhj->rhi", states, normed[:, position], precision=highest)
-        states = (
-            states * decays[:, position][:, :, None, :]
-            - jnp.einsum(
-                "rhi,rhj->rhij",
-                pulled,
-                normed[:, position] * learn_heads[:, position],
-                precision=highest,
-            )
-            + jnp.einsum(
-                "rhi,rhj->rhij",
-                content_part_lines[:, position],
-                erasing_address[:, position],
-                precision=highest,
-            )
+    steps_count = acceptor_parts.shape[1]
+
+    def by_step(array_in):
+        return jnp.transpose(array_in, (1, 0, 2, 3)).reshape(
+            steps_count, batch_rows * stored_memory_parts, 1, subspace_span
         )
-        readout.append(
-            jnp.einsum("rhij,rhj->rhi", states, acceptor_parts[:, position], precision=highest)
-        )
-    read_all = jnp.stack(readout, axis=1)
+
+    vectors = jnp.stack(
+        [
+            by_step(decays),
+            by_step(normed),
+            by_step(normed * learn_heads),
+            by_step(erasing_address),
+            by_step(acceptor_parts),
+        ],
+        axis=1,
+    )
+    content = by_step(content_part_lines).reshape(
+        steps_count, batch_rows * stored_memory_parts, subspace_span, 1
+    )
+    read = run_recurrence(
+        starting_memory.reshape(batch_rows * stored_memory_parts, subspace_span, subspace_span),
+        vectors,
+        content,
+    )
+    read_all = jnp.transpose(
+        read.reshape(steps_count, batch_rows, stored_memory_parts, subspace_span), (1, 0, 2, 3)
+    )
     center = read_all - jnp.mean(read_all, axis=-1, keepdims=True)
     variance = jnp.mean(center * center, axis=-1, keepdims=True)
     gain_heads = section_standard_gains.reshape(stored_memory_parts, subspace_span)
@@ -190,10 +221,24 @@
     return jnp.dot(lagged_features, params[4], preferred_element_type=jnp.float32)
 
 
+def gather_start(last_use, fading_first, adapt_first):
+    n = lax.axis_size("head")
+    packed = jnp.concatenate([fading_first.reshape(-1), adapt_first.reshape(-1), last_use.reshape(-1)])
+    whole = gather_heads(packed, 0).reshape(n, -1)
+    first_size = fading_first.size
+    fading_full = whole[:, :first_size].reshape((n * fading_first.shape[0],) + fading_first.shape[1:])
+    adapt_full = whole[:, first_size : 2 * first_size].reshape(fading_full.shape)
+    prev_full = jnp.transpose(
+        whole[:, 2 * first_size :].reshape((n,) + last_use.shape), (1, 0, 2)
+    ).reshape(last_use.shape[0], n * last_use.shape[1])
+    return prev_full, fading_full, adapt_full
+
+
 def run_sections(inputs, states_use, last_use, params):
     section_num = lax.axis_index("section")
     batch_rows, steps_count, shard_width = inputs.shape
-    full_prev = gather_heads(last_use, 1)
+    full_prev, fading_full, adapt_full = gather_start(last_use, params[5], params[7])
+    params = params[:5] + (fading_full, params[6], adapt_full) + params[8:]
     full_first = gather_heads(inputs, 2)
     partial_first = layer_partial(full_first, full_prev, states_use, params)
     own_first = scatter_heads(partial_first).reshape(batch_rows, steps_count, shard_width)
@@ -262,9 +307,9 @@
         address_projection[0],
         content_projection[0],
         readout_projection[0],
-        gather_heads(fading_first_lowrank[0], 0),
+        fading_first_lowrank[0],
         fading_second_lowrank[0],
-        gather_heads(adapt_first_lowrank[0], 0),
+        adapt_first_lowrank[0],
         adapt_second_lowrank[0],
         fading_baseline[0],
         adapt_baseline[0],

time: 225 us -> 170 us (0.76)
  matrix products: 43.7 us -> 3.37 us
  starting transfers between devices: 92.2 us -> 74.5 us
  Pallas kernels: 0 us -> 16.1 us
  local copies, waits for them, and re-layouts: 42.1 us -> 34.4 us
  waiting for transfers between devices: 25.8 us -> 22 us
    dot_general x16 -> x0, matrix products: 34.9 us -> none  [the longest x8 18.2 us: sequence_recurrence(): jnp.einsum('rhij,rhj->rhi', states, acceptor_parts[:, position], precisio...]
    ppermute x12 -> x6, starting transfers between devices: 43.5 us -> 23.7 us  [gather_heads(): lax.ppermute(block, 'head', [(i, (i + k) % n) for i in range(n)])]
    pallas_call x0 -> x2, Pallas kernels: none -> 16.1 us  [run_recurrence(): pl.pallas_call(recurrence_kernel, out_shape=jax.ShapeDtypeStruct((steps,...]
    unnamed x166 -> x89, local copies, waits for them, and re-layouts: 22.1 us -> 7.97 us
    pallas_call x0 -> x2, other arithmetic: none -> 6.7 us  [run_recurrence(): pl.pallas_call(recurrence_kernel, out_shape=jax.ShapeDtypeStruct((steps,...]
    concatenate x1, local copies, waits for them, and re-layouts: 0.01 us -> 6.38 us  [gather_heads(): ordered = jnp.roll(stacked, me + 1, axis=0)]
    another operation x2 -> x12, local copies, waits for them, and re-layouts: 1.38 us -> 7.55 us  [the longest x2 5.44 us: sequence_recurrence(): by_step(content_part_lines)]
    ppermute x12 -> x6, waiting for transfers between devices: 5.62 us -> 1.17 us  [gather_heads(): lax.ppermute(block, 'head', [(i, (i + k) % n) for i in range(n)])]
  transfers between devices with their start and end apart: 24 -> 18, of which waited for: 8 -> 6; matrix products, arithmetic and copies ran while one was open for 6% -> 15% of each run, Pallas kernels for 0% -> 0%
where the time goes in v2:
time: 170 us; the launch traced here: 168 us
  starting transfers between devices  74.5 us (44%)
  local copies, waits for them, and re-layouts  34.4 us (20%)
  waiting for transfers between devices  22 us (13%)
  other arithmetic  16.7 us (10%)
  Pallas kernels  16.1 us (9%)
  matrix products  3.37 us (2%)
    ppermute x6, starting transfers between devices, gather_heads(): lax.ppermute(block, 'head', [(i, (i + k) % n) for i in range(n)])  23.7 us
    ppermute x6, starting transfers between devices, scatter_heads(): lax.ppermute(chunk, 'head', [(i, (i + k) % n) for i in range(n)])  19.4 us
    pallas_call x2, Pallas kernels, run_recurrence(): pl.pallas_call(recurrence_kernel, out_shape=jax.ShapeDtypeStruct((steps,...  16.1 us
    all_to_all x1, starting transfers between devices, body(): lax.all_to_all(outgoing, 'req', split_axis=0, concat_axis=0, tiled=True)  13.3 us
    all_to_all x1, starting transfers between devices, body(): lax.all_to_all(going_back, 'req', split_axis=0, concat_axis=0, tiled=True)  12.7 us
    all_to_all x1, waiting for transfers between devices, body(): lax.all_to_all(going_back, 'req', split_axis=0, concat_axis=0, tiled=True)  12.7 us
    unnamed x89, local copies, waits for them, and re-layouts  7.97 us
    ppermute x6, waiting for transfers between devices, scatter_heads(): lax.ppermute(chunk, 'head', [(i, (i + k) % n) for i in range(n)])  7.62 us
  transfers between devices with their start and end apart: 18, of which 6 were waited for; matrix products, arithmetic and copies ran while one was open for 15% of the time, Pallas kernels for 0%

profile of v2, /device:TPU:6, one launch (start us, length us, event | category | flops | bytes accessed | tf_op | source)
XLA Modules:
  0.0 168.5 jit_solution(10246842124834782226)
XLA Ops:
  2.9 2.7 %collective-permute-start.3 = (bf16[51200]{0:T(1024)(128)(2,1)S(1)}, bf16[51200]{0:T(1024)(128)(2,1)S(1)}, u32[]{:S(2)}, u32[]{:S(2)}) collective-permute-start(bf16[51200]{0:T(1024)(128)(2,1)S(1)} %constant_dynamic-update-slice_fusion.11), channel_id=1, source_target_pairs={{0,3},{1,0},{2,1},{3,2},{4,7},{5,4},{6,5},{7,6},{8,11},{9,8},{10,9... | collective-permute-start | bytes 307208 | tf_op jit(solution)/shard_map/ppermute | solution.py:136
  5.7 8.4 %collective-permute-start.4 = (bf16[51200]{0:T(1024)(128)(2,1)S(1)}, bf16[51200]{0:T(1024)(128)(2,1)S(1)}, u32[]{:S(2)}, u32[]{:S(2)}) collective-permute-start(bf16[51200]{0:T(1024)(128)(2,1)S(1)} %constant_dynamic-update-slice_fusion.11), channel_id=1, source_target_pairs={{0,2},{1,3},{2,0},{3,1},{4,6},{5,7},{6,4},{7,5},{8,10},{9,11},{10,... | collective-permute-start | bytes 307208 | tf_op jit(solution)/shard_map/ppermute | solution.py:136
  14.1 1.9 %collective-permute-start.5 = (bf16[51200]{0:T(1024)(128)(2,1)S(1)}, bf16[51200]{0:T(1024)(128)(2,1)S(1)}, u32[]{:S(2)}, u32[]{:S(2)}) collective-permute-start(bf16[51200]{0:T(1024)(128)(2,1)S(1)} %constant_dynamic-update-slice_fusion.11), channel_id=1, source_target_pairs={{0,1},{1,2},{2,3},{3,0},{4,5},{5,6},{6,7},{7,4},{8,9},{9,10},{10,1... | collective-permute-start | bytes 307208 | tf_op jit(solution)/shard_map/ppermute | solution.py:136
  17.7 2.0 %scatter_fusion = bf16[64,4,256]{2,1,0:T(4,128)(2,1)} fusion(bf16[64,4,256]{2,1,0:T(4,128)(2,1)} %broadcast.445.clone, s32[8]{0:T(128)S(1)} %fusion.82, bf16[8,4,256]{2,1,0:T(4,128)(2,1)} %param.25), kind=kCustom, calls=%fused_computation.3 | custom fusion | bytes 49184 | tf_op jit(solution)/shard_map/scatter | solution.py:327
  19.7 13.3 %all-to-all-start = ((bf16[64,4,256]{2,1,0:T(4,128)(2,1)}), bf16[64,4,256]{2,1,0:T(4,128)(2,1)S(1)}, u32[]{:S(2)}, u32[]{:S(2)}) async-start(bf16[64,4,256]{2,1,0:T(4,128)(2,1)} %scatter_fusion), calls=%async_computation | async-start | bytes 262144 | tf_op jit(solution)/shard_map/all_to_all | solution.py:329
  38.7 1.3 reduce.31
  40.7 1.3 reduce.32
  42.7 1.3 reduce.33
  45.9 6.4 %concatenate.30 = bf16[8,51200]{1,0:T(8,128)(2,1)} concatenate(bf16[1,51200]{1,0:T(2,128)(2,1)S(1)} %stack.54, bf16[1,51200]{1,0:T(2,128)(2,1)S(1)} %stack.55, bf16[1,51200]{1,0:T(2,128)(2,1)S(1)} %stack.56, bf16[1,51200]{1,0:T(2,128)(2,1)S(1)} %stack.57, bf16[1,51200]{1,0:T(2,128)(2,1)S(1)} %stack.54, bf16[1,51200]{1,0:T(2,128)(2,1)S(1)} %stack.55, bf16[1,51200]{1,0:T(2,128)(2,1)S(1)} %stack.56, ...), dimensions={0} | concatenate | bytes 1638400 | tf_op jit(solution)/shard_map/jit(_roll_dynamic)/concatenate | solution.py:138
  52.3 1.4 fusion.87
  55.6 2.0 %collective-permute-start = (bf16[8,4,256]{2,0,1:T(8,128)(2,1)S(1)}, bf16[8,4,256]{2,0,1:T(8,128)(2,1)S(1)}, u32[]{:S(2)}, u32[]{:S(2)}) collective-permute-start(bf16[8,4,256]{2,0,1:T(8,128)(2,1)S(1)} %copy_select_fusion), channel_id=1, source_target_pairs={{0,3},{1,0},{2,1},{3,2},{4,7},{5,4},{6,5},{7,6},{8,11},{9,8},{10,9... | collective-permute-start | bytes 49160 | tf_op jit(solution)/shard_map/ppermute | solution.py:136
  57.6 4.2 %collective-permute-start.1 = (bf16[8,4,256]{2,0,1:T(8,128)(2,1)S(1)}, bf16[8,4,256]{2,0,1:T(8,128)(2,1)S(1)}, u32[]{:S(2)}, u32[]{:S(2)}) collective-permute-start(bf16[8,4,256]{2,0,1:T(8,128)(2,1)S(1)} %copy_select_fusion), channel_id=1, source_target_pairs={{0,2},{1,3},{2,0},{3,1},{4,6},{5,7},{6,4},{7,5},{8,10},{9,11},{10,... | collective-permute-start | bytes 49160 | tf_op jit(solution)/shard_map/ppermute | solution.py:136
  61.8 4.5 %collective-permute-start.2 = (bf16[8,4,256]{2,0,1:T(8,128)(2,1)S(1)}, bf16[8,4,256]{2,0,1:T(8,128)(2,1)S(1)}, u32[]{:S(2)}, u32[]{:S(2)}) collective-permute-start(bf16[8,4,256]{2,0,1:T(8,128)(2,1)S(1)} %copy_select_fusion), channel_id=1, source_target_pairs={{0,1},{1,2},{2,3},{3,0},{4,5},{5,6},{6,7},{7,4},{8,9},{9,10},{10,1... | collective-permute-start | bytes 49160 | tf_op jit(solution)/shard_map/ppermute | solution.py:136
  70.4 2.7 %copy.262.content_ref = f32[4,32,64,1]{3,2,1,0:T(8,128)} copy(f32[4,32,64,1]{2,1,0,3:T(8,128)S(1)} %bitcast.255) | data formatting | bytes 65536 | tf_op jit(solution)/shard_map/reshape;reshape | solution.py:98
  74.0 8.0 %shard_map.199 = f32[4,32,64,1]{3,2,1,0:T(8,128)} custom-call(f32[32,64,64]{2,1,0:T(8,128)} %bitcast.247, f32[4,5,32,1,64]{4,3,2,1,0:T(1,128)} %copy-done.2, f32[4,32,64,1]{3,2,1,0:T(8,128)} %copy.262.content_ref), custom_call_target="tpu_custom_call" | custom-call | tf_op jit(solution)/shard_map/pallas_call | solution.py:27
  82.1 3.3 %reduce.5 = f32[4,32,64]{2,1,0:T(8,128)S(1)} reduce(f32[4,32,64,1]{3,2,1,0:T(8,128)} %shard_map.199, f32[]{:T(128)} %constant.205), dimensions={3}, to_apply=%pallas_call.6.reduce_sub_computation | reduce | bytes 65540 | tf_op jit(solution)/shard_map/pallas_call | solution.py:27
  86.4 5.4 %collective-permute-start.6 = (f32[32,256]{1,0:T(8,128)S(1)}, f32[32,256]{1,0:T(8,128)S(1)}, u32[]{:S(2)}, u32[]{:S(2)}) collective-permute-start(f32[32,256]{1,0:T(8,128)S(1)} %get-tuple-element.30), channel_id=1, source_target_pairs={{0,1},{1,2},{2,3},{3,0},{4,5},{5,6},{6,7},{7,4},{8,9},{9,10},{10,1... | collective-permute-start | bytes 98312 | tf_op jit(solution)/shard_map/ppermute | solution.py:152
  91.9 2.1 %collective-permute-start.7 = (f32[32,256]{1,0:T(8,128)S(1)}, f32[32,256]{1,0:T(8,128)S(1)}, u32[]{:S(2)}, u32[]{:S(2)}) collective-permute-start(f32[32,256]{1,0:T(8,128)S(1)} %get-tuple-element.32), channel_id=1, source_target_pairs={{0,2},{1,3},{2,0},{3,1},{4,6},{5,7},{6,4},{7,5},{8,10},{9,11},{10,... | collective-permute-start | bytes 98312 | tf_op jit(solution)/shard_map/ppermute | solution.py:152
  94.0 2.6 %collective-permute-start.8 = (f32[32,256]{1,0:T(8,128)S(1)}, f32[32,256]{1,0:T(8,128)S(1)}, u32[]{:S(2)}, u32[]{:S(2)}) collective-permute-start(f32[32,256]{1,0:T(8,128)S(1)} %get-tuple-element.31), channel_id=1, source_target_pairs={{0,3},{1,0},{2,1},{3,2},{4,7},{5,4},{6,5},{7,6},{8,11},{9,8},{10,9... | collective-permute-start | bytes 98312 | tf_op jit(solution)/shard_map/ppermute | solution.py:152
  96.6 2.6 %collective-permute-done.7 = f32[32,256]{1,0:T(8,128)S(1)} collective-permute-done((f32[32,256]{1,0:T(8,128)S(1)}, f32[32,256]{1,0:T(8,128)S(1)}, u32[]{:S(2)}, u32[]{:S(2)}) %collective-permute-start.7) | collective-permute-done | bytes 32800 | tf_op jit(solution)/shard_map/ppermute | solution.py:152
  99.2 1.8 %collective-permute-done.8 = f32[32,256]{1,0:T(8,128)S(1)} collective-permute-done((f32[32,256]{1,0:T(8,128)S(1)}, f32[32,256]{1,0:T(8,128)S(1)}, u32[]{:S(2)}, u32[]{:S(2)}) %collective-permute-start.8) | collective-permute-done | bytes 32800 | tf_op jit(solution)/shard_map/ppermute | solution.py:152
  105.0 1.5 collective-permute-start.9
  107.7 2.7 %copy.284.content_ref = f32[4,32,64,1]{3,2,1,0:T(8,128)} copy(f32[4,32,64,1]{2,1,0,3:T(8,128)S(1)} %bitcast.256) | data formatting | bytes 65536 | tf_op jit(solution)/shard_map/reshape;reshape | solution.py:98
  113.5 8.0 %shard_map.200 = f32[4,32,64,1]{3,2,1,0:T(8,128)} custom-call(f32[32,64,64]{2,1,0:T(8,128)} %bitcast.248, f32[4,5,32,1,64]{4,3,2,1,0:T(1,128)} %copy-done.3, f32[4,32,64,1]{3,2,1,0:T(8,128)} %copy.284.content_ref), custom_call_target="tpu_custom_call" | custom-call | tf_op jit(solution)/shard_map/pallas_call | solution.py:27
  121.5 3.4 %reduce.9 = f32[4,32,64]{2,1,0:T(8,128)S(1)} reduce(f32[4,32,64,1]{3,2,1,0:T(8,128)} %shard_map.200, f32[]{:T(128)} %constant.205), dimensions={3}, to_apply=%pallas_call.7.reduce_sub_computation | reduce | bytes 65540 | tf_op jit(solution)/shard_map/pallas_call | solution.py:27
  125.8 2.6 %collective-permute-start.13 = (f32[32,256]{1,0:T(8,128)S(1)}, f32[32,256]{1,0:T(8,128)S(1)}, u32[]{:S(2)}, u32[]{:S(2)}) collective-permute-start(f32[32,256]{1,0:T(8,128)S(1)} %get-tuple-element.27), channel_id=1, source_target_pairs={{0,1},{1,2},{2,3},{3,0},{4,5},{5,6},{6,7},{7,4},{8,9},{9,10},{10,1... | collective-permute-start | bytes 98312 | tf_op jit(solution)/shard_map/ppermute | solution.py:152
  128.4 3.4 %collective-permute-start.14 = (f32[32,256]{1,0:T(8,128)S(1)}, f32[32,256]{1,0:T(8,128)S(1)}, u32[]{:S(2)}, u32[]{:S(2)}) collective-permute-start(f32[32,256]{1,0:T(8,128)S(1)} %get-tuple-element.29), channel_id=1, source_target_pairs={{0,2},{1,3},{2,0},{3,1},{4,6},{5,7},{6,4},{7,5},{8,10},{9,11},{10,... | collective-permute-start | bytes 98312 | tf_op jit(solution)/shard_map/ppermute | solution.py:152
  131.8 3.3 %collective-permute-start.15 = (f32[32,256]{1,0:T(8,128)S(1)}, f32[32,256]{1,0:T(8,128)S(1)}, u32[]{:S(2)}, u32[]{:S(2)}) collective-permute-start(f32[32,256]{1,0:T(8,128)S(1)} %get-tuple-element.28), channel_id=1, source_target_pairs={{0,3},{1,0},{2,1},{3,2},{4,7},{5,4},{6,5},{7,6},{8,11},{9,8},{10,9... | collective-permute-start | bytes 98312 | tf_op jit(solution)/shard_map/ppermute | solution.py:152
  135.8 3.2 %collective-permute-done.15 = f32[32,256]{1,0:T(8,128)S(1)} collective-permute-done((f32[32,256]{1,0:T(8,128)S(1)}, f32[32,256]{1,0:T(8,128)S(1)}, u32[]{:S(2)}, u32[]{:S(2)}) %collective-permute-start.15) | collective-permute-done | bytes 32800 | tf_op jit(solution)/shard_map/ppermute | solution.py:152
  139.8 1.9 %scatter_fusion.1 = bf16[64,4,256]{2,1,0:T(4,128)(2,1)} fusion(bf16[64,4,256]{2,1,0:T(4,128)(2,1)} %broadcast.445, s32[8]{0:T(128)S(1)} %fusion.81, bf16[8,4,256]{2,1,0:T(4,128)(2,1)S(1)} %copy.289), kind=kCustom, calls=%fused_computation.4 | custom fusion | bytes 49184 | tf_op jit(solution)/shard_map/scatter | solution.py:333
  141.7 12.7 %all-to-all-start.1 = ((bf16[64,4,256]{2,1,0:T(4,128)(2,1)}), bf16[64,4,256]{2,1,0:T(4,128)(2,1)S(1)}, u32[]{:S(2)}, u32[]{:S(2)}) async-start(bf16[64,4,256]{2,1,0:T(4,128)(2,1)} %scatter_fusion.1), calls=%async_computation.1 | async-start | bytes 262144 | tf_op jit(solution)/shard_map/all_to_all | solution.py:335
  154.5 12.7 %all-to-all-done.1 = bf16[64,4,256]{2,1,0:T(4,128)(2,1)S(1)} async-done(((bf16[64,4,256]{2,1,0:T(4,128)(2,1)}), bf16[64,4,256]{2,1,0:T(4,128)(2,1)S(1)}, u32[]{:S(2)}, u32[]{:S(2)}) %all-to-all-start.1) | async-done | bytes 131104 | tf_op jit(solution)/shard_map/all_to_all | solution.py:335
  (228 shorter events, 32.3 us)
Async XLA Ops:
  0.0 86.2 %copy-start = (bf16[1,256,1024]{2,1,0:T(8,128)(2,1)S(1)}, bf16[1,256,1024]{2,1,0:T(8,128)(2,1)}, u32[]{:S(2)}) copy-start(bf16[1,256,1024]{2,1,0:T(8,128)(2,1)} %param.34) | copy-start | bytes 1572868
  2.9 42.6 %collective-permute-start.3 = (bf16[51200]{0:T(1024)(128)(2,1)S(1)}, bf16[51200]{0:T(1024)(128)(2,1)S(1)}, u32[]{:S(2)}, u32[]{:S(2)}) collective-permute-start(bf16[51200]{0:T(1024)(128)(2,1)S(1)} %constant_dynamic-update-slice_fusion.11), channel_id=1, source_target_pairs={{0,3},{1,0},{2,1},{3,2},{4,7},{5,4},{6,5},{7,6},{8,11},{9,8},{10,9... | collective-permute-start | bytes 307208 | tf_op jit(solution)/shard_map/ppermute | solution.py:136
  5.7 40.0 %collective-permute-start.4 = (bf16[51200]{0:T(1024)(128)(2,1)S(1)}, bf16[51200]{0:T(1024)(128)(2,1)S(1)}, u32[]{:S(2)}, u32[]{:S(2)}) collective-permute-start(bf16[51200]{0:T(1024)(128)(2,1)S(1)} %constant_dynamic-update-slice_fusion.11), channel_id=1, source_target_pairs={{0,2},{1,3},{2,0},{3,1},{4,6},{5,7},{6,4},{7,5},{8,10},{9,11},{10,... | collective-permute-start | bytes 307208 | tf_op jit(solution)/shard_map/ppermute | solution.py:136
  14.1 31.7 %collective-permute-start.5 = (bf16[51200]{0:T(1024)(128)(2,1)S(1)}, bf16[51200]{0:T(1024)(128)(2,1)S(1)}, u32[]{:S(2)}, u32[]{:S(2)}) collective-permute-start(bf16[51200]{0:T(1024)(128)(2,1)S(1)} %constant_dynamic-update-slice_fusion.11), channel_id=1, source_target_pairs={{0,1},{1,2},{2,3},{3,0},{4,5},{5,6},{6,7},{7,4},{8,9},{9,10},{10,1... | collective-permute-start | bytes 307208 | tf_op jit(solution)/shard_map/ppermute | solution.py:136
  16.8 28.7 %copy-start.10 = (s32[64,8]{1,0:T(8,128)}, s32[64,8]{1,0:T(8,128)S(1)}, u32[]{:S(2)}) copy-start(s32[64,8]{1,0:T(8,128)S(1)} %reshape.493) | copy-start | bytes 6148
  19.7 35.3 %all-to-all-start = ((bf16[64,4,256]{2,1,0:T(4,128)(2,1)}), bf16[64,4,256]{2,1,0:T(4,128)(2,1)S(1)}, u32[]{:S(2)}, u32[]{:S(2)}) async-start(bf16[64,4,256]{2,1,0:T(4,128)(2,1)} %scatter_fusion), calls=%async_computation | async-start | bytes 262144 | tf_op jit(solution)/shard_map/all_to_all | solution.py:329
  35.5 32.4 %copy-start.11 = (f32[4,256]{1,0:T(4,128)}, f32[4,256]{1,0:T(4,128)S(1)}, u32[]{:S(2)}) copy-start(f32[4,256]{1,0:T(4,128)S(1)} %mul.255) | copy-start | bytes 12292
  35.5 32.4 %copy-start.4 = (bf16[1,96,256]{2,1,0:T(8,128)(2,1)S(1)}, bf16[1,96,256]{2,1,0:T(8,128)(2,1)}, u32[]{:S(2)}) copy-start(bf16[1,96,256]{2,1,0:T(8,128)(2,1)} %param.38) | copy-start | bytes 147460
  35.5 32.4 %copy-start.15 = (f32[1,256]{1,0:T(1,128)S(1)}, f32[1,256]{1,0:T(1,128)}, u32[]{:S(2)}) copy-start(f32[1,256]{1,0:T(1,128)} %param.40) | copy-start | bytes 3076
  36.8 31.6 %copy-start.1 = (bf16[1,1024,256]{2,1,0:T(8,128)(2,1)S(1)}, bf16[1,1024,256]{2,1,0:T(8,128)(2,1)}, u32[]{:S(2)}) copy-start(bf16[1,1024,256]{2,1,0:T(8,128)(2,1)} %param.32) | copy-start | bytes 1572868
  36.8 31.6 %copy-start.17 = (f32[1,256]{1,0:T(1,128)S(1)}, f32[1,256]{1,0:T(1,128)}, u32[]{:S(2)}) copy-start(f32[1,256]{1,0:T(1,128)} %param.42) | copy-start | bytes 3076
  36.9 31.6 %copy-start.19 = (f32[1,256]{1,0:T(1,128)S(1)}, f32[1,256]{1,0:T(1,128)}, u32[]{:S(2)}) copy-start(f32[1,256]{1,0:T(1,128)} %param.41) | copy-start | bytes 3076
  55.6 10.8 %collective-permute-start = (bf16[8,4,256]{2,0,1:T(8,128)(2,1)S(1)}, bf16[8,4,256]{2,0,1:T(8,128)(2,1)S(1)}, u32[]{:S(2)}, u32[]{:S(2)}) collective-permute-start(bf16[8,4,256]{2,0,1:T(8,128)(2,1)S(1)} %copy_select_fusion), channel_id=1, source_target_pairs={{0,3},{1,0},{2,1},{3,2},{4,7},{5,4},{6,5},{7,6},{8,11},{9,8},{10,9... | collective-permute-start | bytes 49160 | tf_op jit(solution)/shard_map/ppermute | solution.py:136
  57.6 8.8 %collective-permute-start.1 = (bf16[8,4,256]{2,0,1:T(8,128)(2,1)S(1)}, bf16[8,4,256]{2,0,1:T(8,128)(2,1)S(1)}, u32[]{:S(2)}, u32[]{:S(2)}) collective-permute-start(bf16[8,4,256]{2,0,1:T(8,128)(2,1)S(1)} %copy_select_fusion), channel_id=1, source_target_pairs={{0,2},{1,3},{2,0},{3,1},{4,6},{5,7},{6,4},{7,5},{8,10},{9,11},{10,... | collective-permute-start | bytes 49160 | tf_op jit(solution)/shard_map/ppermute | solution.py:136
  61.8 5.7 %collective-permute-start.2 = (bf16[8,4,256]{2,0,1:T(8,128)(2,1)S(1)}, bf16[8,4,256]{2,0,1:T(8,128)(2,1)S(1)}, u32[]{:S(2)}, u32[]{:S(2)}) collective-permute-start(bf16[8,4,256]{2,0,1:T(8,128)(2,1)S(1)} %copy_select_fusion), channel_id=1, source_target_pairs={{0,1},{1,2},{2,3},{3,0},{4,5},{5,6},{6,7},{7,4},{8,9},{9,10},{10,1... | collective-permute-start | bytes 49160 | tf_op jit(solution)/shard_map/ppermute | solution.py:136
  82.0 25.2 %copy-start.9 = (bf16[1,4,8,256]{3,2,1,0:T(8,128)(2,1)S(1)}, bf16[1,4,8,256]{3,2,1,0:T(8,128)(2,1)}, u32[]{:S(2)}) copy-start(bf16[1,4,8,256]{3,2,1,0:T(8,128)(2,1)} %copy-done.8) | copy-start | bytes 49156
  82.0 25.2 %copy-start.12 = (f32[4,256]{1,0:T(4,128)S(1)}, f32[4,256]{1,0:T(4,128)}, u32[]{:S(2)}) copy-start(f32[4,256]{1,0:T(4,128)} %copy-done.11) | copy-start | bytes 12292
  85.4 25.1 %copy-start.5 = (bf16[1,96,256]{2,1,0:T(8,128)(2,1)S(1)}, bf16[1,96,256]{2,1,0:T(8,128)(2,1)}, u32[]{:S(2)}) copy-start(bf16[1,96,256]{2,1,0:T(8,128)(2,1)} %param.38) | copy-start | bytes 147460
  85.4 25.1 %copy-start.16 = (f32[1,256]{1,0:T(1,128)S(1)}, f32[1,256]{1,0:T(1,128)}, u32[]{:S(2)}) copy-start(f32[1,256]{1,0:T(1,128)} %param.40) | copy-start | bytes 3076
  86.1 24.9 %copy-start.18 = (f32[1,256]{1,0:T(1,128)S(1)}, f32[1,256]{1,0:T(1,128)}, u32[]{:S(2)}) copy-start(f32[1,256]{1,0:T(1,128)} %param.42) | copy-start | bytes 3076
  86.4 10.1 %collective-permute-start.6 = (f32[32,256]{1,0:T(8,128)S(1)}, f32[32,256]{1,0:T(8,128)S(1)}, u32[]{:S(2)}, u32[]{:S(2)}) collective-permute-start(f32[32,256]{1,0:T(8,128)S(1)} %get-tuple-element.30), channel_id=1, source_target_pairs={{0,1},{1,2},{2,3},{3,0},{4,5},{5,6},{6,7},{7,4},{8,9},{9,10},{10,1... | collective-permute-start | bytes 98312 | tf_op jit(solution)/shard_map/ppermute | solution.py:152
  91.9 7.3 %collective-permute-start.7 = (f32[32,256]{1,0:T(8,128)S(1)}, f32[32,256]{1,0:T(8,128)S(1)}, u32[]{:S(2)}, u32[]{:S(2)}) collective-permute-start(f32[32,256]{1,0:T(8,128)S(1)} %get-tuple-element.32), channel_id=1, source_target_pairs={{0,2},{1,3},{2,0},{3,1},{4,6},{5,7},{6,4},{7,5},{8,10},{9,11},{10,... | collective-permute-start | bytes 98312 | tf_op jit(solution)/shard_map/ppermute | solution.py:152
  94.0 7.0 %collective-permute-start.8 = (f32[32,256]{1,0:T(8,128)S(1)}, f32[32,256]{1,0:T(8,128)S(1)}, u32[]{:S(2)}, u32[]{:S(2)}) collective-permute-start(f32[32,256]{1,0:T(8,128)S(1)} %get-tuple-element.31), channel_id=1, source_target_pairs={{0,3},{1,0},{2,1},{3,2},{4,7},{5,4},{6,5},{7,6},{8,11},{9,8},{10,9... | collective-permute-start | bytes 98312 | tf_op jit(solution)/shard_map/ppermute | solution.py:152
  101.1 5.4 %collective-permute-start.10 = (bf16[8,4,256]{2,0,1:T(8,128)(2,1)S(1)}, bf16[8,4,256]{2,0,1:T(8,128)(2,1)S(1)}, u32[]{:S(2)}, u32[]{:S(2)}) collective-permute-start(bf16[8,4,256]{2,0,1:T(8,128)(2,1)S(1)} %fusion.64), channel_id=1, source_target_pairs={{0,259},{1,256},{2,257},{3,258},{4,263},{5,260},{6,261},{7,262},{8... | collective-permute-start | bytes 49160 | tf_op jit(solution)/shard_map/ppermute | solution.py:162
  102.4 4.2 %collective-permute-start.11 = (bf16[8,4,256]{2,0,1:T(8,128)(2,1)S(1)}, bf16[8,4,256]{2,0,1:T(8,128)(2,1)S(1)}, u32[]{:S(2)}, u32[]{:S(2)}) collective-permute-start(bf16[8,4,256]{2,0,1:T(8,128)(2,1)S(1)} %fusion.64), channel_id=1, source_target_pairs={{0,258},{1,259},{2,256},{3,257},{4,262},{5,263},{6,260},{7,261},{8... | collective-permute-start | bytes 49160 | tf_op jit(solution)/shard_map/ppermute | solution.py:162
  103.7 2.9 %collective-permute-start.12 = (bf16[8,4,256]{2,0,1:T(8,128)(2,1)S(1)}, bf16[8,4,256]{2,0,1:T(8,128)(2,1)S(1)}, u32[]{:S(2)}, u32[]{:S(2)}) collective-permute-start(bf16[8,4,256]{2,0,1:T(8,128)(2,1)S(1)} %fusion.64), channel_id=1, source_target_pairs={{0,257},{1,258},{2,259},{3,256},{4,261},{5,262},{6,263},{7,260},{8... | collective-permute-start | bytes 49160 | tf_op jit(solution)/shard_map/ppermute | solution.py:162
  105.0 2.1 %collective-permute-start.9 = (bf16[8,4,256]{2,0,1:T(8,128)(2,1)S(1)}, bf16[8,4,256]{2,0,1:T(8,128)(2,1)S(1)}, u32[]{:S(2)}, u32[]{:S(2)}) collective-permute-start(bf16[8,4,256]{2,0,1:T(8,128)(2,1)S(1)} %fusion.64), channel_id=1, source_target_pairs={{0,256},{1,257},{2,258},{3,259},{4,260},{5,261},{6,262},{7,263},{8... | collective-permute-start | bytes 49160 | tf_op jit(solution)/shard_map/ppermute | solution.py:162
  121.5 32.9 %copy-start.32 = (s32[8]{0:T(128)S(1)}, s32[8]{0:T(128)}, u32[]{:S(2)}) copy-start(s32[8]{0:T(128)} %param.26) | copy-start | bytes 100
  125.8 10.0 %collective-permute-start.13 = (f32[32,256]{1,0:T(8,128)S(1)}, f32[32,256]{1,0:T(8,128)S(1)}, u32[]{:S(2)}, u32[]{:S(2)}) collective-permute-start(f32[32,256]{1,0:T(8,128)S(1)} %get-tuple-element.27), channel_id=1, source_target_pairs={{0,1},{1,2},{2,3},{3,0},{4,5},{5,6},{6,7},{7,4},{8,9},{9,10},{10,1... | collective-permute-start | bytes 98312 | tf_op jit(solution)/shard_map/ppermute | solution.py:152
  128.4 7.4 %collective-permute-start.14 = (f32[32,256]{1,0:T(8,128)S(1)}, f32[32,256]{1,0:T(8,128)S(1)}, u32[]{:S(2)}, u32[]{:S(2)}) collective-permute-start(f32[32,256]{1,0:T(8,128)S(1)} %get-tuple-element.29), channel_id=1, source_target_pairs={{0,2},{1,3},{2,0},{3,1},{4,6},{5,7},{6,4},{7,5},{8,10},{9,11},{10,... | collective-permute-start | bytes 98312 | tf_op jit(solution)/shard_map/ppermute | solution.py:152
  131.8 7.3 %collective-permute-start.15 = (f32[32,256]{1,0:T(8,128)S(1)}, f32[32,256]{1,0:T(8,128)S(1)}, u32[]{:S(2)}, u32[]{:S(2)}) collective-permute-start(f32[32,256]{1,0:T(8,128)S(1)} %get-tuple-element.28), channel_id=1, source_target_pairs={{0,3},{1,0},{2,1},{3,2},{4,7},{5,4},{6,5},{7,6},{8,11},{9,8},{10,9... | collective-permute-start | bytes 98312 | tf_op jit(solution)/shard_map/ppermute | solution.py:152
  141.7 25.5 %all-to-all-start.1 = ((bf16[64,4,256]{2,1,0:T(4,128)(2,1)}), bf16[64,4,256]{2,1,0:T(4,128)(2,1)S(1)}, u32[]{:S(2)}, u32[]{:S(2)}) async-start(bf16[64,4,256]{2,1,0:T(4,128)(2,1)} %scatter_fusion.1), calls=%async_computation.1 | async-start | bytes 262144 | tf_op jit(solution)/shard_map/all_to_all | solution.py:335
  (19 other events, 244.9 us)

commit v3 on v2

--- a/solution.py
+++ b/solution.py
@@ -128,18 +128,24 @@
     )
 
 
-def gather_heads(block, axis):
-    n = lax.axis_size("head")
+def in_device_order(pieces):
+    n = len(pieces)
     me = lax.axis_index("head")
+    ordered = []
+    for d in range(n):
+        chosen = pieces[0]
+        for k in range(1, n):
+            chosen = jnp.where((me - k) % n == d, pieces[k], chosen)
+        ordered.append(chosen)
+    return ordered
+
+
+def gather_heads(block):
+    n = lax.axis_size("head")
     pieces = [block]
     for k in range(1, n):
         pieces.append(lax.ppermute(block, "head", [(i, (i + k) % n) for i in range(n)]))
-    stacked = jnp.stack(pieces[::-1], axis=0)
-    ordered = jnp.roll(stacked, me + 1, axis=0)
-    moved = jnp.moveaxis(ordered, 0, axis)
-    shape = list(block.shape)
-    shape[axis] = shape[axis] * n
-    return moved.reshape(shape)
+    return in_device_order(pieces)
 
 
 def scatter_heads(partial):
@@ -153,18 +159,18 @@
     return total
 
 
-def hand_over(block):
-    n = lax.axis_size("head")
-    me = lax.axis_index("head")
-    pieces = []
+def hand_over(partial):
+    n = lax.axis_size("head")
+    total = None
     for k in range(n):
-        pieces.append(
-            lax.ppermute(block, ("section", "head"), [(i, n + (i + k) % n) for i in range(n)])
-        )
-    stacked = jnp.stack(pieces[::-1], axis=0)
-    ordered = jnp.roll(stacked, me + 1, axis=0)
-    moved = jnp.moveaxis(ordered, 0, 2)
-    return moved.reshape(block.shape[:2] + (block.shape[2] * n,)), pieces[0]
+        piece = lax.ppermute(partial, ("section", "head"), [(i, n + (i + k) % n) for i in range(n)])
+        total = piece if total is None else total + piece
+    return total
+
+
+def hand_back(block):
+    n = lax.axis_size("head")
+    return lax.ppermute(block, ("section", "head"), [(n + i, i) for i in range(n)])
 
 
 def run_layer(full_now, full_prev_row, params):
@@ -221,29 +227,37 @@
     return jnp.dot(lagged_features, params[4], preferred_element_type=jnp.float32)
 
 
-def gather_start(last_use, fading_first, adapt_first):
-    n = lax.axis_size("head")
-    packed = jnp.concatenate([fading_first.reshape(-1), adapt_first.reshape(-1), last_use.reshape(-1)])
-    whole = gather_heads(packed, 0).reshape(n, -1)
-    first_size = fading_first.size
-    fading_full = whole[:, :first_size].reshape((n * fading_first.shape[0],) + fading_first.shape[1:])
-    adapt_full = whole[:, first_size : 2 * first_size].reshape(fading_full.shape)
-    prev_full = jnp.transpose(
-        whole[:, 2 * first_size :].reshape((n,) + last_use.shape), (1, 0, 2)
-    ).reshape(last_use.shape[0], n * last_use.shape[1])
-    return prev_full, fading_full, adapt_full
-
-
 def run_sections(inputs, states_use, last_use, params):
     section_num = lax.axis_index("section")
+    n = lax.axis_size("head")
     batch_rows, steps_count, shard_width = inputs.shape
-    full_prev, fading_full, adapt_full = gather_start(last_use, params[5], params[7])
+    fading_first, adapt_first = params[5], params[7]
+    sizes = [inputs.size, last_use.size, fading_first.size, adapt_first.size]
+    packed = jnp.concatenate(
+        [inputs.reshape(-1), last_use.reshape(-1), fading_first.reshape(-1), adapt_first.reshape(-1)]
+    )
+    ordered = gather_heads(packed)
+    cuts = [0]
+    for size in sizes:
+        cuts.append(cuts[-1] + size)
+
+    def joined(index, shape, axis):
+        parts = [piece[cuts[index] : cuts[index + 1]].reshape(shape) for piece in ordered]
+        return jnp.concatenate(parts, axis=axis)
+
+    full_first = joined(0, inputs.shape, 2)
+    full_prev = joined(1, last_use.shape, 1)
+    fading_full = joined(2, fading_first.shape, 0)
+    adapt_full = joined(3, adapt_first.shape, 0)
     params = params[:5] + (fading_full, params[6], adapt_full) + params[8:]
-    full_first = gather_heads(inputs, 2)
     partial_first = layer_partial(full_first, full_prev, states_use, params)
-    own_first = scatter_heads(partial_first).reshape(batch_rows, steps_count, shard_width)
-    first_out = (inputs.astype(jnp.float32) + own_first).astype(jnp.bfloat16)
-    full_second, second_in = hand_over(first_out)
+    total_first = hand_over(partial_first)
+    full_second = (
+        full_first.astype(jnp.float32) + total_first.reshape(full_first.shape)
+    ).astype(jnp.bfloat16)
+    me = lax.axis_index("head")
+    second_in = lax.dynamic_slice_in_dim(full_second, me * shard_width, shard_width, 2)
+    first_out = hand_back(second_in)
     partial_second = layer_partial(full_second, full_prev, states_use, params)
     own_second = scatter_heads(partial_second).reshape(batch_rows, steps_count, shard_width)
     second_out = (second_in.astype(jnp.float32) + own_second).astype(jnp.bfloat16)
@@ -302,25 +316,25 @@
     home_slot = source * capacity + home_rank
     buffer_rows = groups * capacity
     params = (
-        lag_interpolants[0],
-        acceptor_projection[0],
-        address_projection[0],
-        content_projection[0],
-        readout_projection[0],
-        fading_first_lowrank[0],
-        fading_second_lowrank[0],
-        adapt_first_lowrank[0],
-        adapt_second_lowrank[0],
-        fading_baseline[0],
-        adapt_baseline[0],
-        erasing_address_gains[0],
-        address_rate_coupling[0],
-        present_extra_gain[0],
-        section_standard_gains[0],
-        section_standard_shift_terms[0],
-    )
-    states_local = memory_per_request[0]
-    last_local = previous_step_feature[0]
+        lag_interpolants.reshape(lag_interpolants.shape[1:]),
+        acceptor_projection.reshape(acceptor_projection.shape[1:]),
+        address_projection.reshape(address_projection.shape[1:]),
+        content_projection.reshape(content_projection.shape[1:]),
+        readout_projection.reshape(readout_projection.shape[1:]),
+        fading_first_lowrank.reshape(fading_first_lowrank.shape[1:]),
+        fading_second_lowrank.reshape(fading_second_lowrank.shape[1:]),
+        adapt_first_lowrank.reshape(adapt_first_lowrank.shape[1:]),
+        adapt_second_lowrank.reshape(adapt_second_lowrank.shape[1:]),
+        fading_baseline.reshape(fading_baseline.shape[1:]),
+        adapt_baseline.reshape(adapt_baseline.shape[1:]),
+        erasing_address_gains.reshape(erasing_address_gains.shape[1:]),
+        address_rate_coupling.reshape(address_rate_coupling.shape[1:]),
+        present_extra_gain.reshape(present_extra_gain.shape[1:]),
+        section_standard_gains.reshape(section_standard_gains.shape[1:]),
+        section_standard_shift_terms.reshape(section_standard_shift_terms.shape[1:]),
+    )
+    states_local = memory_per_request.reshape(memory_per_request.shape[1:])
+    last_local = previous_step_feature.reshape(previous_step_feature.shape[1:])
     outgoing = (
         jnp.zeros((buffer_rows,) + embedding_per_slot.shape[1:], jnp.bfloat16)
         .at[arrival_slot]

time: 170 us -> 150 us (0.88)
  starting transfers between devices: 74.5 us -> 56.9 us
  local copies, waits for them, and re-layouts: 34.4 us -> 29.1 us
  matrix products: 3.37 us -> 6.53 us
    ppermute x6 -> x3, starting transfers between devices: 23.7 us -> 9.76 us  [gather_heads(): lax.ppermute(block, 'head', [(i, (i + k) % n) for i in range(n)])]
    ppermute x6 -> x3, starting transfers between devices: 19.4 us -> 9.27 us  [scatter_heads(): lax.ppermute(chunk, 'head', [(i, (i + k) % n) for i in range(n)])]
    concatenate x2 -> x4, local copies, waits for them, and re-layouts: 6.38 us -> 0.05 us  [the longest x3 0.04 us: joined(): return jnp.concatenate(parts, axis=axis)]
    ppermute x6 -> x3, waiting for transfers between devices: 7.62 us -> 3.75 us  [scatter_heads(): lax.ppermute(chunk, 'head', [(i, (i + k) % n) for i in range(n)])]
    ppermute x4 -> x5, starting transfers between devices: 5.37 us -> 8.66 us  [the longest x4 7.36 us: hand_over(): lax.ppermute(partial, ('section', 'head'), [(i, n + (i + k) % n) for i in...]
    all_to_all x1, starting transfers between devices: 13.3 us -> 16.6 us  [body(): lax.all_to_all(outgoing, 'req', split_axis=0, concat_axis=0, tiled=True)]
    slice x4 -> x22, local copies, waits for them, and re-layouts: 2.23 us -> 0.22 us  [joined(): piece[cuts[index]:cuts[index + 1]].reshape(shape)]
    ppermute x6 -> x3, waiting for transfers between devices: 1.17 us -> 2.98 us  [gather_heads(): lax.ppermute(block, 'head', [(i, (i + k) % n) for i in range(n)])]
  transfers between devices with their start and end apart: 18 -> 13, of which waited for: 6 -> 6; matrix products, arithmetic and copies ran while one was open for 15% -> 10% of each run, Pallas kernels for 0% -> 0%
where the time goes in v3:
time: 150 us; the launch traced here: 149 us
  starting transfers between devices  56.9 us (38%)
  local copies, waits for them, and re-layouts  29.1 us (19%)
  waiting for transfers between devices  21.6 us (14%)
  other arithmetic  17 us (11%)
  Pallas kernels  16.1 us (11%)
  matrix products  6.53 us (4%)
    all_to_all x1, starting transfers between devices, body(): lax.all_to_all(outgoing, 'req', split_axis=0, concat_axis=0, tiled=True)  16.6 us
    pallas_call x2, Pallas kernels, run_recurrence(): pl.pallas_call(recurrence_kernel, out_shape=jax.ShapeDtypeStruct((steps,...  16.1 us
    all_to_all x1, starting transfers between devices, body(): lax.all_to_all(going_back, 'req', split_axis=0, concat_axis=0, tiled=True)  12.6 us
    all_to_all x1, waiting for transfers between devices, body(): lax.all_to_all(going_back, 'req', split_axis=0, concat_axis=0, tiled=True)  12.5 us
    ppermute x3, starting transfers between devices, gather_heads(): lax.ppermute(block, 'head', [(i, (i + k) % n) for i in range(n)])  9.76 us
    ppermute x3, starting transfers between devices, scatter_heads(): lax.ppermute(chunk, 'head', [(i, (i + k) % n) for i in range(n)])  9.27 us
    unnamed x85, local copies, waits for them, and re-layouts  7.42 us
    ppermute x4, starting transfers between devices, hand_over(): lax.ppermute(partial, ('section', 'head'), [(i, n + (i + k) % n) for i in...  7.36 us
  transfers between devices with their start and end apart: 13, of which 6 were waited for; matrix products, arithmetic and copies ran while one was open for 10% of the time, Pallas kernels for 0%

profile of v3, /device:TPU:6, one launch (start us, length us, event | category | flops | bytes accessed | tf_op | source)
XLA Modules:
  0.0 148.7 jit_solution(2413495182342247860)
XLA Ops:
  1.8 2.0 %scatter_fusion = bf16[64,4,256]{2,1,0:T(4,128)(2,1)} fusion(bf16[64,4,256]{2,1,0:T(4,128)(2,1)} %broadcast.418.clone, s32[8]{0:T(128)S(1)} %fusion.107, bf16[8,4,256]{2,1,0:T(4,128)(2,1)} %param.23), kind=kCustom, calls=%fused_computation.3 | custom fusion | bytes 49184 | tf_op jit(solution)/shard_map/scatter | solution.py:341
  3.8 16.6 %all-to-all-start = ((bf16[64,4,256]{2,1,0:T(4,128)(2,1)}), bf16[64,4,256]{2,1,0:T(4,128)(2,1)S(1)}, u32[]{:S(2)}, u32[]{:S(2)}) async-start(bf16[64,4,256]{2,1,0:T(4,128)(2,1)} %scatter_fusion), calls=%async_computation | async-start | bytes 262144 | tf_op jit(solution)/shard_map/all_to_all | solution.py:343
  25.1 1.2 copy.143
  26.3 1.2 copy.146
  28.1 1.3 reduce.11
  30.0 1.3 reduce.12
  32.0 1.3 reduce.13
  34.0 1.5 %fusion.116 = (f32[1,1,1024]{2,1,0:T(1,128)S(1)}, f32[1,1,1024]{2,1,0:T(1,128)S(1)}, f32[1,1,1024]{2,1,0:T(1,128)S(1)}, f32[1,1,1024]{2,1,0:T(1,128)}, f32[1,1,1024]{2,1,0:T(1,128)S(1)}) fusion(bf16[1,5,1024]{2,1,0:T(8,128)(2,1)} %param.28), kind=kLoop, calls=%fused_computation.240 | loop fusion | bytes 40960 | tf_op jit(solution)/shard_map/slice | solution.py:201
  36.3 2.7 %collective-permute-start = (bf16[59392]{0:T(1024)(128)(2,1)S(1)}, bf16[59392]{0:T(1024)(128)(2,1)S(1)}, u32[]{:S(2)}, u32[]{:S(2)}) collective-permute-start(bf16[59392]{0:T(1024)(128)(2,1)S(1)} %constant_dynamic-update-slice_fusion.23), channel_id=1, source_target_pairs={{0,3},{1,0},{2,1},{3,2},{4,7},{5,4},{6,5},{7,6},{8,11},{9,8},{10,9... | collective-permute-start | bytes 356360 | tf_op jit(solution)/shard_map/ppermute | solution.py:147
  39.1 3.0 %collective-permute-start.1 = (bf16[59392]{0:T(1024)(128)(2,1)S(1)}, bf16[59392]{0:T(1024)(128)(2,1)S(1)}, u32[]{:S(2)}, u32[]{:S(2)}) collective-permute-start(bf16[59392]{0:T(1024)(128)(2,1)S(1)} %constant_dynamic-update-slice_fusion.23), channel_id=1, source_target_pairs={{0,2},{1,3},{2,0},{3,1},{4,6},{5,7},{6,4},{7,5},{8,10},{9,11},{10,... | collective-permute-start | bytes 356360 | tf_op jit(solution)/shard_map/ppermute | solution.py:147
  42.1 4.0 %collective-permute-start.2 = (bf16[59392]{0:T(1024)(128)(2,1)S(1)}, bf16[59392]{0:T(1024)(128)(2,1)S(1)}, u32[]{:S(2)}, u32[]{:S(2)}) collective-permute-start(bf16[59392]{0:T(1024)(128)(2,1)S(1)} %constant_dynamic-update-slice_fusion.23), channel_id=1, source_target_pairs={{0,1},{1,2},{2,3},{3,0},{4,5},{5,6},{6,7},{7,4},{8,9},{9,10},{10,1... | collective-permute-start | bytes 356360 | tf_op jit(solution)/shard_map/ppermute | solution.py:147
  47.3 2.3 %collective-permute-done.2 = bf16[59392]{0:T(1024)(128)(2,1)S(1)} collective-permute-done((bf16[59392]{0:T(1024)(128)(2,1)S(1)}, bf16[59392]{0:T(1024)(128)(2,1)S(1)}, u32[]{:S(2)}, u32[]{:S(2)}) %collective-permute-start.2) | collective-permute-done | bytes 118816 | tf_op jit(solution)/shard_map/ppermute | solution.py:147
  52.6 1.2 fusion.80
  56.1 2.7 %copy.149.content_ref = f32[4,32,64,1]{3,2,1,0:T(8,128)} copy(f32[4,32,64,1]{2,1,0,3:T(8,128)S(1)} %bitcast.191) | data formatting | bytes 65536 | tf_op jit(solution)/shard_map/reshape;reshape | solution.py:98
  60.5 8.0 %shard_map.199 = f32[4,32,64,1]{3,2,1,0:T(8,128)} custom-call(f32[32,64,64]{2,1,0:T(8,128)} %bitcast.180, f32[4,5,32,1,64]{4,3,2,1,0:T(1,128)} %copy-done.2, f32[4,32,64,1]{3,2,1,0:T(8,128)} %copy.149.content_ref), custom_call_target="tpu_custom_call" | custom-call | tf_op jit(solution)/shard_map/pallas_call | solution.py:27
  68.6 3.4 %reduce = f32[4,32,64]{2,1,0:T(8,128)S(1)} reduce(f32[4,32,64,1]{3,2,1,0:T(8,128)} %shard_map.199, f32[]{:T(128)} %constant.200), dimensions={3}, to_apply=%pallas_call.6.reduce_sub_computation | reduce | bytes 65540 | tf_op jit(solution)/shard_map/pallas_call | solution.py:27
  72.9 1.3 collective-permute-start.3
  74.2 3.3 %collective-permute-start.4 = (f32[32,1024]{1,0:T(8,128)S(1)}, f32[32,1024]{1,0:T(8,128)S(1)}, u32[]{:S(2)}, u32[]{:S(2)}) collective-permute-start(f32[32,1024]{1,0:T(8,128)S(1)} %fusion.22), channel_id=1, source_target_pairs={{0,257},{1,258},{2,259},{3,256},{4,261},{5,262},{6,263},{7,260},{8... | collective-permute-start | bytes 393224 | tf_op jit(solution)/shard_map/ppermute | solution.py:166
  77.5 1.3 collective-permute-start.5
  78.8 1.5 collective-permute-start.6
  81.3 1.4 collective-permute-done.6
  88.0 2.7 %copy.162.content_ref = f32[4,32,64,1]{3,2,1,0:T(8,128)} copy(f32[4,32,64,1]{2,1,0,3:T(8,128)S(1)} %bitcast.192) | data formatting | bytes 65536 | tf_op jit(solution)/shard_map/reshape;reshape | solution.py:98
  92.7 8.0 %shard_map.200 = f32[4,32,64,1]{3,2,1,0:T(8,128)} custom-call(f32[32,64,64]{2,1,0:T(8,128)} %bitcast.181, f32[4,5,32,1,64]{4,3,2,1,0:T(1,128)} %copy-done.3, f32[4,32,64,1]{3,2,1,0:T(8,128)} %copy.162.content_ref), custom_call_target="tpu_custom_call" | custom-call | tf_op jit(solution)/shard_map/pallas_call | solution.py:27
  100.7 3.3 %reduce.4 = f32[4,32,64]{2,1,0:T(8,128)S(1)} reduce(f32[4,32,64,1]{3,2,1,0:T(8,128)} %shard_map.200, f32[]{:T(128)} %constant.200), dimensions={3}, to_apply=%pallas_call.7.reduce_sub_computation | reduce | bytes 65540 | tf_op jit(solution)/shard_map/pallas_call | solution.py:27
  105.1 3.4 %collective-permute-start.10 = (f32[32,256]{1,0:T(8,128)S(1)}, f32[32,256]{1,0:T(8,128)S(1)}, u32[]{:S(2)}, u32[]{:S(2)}) collective-permute-start(f32[32,256]{1,0:T(8,128)S(1)} %get-tuple-element.22), channel_id=1, source_target_pairs={{0,3},{1,0},{2,1},{3,2},{4,7},{5,4},{6,5},{7,6},{8,11},{9,8},{10,9... | collective-permute-start | bytes 98312 | tf_op jit(solution)/shard_map/ppermute | solution.py:158
  108.4 3.7 %collective-permute-start.8 = (f32[32,256]{1,0:T(8,128)S(1)}, f32[32,256]{1,0:T(8,128)S(1)}, u32[]{:S(2)}, u32[]{:S(2)}) collective-permute-start(f32[32,256]{1,0:T(8,128)S(1)} %get-tuple-element.21), channel_id=1, source_target_pairs={{0,1},{1,2},{2,3},{3,0},{4,5},{5,6},{6,7},{7,4},{8,9},{9,10},{10,1... | collective-permute-start | bytes 98312 | tf_op jit(solution)/shard_map/ppermute | solution.py:158
  112.1 2.2 %collective-permute-start.9 = (f32[32,256]{1,0:T(8,128)S(1)}, f32[32,256]{1,0:T(8,128)S(1)}, u32[]{:S(2)}, u32[]{:S(2)}) collective-permute-start(f32[32,256]{1,0:T(8,128)S(1)} %get-tuple-element.23), channel_id=1, source_target_pairs={{0,2},{1,3},{2,0},{3,1},{4,6},{5,7},{6,4},{7,5},{8,10},{9,11},{10,... | collective-permute-start | bytes 98312 | tf_op jit(solution)/shard_map/ppermute | solution.py:158
  114.4 1.3 collective-permute-start.7
  115.7 3.7 %collective-permute-done.9 = f32[32,256]{1,0:T(8,128)S(1)} collective-permute-done((f32[32,256]{1,0:T(8,128)S(1)}, f32[32,256]{1,0:T(8,128)S(1)}, u32[]{:S(2)}, u32[]{:S(2)}) %collective-permute-start.9) | collective-permute-done | bytes 32800 | tf_op jit(solution)/shard_map/ppermute | solution.py:158
  120.2 1.9 %scatter_fusion.1 = bf16[64,4,256]{2,1,0:T(4,128)(2,1)} fusion(bf16[64,4,256]{2,1,0:T(4,128)(2,1)} %broadcast.418, s32[8]{0:T(128)S(1)} %copy-done.27, bf16[8,4,256]{2,1,0:T(4,128)(2,1)S(1)} %fusion.98), kind=kCustom, calls=%fused_computation.4 | custom fusion | bytes 49184 | tf_op jit(solution)/shard_map/scatter | solution.py:347
  122.1 12.6 %all-to-all-start.1 = ((bf16[64,4,256]{2,1,0:T(4,128)(2,1)}), bf16[64,4,256]{2,1,0:T(4,128)(2,1)S(1)}, u32[]{:S(2)}, u32[]{:S(2)}) async-start(bf16[64,4,256]{2,1,0:T(4,128)(2,1)} %scatter_fusion.1), calls=%async_computation.1 | async-start | bytes 262144 | tf_op jit(solution)/shard_map/all_to_all | solution.py:349
  134.8 12.5 %all-to-all-done.1 = bf16[64,4,256]{2,1,0:T(4,128)(2,1)S(1)} async-done(((bf16[64,4,256]{2,1,0:T(4,128)(2,1)}), bf16[64,4,256]{2,1,0:T(4,128)(2,1)S(1)}, u32[]{:S(2)}, u32[]{:S(2)}) %all-to-all-start.1) | async-done | bytes 131104 | tf_op jit(solution)/shard_map/all_to_all | solution.py:349
  (230 shorter events, 29.0 us)
Async XLA Ops:
  0.0 72.7 %copy-start = (bf16[1,256,1024]{2,1,0:T(8,128)(2,1)S(1)}, bf16[1,256,1024]{2,1,0:T(8,128)(2,1)}, u32[]{:S(2)}) copy-start(bf16[1,256,1024]{2,1,0:T(8,128)(2,1)} %param.32) | copy-start | bytes 1572868
  0.0 51.0 %copy-start.26 = (f32[1,256]{1,0:T(1,128)S(1)}, f32[1,256]{1,0:T(1,128)}, u32[]{:S(2)}) copy-start(f32[1,256]{1,0:T(1,128)} %param.38) | copy-start | bytes 3076
  0.0 51.0 %copy-start.11 = (bf16[1,96,256]{2,1,0:T(8,128)(2,1)S(1)}, bf16[1,96,256]{2,1,0:T(8,128)(2,1)}, u32[]{:S(2)}) copy-start(bf16[1,96,256]{2,1,0:T(8,128)(2,1)} %param.36) | copy-start | bytes 147460
  1.1 21.0 %copy-start.24 = (s32[8]{0:T(128)}, s32[8]{0:T(128)S(1)}, u32[]{:S(2)}) copy-start(s32[8]{0:T(128)S(1)} %convert_reduce_fusion) | copy-start | bytes 100
  3.8 31.8 %all-to-all-start = ((bf16[64,4,256]{2,1,0:T(4,128)(2,1)}), bf16[64,4,256]{2,1,0:T(4,128)(2,1)S(1)}, u32[]{:S(2)}, u32[]{:S(2)}) async-start(bf16[64,4,256]{2,1,0:T(4,128)(2,1)} %scatter_fusion), calls=%async_computation | async-start | bytes 262144 | tf_op jit(solution)/shard_map/all_to_all | solution.py:343
  21.9 29.6 %copy-start.1 = (bf16[1,1024,256]{2,1,0:T(8,128)(2,1)S(1)}, bf16[1,1024,256]{2,1,0:T(8,128)(2,1)}, u32[]{:S(2)}) copy-start(bf16[1,1024,256]{2,1,0:T(8,128)(2,1)} %param.30) | copy-start | bytes 1572868
  21.9 29.6 %copy-start.16 = (f32[1,256]{1,0:T(1,128)S(1)}, f32[1,256]{1,0:T(1,128)}, u32[]{:S(2)}) copy-start(f32[1,256]{1,0:T(1,128)} %param.40) | copy-start | bytes 3076
  21.9 29.6 %copy-start.17 = (f32[1,256]{1,0:T(1,128)S(1)}, f32[1,256]{1,0:T(1,128)}, u32[]{:S(2)}) copy-start(f32[1,256]{1,0:T(1,128)} %param.39) | copy-start | bytes 3076
  35.5 15.5 %copy-start.12 = (f32[1,1,1024]{2,1,0:T(1,128)}, f32[1,1,1024]{2,1,0:T(1,128)S(1)}, u32[]{:S(2)}) copy-start(f32[1,1,1024]{2,1,0:T(1,128)S(1)} %get-tuple-element.42) | copy-start | bytes 12292
  35.5 15.5 %copy-start.13 = (f32[1,1,1024]{2,1,0:T(1,128)}, f32[1,1,1024]{2,1,0:T(1,128)S(1)}, u32[]{:S(2)}) copy-start(f32[1,1,1024]{2,1,0:T(1,128)S(1)} %get-tuple-element.44) | copy-start | bytes 12292
  35.6 15.5 %copy-start.14 = (f32[1,1,1024]{2,1,0:T(1,128)}, f32[1,1,1024]{2,1,0:T(1,128)S(1)}, u32[]{:S(2)}) copy-start(f32[1,1,1024]{2,1,0:T(1,128)S(1)} %get-tuple-element.40) | copy-start | bytes 12292
  35.6 16.5 %copy-start.15 = (f32[1,1,1024]{2,1,0:T(1,128)}, f32[1,1,1024]{2,1,0:T(1,128)S(1)}, u32[]{:S(2)}) copy-start(f32[1,1,1024]{2,1,0:T(1,128)S(1)} %get-tuple-element.41) | copy-start | bytes 12292
  36.3 10.3 %collective-permute-start = (bf16[59392]{0:T(1024)(128)(2,1)S(1)}, bf16[59392]{0:T(1024)(128)(2,1)S(1)}, u32[]{:S(2)}, u32[]{:S(2)}) collective-permute-start(bf16[59392]{0:T(1024)(128)(2,1)S(1)} %constant_dynamic-update-slice_fusion.23), channel_id=1, source_target_pairs={{0,3},{1,0},{2,1},{3,2},{4,7},{5,4},{6,5},{7,6},{8,11},{9,8},{10,9... | collective-permute-start | bytes 356360 | tf_op jit(solution)/shard_map/ppermute | solution.py:147
  39.1 8.2 %collective-permute-start.1 = (bf16[59392]{0:T(1024)(128)(2,1)S(1)}, bf16[59392]{0:T(1024)(128)(2,1)S(1)}, u32[]{:S(2)}, u32[]{:S(2)}) collective-permute-start(bf16[59392]{0:T(1024)(128)(2,1)S(1)} %constant_dynamic-update-slice_fusion.23), channel_id=1, source_target_pairs={{0,2},{1,3},{2,0},{3,1},{4,6},{5,7},{6,4},{7,5},{8,10},{9,11},{10,... | collective-permute-start | bytes 356360 | tf_op jit(solution)/shard_map/ppermute | solution.py:147
  42.1 7.5 %collective-permute-start.2 = (bf16[59392]{0:T(1024)(128)(2,1)S(1)}, bf16[59392]{0:T(1024)(128)(2,1)S(1)}, u32[]{:S(2)}, u32[]{:S(2)}) collective-permute-start(bf16[59392]{0:T(1024)(128)(2,1)S(1)} %constant_dynamic-update-slice_fusion.23), channel_id=1, source_target_pairs={{0,1},{1,2},{2,3},{3,0},{4,5},{5,6},{6,7},{7,4},{8,9},{9,10},{10,1... | collective-permute-start | bytes 356360 | tf_op jit(solution)/shard_map/ppermute | solution.py:147
  68.5 3.8 %copy-start.20 = (f32[4,64]{1,0:T(4,128)S(1)}, f32[4,64]{1,0:T(4,128)}, u32[]{:S(2)}) copy-start(f32[4,64]{1,0:T(4,128)} %mul.257) | copy-start | bytes 3076
  68.5 3.8 %copy-start.22 = (f32[4,64]{1,0:T(4,128)S(1)}, f32[4,64]{1,0:T(4,128)}, u32[]{:S(2)}) copy-start(f32[4,64]{1,0:T(4,128)} %mul.261) | copy-start | bytes 3076
  68.5 11.8 %copy-start.25 = (s32[8]{0:T(128)S(1)}, s32[8]{0:T(128)}, u32[]{:S(2)}) copy-start(s32[8]{0:T(128)} %copy-done.24) | copy-start | bytes 100
  68.5 14.4 %copy-start.6 = (bf16[32,256]{1,0:T(8,128)(2,1)S(1)}, bf16[32,256]{1,0:T(8,128)(2,1)}, u32[]{:S(2)}) copy-start(bf16[32,256]{1,0:T(8,128)(2,1)} %copy-done.5) | copy-start | bytes 49156
  68.5 14.4 %copy-start.8 = (bf16[32,256]{1,0:T(8,128)(2,1)S(1)}, bf16[32,256]{1,0:T(8,128)(2,1)}, u32[]{:S(2)}) copy-start(bf16[32,256]{1,0:T(8,128)(2,1)} %copy-done.7) | copy-start | bytes 49156
  68.5 14.4 %copy-start.10 = (bf16[32,256]{1,0:T(8,128)(2,1)S(1)}, bf16[32,256]{1,0:T(8,128)(2,1)}, u32[]{:S(2)}) copy-start(bf16[32,256]{1,0:T(8,128)(2,1)} %copy-done.9) | copy-start | bytes 49156
  72.9 7.4 %collective-permute-start.3 = (f32[32,1024]{1,0:T(8,128)S(1)}, f32[32,1024]{1,0:T(8,128)S(1)}, u32[]{:S(2)}, u32[]{:S(2)}) collective-permute-start(f32[32,1024]{1,0:T(8,128)S(1)} %fusion.22), channel_id=1, source_target_pairs={{0,256},{1,257},{2,258},{3,259},{4,260},{5,261},{6,262},{7,263},{8... | collective-permute-start | bytes 393224 | tf_op jit(solution)/shard_map/ppermute | solution.py:166
  74.2 6.1 %collective-permute-start.4 = (f32[32,1024]{1,0:T(8,128)S(1)}, f32[32,1024]{1,0:T(8,128)S(1)}, u32[]{:S(2)}, u32[]{:S(2)}) collective-permute-start(f32[32,1024]{1,0:T(8,128)S(1)} %fusion.22), channel_id=1, source_target_pairs={{0,257},{1,258},{2,259},{3,256},{4,261},{5,262},{6,263},{7,260},{8... | collective-permute-start | bytes 393224 | tf_op jit(solution)/shard_map/ppermute | solution.py:166
  77.5 3.8 %collective-permute-start.5 = (f32[32,1024]{1,0:T(8,128)S(1)}, f32[32,1024]{1,0:T(8,128)S(1)}, u32[]{:S(2)}, u32[]{:S(2)}) collective-permute-start(f32[32,1024]{1,0:T(8,128)S(1)} %fusion.22), channel_id=1, source_target_pairs={{0,258},{1,259},{2,256},{3,257},{4,262},{5,263},{6,260},{7,261},{8... | collective-permute-start | bytes 393224 | tf_op jit(solution)/shard_map/ppermute | solution.py:166
  78.8 3.9 %collective-permute-start.6 = (f32[32,1024]{1,0:T(8,128)S(1)}, f32[32,1024]{1,0:T(8,128)S(1)}, u32[]{:S(2)}, u32[]{:S(2)}) collective-permute-start(f32[32,1024]{1,0:T(8,128)S(1)} %fusion.22), channel_id=1, source_target_pairs={{0,259},{1,256},{2,257},{3,258},{4,263},{5,260},{6,261},{7,262},{8... | collective-permute-start | bytes 393224 | tf_op jit(solution)/shard_map/ppermute | solution.py:166
  100.7 19.5 %copy-start.27 = (s32[8]{0:T(128)S(1)}, s32[8]{0:T(128)}, u32[]{:S(2)}) copy-start(s32[8]{0:T(128)} %fusion.106) | copy-start | bytes 100
  100.7 34.0 %copy-start.28 = (s32[8]{0:T(128)S(1)}, s32[8]{0:T(128)}, u32[]{:S(2)}) copy-start(s32[8]{0:T(128)} %param.24) | copy-start | bytes 100
  105.1 10.6 %collective-permute-start.10 = (f32[32,256]{1,0:T(8,128)S(1)}, f32[32,256]{1,0:T(8,128)S(1)}, u32[]{:S(2)}, u32[]{:S(2)}) collective-permute-start(f32[32,256]{1,0:T(8,128)S(1)} %get-tuple-element.22), channel_id=1, source_target_pairs={{0,3},{1,0},{2,1},{3,2},{4,7},{5,4},{6,5},{7,6},{8,11},{9,8},{10,9... | collective-permute-start | bytes 98312 | tf_op jit(solution)/shard_map/ppermute | solution.py:158
  108.4 7.2 %collective-permute-start.8 = (f32[32,256]{1,0:T(8,128)S(1)}, f32[32,256]{1,0:T(8,128)S(1)}, u32[]{:S(2)}, u32[]{:S(2)}) collective-permute-start(f32[32,256]{1,0:T(8,128)S(1)} %get-tuple-element.21), channel_id=1, source_target_pairs={{0,1},{1,2},{2,3},{3,0},{4,5},{5,6},{6,7},{7,4},{8,9},{9,10},{10,1... | collective-permute-start | bytes 98312 | tf_op jit(solution)/shard_map/ppermute | solution.py:158
  112.1 7.3 %collective-permute-start.9 = (f32[32,256]{1,0:T(8,128)S(1)}, f32[32,256]{1,0:T(8,128)S(1)}, u32[]{:S(2)}, u32[]{:S(2)}) collective-permute-start(f32[32,256]{1,0:T(8,128)S(1)} %get-tuple-element.23), channel_id=1, source_target_pairs={{0,2},{1,3},{2,0},{3,1},{4,6},{5,7},{6,4},{7,5},{8,10},{9,11},{10,... | collective-permute-start | bytes 98312 | tf_op jit(solution)/shard_map/ppermute | solution.py:158
  114.4 5.1 %collective-permute-start.7 = (bf16[8,4,256]{2,1,0:T(4,128)(2,1)S(1)}, bf16[8,4,256]{2,1,0:T(4,128)(2,1)S(1)}, u32[]{:S(2)}, u32[]{:S(2)}) collective-permute-start(bf16[8,4,256]{2,1,0:T(4,128)(2,1)S(1)} %constant_dynamic-slice_fusion.2), channel_id=1, source_target_pairs={{256,0},{257,1},{258,2},{259,3},{260,4},{261,5},{262,6},{263,7},{2... | collective-permute-start | bytes 49160 | tf_op jit(solution)/shard_map/ppermute | solution.py:173
  122.1 25.2 %all-to-all-start.1 = ((bf16[64,4,256]{2,1,0:T(4,128)(2,1)}), bf16[64,4,256]{2,1,0:T(4,128)(2,1)S(1)}, u32[]{:S(2)}, u32[]{:S(2)}) async-start(bf16[64,4,256]{2,1,0:T(4,128)(2,1)} %scatter_fusion.1), calls=%async_computation.1 | async-start | bytes 262144 | tf_op jit(solution)/shard_map/all_to_all | solution.py:349
  (10 other events, 25.0 us)

commit v4 on v3

--- a/solution.py
+++ b/solution.py
@@ -142,20 +142,19 @@
 
 def gather_heads(block):
     n = lax.axis_size("head")
-    pieces = [block]
-    for k in range(1, n):
-        pieces.append(lax.ppermute(block, "head", [(i, (i + k) % n) for i in range(n)]))
-    return in_device_order(pieces)
+    copies = jnp.broadcast_to(block[None], (n,) + block.shape)
+    arrived = lax.all_to_all(copies, "head", split_axis=0, concat_axis=0, tiled=True)
+    return [arrived[d] for d in range(n)]
 
 
 def scatter_heads(partial):
     n = lax.axis_size("head")
-    me = lax.axis_index("head")
-    width = partial.shape[1] // n
-    total = lax.dynamic_slice_in_dim(partial, me * width, width, 1)
-    for k in range(1, n):
-        chunk = lax.dynamic_slice_in_dim(partial, ((me + k) % n) * width, width, 1)
-        total = total + lax.ppermute(chunk, "head", [(i, (i + k) % n) for i in range(n)])
+    rows, columns = partial.shape
+    chunks = jnp.transpose(partial.reshape(rows, n, columns // n), (1, 0, 2))
+    arrived = lax.all_to_all(chunks, "head", split_axis=0, concat_axis=0, tiled=True)
+    total = arrived[0]
+    for d in range(1, n):
+        total = total + arrived[d]
     return total
 
 

time: 150 us -> 156 us (1.040)
  starting transfers between devices: 56.9 us -> 45.9 us
  local copies, waits for them, and re-layouts: 29.1 us -> 35.8 us
  other arithmetic: 17 us -> 22.8 us
  matrix products: 6.53 us -> 8.62 us
    ppermute x6 -> x0, starting transfers between devices: 19 us -> none  [the longest x3 9.76 us: gather_heads(): lax.ppermute(block, 'head', [(i, (i + k) % n) for i in range(n)])]
    all_to_all x0 -> x2, starting transfers between devices: none -> 10.2 us  [the longest x1 5.4 us: scatter_heads(): lax.all_to_all(chunks, 'head', split_axis=0, concat_axis=0, tiled=True)]
    all_to_all x0 -> x2, waiting for transfers between devices: none -> 8.64 us  [the longest x1 5.48 us: gather_heads(): lax.all_to_all(copies, 'head', split_axis=0, concat_axis=0, tiled=True)]
    ppermute x6 -> x0, waiting for transfers between devices: 6.73 us -> none  [the longest x3 3.75 us: scatter_heads(): lax.ppermute(chunk, 'head', [(i, (i + k) % n) for i in range(n)])]
    broadcast_in_dim x0 -> x1, other arithmetic: none -> 3.7 us  [gather_heads(): copies = jnp.broadcast_to(block[None], (n,) + block.shape)]
    slice x22 -> x6, local copies, waits for them, and re-layouts: 0.22 us -> 2.68 us  [joined(): piece[cuts[index]:cuts[index + 1]].reshape(shape)]
    unnamed x85 -> x80, local copies, waits for them, and re-layouts: 7.42 us -> 9.41 us
    ppermute x4, starting transfers between devices: 7.36 us -> 5.75 us  [hand_over(): lax.ppermute(partial, ('section', 'head'), [(i, n + (i + k) % n) for i in...]
  transfers between devices with their start and end apart: 13 -> 9, of which waited for: 6 -> 5; matrix products, arithmetic and copies ran while one was open for 10% -> 11% of each run, Pallas kernels for 0% -> 0%
where the time goes in v4:
time: 156 us; the launch traced here: 154 us
  starting transfers between devices  45.9 us (29%)
  local copies, waits for them, and re-layouts  35.8 us (23%)
  waiting for transfers between devices  23.1 us (15%)
  other arithmetic  22.8 us (15%)
  Pallas kernels  16.1 us (10%)
  matrix products  8.62 us (6%)
    all_to_all x1, starting transfers between devices, body(): lax.all_to_all(outgoing, 'req', split_axis=0, concat_axis=0, tiled=True)  16.6 us
    pallas_call x2, Pallas kernels, run_recurrence(): pl.pallas_call(recurrence_kernel, out_shape=jax.ShapeDtypeStruct((steps,...  16.1 us
    all_to_all x1, waiting for transfers between devices, body(): lax.all_to_all(going_back, 'req', split_axis=0, concat_axis=0, tiled=True)  12.8 us
    all_to_all x1, starting transfers between devices, body(): lax.all_to_all(going_back, 'req', split_axis=0, concat_axis=0, tiled=True)  12.1 us
    unnamed x80, local copies, waits for them, and re-layouts  9.41 us
    pallas_call x2, other arithmetic, run_recurrence(): pl.pallas_call(recurrence_kernel, out_shape=jax.ShapeDtypeStruct((steps,...  6.75 us
    ppermute x4, starting transfers between devices, hand_over(): lax.ppermute(partial, ('section', 'head'), [(i, n + (i + k) % n) for i in...  5.75 us
    all_to_all x1, waiting for transfers between devices, gather_heads(): lax.all_to_all(copies, 'head', split_axis=0, concat_axis=0, tiled=True)  5.48 us
  transfers between devices with their start and end apart: 9, of which 5 were waited for; matrix products, arithmetic and copies ran while one was open for 11% of the time, Pallas kernels for 0%

profile of v4, /device:TPU:6, one launch (start us, length us, event | category | flops | bytes accessed | tf_op | source)
XLA Modules:
  0.0 153.5 jit_solution(8237587082522191892)
XLA Ops:
  1.8 2.0 %scatter_fusion = bf16[64,4,256]{2,1,0:T(4,128)(2,1)} fusion(bf16[64,4,256]{2,1,0:T(4,128)(2,1)} %broadcast.407.clone, s32[8]{0:T(128)S(1)} %fusion.105, bf16[8,4,256]{2,1,0:T(4,128)(2,1)} %param.23), kind=kCustom, calls=%fused_computation.3 | custom fusion | bytes 49184 | tf_op jit(solution)/shard_map/scatter | solution.py:340
  3.7 16.6 %all-to-all-start = ((bf16[64,4,256]{2,1,0:T(4,128)(2,1)}), bf16[64,4,256]{2,1,0:T(4,128)(2,1)S(1)}, u32[]{:S(2)}, u32[]{:S(2)}) async-start(bf16[64,4,256]{2,1,0:T(4,128)(2,1)} %scatter_fusion), calls=%async_computation | async-start | bytes 262144 | tf_op jit(solution)/shard_map/all_to_all | solution.py:342
  24.7 1.2 copy.147
  25.9 1.2 copy.150
  27.7 1.3 reduce.47
  29.7 1.3 reduce.48
  31.7 1.3 reduce.49
  33.7 1.2 copy.183
  36.9 3.7 %reduce.50 = bf16[4,59392]{1,0:T(4,128)(2,1)S(1)} reduce(bf16[4,1,59392]{2,1,0:T(2,128)(2,1)S(1)} %broadcast_in_dim.49, bf16[]{:T(256)} %broadcast.530), dimensions={1}, to_apply=%broadcast_in_dim.49.reduce_sub_computation | reduce | bytes 950274 | tf_op jit(solution)/shard_map/broadcast_in_dim | solution.py:145
  41.6 4.8 %all-to-all-start.1 = ((bf16[4,2,29696]{2,1,0:T(2,128)(2,1)}), bf16[4,2,29696]{2,1,0:T(2,128)(2,1)S(1)}, u32[]{:S(2)}, u32[]{:S(2)}) async-start(bf16[4,2,29696]{2,1,0:T(2,128)(2,1)} %reshape.806), calls=%async_computation.1 | async-start | bytes 950272 | tf_op jit(solution)/shard_map/all_to_all | solution.py:146
  47.5 5.5 %all-to-all-done.1 = bf16[4,2,29696]{2,1,0:T(2,128)(2,1)S(1)} async-done(((bf16[4,2,29696]{2,1,0:T(2,128)(2,1)}), bf16[4,2,29696]{2,1,0:T(2,128)(2,1)S(1)}, u32[]{:S(2)}, u32[]{:S(2)}) %all-to-all-start.1) | async-done | bytes 475168 | tf_op jit(solution)/shard_map/all_to_all | solution.py:146
  54.4 1.1 slice_reduce_fusion.2
  55.6 1.1 slice_reduce_fusion
  60.3 1.5 add_multiply_fusion.1
  63.3 1.3 fusion.78
  67.6 2.7 %copy.153.content_ref = f32[4,32,64,1]{3,2,1,0:T(8,128)} copy(f32[4,32,64,1]{2,1,0,3:T(8,128)S(1)} %bitcast.205) | data formatting | bytes 65536 | tf_op jit(solution)/shard_map/reshape;reshape | solution.py:98
  71.1 8.0 %shard_map.199 = f32[4,32,64,1]{3,2,1,0:T(8,128)} custom-call(f32[32,64,64]{2,1,0:T(8,128)} %bitcast.192, f32[4,5,32,1,64]{4,3,2,1,0:T(1,128)} %copy-done.2, f32[4,32,64,1]{3,2,1,0:T(8,128)} %copy.153.content_ref), custom_call_target="tpu_custom_call" | custom-call | tf_op jit(solution)/shard_map/pallas_call | solution.py:27
  79.2 3.4 %reduce.20 = f32[4,32,64]{2,1,0:T(8,128)S(1)} reduce(f32[4,32,64,1]{3,2,1,0:T(8,128)} %shard_map.199, f32[]{:T(128)} %constant.162), dimensions={3}, to_apply=%pallas_call.6.reduce_sub_computation | reduce | bytes 65540 | tf_op jit(solution)/shard_map/pallas_call | solution.py:27
  84.2 1.3 collective-permute-start
  85.5 1.6 %collective-permute-start.1 = (f32[32,1024]{1,0:T(8,128)S(1)}, f32[32,1024]{1,0:T(8,128)S(1)}, u32[]{:S(2)}, u32[]{:S(2)}) collective-permute-start(f32[32,1024]{1,0:T(8,128)S(1)} %fusion.20), channel_id=1, source_target_pairs={{0,257},{1,258},{2,259},{3,256},{4,261},{5,262},{6,263},{7,260},{8... | collective-permute-start | bytes 393224 | tf_op jit(solution)/shard_map/ppermute | solution.py:165
  87.2 1.3 collective-permute-start.2
  88.5 1.5 collective-permute-start.3
  91.0 1.4 collective-permute-done.3
  97.0 2.7 %copy.166.content_ref = f32[4,32,64,1]{3,2,1,0:T(8,128)} copy(f32[4,32,64,1]{2,1,0,3:T(8,128)S(1)} %bitcast.206) | data formatting | bytes 65536 | tf_op jit(solution)/shard_map/reshape;reshape | solution.py:98
  101.6 8.0 %shard_map.200 = f32[4,32,64,1]{3,2,1,0:T(8,128)} custom-call(f32[32,64,64]{2,1,0:T(8,128)} %bitcast.193, f32[4,5,32,1,64]{4,3,2,1,0:T(1,128)} %copy-done.3, f32[4,32,64,1]{3,2,1,0:T(8,128)} %copy.166.content_ref), custom_call_target="tpu_custom_call" | custom-call | tf_op jit(solution)/shard_map/pallas_call | solution.py:27
  109.6 3.3 %reduce.24 = f32[4,32,64]{2,1,0:T(8,128)S(1)} reduce(f32[4,32,64,1]{3,2,1,0:T(8,128)} %shard_map.200, f32[]{:T(128)} %constant.162), dimensions={3}, to_apply=%pallas_call.7.reduce_sub_computation | reduce | bytes 65540 | tf_op jit(solution)/shard_map/pallas_call | solution.py:27
  114.7 5.4 %all-to-all-start.2 = ((f32[4,32,256]{2,1,0:T(8,128)}), f32[4,32,256]{2,1,0:T(8,128)S(1)}, u32[]{:S(2)}, u32[]{:S(2)}) async-start(f32[4,32,256]{2,1,0:T(8,128)} %convolution_bitcast_fusion), calls=%async_computation.2 | async-start | bytes 262144 | tf_op jit(solution)/shard_map/all_to_all | solution.py:154
  120.1 1.3 collective-permute-start.4
  121.4 3.2 %all-to-all-done.2 = f32[4,32,256]{2,1,0:T(8,128)S(1)} async-done(((f32[4,32,256]{2,1,0:T(8,128)}), f32[4,32,256]{2,1,0:T(8,128)S(1)}, u32[]{:S(2)}, u32[]{:S(2)}) %all-to-all-start.2) | async-done | bytes 131104 | tf_op jit(solution)/shard_map/all_to_all | solution.py:154
  125.3 1.9 %scatter_fusion.1 = bf16[64,4,256]{2,1,0:T(4,128)(2,1)} fusion(bf16[64,4,256]{2,1,0:T(4,128)(2,1)} %broadcast.407, s32[8]{0:T(128)S(1)} %copy-done.25, bf16[8,4,256]{2,1,0:T(4,128)(2,1)S(1)} %fusion.96), kind=kCustom, calls=%fused_computation.4 | custom fusion | bytes 49184 | tf_op jit(solution)/shard_map/scatter | solution.py:346
  127.2 12.1 %all-to-all-start.3 = ((bf16[64,4,256]{2,1,0:T(4,128)(2,1)}), bf16[64,4,256]{2,1,0:T(4,128)(2,1)S(1)}, u32[]{:S(2)}, u32[]{:S(2)}) async-start(bf16[64,4,256]{2,1,0:T(4,128)(2,1)} %scatter_fusion.1), calls=%async_computation.3 | async-start | bytes 262144 | tf_op jit(solution)/shard_map/all_to_all | solution.py:348
  139.4 12.8 %all-to-all-done.3 = bf16[64,4,256]{2,1,0:T(4,128)(2,1)S(1)} async-done(((bf16[64,4,256]{2,1,0:T(4,128)(2,1)}), bf16[64,4,256]{2,1,0:T(4,128)(2,1)S(1)}, u32[]{:S(2)}, u32[]{:S(2)}) %all-to-all-start.3) | async-done | bytes 131104 | tf_op jit(solution)/shard_map/all_to_all | solution.py:348
  (216 shorter events, 35.0 us)
Async XLA Ops:
  0.0 60.3 %copy-start = (bf16[1,1024,256]{2,1,0:T(8,128)(2,1)S(1)}, bf16[1,1024,256]{2,1,0:T(8,128)(2,1)}, u32[]{:S(2)}) copy-start(bf16[1,1024,256]{2,1,0:T(8,128)(2,1)} %param.30) | copy-start | bytes 1572868
  0.8 21.0 %copy-start.8 = (s32[64,8]{1,0:T(8,128)}, s32[64,8]{1,0:T(8,128)S(1)}, u32[]{:S(2)}) copy-start(s32[64,8]{1,0:T(8,128)S(1)} %reshape.668) | copy-start | bytes 6148
  1.1 20.2 %copy-start.23 = (s32[8]{0:T(128)}, s32[8]{0:T(128)S(1)}, u32[]{:S(2)}) copy-start(s32[8]{0:T(128)S(1)} %convert_reduce_fusion) | copy-start | bytes 100
  3.7 31.4 %all-to-all-start = ((bf16[64,4,256]{2,1,0:T(4,128)(2,1)}), bf16[64,4,256]{2,1,0:T(4,128)(2,1)S(1)}, u32[]{:S(2)}, u32[]{:S(2)}) async-start(bf16[64,4,256]{2,1,0:T(4,128)(2,1)} %scatter_fusion), calls=%async_computation | async-start | bytes 262144 | tf_op jit(solution)/shard_map/all_to_all | solution.py:342
  21.9 25.1 %copy-start.18 = (bf16[1,5,1024]{2,1,0:T(8,128)(2,1)S(1)}, bf16[1,5,1024]{2,1,0:T(8,128)(2,1)}, u32[]{:S(2)}) copy-start(bf16[1,5,1024]{2,1,0:T(8,128)(2,1)} %param.28) | copy-start | bytes 30724
  41.6 11.4 %all-to-all-start.1 = ((bf16[4,2,29696]{2,1,0:T(2,128)(2,1)}), bf16[4,2,29696]{2,1,0:T(2,128)(2,1)S(1)}, u32[]{:S(2)}, u32[]{:S(2)}) async-start(bf16[4,2,29696]{2,1,0:T(2,128)(2,1)} %reshape.806), calls=%async_computation.1 | async-start | bytes 950272 | tf_op jit(solution)/shard_map/all_to_all | solution.py:146
  57.1 5.7 %copy-start.10 = (bf16[32,256]{1,0:T(8,128)(2,1)}, bf16[32,256]{1,0:T(8,128)(2,1)S(1)}, u32[]{:S(2)}) copy-start(bf16[32,256]{1,0:T(8,128)(2,1)S(1)} %concatenate.54) | copy-start | bytes 49156
  57.2 3.1 %copy-start.12 = (bf16[32,256]{1,0:T(8,128)(2,1)}, bf16[32,256]{1,0:T(8,128)(2,1)S(1)}, u32[]{:S(2)}) copy-start(bf16[32,256]{1,0:T(8,128)(2,1)S(1)} %concatenate.55) | copy-start | bytes 49156
  57.3 5.5 %copy-start.14 = (bf16[32,256]{1,0:T(8,128)(2,1)}, bf16[32,256]{1,0:T(8,128)(2,1)S(1)}, u32[]{:S(2)}) copy-start(bf16[32,256]{1,0:T(8,128)(2,1)S(1)} %concatenate.52) | copy-start | bytes 49156
  57.3 3.0 %copy-start.16 = (bf16[32,256]{1,0:T(8,128)(2,1)}, bf16[32,256]{1,0:T(8,128)(2,1)S(1)}, u32[]{:S(2)}) copy-start(bf16[32,256]{1,0:T(8,128)(2,1)S(1)} %concatenate.53) | copy-start | bytes 49156
  58.1 4.8 %copy-start.9 = (f32[32,1024]{1,0:T(8,128)}, f32[32,1024]{1,0:T(8,128)S(1)}, u32[]{:S(2)}) copy-start(f32[32,1024]{1,0:T(8,128)S(1)} %reshape.705) | copy-start | bytes 393220
  63.3 7.0 %copy-start.4 = (f32[4,8,4,64]{3,2,1,0:T(4,128)S(1)}, f32[4,8,4,64]{3,2,1,0:T(4,128)}, u32[]{:S(2)}) copy-start(f32[4,8,4,64]{3,2,1,0:T(4,128)} %copy.144) | copy-start | bytes 98308
  79.2 3.7 %copy-start.6 = (f32[8,4,4,64]{3,2,1,0:T(4,128)S(1)}, f32[8,4,4,64]{3,2,1,0:T(4,128)}, u32[]{:S(2)}) copy-start(f32[8,4,4,64]{3,2,1,0:T(4,128)} %copy-done.5) | copy-start | bytes 98308
  79.2 4.9 %copy-start.1 = (bf16[1,256,1024]{2,1,0:T(8,128)(2,1)S(1)}, bf16[1,256,1024]{2,1,0:T(8,128)(2,1)}, u32[]{:S(2)}) copy-start(bf16[1,256,1024]{2,1,0:T(8,128)(2,1)} %param.32) | copy-start | bytes 1572868
  79.2 13.5 %copy-start.11 = (bf16[32,256]{1,0:T(8,128)(2,1)S(1)}, bf16[32,256]{1,0:T(8,128)(2,1)}, u32[]{:S(2)}) copy-start(bf16[32,256]{1,0:T(8,128)(2,1)} %copy-done.10) | copy-start | bytes 49156
  79.2 13.5 %copy-start.13 = (bf16[32,256]{1,0:T(8,128)(2,1)S(1)}, bf16[32,256]{1,0:T(8,128)(2,1)}, u32[]{:S(2)}) copy-start(bf16[32,256]{1,0:T(8,128)(2,1)} %copy-done.12) | copy-start | bytes 49156
  79.2 13.5 %copy-start.15 = (bf16[32,256]{1,0:T(8,128)(2,1)S(1)}, bf16[32,256]{1,0:T(8,128)(2,1)}, u32[]{:S(2)}) copy-start(bf16[32,256]{1,0:T(8,128)(2,1)} %copy-done.14) | copy-start | bytes 49156
  83.9 12.3 %copy-start.17 = (bf16[1,96,256]{2,1,0:T(8,128)(2,1)S(1)}, bf16[1,96,256]{2,1,0:T(8,128)(2,1)}, u32[]{:S(2)}) copy-start(bf16[1,96,256]{2,1,0:T(8,128)(2,1)} %param.34) | copy-start | bytes 147460
  83.9 12.3 %copy-start.19 = (f32[1,1,1024]{2,1,0:T(1,128)S(1)}, f32[1,1,1024]{2,1,0:T(1,128)}, u32[]{:S(2)}) copy-start(f32[1,1,1024]{2,1,0:T(1,128)} %get-tuple-element.40) | copy-start | bytes 12292
  83.9 12.3 %copy-start.24 = (f32[1,256]{1,0:T(1,128)S(1)}, f32[1,256]{1,0:T(1,128)}, u32[]{:S(2)}) copy-start(f32[1,256]{1,0:T(1,128)} %param.37) | copy-start | bytes 3076
  84.2 6.5 %collective-permute-start = (f32[32,1024]{1,0:T(8,128)S(1)}, f32[32,1024]{1,0:T(8,128)S(1)}, u32[]{:S(2)}, u32[]{:S(2)}) collective-permute-start(f32[32,1024]{1,0:T(8,128)S(1)} %fusion.20), channel_id=1, source_target_pairs={{0,256},{1,257},{2,258},{3,259},{4,260},{5,261},{6,262},{7,263},{8... | collective-permute-start | bytes 393224 | tf_op jit(solution)/shard_map/ppermute | solution.py:165
  85.5 5.2 %collective-permute-start.1 = (f32[32,1024]{1,0:T(8,128)S(1)}, f32[32,1024]{1,0:T(8,128)S(1)}, u32[]{:S(2)}, u32[]{:S(2)}) collective-permute-start(f32[32,1024]{1,0:T(8,128)S(1)} %fusion.20), channel_id=1, source_target_pairs={{0,257},{1,258},{2,259},{3,256},{4,261},{5,262},{6,263},{7,260},{8... | collective-permute-start | bytes 393224 | tf_op jit(solution)/shard_map/ppermute | solution.py:165
  87.2 3.8 %collective-permute-start.2 = (f32[32,1024]{1,0:T(8,128)S(1)}, f32[32,1024]{1,0:T(8,128)S(1)}, u32[]{:S(2)}, u32[]{:S(2)}) collective-permute-start(f32[32,1024]{1,0:T(8,128)S(1)} %fusion.20), channel_id=1, source_target_pairs={{0,258},{1,259},{2,256},{3,257},{4,262},{5,263},{6,260},{7,261},{8... | collective-permute-start | bytes 393224 | tf_op jit(solution)/shard_map/ppermute | solution.py:165
  88.5 3.9 %collective-permute-start.3 = (f32[32,1024]{1,0:T(8,128)S(1)}, f32[32,1024]{1,0:T(8,128)S(1)}, u32[]{:S(2)}, u32[]{:S(2)}) collective-permute-start(f32[32,1024]{1,0:T(8,128)S(1)} %fusion.20), channel_id=1, source_target_pairs={{0,259},{1,256},{2,257},{3,258},{4,263},{5,260},{6,261},{7,262},{8... | collective-permute-start | bytes 393224 | tf_op jit(solution)/shard_map/ppermute | solution.py:165
  109.6 3.7 %copy-start.20 = (f32[4,64]{1,0:T(4,128)S(1)}, f32[4,64]{1,0:T(4,128)}, u32[]{:S(2)}) copy-start(f32[4,64]{1,0:T(4,128)} %add.340) | copy-start | bytes 3076
  109.6 3.7 %copy-start.21 = (f32[4,64]{1,0:T(4,128)S(1)}, f32[4,64]{1,0:T(4,128)}, u32[]{:S(2)}) copy-start(f32[4,64]{1,0:T(4,128)} %mul.247) | copy-start | bytes 3076
  109.6 3.7 %copy-start.22 = (f32[4,64]{1,0:T(4,128)S(1)}, f32[4,64]{1,0:T(4,128)}, u32[]{:S(2)}) copy-start(f32[4,64]{1,0:T(4,128)} %mul.251) | copy-start | bytes 3076
  109.6 15.7 %copy-start.25 = (s32[8]{0:T(128)S(1)}, s32[8]{0:T(128)}, u32[]{:S(2)}) copy-start(s32[8]{0:T(128)} %fusion.104) | copy-start | bytes 100
  109.6 29.7 %copy-start.26 = (s32[8]{0:T(128)S(1)}, s32[8]{0:T(128)}, u32[]{:S(2)}) copy-start(s32[8]{0:T(128)} %param.24) | copy-start | bytes 100
  114.7 9.9 %all-to-all-start.2 = ((f32[4,32,256]{2,1,0:T(8,128)}), f32[4,32,256]{2,1,0:T(8,128)S(1)}, u32[]{:S(2)}, u32[]{:S(2)}) async-start(f32[4,32,256]{2,1,0:T(8,128)} %convolution_bitcast_fusion), calls=%async_computation.2 | async-start | bytes 262144 | tf_op jit(solution)/shard_map/all_to_all | solution.py:154
  120.1 4.5 %collective-permute-start.4 = (bf16[8,4,256]{2,1,0:T(4,128)(2,1)S(1)}, bf16[8,4,256]{2,1,0:T(4,128)(2,1)S(1)}, u32[]{:S(2)}, u32[]{:S(2)}) collective-permute-start(bf16[8,4,256]{2,1,0:T(4,128)(2,1)S(1)} %constant_dynamic-slice_fusion.1), channel_id=1, source_target_pairs={{256,0},{257,1},{258,2},{259,3},{260,4},{261,5},{262,6},{263,7},{2... | collective-permute-start | bytes 49160 | tf_op jit(solution)/shard_map/ppermute | solution.py:172
  127.2 25.1 %all-to-all-start.3 = ((bf16[64,4,256]{2,1,0:T(4,128)(2,1)}), bf16[64,4,256]{2,1,0:T(4,128)(2,1)S(1)}, u32[]{:S(2)}, u32[]{:S(2)}) async-start(bf16[64,4,256]{2,1,0:T(4,128)(2,1)} %scatter_fusion.1), calls=%async_computation.3 | async-start | bytes 262144 | tf_op jit(solution)/shard_map/all_to_all | solution.py:348
  (4 other events, 4.9 us)

commit v5 on v3

--- a/solution.py
+++ b/solution.py
@@ -9,24 +9,27 @@
 
 
 def recurrence_kernel(memory_ref, vector_ref, content_ref, read_ref):
-    states = memory_ref[...]
-    for position in range(vector_ref.shape[0]):
-        decay = vector_ref[position, 0]
-        normed = vector_ref[position, 1]
-        normed_learn = vector_ref[position, 2]
-        erasing = vector_ref[position, 3]
-        acceptor = vector_ref[position, 4]
-        pulled = jnp.sum(states * normed, axis=-1, keepdims=True)
-        states = states * decay - pulled * normed_learn + content_ref[position] * erasing
-        read_ref[position] = jnp.sum(states * acceptor, axis=-1, keepdims=True)
+    steps, _, blocks, _ = vector_ref.shape
+    for block in range(blocks):
+        states = memory_ref[block]
+        for position in range(steps):
+            row = slice(block, block + 1)
+            column = slice(position * blocks + block, position * blocks + block + 1)
+            decay = vector_ref[position, 0, row, :]
+            normed = vector_ref[position, 1, row, :]
+            normed_learn = vector_ref[position, 2, row, :]
+            erasing = vector_ref[position, 3, row, :]
+            acceptor = vector_ref[position, 4, row, :]
+            content = content_ref[:, column]
+            pulled = jnp.sum(states * normed, axis=1, keepdims=True)
+            states = states * decay - pulled * normed_learn + content * erasing
+            read_ref[:, column] = jnp.sum(states * acceptor, axis=1, keepdims=True)
 
 
 def run_recurrence(starting_memory, vectors, content):
-    steps = vectors.shape[0]
-    blocks, span, _ = starting_memory.shape
     return pl.pallas_call(
         recurrence_kernel,
-        out_shape=jax.ShapeDtypeStruct((steps, blocks, span, 1), jnp.float32),
+        out_shape=jax.ShapeDtypeStruct(content.shape, jnp.float32),
         in_specs=[pl.BlockSpec(memory_space=pltpu.VMEM)] * 3,
         out_specs=pl.BlockSpec(memory_space=pltpu.VMEM),
     )(starting_memory, vectors, content)
@@ -82,7 +85,7 @@
 
     def by_step(array_in):
         return jnp.transpose(array_in, (1, 0, 2, 3)).reshape(
-            steps_count, batch_rows * stored_memory_parts, 1, subspace_span
+            steps_count, batch_rows * stored_memory_parts, subspace_span
         )
 
     vectors = jnp.stack(
@@ -95,16 +98,14 @@
         ],
         axis=1,
     )
-    content = by_step(content_part_lines).reshape(
-        steps_count, batch_rows * stored_memory_parts, subspace_span, 1
-    )
+    content = jnp.transpose(content_part_lines, (3, 1, 0, 2)).reshape(subspace_span, -1)
     read = run_recurrence(
         starting_memory.reshape(batch_rows * stored_memory_parts, subspace_span, subspace_span),
         vectors,
         content,
     )
     read_all = jnp.transpose(
-        read.reshape(steps_count, batch_rows, stored_memory_parts, subspace_span), (1, 0, 2, 3)
+        read.reshape(subspace_span, steps_count, batch_rows, stored_memory_parts), (2, 1, 3, 0)
     )
     center = read_all - jnp.mean(read_all, axis=-1, keepdims=True)
     variance = jnp.mean(center * center, axis=-1, keepdims=True)
@@ -325,13 +326,13 @@
         fading_second_lowrank.reshape(fading_second_lowrank.shape[1:]),
         adapt_first_lowrank.reshape(adapt_first_lowrank.shape[1:]),
         adapt_second_lowrank.reshape(adapt_second_lowrank.shape[1:]),
-        fading_baseline.reshape(fading_baseline.shape[1:]),
-        adapt_baseline.reshape(adapt_baseline.shape[1:]),
-        erasing_address_gains.reshape(erasing_address_gains.shape[1:]),
-        address_rate_coupling.reshape(address_rate_coupling.shape[1:]),
-        present_extra_gain.reshape(present_extra_gain.shape[1:]),
-        section_standard_gains.reshape(section_standard_gains.shape[1:]),
-        section_standard_shift_terms.reshape(section_standard_shift_terms.shape[1:]),
+        fading_baseline,
+        adapt_baseline,
+        erasing_address_gains,
+        address_rate_coupling,
+        present_extra_gain,
+        section_standard_gains,
+        section_standard_shift_terms,
     )
     states_local = memory_per_request.reshape(memory_per_request.shape[1:])
     last_local = previous_step_feature.reshape(previous_step_feature.shape[1:])

time: 150 us -> 153 us (1.020)
  Pallas kernels: 16.1 us -> 29.4 us
  other arithmetic: 17 us -> 6.9 us
  local copies, waits for them, and re-layouts: 29.1 us -> 32.5 us
  matrix products: 6.53 us -> 3.98 us
  starting transfers between devices: 56.9 us -> 54.5 us
    pallas_call x2, Pallas kernels: 16.1 us -> 29.4 us  [run_recurrence(): pl.pallas_call(recurrence_kernel, out_shape=jax.ShapeDtypeStruct(content....]
    unnamed x85 -> x149, local copies, waits for them, and re-layouts: 7.42 us -> 16.3 us
    pallas_call x2 -> x0, other arithmetic: 6.74 us -> none  [run_recurrence(): pl.pallas_call(recurrence_kernel, out_shape=jax.ShapeDtypeStruct((steps,...]
    another operation x4 -> x2, local copies, waits for them, and re-layouts: 6.82 us -> 1.38 us  [the longest x2 5.45 us: sequence_recurrence(): by_step(content_part_lines)]
    all_to_all x1, waiting for transfers between devices: 0.01 us -> 3 us  [body(): lax.all_to_all(outgoing, 'req', split_axis=0, concat_axis=0, tiled=True)]
    unnamed x4, other arithmetic: 4.1 us -> 2.08 us
    all_to_all x1, starting transfers between devices: 12.6 us -> 10.8 us  [body(): lax.all_to_all(going_back, 'req', split_axis=0, concat_axis=0, tiled=True)]
    pallas_call x0 -> x2, local copies, waits for them, and re-layouts: none -> 1.69 us  [run_recurrence(): pl.pallas_call(recurrence_kernel, out_shape=jax.ShapeDtypeStruct(content....]
  transfers between devices with their start and end apart: 13 -> 13, of which waited for: 6 -> 7; matrix products, arithmetic and copies ran while one was open for 10% -> 6% of each run, Pallas kernels for 0% -> 0%
where the time goes in v5:
time: 153 us; the launch traced here: 151 us
  starting transfers between devices  54.5 us (36%)
  local copies, waits for them, and re-layouts  32.5 us (21%)
  Pallas kernels  29.4 us (19%)
  waiting for transfers between devices  22.1 us (14%)
  other arithmetic  6.9 us (5%)
  matrix products  3.98 us (3%)
  between operations  1.59 us (1%)
    pallas_call x2, Pallas kernels, run_recurrence(): pl.pallas_call(recurrence_kernel, out_shape=jax.ShapeDtypeStruct(content....  29.4 us
    all_to_all x1, starting transfers between devices, body(): lax.all_to_all(outgoing, 'req', split_axis=0, concat_axis=0, tiled=True)  16.6 us
    unnamed x149, local copies, waits for them, and re-layouts  16.3 us
    all_to_all x1, waiting for transfers between devices, body(): lax.all_to_all(going_back, 'req', split_axis=0, concat_axis=0, tiled=True)  11.3 us
    all_to_all x1, starting transfers between devices, body(): lax.all_to_all(going_back, 'req', split_axis=0, concat_axis=0, tiled=True)  10.8 us
    ppermute x3, starting transfers between devices, gather_heads(): lax.ppermute(block, 'head', [(i, (i + k) % n) for i in range(n)])  9.76 us
    ppermute x3, starting transfers between devices, scatter_heads(): lax.ppermute(chunk, 'head', [(i, (i + k) % n) for i in range(n)])  9.27 us
    ppermute x4, starting transfers between devices, hand_over(): lax.ppermute(partial, ('section', 'head'), [(i, n + (i + k) % n) for i in...  6.74 us
  transfers between devices with their start and end apart: 13, of which 7 were waited for; matrix products, arithmetic and copies ran while one was open for 6% of the time, Pallas kernels for 0%

profile of v5, /device:TPU:6, one launch (start us, length us, event | category | flops | bytes accessed | tf_op | source)
XLA Modules:
  0.0 150.9 jit_solution(8467062279053152475)
XLA Ops:
  0.0 0.7 copy-done.36
  2.3 1.9 %scatter_fusion = bf16[64,4,256]{2,1,0:T(4,128)(2,1)} fusion(bf16[64,4,256]{2,1,0:T(4,128)(2,1)} %broadcast.418.clone, s32[8]{0:T(128)S(1)} %fusion.107, bf16[8,4,256]{2,1,0:T(4,128)(2,1)S(1)} %copy-done.35), kind=kCustom, calls=%fused_computation.3 | custom fusion | bytes 49184 | tf_op jit(solution)/shard_map/scatter | solution.py:342
  4.2 16.6 %all-to-all-start = ((bf16[64,4,256]{2,1,0:T(4,128)(2,1)}), bf16[64,4,256]{2,1,0:T(4,128)(2,1)S(1)}, u32[]{:S(2)}, u32[]{:S(2)}) async-start(bf16[64,4,256]{2,1,0:T(4,128)(2,1)} %scatter_fusion), calls=%async_computation | async-start | bytes 262144 | tf_op jit(solution)/shard_map/all_to_all | solution.py:344
  24.2 0.8 copy-done.3
  30.6 3.0 %all-to-all-done = bf16[64,4,256]{2,1,0:T(4,128)(2,1)S(1)} async-done(((bf16[64,4,256]{2,1,0:T(4,128)(2,1)}), bf16[64,4,256]{2,1,0:T(4,128)(2,1)S(1)}, u32[]{:S(2)}, u32[]{:S(2)}) %all-to-all-start) | async-done | bytes 131104 | tf_op jit(solution)/shard_map/all_to_all | solution.py:344
  34.3 2.7 %collective-permute-start = (bf16[59392]{0:T(1024)(128)(2,1)S(1)}, bf16[59392]{0:T(1024)(128)(2,1)S(1)}, u32[]{:S(2)}, u32[]{:S(2)}) collective-permute-start(bf16[59392]{0:T(1024)(128)(2,1)S(1)} %constant_dynamic-update-slice_fusion.17), channel_id=1, source_target_pairs={{0,3},{1,0},{2,1},{3,2},{4,7},{5,4},{6,5},{7,6},{8,11},{9,8},{10,9... | collective-permute-start | bytes 356360 | tf_op jit(solution)/shard_map/ppermute | solution.py:148
  37.0 3.0 %collective-permute-start.1 = (bf16[59392]{0:T(1024)(128)(2,1)S(1)}, bf16[59392]{0:T(1024)(128)(2,1)S(1)}, u32[]{:S(2)}, u32[]{:S(2)}) collective-permute-start(bf16[59392]{0:T(1024)(128)(2,1)S(1)} %constant_dynamic-update-slice_fusion.17), channel_id=1, source_target_pairs={{0,2},{1,3},{2,0},{3,1},{4,6},{5,7},{6,4},{7,5},{8,10},{9,11},{10,... | collective-permute-start | bytes 356360 | tf_op jit(solution)/shard_map/ppermute | solution.py:148
  40.1 4.0 %collective-permute-start.2 = (bf16[59392]{0:T(1024)(128)(2,1)S(1)}, bf16[59392]{0:T(1024)(128)(2,1)S(1)}, u32[]{:S(2)}, u32[]{:S(2)}) collective-permute-start(bf16[59392]{0:T(1024)(128)(2,1)S(1)} %constant_dynamic-update-slice_fusion.17), channel_id=1, source_target_pairs={{0,1},{1,2},{2,3},{3,0},{4,5},{5,6},{6,7},{7,4},{8,9},{9,10},{10,1... | collective-permute-start | bytes 356360 | tf_op jit(solution)/shard_map/ppermute | solution.py:148
  45.3 1.7 %collective-permute-done.2 = bf16[59392]{0:T(1024)(128)(2,1)S(1)} collective-permute-done((bf16[59392]{0:T(1024)(128)(2,1)S(1)}, bf16[59392]{0:T(1024)(128)(2,1)S(1)}, u32[]{:S(2)}, u32[]{:S(2)}) %collective-permute-start.2) | collective-permute-done | bytes 118816 | tf_op jit(solution)/shard_map/ppermute | solution.py:148
  50.2 0.8 add_multiply_fusion.1
  52.0 0.8 copy-done.8
  53.3 0.7 copy-done.9
  56.3 0.8 copy-done.6
  57.1 0.7 copy-done.5
  57.8 14.7 %shard_map.199 = f32[64,128]{1,0:T(8,128)} custom-call(f32[32,64,64]{2,1,0:T(8,128)} %bitcast.192, f32[4,5,32,64]{3,2,1,0:T(8,128)} %copy-done.5, f32[64,128]{1,0:T(8,128)} %copy.155.content_ref), custom_call_target="tpu_custom_call" | custom-call | tf_op jit(solution)/shard_map/pallas_call | solution.py:30
  72.5 0.8 copy.156
  75.0 1.3 collective-permute-start.3
  76.3 2.7 %collective-permute-start.4 = (f32[32,1024]{1,0:T(8,128)S(1)}, f32[32,1024]{1,0:T(8,128)S(1)}, u32[]{:S(2)}, u32[]{:S(2)}) collective-permute-start(f32[32,1024]{1,0:T(8,128)S(1)} %fusion.22), channel_id=1, source_target_pairs={{0,257},{1,258},{2,259},{3,256},{4,261},{5,262},{6,263},{7,260},{8... | collective-permute-start | bytes 393224 | tf_op jit(solution)/shard_map/ppermute | solution.py:167
  79.0 1.3 collective-permute-start.5
  80.3 1.5 collective-permute-start.6
  82.8 1.4 collective-permute-done.6
  85.2 0.7 copy-done.21
  91.3 14.7 %shard_map.200 = f32[64,128]{1,0:T(8,128)} custom-call(f32[32,64,64]{2,1,0:T(8,128)} %bitcast.193, f32[4,5,32,64]{3,2,1,0:T(8,128)} %copy-done.4, f32[64,128]{1,0:T(8,128)} %copy.169.content_ref), custom_call_target="tpu_custom_call" | custom-call | tf_op jit(solution)/shard_map/pallas_call | solution.py:30
  106.0 0.8 copy.170
  108.4 3.4 %collective-permute-start.10 = (f32[32,256]{1,0:T(8,128)S(1)}, f32[32,256]{1,0:T(8,128)S(1)}, u32[]{:S(2)}, u32[]{:S(2)}) collective-permute-start(f32[32,256]{1,0:T(8,128)S(1)} %get-tuple-element.22), channel_id=1, source_target_pairs={{0,3},{1,0},{2,1},{3,2},{4,7},{5,4},{6,5},{7,6},{8,11},{9,8},{10,9... | collective-permute-start | bytes 98312 | tf_op jit(solution)/shard_map/ppermute | solution.py:159
  111.8 3.7 %collective-permute-start.8 = (f32[32,256]{1,0:T(8,128)S(1)}, f32[32,256]{1,0:T(8,128)S(1)}, u32[]{:S(2)}, u32[]{:S(2)}) collective-permute-start(f32[32,256]{1,0:T(8,128)S(1)} %get-tuple-element.21), channel_id=1, source_target_pairs={{0,1},{1,2},{2,3},{3,0},{4,5},{5,6},{6,7},{7,4},{8,9},{9,10},{10,1... | collective-permute-start | bytes 98312 | tf_op jit(solution)/shard_map/ppermute | solution.py:159
  115.5 2.2 %collective-permute-start.9 = (f32[32,256]{1,0:T(8,128)S(1)}, f32[32,256]{1,0:T(8,128)S(1)}, u32[]{:S(2)}, u32[]{:S(2)}) collective-permute-start(f32[32,256]{1,0:T(8,128)S(1)} %get-tuple-element.23), channel_id=1, source_target_pairs={{0,2},{1,3},{2,0},{3,1},{4,6},{5,7},{6,4},{7,5},{8,10},{9,11},{10,... | collective-permute-start | bytes 98312 | tf_op jit(solution)/shard_map/ppermute | solution.py:159
  117.8 1.3 collective-permute-start.7
  119.1 3.7 %collective-permute-done.9 = f32[32,256]{1,0:T(8,128)S(1)} collective-permute-done((f32[32,256]{1,0:T(8,128)S(1)}, f32[32,256]{1,0:T(8,128)S(1)}, u32[]{:S(2)}, u32[]{:S(2)}) %collective-permute-start.9) | collective-permute-done | bytes 32800 | tf_op jit(solution)/shard_map/ppermute | solution.py:159
  123.6 1.9 %scatter_fusion.1 = bf16[64,4,256]{2,1,0:T(4,128)(2,1)} fusion(bf16[64,4,256]{2,1,0:T(4,128)(2,1)} %broadcast.418, s32[8]{0:T(128)S(1)} %copy-done.59, bf16[8,4,256]{2,1,0:T(4,128)(2,1)S(1)} %fusion.98), kind=kCustom, calls=%fused_computation.4 | custom fusion | bytes 49184 | tf_op jit(solution)/shard_map/scatter | solution.py:348
  125.5 10.8 %all-to-all-start.1 = ((bf16[64,4,256]{2,1,0:T(4,128)(2,1)}), bf16[64,4,256]{2,1,0:T(4,128)(2,1)S(1)}, u32[]{:S(2)}, u32[]{:S(2)}) async-start(bf16[64,4,256]{2,1,0:T(4,128)(2,1)} %scatter_fusion.1), calls=%async_computation.1 | async-start | bytes 262144 | tf_op jit(solution)/shard_map/all_to_all | solution.py:350
  137.7 11.3 %all-to-all-done.1 = bf16[64,4,256]{2,1,0:T(4,128)(2,1)S(1)} async-done(((bf16[64,4,256]{2,1,0:T(4,128)(2,1)}), bf16[64,4,256]{2,1,0:T(4,128)(2,1)S(1)}, u32[]{:S(2)}, u32[]{:S(2)}) %all-to-all-start.1) | async-done | bytes 131104 | tf_op jit(solution)/shard_map/all_to_all | solution.py:350
  (294 shorter events, 32.7 us)
Async XLA Ops:
  0.0 74.8 %copy-start = (bf16[1,256,1024]{2,1,0:T(8,128)(2,1)S(1)}, bf16[1,256,1024]{2,1,0:T(8,128)(2,1)}, u32[]{:S(2)}) copy-start(bf16[1,256,1024]{2,1,0:T(8,128)(2,1)} %param.32) | copy-start | bytes 1572868
  2.3 21.6 %copy-start.2 = (bf16[1,1024,256]{2,1,0:T(8,128)(2,1)S(1)}, bf16[1,1024,256]{2,1,0:T(8,128)(2,1)}, u32[]{:S(2)}) copy-start(bf16[1,1024,256]{2,1,0:T(8,128)(2,1)} %param.29) | copy-start | bytes 1572868
  4.2 29.3 %all-to-all-start = ((bf16[64,4,256]{2,1,0:T(4,128)(2,1)}), bf16[64,4,256]{2,1,0:T(4,128)(2,1)S(1)}, u32[]{:S(2)}, u32[]{:S(2)}) async-start(bf16[64,4,256]{2,1,0:T(4,128)(2,1)} %scatter_fusion), calls=%async_computation | async-start | bytes 262144 | tf_op jit(solution)/shard_map/all_to_all | solution.py:344
  24.0 1.0 copy-start.3
  25.0 2.3 %copy-start.57 = (f32[1,256]{1,0:T(1,128)S(1)}, f32[1,256]{1,0:T(1,128)}, u32[]{:S(2)}) copy-start(f32[1,256]{1,0:T(1,128)} %param.42) | copy-start | bytes 3076
  25.0 3.6 %copy-start.58 = (f32[1,256]{1,0:T(1,128)S(1)}, f32[1,256]{1,0:T(1,128)}, u32[]{:S(2)}) copy-start(f32[1,256]{1,0:T(1,128)} %param.41) | copy-start | bytes 3076
  25.9 4.0 %copy-start.30 = (bf16[1,5,1024]{2,1,0:T(8,128)(2,1)S(1)}, bf16[1,5,1024]{2,1,0:T(8,128)(2,1)}, u32[]{:S(2)}) copy-start(bf16[1,5,1024]{2,1,0:T(8,128)(2,1)} %param.28) | copy-start | bytes 30724
  30.5 17.6 %copy-start.24 = (f32[1,1,1024]{2,1,0:T(1,128)}, f32[1,1,1024]{2,1,0:T(1,128)S(1)}, u32[]{:S(2)}) copy-start(f32[1,1,1024]{2,1,0:T(1,128)S(1)} %get-tuple-element.44) | copy-start | bytes 12292
  30.5 17.6 %copy-start.26 = (f32[1,1,1024]{2,1,0:T(1,128)}, f32[1,1,1024]{2,1,0:T(1,128)S(1)}, u32[]{:S(2)}) copy-start(f32[1,1,1024]{2,1,0:T(1,128)S(1)} %get-tuple-element.42) | copy-start | bytes 12292
  30.5 17.6 %copy-start.28 = (f32[1,1,1024]{2,1,0:T(1,128)}, f32[1,1,1024]{2,1,0:T(1,128)S(1)}, u32[]{:S(2)}) copy-start(f32[1,1,1024]{2,1,0:T(1,128)S(1)} %get-tuple-element.40) | copy-start | bytes 12292
  30.5 17.9 %copy-start.33 = (f32[1,1,1024]{2,1,0:T(1,128)}, f32[1,1,1024]{2,1,0:T(1,128)S(1)}, u32[]{:S(2)}) copy-start(f32[1,1,1024]{2,1,0:T(1,128)S(1)} %get-tuple-element.41) | copy-start | bytes 12292
  34.3 10.4 %collective-permute-start = (bf16[59392]{0:T(1024)(128)(2,1)S(1)}, bf16[59392]{0:T(1024)(128)(2,1)S(1)}, u32[]{:S(2)}, u32[]{:S(2)}) collective-permute-start(bf16[59392]{0:T(1024)(128)(2,1)S(1)} %constant_dynamic-update-slice_fusion.17), channel_id=1, source_target_pairs={{0,3},{1,0},{2,1},{3,2},{4,7},{5,4},{6,5},{7,6},{8,11},{9,8},{10,9... | collective-permute-start | bytes 356360 | tf_op jit(solution)/shard_map/ppermute | solution.py:148
  37.0 8.2 %collective-permute-start.1 = (bf16[59392]{0:T(1024)(128)(2,1)S(1)}, bf16[59392]{0:T(1024)(128)(2,1)S(1)}, u32[]{:S(2)}, u32[]{:S(2)}) collective-permute-start(bf16[59392]{0:T(1024)(128)(2,1)S(1)} %constant_dynamic-update-slice_fusion.17), channel_id=1, source_target_pairs={{0,2},{1,3},{2,0},{3,1},{4,6},{5,7},{6,4},{7,5},{8,10},{9,11},{10,... | collective-permute-start | bytes 356360 | tf_op jit(solution)/shard_map/ppermute | solution.py:148
  40.1 6.9 %collective-permute-start.2 = (bf16[59392]{0:T(1024)(128)(2,1)S(1)}, bf16[59392]{0:T(1024)(128)(2,1)S(1)}, u32[]{:S(2)}, u32[]{:S(2)}) collective-permute-start(bf16[59392]{0:T(1024)(128)(2,1)S(1)} %constant_dynamic-update-slice_fusion.17), channel_id=1, source_target_pairs={{0,1},{1,2},{2,3},{3,0},{4,5},{5,6},{6,7},{7,4},{8,9},{9,10},{10,1... | collective-permute-start | bytes 356360 | tf_op jit(solution)/shard_map/ppermute | solution.py:148
  47.2 4.8 %copy-start.10 = (bf16[32,256]{1,0:T(8,128)(2,1)}, bf16[32,256]{1,0:T(8,128)(2,1)S(1)}, u32[]{:S(2)}) copy-start(bf16[32,256]{1,0:T(8,128)(2,1)S(1)} %slice.200) | copy-start | bytes 49156
  47.3 1.2 copy-start.12
  47.3 1.1 copy-start.15
  48.4 1.2 copy-start.1
  51.9 0.9 copy-start.8
  51.9 0.9 copy-start.13
  51.9 0.9 copy-start.16
  52.0 0.9 copy-start.22
  74.8 7.0 %copy-start.51 = (s32[8]{0:T(128)S(1)}, s32[8]{0:T(128)}, u32[]{:S(2)}) copy-start(s32[8]{0:T(128)} %copy-done.50) | copy-start | bytes 100
  75.0 7.4 %collective-permute-start.3 = (f32[32,1024]{1,0:T(8,128)S(1)}, f32[32,1024]{1,0:T(8,128)S(1)}, u32[]{:S(2)}, u32[]{:S(2)}) collective-permute-start(f32[32,1024]{1,0:T(8,128)S(1)} %fusion.22), channel_id=1, source_target_pairs={{0,256},{1,257},{2,258},{3,259},{4,260},{5,261},{6,262},{7,263},{8... | collective-permute-start | bytes 393224 | tf_op jit(solution)/shard_map/ppermute | solution.py:167
  76.3 6.1 %collective-permute-start.4 = (f32[32,1024]{1,0:T(8,128)S(1)}, f32[32,1024]{1,0:T(8,128)S(1)}, u32[]{:S(2)}, u32[]{:S(2)}) collective-permute-start(f32[32,1024]{1,0:T(8,128)S(1)} %fusion.22), channel_id=1, source_target_pairs={{0,257},{1,258},{2,259},{3,256},{4,261},{5,262},{6,263},{7,260},{8... | collective-permute-start | bytes 393224 | tf_op jit(solution)/shard_map/ppermute | solution.py:167
  79.0 3.8 %collective-permute-start.5 = (f32[32,1024]{1,0:T(8,128)S(1)}, f32[32,1024]{1,0:T(8,128)S(1)}, u32[]{:S(2)}, u32[]{:S(2)}) collective-permute-start(f32[32,1024]{1,0:T(8,128)S(1)} %fusion.22), channel_id=1, source_target_pairs={{0,258},{1,259},{2,256},{3,257},{4,262},{5,263},{6,260},{7,261},{8... | collective-permute-start | bytes 393224 | tf_op jit(solution)/shard_map/ppermute | solution.py:167
  80.3 3.9 %collective-permute-start.6 = (f32[32,1024]{1,0:T(8,128)S(1)}, f32[32,1024]{1,0:T(8,128)S(1)}, u32[]{:S(2)}, u32[]{:S(2)}) collective-permute-start(f32[32,1024]{1,0:T(8,128)S(1)} %fusion.22), channel_id=1, source_target_pairs={{0,259},{1,256},{2,257},{3,258},{4,263},{5,260},{6,261},{7,262},{8... | collective-permute-start | bytes 393224 | tf_op jit(solution)/shard_map/ppermute | solution.py:167
  108.4 10.6 %collective-permute-start.10 = (f32[32,256]{1,0:T(8,128)S(1)}, f32[32,256]{1,0:T(8,128)S(1)}, u32[]{:S(2)}, u32[]{:S(2)}) collective-permute-start(f32[32,256]{1,0:T(8,128)S(1)} %get-tuple-element.22), channel_id=1, source_target_pairs={{0,3},{1,0},{2,1},{3,2},{4,7},{5,4},{6,5},{7,6},{8,11},{9,8},{10,9... | collective-permute-start | bytes 98312 | tf_op jit(solution)/shard_map/ppermute | solution.py:159
  111.8 7.2 %collective-permute-start.8 = (f32[32,256]{1,0:T(8,128)S(1)}, f32[32,256]{1,0:T(8,128)S(1)}, u32[]{:S(2)}, u32[]{:S(2)}) collective-permute-start(f32[32,256]{1,0:T(8,128)S(1)} %get-tuple-element.21), channel_id=1, source_target_pairs={{0,1},{1,2},{2,3},{3,0},{4,5},{5,6},{6,7},{7,4},{8,9},{9,10},{10,1... | collective-permute-start | bytes 98312 | tf_op jit(solution)/shard_map/ppermute | solution.py:159
  115.5 7.3 %collective-permute-start.9 = (f32[32,256]{1,0:T(8,128)S(1)}, f32[32,256]{1,0:T(8,128)S(1)}, u32[]{:S(2)}, u32[]{:S(2)}) collective-permute-start(f32[32,256]{1,0:T(8,128)S(1)} %get-tuple-element.23), channel_id=1, source_target_pairs={{0,2},{1,3},{2,0},{3,1},{4,6},{5,7},{6,4},{7,5},{8,10},{9,11},{10,... | collective-permute-start | bytes 98312 | tf_op jit(solution)/shard_map/ppermute | solution.py:159
  117.8 5.1 %collective-permute-start.7 = (bf16[8,4,256]{2,1,0:T(4,128)(2,1)S(1)}, bf16[8,4,256]{2,1,0:T(4,128)(2,1)S(1)}, u32[]{:S(2)}, u32[]{:S(2)}) collective-permute-start(bf16[8,4,256]{2,1,0:T(4,128)(2,1)S(1)} %constant_dynamic-slice_fusion.2), channel_id=1, source_target_pairs={{256,0},{257,1},{258,2},{259,3},{260,4},{261,5},{262,6},{263,7},{2... | collective-permute-start | bytes 49160 | tf_op jit(solution)/shard_map/ppermute | solution.py:174
  125.5 23.5 %all-to-all-start.1 = ((bf16[64,4,256]{2,1,0:T(4,128)(2,1)}), bf16[64,4,256]{2,1,0:T(4,128)(2,1)S(1)}, u32[]{:S(2)}, u32[]{:S(2)}) async-start(bf16[64,4,256]{2,1,0:T(4,128)(2,1)} %scatter_fusion.1), calls=%async_computation.1 | async-start | bytes 262144 | tf_op jit(solution)/shard_map/all_to_all | solution.py:350
  (42 other events, 30.4 us)

commit v6 on v3

--- a/solution.py
+++ b/solution.py
@@ -325,13 +325,13 @@
         fading_second_lowrank.reshape(fading_second_lowrank.shape[1:]),
         adapt_first_lowrank.reshape(adapt_first_lowrank.shape[1:]),
         adapt_second_lowrank.reshape(adapt_second_lowrank.shape[1:]),
-        fading_baseline.reshape(fading_baseline.shape[1:]),
-        adapt_baseline.reshape(adapt_baseline.shape[1:]),
-        erasing_address_gains.reshape(erasing_address_gains.shape[1:]),
-        address_rate_coupling.reshape(address_rate_coupling.shape[1:]),
-        present_extra_gain.reshape(present_extra_gain.shape[1:]),
-        section_standard_gains.reshape(section_standard_gains.shape[1:]),
-        section_standard_shift_terms.reshape(section_standard_shift_terms.shape[1:]),
+        fading_baseline,
+        adapt_baseline,
+        erasing_address_gains,
+        address_rate_coupling,
+        present_extra_gain,
+        section_standard_gains,
+        section_standard_shift_terms,
     )
     states_local = memory_per_request.reshape(memory_per_request.shape[1:])
     last_local = previous_step_feature.reshape(previous_step_feature.shape[1:])

time: 150 us -> 150 us (level)
  no operation moved by 1% of the time
where the time goes in v6:
time: 150 us; the launch traced here: 149 us
  starting transfers between devices  56.9 us (38%)
  local copies, waits for them, and re-layouts  29 us (19%)
  waiting for transfers between devices  21.6 us (14%)
  other arithmetic  17 us (11%)
  Pallas kernels  16.1 us (11%)
  matrix products  6.53 us (4%)
    all_to_all x1, starting transfers between devices, body(): lax.all_to_all(outgoing, 'req', split_axis=0, concat_axis=0, tiled=True)  16.6 us
    pallas_call x2, Pallas kernels, run_recurrence(): pl.pallas_call(recurrence_kernel, out_shape=jax.ShapeDtypeStruct((steps,...  16.1 us
    all_to_all x1, starting transfers between devices, body(): lax.all_to_all(going_back, 'req', split_axis=0, concat_axis=0, tiled=True)  12.6 us
    all_to_all x1, waiting for transfers between devices, body(): lax.all_to_all(going_back, 'req', split_axis=0, concat_axis=0, tiled=True)  12.5 us
    ppermute x3, starting transfers between devices, gather_heads(): lax.ppermute(block, 'head', [(i, (i + k) % n) for i in range(n)])  9.76 us
    ppermute x3, starting transfers between devices, scatter_heads(): lax.ppermute(chunk, 'head', [(i, (i + k) % n) for i in range(n)])  9.27 us
    unnamed x85, local copies, waits for them, and re-layouts  7.42 us
    ppermute x4, starting transfers between devices, hand_over(): lax.ppermute(partial, ('section', 'head'), [(i, n + (i + k) % n) for i in...  7.36 us
  transfers between devices with their start and end apart: 13, of which 6 were waited for; matrix products, arithmetic and copies ran while one was open for 10% of the time, Pallas kernels for 0%

profile of v6, /device:TPU:6, one launch (start us, length us, event | category | flops | bytes accessed | tf_op | source)
XLA Modules:
  0.0 148.6 jit_solution(2413495182342247860)
XLA Ops:
  1.8 1.9 %scatter_fusion = bf16[64,4,256]{2,1,0:T(4,128)(2,1)} fusion(bf16[64,4,256]{2,1,0:T(4,128)(2,1)} %broadcast.418.clone, s32[8]{0:T(128)S(1)} %fusion.107, bf16[8,4,256]{2,1,0:T(4,128)(2,1)} %param.23), kind=kCustom, calls=%fused_computation.3 | custom fusion | bytes 49184 | tf_op jit(solution)/shard_map/scatter | solution.py:341
  3.7 16.6 %all-to-all-start = ((bf16[64,4,256]{2,1,0:T(4,128)(2,1)}), bf16[64,4,256]{2,1,0:T(4,128)(2,1)S(1)}, u32[]{:S(2)}, u32[]{:S(2)}) async-start(bf16[64,4,256]{2,1,0:T(4,128)(2,1)} %scatter_fusion), calls=%async_computation | async-start | bytes 262144 | tf_op jit(solution)/shard_map/all_to_all | solution.py:343
  25.0 1.2 copy.143
  26.3 1.2 copy.146
  28.1 1.3 reduce.11
  30.0 1.3 reduce.12
  32.0 1.3 reduce.13
  34.0 1.5 %fusion.116 = (f32[1,1,1024]{2,1,0:T(1,128)S(1)}, f32[1,1,1024]{2,1,0:T(1,128)S(1)}, f32[1,1,1024]{2,1,0:T(1,128)S(1)}, f32[1,1,1024]{2,1,0:T(1,128)}, f32[1,1,1024]{2,1,0:T(1,128)S(1)}) fusion(bf16[1,5,1024]{2,1,0:T(8,128)(2,1)} %param.28), kind=kLoop, calls=%fused_computation.240 | loop fusion | bytes 40960 | tf_op jit(solution)/shard_map/slice | solution.py:201
  36.3 2.7 %collective-permute-start = (bf16[59392]{0:T(1024)(128)(2,1)S(1)}, bf16[59392]{0:T(1024)(128)(2,1)S(1)}, u32[]{:S(2)}, u32[]{:S(2)}) collective-permute-start(bf16[59392]{0:T(1024)(128)(2,1)S(1)} %constant_dynamic-update-slice_fusion.23), channel_id=1, source_target_pairs={{0,3},{1,0},{2,1},{3,2},{4,7},{5,4},{6,5},{7,6},{8,11},{9,8},{10,9... | collective-permute-start | bytes 356360 | tf_op jit(solution)/shard_map/ppermute | solution.py:147
  39.0 3.0 %collective-permute-start.1 = (bf16[59392]{0:T(1024)(128)(2,1)S(1)}, bf16[59392]{0:T(1024)(128)(2,1)S(1)}, u32[]{:S(2)}, u32[]{:S(2)}) collective-permute-start(bf16[59392]{0:T(1024)(128)(2,1)S(1)} %constant_dynamic-update-slice_fusion.23), channel_id=1, source_target_pairs={{0,2},{1,3},{2,0},{3,1},{4,6},{5,7},{6,4},{7,5},{8,10},{9,11},{10,... | collective-permute-start | bytes 356360 | tf_op jit(solution)/shard_map/ppermute | solution.py:147
  42.1 4.0 %collective-permute-start.2 = (bf16[59392]{0:T(1024)(128)(2,1)S(1)}, bf16[59392]{0:T(1024)(128)(2,1)S(1)}, u32[]{:S(2)}, u32[]{:S(2)}) collective-permute-start(bf16[59392]{0:T(1024)(128)(2,1)S(1)} %constant_dynamic-update-slice_fusion.23), channel_id=1, source_target_pairs={{0,1},{1,2},{2,3},{3,0},{4,5},{5,6},{6,7},{7,4},{8,9},{9,10},{10,1... | collective-permute-start | bytes 356360 | tf_op jit(solution)/shard_map/ppermute | solution.py:147
  47.3 2.3 %collective-permute-done.2 = bf16[59392]{0:T(1024)(128)(2,1)S(1)} collective-permute-done((bf16[59392]{0:T(1024)(128)(2,1)S(1)}, bf16[59392]{0:T(1024)(128)(2,1)S(1)}, u32[]{:S(2)}, u32[]{:S(2)}) %collective-permute-start.2) | collective-permute-done | bytes 118816 | tf_op jit(solution)/shard_map/ppermute | solution.py:147
  52.6 1.2 fusion.80
  56.0 2.7 %copy.149.content_ref = f32[4,32,64,1]{3,2,1,0:T(8,128)} copy(f32[4,32,64,1]{2,1,0,3:T(8,128)S(1)} %bitcast.191) | data formatting | bytes 65536 | tf_op jit(solution)/shard_map/reshape;reshape | solution.py:98
  60.5 8.0 %shard_map.199 = f32[4,32,64,1]{3,2,1,0:T(8,128)} custom-call(f32[32,64,64]{2,1,0:T(8,128)} %bitcast.180, f32[4,5,32,1,64]{4,3,2,1,0:T(1,128)} %copy-done.2, f32[4,32,64,1]{3,2,1,0:T(8,128)} %copy.149.content_ref), custom_call_target="tpu_custom_call" | custom-call | tf_op jit(solution)/shard_map/pallas_call | solution.py:27
  68.5 3.4 %reduce = f32[4,32,64]{2,1,0:T(8,128)S(1)} reduce(f32[4,32,64,1]{3,2,1,0:T(8,128)} %shard_map.199, f32[]{:T(128)} %constant.200), dimensions={3}, to_apply=%pallas_call.6.reduce_sub_computation | reduce | bytes 65540 | tf_op jit(solution)/shard_map/pallas_call | solution.py:27
  72.9 1.3 collective-permute-start.3
  74.2 3.3 %collective-permute-start.4 = (f32[32,1024]{1,0:T(8,128)S(1)}, f32[32,1024]{1,0:T(8,128)S(1)}, u32[]{:S(2)}, u32[]{:S(2)}) collective-permute-start(f32[32,1024]{1,0:T(8,128)S(1)} %fusion.22), channel_id=1, source_target_pairs={{0,257},{1,258},{2,259},{3,256},{4,261},{5,262},{6,263},{7,260},{8... | collective-permute-start | bytes 393224 | tf_op jit(solution)/shard_map/ppermute | solution.py:166
  77.5 1.3 collective-permute-start.5
  78.8 1.5 collective-permute-start.6
  81.3 1.4 collective-permute-done.6
  88.0 2.7 %copy.162.content_ref = f32[4,32,64,1]{3,2,1,0:T(8,128)} copy(f32[4,32,64,1]{2,1,0,3:T(8,128)S(1)} %bitcast.192) | data formatting | bytes 65536 | tf_op jit(solution)/shard_map/reshape;reshape | solution.py:98
  92.7 8.0 %shard_map.200 = f32[4,32,64,1]{3,2,1,0:T(8,128)} custom-call(f32[32,64,64]{2,1,0:T(8,128)} %bitcast.181, f32[4,5,32,1,64]{4,3,2,1,0:T(1,128)} %copy-done.3, f32[4,32,64,1]{3,2,1,0:T(8,128)} %copy.162.content_ref), custom_call_target="tpu_custom_call" | custom-call | tf_op jit(solution)/shard_map/pallas_call | solution.py:27
  100.7 3.3 %reduce.4 = f32[4,32,64]{2,1,0:T(8,128)S(1)} reduce(f32[4,32,64,1]{3,2,1,0:T(8,128)} %shard_map.200, f32[]{:T(128)} %constant.200), dimensions={3}, to_apply=%pallas_call.7.reduce_sub_computation | reduce | bytes 65540 | tf_op jit(solution)/shard_map/pallas_call | solution.py:27
  105.1 3.4 %collective-permute-start.10 = (f32[32,256]{1,0:T(8,128)S(1)}, f32[32,256]{1,0:T(8,128)S(1)}, u32[]{:S(2)}, u32[]{:S(2)}) collective-permute-start(f32[32,256]{1,0:T(8,128)S(1)} %get-tuple-element.22), channel_id=1, source_target_pairs={{0,3},{1,0},{2,1},{3,2},{4,7},{5,4},{6,5},{7,6},{8,11},{9,8},{10,9... | collective-permute-start | bytes 98312 | tf_op jit(solution)/shard_map/ppermute | solution.py:158
  108.4 3.7 %collective-permute-start.8 = (f32[32,256]{1,0:T(8,128)S(1)}, f32[32,256]{1,0:T(8,128)S(1)}, u32[]{:S(2)}, u32[]{:S(2)}) collective-permute-start(f32[32,256]{1,0:T(8,128)S(1)} %get-tuple-element.21), channel_id=1, source_target_pairs={{0,1},{1,2},{2,3},{3,0},{4,5},{5,6},{6,7},{7,4},{8,9},{9,10},{10,1... | collective-permute-start | bytes 98312 | tf_op jit(solution)/shard_map/ppermute | solution.py:158
  112.1 2.2 %collective-permute-start.9 = (f32[32,256]{1,0:T(8,128)S(1)}, f32[32,256]{1,0:T(8,128)S(1)}, u32[]{:S(2)}, u32[]{:S(2)}) collective-permute-start(f32[32,256]{1,0:T(8,128)S(1)} %get-tuple-element.23), channel_id=1, source_target_pairs={{0,2},{1,3},{2,0},{3,1},{4,6},{5,7},{6,4},{7,5},{8,10},{9,11},{10,... | collective-permute-start | bytes 98312 | tf_op jit(solution)/shard_map/ppermute | solution.py:158
  114.4 1.3 collective-permute-start.7
  115.7 3.7 %collective-permute-done.9 = f32[32,256]{1,0:T(8,128)S(1)} collective-permute-done((f32[32,256]{1,0:T(8,128)S(1)}, f32[32,256]{1,0:T(8,128)S(1)}, u32[]{:S(2)}, u32[]{:S(2)}) %collective-permute-start.9) | collective-permute-done | bytes 32800 | tf_op jit(solution)/shard_map/ppermute | solution.py:158
  120.2 1.9 %scatter_fusion.1 = bf16[64,4,256]{2,1,0:T(4,128)(2,1)} fusion(bf16[64,4,256]{2,1,0:T(4,128)(2,1)} %broadcast.418, s32[8]{0:T(128)S(1)} %copy-done.27, bf16[8,4,256]{2,1,0:T(4,128)(2,1)S(1)} %fusion.98), kind=kCustom, calls=%fused_computation.4 | custom fusion | bytes 49184 | tf_op jit(solution)/shard_map/scatter | solution.py:347
  122.1 12.6 %all-to-all-start.1 = ((bf16[64,4,256]{2,1,0:T(4,128)(2,1)}), bf16[64,4,256]{2,1,0:T(4,128)(2,1)S(1)}, u32[]{:S(2)}, u32[]{:S(2)}) async-start(bf16[64,4,256]{2,1,0:T(4,128)(2,1)} %scatter_fusion.1), calls=%async_computation.1 | async-start | bytes 262144 | tf_op jit(solution)/shard_map/all_to_all | solution.py:349
  134.8 12.5 %all-to-all-done.1 = bf16[64,4,256]{2,1,0:T(4,128)(2,1)S(1)} async-done(((bf16[64,4,256]{2,1,0:T(4,128)(2,1)}), bf16[64,4,256]{2,1,0:T(4,128)(2,1)S(1)}, u32[]{:S(2)}, u32[]{:S(2)}) %all-to-all-start.1) | async-done | bytes 131104 | tf_op jit(solution)/shard_map/all_to_all | solution.py:349
  (230 shorter events, 29.0 us)
Async XLA Ops:
  0.0 72.7 %copy-start = (bf16[1,256,1024]{2,1,0:T(8,128)(2,1)S(1)}, bf16[1,256,1024]{2,1,0:T(8,128)(2,1)}, u32[]{:S(2)}) copy-start(bf16[1,256,1024]{2,1,0:T(8,128)(2,1)} %param.32) | copy-start | bytes 1572868
  0.0 51.0 %copy-start.26 = (f32[1,256]{1,0:T(1,128)S(1)}, f32[1,256]{1,0:T(1,128)}, u32[]{:S(2)}) copy-start(f32[1,256]{1,0:T(1,128)} %param.38) | copy-start | bytes 3076
  0.0 51.0 %copy-start.11 = (bf16[1,96,256]{2,1,0:T(8,128)(2,1)S(1)}, bf16[1,96,256]{2,1,0:T(8,128)(2,1)}, u32[]{:S(2)}) copy-start(bf16[1,96,256]{2,1,0:T(8,128)(2,1)} %param.36) | copy-start | bytes 147460
  1.1 21.0 %copy-start.24 = (s32[8]{0:T(128)}, s32[8]{0:T(128)S(1)}, u32[]{:S(2)}) copy-start(s32[8]{0:T(128)S(1)} %convert_reduce_fusion) | copy-start | bytes 100
  3.7 31.8 %all-to-all-start = ((bf16[64,4,256]{2,1,0:T(4,128)(2,1)}), bf16[64,4,256]{2,1,0:T(4,128)(2,1)S(1)}, u32[]{:S(2)}, u32[]{:S(2)}) async-start(bf16[64,4,256]{2,1,0:T(4,128)(2,1)} %scatter_fusion), calls=%async_computation | async-start | bytes 262144 | tf_op jit(solution)/shard_map/all_to_all | solution.py:343
  21.9 29.6 %copy-start.1 = (bf16[1,1024,256]{2,1,0:T(8,128)(2,1)S(1)}, bf16[1,1024,256]{2,1,0:T(8,128)(2,1)}, u32[]{:S(2)}) copy-start(bf16[1,1024,256]{2,1,0:T(8,128)(2,1)} %param.30) | copy-start | bytes 1572868
  21.9 29.6 %copy-start.16 = (f32[1,256]{1,0:T(1,128)S(1)}, f32[1,256]{1,0:T(1,128)}, u32[]{:S(2)}) copy-start(f32[1,256]{1,0:T(1,128)} %param.40) | copy-start | bytes 3076
  21.9 29.6 %copy-start.17 = (f32[1,256]{1,0:T(1,128)S(1)}, f32[1,256]{1,0:T(1,128)}, u32[]{:S(2)}) copy-start(f32[1,256]{1,0:T(1,128)} %param.39) | copy-start | bytes 3076
  35.5 15.5 %copy-start.12 = (f32[1,1,1024]{2,1,0:T(1,128)}, f32[1,1,1024]{2,1,0:T(1,128)S(1)}, u32[]{:S(2)}) copy-start(f32[1,1,1024]{2,1,0:T(1,128)S(1)} %get-tuple-element.42) | copy-start | bytes 12292
  35.5 15.5 %copy-start.13 = (f32[1,1,1024]{2,1,0:T(1,128)}, f32[1,1,1024]{2,1,0:T(1,128)S(1)}, u32[]{:S(2)}) copy-start(f32[1,1,1024]{2,1,0:T(1,128)S(1)} %get-tuple-element.44) | copy-start | bytes 12292
  35.5 15.5 %copy-start.14 = (f32[1,1,1024]{2,1,0:T(1,128)}, f32[1,1,1024]{2,1,0:T(1,128)S(1)}, u32[]{:S(2)}) copy-start(f32[1,1,1024]{2,1,0:T(1,128)S(1)} %get-tuple-element.40) | copy-start | bytes 12292
  35.5 16.5 %copy-start.15 = (f32[1,1,1024]{2,1,0:T(1,128)}, f32[1,1,1024]{2,1,0:T(1,128)S(1)}, u32[]{:S(2)}) copy-start(f32[1,1,1024]{2,1,0:T(1,128)S(1)} %get-tuple-element.41) | copy-start | bytes 12292
  36.3 10.3 %collective-permute-start = (bf16[59392]{0:T(1024)(128)(2,1)S(1)}, bf16[59392]{0:T(1024)(128)(2,1)S(1)}, u32[]{:S(2)}, u32[]{:S(2)}) collective-permute-start(bf16[59392]{0:T(1024)(128)(2,1)S(1)} %constant_dynamic-update-slice_fusion.23), channel_id=1, source_target_pairs={{0,3},{1,0},{2,1},{3,2},{4,7},{5,4},{6,5},{7,6},{8,11},{9,8},{10,9... | collective-permute-start | bytes 356360 | tf_op jit(solution)/shard_map/ppermute | solution.py:147
  39.0 8.2 %collective-permute-start.1 = (bf16[59392]{0:T(1024)(128)(2,1)S(1)}, bf16[59392]{0:T(1024)(128)(2,1)S(1)}, u32[]{:S(2)}, u32[]{:S(2)}) collective-permute-start(bf16[59392]{0:T(1024)(128)(2,1)S(1)} %constant_dynamic-update-slice_fusion.23), channel_id=1, source_target_pairs={{0,2},{1,3},{2,0},{3,1},{4,6},{5,7},{6,4},{7,5},{8,10},{9,11},{10,... | collective-permute-start | bytes 356360 | tf_op jit(solution)/shard_map/ppermute | solution.py:147
  42.1 7.5 %collective-permute-start.2 = (bf16[59392]{0:T(1024)(128)(2,1)S(1)}, bf16[59392]{0:T(1024)(128)(2,1)S(1)}, u32[]{:S(2)}, u32[]{:S(2)}) collective-permute-start(bf16[59392]{0:T(1024)(128)(2,1)S(1)} %constant_dynamic-update-slice_fusion.23), channel_id=1, source_target_pairs={{0,1},{1,2},{2,3},{3,0},{4,5},{5,6},{6,7},{7,4},{8,9},{9,10},{10,1... | collective-permute-start | bytes 356360 | tf_op jit(solution)/shard_map/ppermute | solution.py:147
  68.5 3.8 %copy-start.20 = (f32[4,64]{1,0:T(4,128)S(1)}, f32[4,64]{1,0:T(4,128)}, u32[]{:S(2)}) copy-start(f32[4,64]{1,0:T(4,128)} %mul.257) | copy-start | bytes 3076
  68.5 3.8 %copy-start.22 = (f32[4,64]{1,0:T(4,128)S(1)}, f32[4,64]{1,0:T(4,128)}, u32[]{:S(2)}) copy-start(f32[4,64]{1,0:T(4,128)} %mul.261) | copy-start | bytes 3076
  68.5 11.8 %copy-start.25 = (s32[8]{0:T(128)S(1)}, s32[8]{0:T(128)}, u32[]{:S(2)}) copy-start(s32[8]{0:T(128)} %copy-done.24) | copy-start | bytes 100
  68.5 14.4 %copy-start.6 = (bf16[32,256]{1,0:T(8,128)(2,1)S(1)}, bf16[32,256]{1,0:T(8,128)(2,1)}, u32[]{:S(2)}) copy-start(bf16[32,256]{1,0:T(8,128)(2,1)} %copy-done.5) | copy-start | bytes 49156
  68.5 14.4 %copy-start.8 = (bf16[32,256]{1,0:T(8,128)(2,1)S(1)}, bf16[32,256]{1,0:T(8,128)(2,1)}, u32[]{:S(2)}) copy-start(bf16[32,256]{1,0:T(8,128)(2,1)} %copy-done.7) | copy-start | bytes 49156
  68.5 14.4 %copy-start.10 = (bf16[32,256]{1,0:T(8,128)(2,1)S(1)}, bf16[32,256]{1,0:T(8,128)(2,1)}, u32[]{:S(2)}) copy-start(bf16[32,256]{1,0:T(8,128)(2,1)} %copy-done.9) | copy-start | bytes 49156
  72.9 7.4 %collective-permute-start.3 = (f32[32,1024]{1,0:T(8,128)S(1)}, f32[32,1024]{1,0:T(8,128)S(1)}, u32[]{:S(2)}, u32[]{:S(2)}) collective-permute-start(f32[32,1024]{1,0:T(8,128)S(1)} %fusion.22), channel_id=1, source_target_pairs={{0,256},{1,257},{2,258},{3,259},{4,260},{5,261},{6,262},{7,263},{8... | collective-permute-start | bytes 393224 | tf_op jit(solution)/shard_map/ppermute | solution.py:166
  74.2 6.1 %collective-permute-start.4 = (f32[32,1024]{1,0:T(8,128)S(1)}, f32[32,1024]{1,0:T(8,128)S(1)}, u32[]{:S(2)}, u32[]{:S(2)}) collective-permute-start(f32[32,1024]{1,0:T(8,128)S(1)} %fusion.22), channel_id=1, source_target_pairs={{0,257},{1,258},{2,259},{3,256},{4,261},{5,262},{6,263},{7,260},{8... | collective-permute-start | bytes 393224 | tf_op jit(solution)/shard_map/ppermute | solution.py:166
  77.5 3.8 %collective-permute-start.5 = (f32[32,1024]{1,0:T(8,128)S(1)}, f32[32,1024]{1,0:T(8,128)S(1)}, u32[]{:S(2)}, u32[]{:S(2)}) collective-permute-start(f32[32,1024]{1,0:T(8,128)S(1)} %fusion.22), channel_id=1, source_target_pairs={{0,258},{1,259},{2,256},{3,257},{4,262},{5,263},{6,260},{7,261},{8... | collective-permute-start | bytes 393224 | tf_op jit(solution)/shard_map/ppermute | solution.py:166
  78.8 3.9 %collective-permute-start.6 = (f32[32,1024]{1,0:T(8,128)S(1)}, f32[32,1024]{1,0:T(8,128)S(1)}, u32[]{:S(2)}, u32[]{:S(2)}) collective-permute-start(f32[32,1024]{1,0:T(8,128)S(1)} %fusion.22), channel_id=1, source_target_pairs={{0,259},{1,256},{2,257},{3,258},{4,263},{5,260},{6,261},{7,262},{8... | collective-permute-start | bytes 393224 | tf_op jit(solution)/shard_map/ppermute | solution.py:166
  100.7 19.5 %copy-start.27 = (s32[8]{0:T(128)S(1)}, s32[8]{0:T(128)}, u32[]{:S(2)}) copy-start(s32[8]{0:T(128)} %fusion.106) | copy-start | bytes 100
  100.7 34.0 %copy-start.28 = (s32[8]{0:T(128)S(1)}, s32[8]{0:T(128)}, u32[]{:S(2)}) copy-start(s32[8]{0:T(128)} %param.24) | copy-start | bytes 100
  105.1 10.6 %collective-permute-start.10 = (f32[32,256]{1,0:T(8,128)S(1)}, f32[32,256]{1,0:T(8,128)S(1)}, u32[]{:S(2)}, u32[]{:S(2)}) collective-permute-start(f32[32,256]{1,0:T(8,128)S(1)} %get-tuple-element.22), channel_id=1, source_target_pairs={{0,3},{1,0},{2,1},{3,2},{4,7},{5,4},{6,5},{7,6},{8,11},{9,8},{10,9... | collective-permute-start | bytes 98312 | tf_op jit(solution)/shard_map/ppermute | solution.py:158
  108.4 7.2 %collective-permute-start.8 = (f32[32,256]{1,0:T(8,128)S(1)}, f32[32,256]{1,0:T(8,128)S(1)}, u32[]{:S(2)}, u32[]{:S(2)}) collective-permute-start(f32[32,256]{1,0:T(8,128)S(1)} %get-tuple-element.21), channel_id=1, source_target_pairs={{0,1},{1,2},{2,3},{3,0},{4,5},{5,6},{6,7},{7,4},{8,9},{9,10},{10,1... | collective-permute-start | bytes 98312 | tf_op jit(solution)/shard_map/ppermute | solution.py:158
  112.1 7.3 %collective-permute-start.9 = (f32[32,256]{1,0:T(8,128)S(1)}, f32[32,256]{1,0:T(8,128)S(1)}, u32[]{:S(2)}, u32[]{:S(2)}) collective-permute-start(f32[32,256]{1,0:T(8,128)S(1)} %get-tuple-element.23), channel_id=1, source_target_pairs={{0,2},{1,3},{2,0},{3,1},{4,6},{5,7},{6,4},{7,5},{8,10},{9,11},{10,... | collective-permute-start | bytes 98312 | tf_op jit(solution)/shard_map/ppermute | solution.py:158
  114.4 5.1 %collective-permute-start.7 = (bf16[8,4,256]{2,1,0:T(4,128)(2,1)S(1)}, bf16[8,4,256]{2,1,0:T(4,128)(2,1)S(1)}, u32[]{:S(2)}, u32[]{:S(2)}) collective-permute-start(bf16[8,4,256]{2,1,0:T(4,128)(2,1)S(1)} %constant_dynamic-slice_fusion.2), channel_id=1, source_target_pairs={{256,0},{257,1},{258,2},{259,3},{260,4},{261,5},{262,6},{263,7},{2... | collective-permute-start | bytes 49160 | tf_op jit(solution)/shard_map/ppermute | solution.py:173
  122.1 25.2 %all-to-all-start.1 = ((bf16[64,4,256]{2,1,0:T(4,128)(2,1)}), bf16[64,4,256]{2,1,0:T(4,128)(2,1)S(1)}, u32[]{:S(2)}, u32[]{:S(2)}) async-start(bf16[64,4,256]{2,1,0:T(4,128)(2,1)} %scatter_fusion.1), calls=%async_computation.1 | async-start | bytes 262144 | tf_op jit(solution)/shard_map/all_to_all | solution.py:349
  (10 other events, 25.0 us)

commit v7 on v6

--- a/solution.py
+++ b/solution.py
@@ -75,7 +75,8 @@
     learn_heads = to_heads(learning)
     scaled = to_heads(address_entries * erasing_address_gains)
     normed = scaled / jnp.sqrt(jnp.sum(scaled * scaled, axis=-1, keepdims=True) + 1e-06)
-    erasing_address = to_heads(address_entries * (1.0 + (learning - 1.0) * address_rate_coupling))
+    erasing_flat = address_entries * (1.0 + (learning - 1.0) * address_rate_coupling)
+    erasing_address = to_heads(erasing_flat)
     acceptor_parts = to_heads(acceptor_entries)
     content_part_lines = to_heads(content_entries)
     steps_count = acceptor_parts.shape[1]
@@ -108,24 +109,19 @@
     )
     center = read_all - jnp.mean(read_all, axis=-1, keepdims=True)
     variance = jnp.mean(center * center, axis=-1, keepdims=True)
-    gain_heads = section_standard_gains.reshape(stored_memory_parts, subspace_span)
-    bias_heads = section_standard_shift_terms.reshape(stored_memory_parts, subspace_span)
-    standardized_parts = center / jnp.sqrt(variance + 0.00064) * gain_heads + bias_heads
+    flat_shape = (batch_rows * acceptor_parts.shape[1], stored_memory_parts * subspace_span)
+    standardized_parts = (center / jnp.sqrt(variance + 0.00064)).reshape(
+        flat_shape
+    ) * section_standard_gains + section_standard_shift_terms
     present_extra_term = (
         jnp.sum(
-            acceptor_parts
-            * erasing_address
-            * present_extra_gain.reshape(stored_memory_parts, subspace_span),
+            to_heads(acceptor_entries * erasing_flat * present_extra_gain),
             axis=-1,
             keepdims=True,
         )
         * content_part_lines
-    )
-    return (
-        (standardized_parts + present_extra_term)
-        .astype(jnp.bfloat16)
-        .reshape(-1, stored_memory_parts * subspace_span)
-    )
+    ).reshape(flat_shape)
+    return (standardized_parts + present_extra_term).astype(jnp.bfloat16)
 
 
 def in_device_order(pieces):
@@ -203,9 +199,14 @@
         .reshape(-1, span_width)
         for which_mix in range(5)
     ]
-    acceptor_entries = jnp.dot(blends[0], acceptor_projection, preferred_element_type=jnp.float32)
-    address_entries = jnp.dot(blends[2], address_projection, preferred_element_type=jnp.float32)
-    content_entries = jnp.dot(blends[3], content_projection, preferred_element_type=jnp.float32)
+    def project(blend, weight):
+        return lax.dot_general(
+            weight, blend, (((0,), (1,)), ((), ())), preferred_element_type=jnp.float32
+        ).T
+
+    acceptor_entries = project(blends[0], acceptor_projection)
+    address_entries = project(blends[2], address_projection)
+    content_entries = project(blends[3], content_projection)
     latent_response = jnp.tanh(
         jnp.dot(blends[1], fading_first_full, preferred_element_type=jnp.float32)
     ).astype(jnp.bfloat16)

time: 150 us -> 139 us (0.927)
  starting transfers between devices: 56.9 us -> 51 us
  local copies, waits for them, and re-layouts: 29 us -> 23.4 us
  waiting for transfers between devices: 21.6 us -> 26.9 us
  other arithmetic: 17 us -> 12.3 us
    all_to_all x1, waiting for transfers between devices: 0.01 us -> 6.5 us  [body(): lax.all_to_all(outgoing, 'req', split_axis=0, concat_axis=0, tiled=True)]
    all_to_all x1, starting transfers between devices: 12.6 us -> 7.36 us  [body(): lax.all_to_all(going_back, 'req', split_axis=0, concat_axis=0, tiled=True)]
    unnamed x4 -> x1, other arithmetic: 4.1 us -> 0.08 us
    unnamed x85 -> x94, local copies, waits for them, and re-layouts: 7.42 us -> 4.37 us
  transfers between devices with their start and end apart: 13 -> 13, of which waited for: 6 -> 7; matrix products, arithmetic and copies ran while one was open for 10% -> 5% of each run, Pallas kernels for 0% -> 0%
where the time goes in v7:
time: 139 us; the launch traced here: 138 us
  starting transfers between devices  51 us (37%)
  waiting for transfers between devices  26.9 us (19%)
  local copies, waits for them, and re-layouts  23.4 us (17%)
  Pallas kernels  16.1 us (12%)
  other arithmetic  12.3 us (9%)
  matrix products  6.48 us (5%)
  between operations  1.62 us (1%)
    all_to_all x1, starting transfers between devices, body(): lax.all_to_all(outgoing, 'req', split_axis=0, concat_axis=0, tiled=True)  16.6 us
    pallas_call x2, Pallas kernels, run_recurrence(): pl.pallas_call(recurrence_kernel, out_shape=jax.ShapeDtypeStruct((steps,...  16.1 us
    all_to_all x1, waiting for transfers between devices, body(): lax.all_to_all(going_back, 'req', split_axis=0, concat_axis=0, tiled=True)  12.5 us
    ppermute x3, starting transfers between devices, gather_heads(): lax.ppermute(block, 'head', [(i, (i + k) % n) for i in range(n)])  9.76 us
    ppermute x3, starting transfers between devices, scatter_heads(): lax.ppermute(chunk, 'head', [(i, (i + k) % n) for i in range(n)])  9.27 us
    all_to_all x1, starting transfers between devices, body(): lax.all_to_all(going_back, 'req', split_axis=0, concat_axis=0, tiled=True)  7.36 us
    pallas_call x2, other arithmetic, run_recurrence(): pl.pallas_call(recurrence_kernel, out_shape=jax.ShapeDtypeStruct((steps,...  6.84 us
    ppermute x4, starting transfers between devices, hand_over(): lax.ppermute(partial, ('section', 'head'), [(i, n + (i + k) % n) for i in...  6.74 us
  transfers between devices with their start and end apart: 13, of which 7 were waited for; matrix products, arithmetic and copies ran while one was open for 5% of the time, Pallas kernels for 0%

profile of v7, /device:TPU:6, one launch (start us, length us, event | category | flops | bytes accessed | tf_op | source)
XLA Modules:
  0.0 137.8 jit_solution(16194439868392197037)
XLA Ops:
  1.9 2.0 %scatter_fusion = bf16[64,4,256]{2,1,0:T(4,128)(2,1)} fusion(bf16[64,4,256]{2,1,0:T(4,128)(2,1)} %broadcast.450.clone, s32[8]{0:T(128)S(1)} %fusion.101, bf16[8,4,256]{2,1,0:T(4,128)(2,1)} %param.23), kind=kCustom, calls=%fused_computation.3 | custom fusion | bytes 49184 | tf_op jit(solution)/shard_map/scatter | solution.py:342
  3.9 16.6 %all-to-all-start = ((bf16[64,4,256]{2,1,0:T(4,128)(2,1)}), bf16[64,4,256]{2,1,0:T(4,128)(2,1)S(1)}, u32[]{:S(2)}, u32[]{:S(2)}) async-start(bf16[64,4,256]{2,1,0:T(4,128)(2,1)} %scatter_fusion), calls=%async_computation | async-start | bytes 262144 | tf_op jit(solution)/shard_map/all_to_all | solution.py:344
  23.0 0.9 copy.76
  24.0 0.9 copy.77
  25.1 1.5 %fusion.109 = (f32[1,1,1024]{2,1,0:T(1,128)}, f32[1,1,1024]{2,1,0:T(1,128)S(1)}, f32[1,1,1024]{2,1,0:T(1,128)S(1)}, f32[1,1,1024]{2,1,0:T(1,128)S(1)}, f32[1,1,1024]{2,1,0:T(1,128)S(1)}) fusion(bf16[1,5,1024]{2,1,0:T(8,128)(2,1)} %param.28), kind=kLoop, calls=%fused_computation.234 | loop fusion | bytes 40960 | tf_op jit(solution)/shard_map/slice | solution.py:197
  26.7 6.5 %all-to-all-done = bf16[64,4,256]{2,1,0:T(4,128)(2,1)S(1)} async-done(((bf16[64,4,256]{2,1,0:T(4,128)(2,1)}), bf16[64,4,256]{2,1,0:T(4,128)(2,1)S(1)}, u32[]{:S(2)}, u32[]{:S(2)}) %all-to-all-start) | async-done | bytes 131104 | tf_op jit(solution)/shard_map/all_to_all | solution.py:344
  33.9 2.7 %collective-permute-start = (bf16[59392]{0:T(1024)(128)(2,1)S(1)}, bf16[59392]{0:T(1024)(128)(2,1)S(1)}, u32[]{:S(2)}, u32[]{:S(2)}) collective-permute-start(bf16[59392]{0:T(1024)(128)(2,1)S(1)} %constant_dynamic-update-slice_fusion.23), channel_id=1, source_target_pairs={{0,3},{1,0},{2,1},{3,2},{4,7},{5,4},{6,5},{7,6},{8,11},{9,8},{10,9... | collective-permute-start | bytes 356360 | tf_op jit(solution)/shard_map/ppermute | solution.py:143
  36.6 3.0 %collective-permute-start.1 = (bf16[59392]{0:T(1024)(128)(2,1)S(1)}, bf16[59392]{0:T(1024)(128)(2,1)S(1)}, u32[]{:S(2)}, u32[]{:S(2)}) collective-permute-start(bf16[59392]{0:T(1024)(128)(2,1)S(1)} %constant_dynamic-update-slice_fusion.23), channel_id=1, source_target_pairs={{0,2},{1,3},{2,0},{3,1},{4,6},{5,7},{6,4},{7,5},{8,10},{9,11},{10,... | collective-permute-start | bytes 356360 | tf_op jit(solution)/shard_map/ppermute | solution.py:143
  39.7 4.0 %collective-permute-start.2 = (bf16[59392]{0:T(1024)(128)(2,1)S(1)}, bf16[59392]{0:T(1024)(128)(2,1)S(1)}, u32[]{:S(2)}, u32[]{:S(2)}) collective-permute-start(bf16[59392]{0:T(1024)(128)(2,1)S(1)} %constant_dynamic-update-slice_fusion.23), channel_id=1, source_target_pairs={{0,1},{1,2},{2,3},{3,0},{4,5},{5,6},{6,7},{7,4},{8,9},{9,10},{10,1... | collective-permute-start | bytes 356360 | tf_op jit(solution)/shard_map/ppermute | solution.py:143
  44.9 1.7 %collective-permute-done.2 = bf16[59392]{0:T(1024)(128)(2,1)S(1)} collective-permute-done((bf16[59392]{0:T(1024)(128)(2,1)S(1)}, bf16[59392]{0:T(1024)(128)(2,1)S(1)}, u32[]{:S(2)}, u32[]{:S(2)}) %collective-permute-start.2) | collective-permute-done | bytes 118816 | tf_op jit(solution)/shard_map/ppermute | solution.py:143
  50.4 1.2 fusion.74
  53.2 2.7 %copy.85.content_ref = f32[4,32,64,1]{3,2,1,0:T(8,128)} copy(f32[4,32,64,1]{2,1,0,3:T(8,128)S(1)} %bitcast.172) | data formatting | bytes 65536 | tf_op jit(solution)/shard_map/reshape;reshape | solution.py:99
  56.7 8.1 %shard_map.199 = f32[4,32,64,1]{3,2,1,0:T(8,128)} custom-call(f32[32,64,64]{2,1,0:T(8,128)} %bitcast.161, f32[4,5,32,1,64]{4,3,2,1,0:T(1,128)} %copy-done.4, f32[4,32,64,1]{3,2,1,0:T(8,128)} %copy.85.content_ref), custom_call_target="tpu_custom_call" | custom-call | tf_op jit(solution)/shard_map/pallas_call | solution.py:27
  64.9 3.5 %reduce = f32[4,32,64]{2,1,0:T(8,128)S(1)} reduce(f32[4,32,64,1]{3,2,1,0:T(8,128)} %shard_map.199, f32[]{:T(128)} %constant.200), dimensions={3}, to_apply=%pallas_call.6.reduce_sub_computation | reduce | bytes 65540 | tf_op jit(solution)/shard_map/pallas_call | solution.py:27
  69.5 1.3 collective-permute-start.3
  70.8 2.7 %collective-permute-start.4 = (f32[32,1024]{1,0:T(8,128)S(1)}, f32[32,1024]{1,0:T(8,128)S(1)}, u32[]{:S(2)}, u32[]{:S(2)}) collective-permute-start(f32[32,1024]{1,0:T(8,128)S(1)} %fusion.16), channel_id=1, source_target_pairs={{0,257},{1,258},{2,259},{3,256},{4,261},{5,262},{6,263},{7,260},{8... | collective-permute-start | bytes 393224 | tf_op jit(solution)/shard_map/ppermute | solution.py:162
  73.4 1.3 collective-permute-start.5
  74.7 1.5 %collective-permute-start.6 = (f32[32,1024]{1,0:T(8,128)S(1)}, f32[32,1024]{1,0:T(8,128)S(1)}, u32[]{:S(2)}, u32[]{:S(2)}) collective-permute-start(f32[32,1024]{1,0:T(8,128)S(1)} %fusion.16), channel_id=1, source_target_pairs={{0,259},{1,256},{2,257},{3,258},{4,263},{5,260},{6,261},{7,262},{8... | collective-permute-start | bytes 393224 | tf_op jit(solution)/shard_map/ppermute | solution.py:162
  77.2 1.4 collective-permute-done.6
  79.1 1.0 fusion.5
  80.3 1.1 fusion.79
  82.7 2.7 %copy.94.content_ref = f32[4,32,64,1]{3,2,1,0:T(8,128)} copy(f32[4,32,64,1]{2,1,0,3:T(8,128)S(1)} %bitcast.173) | data formatting | bytes 65536 | tf_op jit(solution)/shard_map/reshape;reshape | solution.py:99
  86.9 8.1 %shard_map.200 = f32[4,32,64,1]{3,2,1,0:T(8,128)} custom-call(f32[32,64,64]{2,1,0:T(8,128)} %bitcast.162, f32[4,5,32,1,64]{4,3,2,1,0:T(1,128)} %copy-done.5, f32[4,32,64,1]{3,2,1,0:T(8,128)} %copy.94.content_ref), custom_call_target="tpu_custom_call" | custom-call | tf_op jit(solution)/shard_map/pallas_call | solution.py:27
  94.9 3.4 %reduce.1 = f32[4,32,64]{2,1,0:T(8,128)S(1)} reduce(f32[4,32,64,1]{3,2,1,0:T(8,128)} %shard_map.200, f32[]{:T(128)} %constant.200), dimensions={3}, to_apply=%pallas_call.7.reduce_sub_computation | reduce | bytes 65540 | tf_op jit(solution)/shard_map/pallas_call | solution.py:27
  99.5 3.4 %collective-permute-start.10 = (f32[32,256]{1,0:T(8,128)S(1)}, f32[32,256]{1,0:T(8,128)S(1)}, u32[]{:S(2)}, u32[]{:S(2)}) collective-permute-start(f32[32,256]{1,0:T(8,128)S(1)} %get-tuple-element.26), channel_id=1, source_target_pairs={{0,3},{1,0},{2,1},{3,2},{4,7},{5,4},{6,5},{7,6},{8,11},{9,8},{10,9... | collective-permute-start | bytes 98312 | tf_op jit(solution)/shard_map/ppermute | solution.py:154
  102.8 3.7 %collective-permute-start.8 = (f32[32,256]{1,0:T(8,128)S(1)}, f32[32,256]{1,0:T(8,128)S(1)}, u32[]{:S(2)}, u32[]{:S(2)}) collective-permute-start(f32[32,256]{1,0:T(8,128)S(1)} %get-tuple-element.25), channel_id=1, source_target_pairs={{0,1},{1,2},{2,3},{3,0},{4,5},{5,6},{6,7},{7,4},{8,9},{9,10},{10,1... | collective-permute-start | bytes 98312 | tf_op jit(solution)/shard_map/ppermute | solution.py:154
  106.5 2.2 %collective-permute-start.9 = (f32[32,256]{1,0:T(8,128)S(1)}, f32[32,256]{1,0:T(8,128)S(1)}, u32[]{:S(2)}, u32[]{:S(2)}) collective-permute-start(f32[32,256]{1,0:T(8,128)S(1)} %get-tuple-element.27), channel_id=1, source_target_pairs={{0,2},{1,3},{2,0},{3,1},{4,6},{5,7},{6,4},{7,5},{8,10},{9,11},{10,... | collective-permute-start | bytes 98312 | tf_op jit(solution)/shard_map/ppermute | solution.py:154
  108.8 1.3 collective-permute-start.7
  110.1 3.7 %collective-permute-done.9 = f32[32,256]{1,0:T(8,128)S(1)} collective-permute-done((f32[32,256]{1,0:T(8,128)S(1)}, f32[32,256]{1,0:T(8,128)S(1)}, u32[]{:S(2)}, u32[]{:S(2)}) %collective-permute-start.9) | collective-permute-done | bytes 32800 | tf_op jit(solution)/shard_map/ppermute | solution.py:154
  114.6 1.9 %scatter_fusion.1 = bf16[64,4,256]{2,1,0:T(4,128)(2,1)} fusion(bf16[64,4,256]{2,1,0:T(4,128)(2,1)} %broadcast.450, s32[8]{0:T(128)S(1)} %copy-done.33, bf16[8,4,256]{2,1,0:T(4,128)(2,1)S(1)} %fusion.88), kind=kCustom, calls=%fused_computation.4 | custom fusion | bytes 49184 | tf_op jit(solution)/shard_map/scatter | solution.py:348
  116.5 7.4 %all-to-all-start.1 = ((bf16[64,4,256]{2,1,0:T(4,128)(2,1)}), bf16[64,4,256]{2,1,0:T(4,128)(2,1)S(1)}, u32[]{:S(2)}, u32[]{:S(2)}) async-start(bf16[64,4,256]{2,1,0:T(4,128)(2,1)} %scatter_fusion.1), calls=%async_computation.1 | async-start | bytes 262144 | tf_op jit(solution)/shard_map/all_to_all | solution.py:350
  124.0 12.5 %all-to-all-done.1 = bf16[64,4,256]{2,1,0:T(4,128)(2,1)S(1)} async-done(((bf16[64,4,256]{2,1,0:T(4,128)(2,1)}), bf16[64,4,256]{2,1,0:T(4,128)(2,1)S(1)}, u32[]{:S(2)}, u32[]{:S(2)}) %all-to-all-start.1) | async-done | bytes 131104 | tf_op jit(solution)/shard_map/all_to_all | solution.py:350
  (241 shorter events, 20.4 us)
Async XLA Ops:
  0.0 69.3 %copy-start = (bf16[1,256,1024]{2,1,0:T(8,128)(2,1)S(1)}, bf16[1,256,1024]{2,1,0:T(8,128)(2,1)}, u32[]{:S(2)}) copy-start(bf16[1,256,1024]{2,1,0:T(8,128)(2,1)} %param.32) | copy-start | bytes 1572868
  0.0 48.0 %copy-start.32 = (f32[1,256]{1,0:T(1,128)S(1)}, f32[1,256]{1,0:T(1,128)}, u32[]{:S(2)}) copy-start(f32[1,256]{1,0:T(1,128)} %param.38) | copy-start | bytes 3076
  0.0 48.0 %copy-start.14 = (bf16[1,96,256]{2,1,0:T(8,128)(2,1)S(1)}, bf16[1,96,256]{2,1,0:T(8,128)(2,1)}, u32[]{:S(2)}) copy-start(bf16[1,96,256]{2,1,0:T(8,128)(2,1)} %param.36) | copy-start | bytes 147460
  0.0 48.4 %copy-start.3 = (bf16[1,1024,256]{2,1,0:T(8,128)(2,1)S(1)}, bf16[1,1024,256]{2,1,0:T(8,128)(2,1)}, u32[]{:S(2)}) copy-start(bf16[1,1024,256]{2,1,0:T(8,128)(2,1)} %param.30) | copy-start | bytes 1572868
  0.0 48.6 %copy-start.30 = (f32[1,256]{1,0:T(1,128)S(1)}, f32[1,256]{1,0:T(1,128)}, u32[]{:S(2)}) copy-start(f32[1,256]{1,0:T(1,128)} %param.39) | copy-start | bytes 3076
  0.0 48.6 %copy-start.29 = (f32[1,256]{1,0:T(1,128)S(1)}, f32[1,256]{1,0:T(1,128)}, u32[]{:S(2)}) copy-start(f32[1,256]{1,0:T(1,128)} %param.40) | copy-start | bytes 3076
  0.0 48.6 %copy-start.28 = (f32[1,256]{1,0:T(1,128)S(1)}, f32[1,256]{1,0:T(1,128)}, u32[]{:S(2)}) copy-start(f32[1,256]{1,0:T(1,128)} %param.41) | copy-start | bytes 3076
  0.1 48.6 %copy-start.2 = (bf16[1,1024,256]{2,1,0:T(8,128)(2,1)S(1)}, bf16[1,1024,256]{2,1,0:T(8,128)(2,1)}, u32[]{:S(2)}) copy-start(bf16[1,1024,256]{2,1,0:T(8,128)(2,1)} %param.29) | copy-start | bytes 1572868
  1.2 23.9 %copy-start.31 = (s32[8]{0:T(128)}, s32[8]{0:T(128)S(1)}, u32[]{:S(2)}) copy-start(s32[8]{0:T(128)S(1)} %convert_reduce_fusion) | copy-start | bytes 100
  3.9 29.3 %all-to-all-start = ((bf16[64,4,256]{2,1,0:T(4,128)(2,1)}), bf16[64,4,256]{2,1,0:T(4,128)(2,1)S(1)}, u32[]{:S(2)}, u32[]{:S(2)}) async-start(bf16[64,4,256]{2,1,0:T(4,128)(2,1)} %scatter_fusion), calls=%async_computation | async-start | bytes 262144 | tf_op jit(solution)/shard_map/all_to_all | solution.py:344
  26.6 23.2 %copy-start.16 = (f32[1,1,1024]{2,1,0:T(1,128)}, f32[1,1,1024]{2,1,0:T(1,128)S(1)}, u32[]{:S(2)}) copy-start(f32[1,1,1024]{2,1,0:T(1,128)S(1)} %get-tuple-element.45) | copy-start | bytes 12292
  26.6 23.2 %copy-start.18 = (f32[1,1,1024]{2,1,0:T(1,128)}, f32[1,1,1024]{2,1,0:T(1,128)S(1)}, u32[]{:S(2)}) copy-start(f32[1,1,1024]{2,1,0:T(1,128)S(1)} %get-tuple-element.46) | copy-start | bytes 12292
  26.6 23.3 %copy-start.20 = (f32[1,1,1024]{2,1,0:T(1,128)}, f32[1,1,1024]{2,1,0:T(1,128)S(1)}, u32[]{:S(2)}) copy-start(f32[1,1,1024]{2,1,0:T(1,128)S(1)} %get-tuple-element.43) | copy-start | bytes 12292
  26.6 23.3 %copy-start.23 = (f32[1,1,1024]{2,1,0:T(1,128)}, f32[1,1,1024]{2,1,0:T(1,128)S(1)}, u32[]{:S(2)}) copy-start(f32[1,1,1024]{2,1,0:T(1,128)S(1)} %get-tuple-element.44) | copy-start | bytes 12292
  33.9 10.3 %collective-permute-start = (bf16[59392]{0:T(1024)(128)(2,1)S(1)}, bf16[59392]{0:T(1024)(128)(2,1)S(1)}, u32[]{:S(2)}, u32[]{:S(2)}) collective-permute-start(bf16[59392]{0:T(1024)(128)(2,1)S(1)} %constant_dynamic-update-slice_fusion.23), channel_id=1, source_target_pairs={{0,3},{1,0},{2,1},{3,2},{4,7},{5,4},{6,5},{7,6},{8,11},{9,8},{10,9... | collective-permute-start | bytes 356360 | tf_op jit(solution)/shard_map/ppermute | solution.py:143
  36.6 8.2 %collective-permute-start.1 = (bf16[59392]{0:T(1024)(128)(2,1)S(1)}, bf16[59392]{0:T(1024)(128)(2,1)S(1)}, u32[]{:S(2)}, u32[]{:S(2)}) collective-permute-start(bf16[59392]{0:T(1024)(128)(2,1)S(1)} %constant_dynamic-update-slice_fusion.23), channel_id=1, source_target_pairs={{0,2},{1,3},{2,0},{3,1},{4,6},{5,7},{6,4},{7,5},{8,10},{9,11},{10,... | collective-permute-start | bytes 356360 | tf_op jit(solution)/shard_map/ppermute | solution.py:143
  39.7 6.9 %collective-permute-start.2 = (bf16[59392]{0:T(1024)(128)(2,1)S(1)}, bf16[59392]{0:T(1024)(128)(2,1)S(1)}, u32[]{:S(2)}, u32[]{:S(2)}) collective-permute-start(bf16[59392]{0:T(1024)(128)(2,1)S(1)} %constant_dynamic-update-slice_fusion.23), channel_id=1, source_target_pairs={{0,1},{1,2},{2,3},{3,0},{4,5},{5,6},{6,7},{7,4},{8,9},{9,10},{10,1... | collective-permute-start | bytes 356360 | tf_op jit(solution)/shard_map/ppermute | solution.py:143
  64.8 14.3 %copy-start.15 = (bf16[1,96,256]{2,1,0:T(8,128)(2,1)S(1)}, bf16[1,96,256]{2,1,0:T(8,128)(2,1)}, u32[]{:S(2)}) copy-start(bf16[1,96,256]{2,1,0:T(8,128)(2,1)} %param.36) | copy-start | bytes 147460
  64.8 15.3 %copy-start.19 = (f32[1,1,1024]{2,1,0:T(1,128)S(1)}, f32[1,1,1024]{2,1,0:T(1,128)}, u32[]{:S(2)}) copy-start(f32[1,1,1024]{2,1,0:T(1,128)} %copy-done.18) | copy-start | bytes 12292
  64.8 15.4 %copy-start.22 = (f32[1,1,1024]{2,1,0:T(1,128)S(1)}, f32[1,1,1024]{2,1,0:T(1,128)}, u32[]{:S(2)}) copy-start(f32[1,1,1024]{2,1,0:T(1,128)} %get-tuple-element.42) | copy-start | bytes 12292
  64.9 16.7 %copy-start.17 = (f32[1,1,1024]{2,1,0:T(1,128)S(1)}, f32[1,1,1024]{2,1,0:T(1,128)}, u32[]{:S(2)}) copy-start(f32[1,1,1024]{2,1,0:T(1,128)} %copy-done.16) | copy-start | bytes 12292
  69.5 7.4 %collective-permute-start.3 = (f32[32,1024]{1,0:T(8,128)S(1)}, f32[32,1024]{1,0:T(8,128)S(1)}, u32[]{:S(2)}, u32[]{:S(2)}) collective-permute-start(f32[32,1024]{1,0:T(8,128)S(1)} %fusion.16), channel_id=1, source_target_pairs={{0,256},{1,257},{2,258},{3,259},{4,260},{5,261},{6,262},{7,263},{8... | collective-permute-start | bytes 393224 | tf_op jit(solution)/shard_map/ppermute | solution.py:162
  70.8 6.1 %collective-permute-start.4 = (f32[32,1024]{1,0:T(8,128)S(1)}, f32[32,1024]{1,0:T(8,128)S(1)}, u32[]{:S(2)}, u32[]{:S(2)}) collective-permute-start(f32[32,1024]{1,0:T(8,128)S(1)} %fusion.16), channel_id=1, source_target_pairs={{0,257},{1,258},{2,259},{3,256},{4,261},{5,262},{6,263},{7,260},{8... | collective-permute-start | bytes 393224 | tf_op jit(solution)/shard_map/ppermute | solution.py:162
  73.4 3.8 %collective-permute-start.5 = (f32[32,1024]{1,0:T(8,128)S(1)}, f32[32,1024]{1,0:T(8,128)S(1)}, u32[]{:S(2)}, u32[]{:S(2)}) collective-permute-start(f32[32,1024]{1,0:T(8,128)S(1)} %fusion.16), channel_id=1, source_target_pairs={{0,258},{1,259},{2,256},{3,257},{4,262},{5,263},{6,260},{7,261},{8... | collective-permute-start | bytes 393224 | tf_op jit(solution)/shard_map/ppermute | solution.py:162
  74.7 3.9 %collective-permute-start.6 = (f32[32,1024]{1,0:T(8,128)S(1)}, f32[32,1024]{1,0:T(8,128)S(1)}, u32[]{:S(2)}, u32[]{:S(2)}) collective-permute-start(f32[32,1024]{1,0:T(8,128)S(1)} %fusion.16), channel_id=1, source_target_pairs={{0,259},{1,256},{2,257},{3,258},{4,263},{5,260},{6,261},{7,262},{8... | collective-permute-start | bytes 393224 | tf_op jit(solution)/shard_map/ppermute | solution.py:162
  94.9 19.7 %copy-start.33 = (s32[8]{0:T(128)S(1)}, s32[8]{0:T(128)}, u32[]{:S(2)}) copy-start(s32[8]{0:T(128)} %fusion.100) | copy-start | bytes 100
  94.9 28.9 %copy-start.34 = (s32[8]{0:T(128)S(1)}, s32[8]{0:T(128)}, u32[]{:S(2)}) copy-start(s32[8]{0:T(128)} %param.24) | copy-start | bytes 100
  99.5 10.6 %collective-permute-start.10 = (f32[32,256]{1,0:T(8,128)S(1)}, f32[32,256]{1,0:T(8,128)S(1)}, u32[]{:S(2)}, u32[]{:S(2)}) collective-permute-start(f32[32,256]{1,0:T(8,128)S(1)} %get-tuple-element.26), channel_id=1, source_target_pairs={{0,3},{1,0},{2,1},{3,2},{4,7},{5,4},{6,5},{7,6},{8,11},{9,8},{10,9... | collective-permute-start | bytes 98312 | tf_op jit(solution)/shard_map/ppermute | solution.py:154
  102.8 7.2 %collective-permute-start.8 = (f32[32,256]{1,0:T(8,128)S(1)}, f32[32,256]{1,0:T(8,128)S(1)}, u32[]{:S(2)}, u32[]{:S(2)}) collective-permute-start(f32[32,256]{1,0:T(8,128)S(1)} %get-tuple-element.25), channel_id=1, source_target_pairs={{0,1},{1,2},{2,3},{3,0},{4,5},{5,6},{6,7},{7,4},{8,9},{9,10},{10,1... | collective-permute-start | bytes 98312 | tf_op jit(solution)/shard_map/ppermute | solution.py:154
  106.5 7.3 %collective-permute-start.9 = (f32[32,256]{1,0:T(8,128)S(1)}, f32[32,256]{1,0:T(8,128)S(1)}, u32[]{:S(2)}, u32[]{:S(2)}) collective-permute-start(f32[32,256]{1,0:T(8,128)S(1)} %get-tuple-element.27), channel_id=1, source_target_pairs={{0,2},{1,3},{2,0},{3,1},{4,6},{5,7},{6,4},{7,5},{8,10},{9,11},{10,... | collective-permute-start | bytes 98312 | tf_op jit(solution)/shard_map/ppermute | solution.py:154
  108.8 5.1 %collective-permute-start.7 = (bf16[8,4,256]{2,1,0:T(4,128)(2,1)S(1)}, bf16[8,4,256]{2,1,0:T(4,128)(2,1)S(1)}, u32[]{:S(2)}, u32[]{:S(2)}) collective-permute-start(bf16[8,4,256]{2,1,0:T(4,128)(2,1)S(1)} %constant_dynamic-slice_fusion.2), channel_id=1, source_target_pairs={{256,0},{257,1},{258,2},{259,3},{260,4},{261,5},{262,6},{263,7},{2... | collective-permute-start | bytes 49160 | tf_op jit(solution)/shard_map/ppermute | solution.py:169
  116.5 20.0 %all-to-all-start.1 = ((bf16[64,4,256]{2,1,0:T(4,128)(2,1)}), bf16[64,4,256]{2,1,0:T(4,128)(2,1)S(1)}, u32[]{:S(2)}, u32[]{:S(2)}) async-start(bf16[64,4,256]{2,1,0:T(4,128)(2,1)} %scatter_fusion.1), calls=%async_computation.1 | async-start | bytes 262144 | tf_op jit(solution)/shard_map/all_to_all | solution.py:350
  (16 other events, 100.1 us)

commit v8 on v7

--- a/solution.py
+++ b/solution.py
@@ -16,9 +16,15 @@
         normed_learn = vector_ref[position, 2]
         erasing = vector_ref[position, 3]
         acceptor = vector_ref[position, 4]
+        content = content_ref[position]
         pulled = jnp.sum(states * normed, axis=-1, keepdims=True)
-        states = states * decay - pulled * normed_learn + content_ref[position] * erasing
-        read_ref[position] = jnp.sum(states * acceptor, axis=-1, keepdims=True)
+        added = jnp.einsum(
+            "bqi,bqj->bij", content, erasing, precision=highest, preferred_element_type=jnp.float32
+        )
+        states = states * decay - pulled * normed_learn + added
+        read_ref[position] = jnp.einsum(
+            "bqj,bij->bqi", acceptor, states, precision=highest, preferred_element_type=jnp.float32
+        )
 
 
 def run_recurrence(starting_memory, vectors, content):
@@ -26,7 +32,7 @@
     blocks, span, _ = starting_memory.shape
     return pl.pallas_call(
         recurrence_kernel,
-        out_shape=jax.ShapeDtypeStruct((steps, blocks, span, 1), jnp.float32),
+        out_shape=jax.ShapeDtypeStruct((steps, blocks, 1, span), jnp.float32),
         in_specs=[pl.BlockSpec(memory_space=pltpu.VMEM)] * 3,
         out_specs=pl.BlockSpec(memory_space=pltpu.VMEM),
     )(starting_memory, vectors, content)
@@ -96,9 +102,7 @@
         ],
         axis=1,
     )
-    content = by_step(content_part_lines).reshape(
-        steps_count, batch_rows * stored_memory_parts, subspace_span, 1
-    )
+    content = by_step(content_part_lines)
     read = run_recurrence(
         starting_memory.reshape(batch_rows * stored_memory_parts, subspace_span, subspace_span),
         vectors,

time: 139 us -> 139 us (level)
  Pallas kernels: 16.1 us -> 24 us
  other arithmetic: 12.3 us -> 6.03 us
  matrix products: 6.48 us -> 3.34 us
  waiting for transfers between devices: 26.9 us -> 29.5 us
  starting transfers between devices: 51 us -> 48.8 us
    unnamed x94 -> x128, local copies, waits for them, and re-layouts: 4.37 us -> 12.9 us
    pallas_call x2, Pallas kernels: 16.1 us -> 24 us  [run_recurrence(): pl.pallas_call(recurrence_kernel, out_shape=jax.ShapeDtypeStruct((steps,...]
    pallas_call x2 -> x0, other arithmetic: 6.84 us -> none  [run_recurrence(): pl.pallas_call(recurrence_kernel, out_shape=jax.ShapeDtypeStruct((steps,...]
    another operation x4 -> x2, local copies, waits for them, and re-layouts: 6.8 us -> 1.38 us  [the longest x2 5.44 us: sequence_recurrence(): by_step(content_part_lines)]
    all_to_all x1, waiting for transfers between devices: 6.5 us -> 8.96 us  [body(): lax.all_to_all(outgoing, 'req', split_axis=0, concat_axis=0, tiled=True)]
    all_to_all x1, starting transfers between devices: 7.36 us -> 4.92 us  [body(): lax.all_to_all(going_back, 'req', split_axis=0, concat_axis=0, tiled=True)]
    reduce_sum x2, other arithmetic: 0.21 us -> 2.03 us  [sequence_recurrence(): center = read_all - jnp.mean(read_all, axis=-1, keepdims=True)]
    dot_general x2, matrix products: 2.36 us -> 0.64 us  [sequence_recurrence(): jnp.dot(latent_response, fading_second_lowrank, preferred_element_type=jn...]
  transfers between devices with their start and end apart: 13 -> 13, of which waited for: 7 -> 7; matrix products, arithmetic and copies ran while one was open for 5% -> 2% of each run, Pallas kernels for 0% -> 0%
where the time goes in v8:
time: 139 us; the launch traced here: 138 us
  starting transfers between devices  48.8 us (35%)
  waiting for transfers between devices  29.5 us (21%)
  local copies, waits for them, and re-layouts  24.7 us (18%)
  Pallas kernels  24 us (17%)
  other arithmetic  6.03 us (4%)
  matrix products  3.34 us (2%)
  between operations  1.63 us (1%)
    pallas_call x2, Pallas kernels, run_recurrence(): pl.pallas_call(recurrence_kernel, out_shape=jax.ShapeDtypeStruct((steps,...  24 us
    all_to_all x1, starting transfers between devices, body(): lax.all_to_all(outgoing, 'req', split_axis=0, concat_axis=0, tiled=True)  16.6 us
    unnamed x128, local copies, waits for them, and re-layouts  12.9 us
    all_to_all x1, waiting for transfers between devices, body(): lax.all_to_all(going_back, 'req', split_axis=0, concat_axis=0, tiled=True)  12.4 us
    ppermute x3, starting transfers between devices, gather_heads(): lax.ppermute(block, 'head', [(i, (i + k) % n) for i in range(n)])  9.94 us
    ppermute x3, starting transfers between devices, scatter_heads(): lax.ppermute(chunk, 'head', [(i, (i + k) % n) for i in range(n)])  9.27 us
    all_to_all x1, waiting for transfers between devices, body(): lax.all_to_all(outgoing, 'req', split_axis=0, concat_axis=0, tiled=True)  8.96 us
    ppermute x4, starting transfers between devices, hand_over(): lax.ppermute(partial, ('section', 'head'), [(i, n + (i + k) % n) for i in...  6.78 us
  transfers between devices with their start and end apart: 13, of which 7 were waited for; matrix products, arithmetic and copies ran while one was open for 2% of the time, Pallas kernels for 0%

profile of v8, /device:TPU:6, one launch (start us, length us, event | category | flops | bytes accessed | tf_op | source)
XLA Modules:
  0.0 138.0 jit_solution(10629867205976887816)
XLA Ops:
  0.0 0.7 copy-done.34
  2.3 1.9 %scatter_fusion = bf16[64,4,256]{2,1,0:T(4,128)(2,1)} fusion(bf16[64,4,256]{2,1,0:T(4,128)(2,1)} %broadcast.450.clone, s32[8]{0:T(128)S(1)} %fusion.101, bf16[8,4,256]{2,1,0:T(4,128)(2,1)S(1)} %copy-done.33), kind=kCustom, calls=%fused_computation.3 | custom fusion | bytes 49184 | tf_op jit(solution)/shard_map/scatter | solution.py:346
  4.2 16.6 %all-to-all-start = ((bf16[64,4,256]{2,1,0:T(4,128)(2,1)}), bf16[64,4,256]{2,1,0:T(4,128)(2,1)S(1)}, u32[]{:S(2)}, u32[]{:S(2)}) async-start(bf16[64,4,256]{2,1,0:T(4,128)(2,1)} %scatter_fusion), calls=%async_computation | async-start | bytes 262144 | tf_op jit(solution)/shard_map/all_to_all | solution.py:348
  24.6 9.0 %all-to-all-done = bf16[64,4,256]{2,1,0:T(4,128)(2,1)S(1)} async-done(((bf16[64,4,256]{2,1,0:T(4,128)(2,1)}), bf16[64,4,256]{2,1,0:T(4,128)(2,1)S(1)}, u32[]{:S(2)}, u32[]{:S(2)}) %all-to-all-start) | async-done | bytes 131104 | tf_op jit(solution)/shard_map/all_to_all | solution.py:348
  34.3 2.7 %collective-permute-start = (bf16[59392]{0:T(1024)(128)(2,1)S(1)}, bf16[59392]{0:T(1024)(128)(2,1)S(1)}, u32[]{:S(2)}, u32[]{:S(2)}) collective-permute-start(bf16[59392]{0:T(1024)(128)(2,1)S(1)} %constant_dynamic-update-slice_fusion.23), channel_id=1, source_target_pairs={{0,3},{1,0},{2,1},{3,2},{4,7},{5,4},{6,5},{7,6},{8,11},{9,8},{10,9... | collective-permute-start | bytes 356360 | tf_op jit(solution)/shard_map/ppermute | solution.py:147
  37.0 3.0 %collective-permute-start.1 = (bf16[59392]{0:T(1024)(128)(2,1)S(1)}, bf16[59392]{0:T(1024)(128)(2,1)S(1)}, u32[]{:S(2)}, u32[]{:S(2)}) collective-permute-start(bf16[59392]{0:T(1024)(128)(2,1)S(1)} %constant_dynamic-update-slice_fusion.23), channel_id=1, source_target_pairs={{0,2},{1,3},{2,0},{3,1},{4,6},{5,7},{6,4},{7,5},{8,10},{9,11},{10,... | collective-permute-start | bytes 356360 | tf_op jit(solution)/shard_map/ppermute | solution.py:147
  40.1 4.2 %collective-permute-start.2 = (bf16[59392]{0:T(1024)(128)(2,1)S(1)}, bf16[59392]{0:T(1024)(128)(2,1)S(1)}, u32[]{:S(2)}, u32[]{:S(2)}) collective-permute-start(bf16[59392]{0:T(1024)(128)(2,1)S(1)} %constant_dynamic-update-slice_fusion.23), channel_id=1, source_target_pairs={{0,1},{1,2},{2,3},{3,0},{4,5},{5,6},{6,7},{7,4},{8,9},{9,10},{10,1... | collective-permute-start | bytes 356360 | tf_op jit(solution)/shard_map/ppermute | solution.py:147
  45.3 1.7 %collective-permute-done.2 = bf16[59392]{0:T(1024)(128)(2,1)S(1)} collective-permute-done((bf16[59392]{0:T(1024)(128)(2,1)S(1)}, bf16[59392]{0:T(1024)(128)(2,1)S(1)}, u32[]{:S(2)}, u32[]{:S(2)}) %collective-permute-start.2) | collective-permute-done | bytes 118816 | tf_op jit(solution)/shard_map/ppermute | solution.py:147
  48.5 0.7 copy-done.18
  50.5 0.8 multiply_multiply_fusion.1
  52.3 0.7 copy-done.20
  55.4 0.7 copy-done.6
  56.1 12.0 %shard_map.199 = f32[4,32,1,64]{3,2,1,0:T(1,128)} custom-call(f32[32,64,64]{2,1,0:T(8,128)} %bitcast.161, f32[4,5,32,1,64]{4,3,2,1,0:T(1,128)} %copy-done.6, f32[4,32,1,64]{3,2,1,0:T(1,128)} %bitcast.172), custom_call_target="tpu_custom_call" | custom-call | tf_op jit(solution)/shard_map/pallas_call | solution.py:33
  68.1 1.0 reduce_sum.112
  71.5 1.3 collective-permute-start.3
  72.8 2.7 %collective-permute-start.4 = (f32[32,1024]{1,0:T(8,128)S(1)}, f32[32,1024]{1,0:T(8,128)S(1)}, u32[]{:S(2)}, u32[]{:S(2)}) collective-permute-start(f32[32,1024]{1,0:T(8,128)S(1)} %fusion.16), channel_id=1, source_target_pairs={{0,257},{1,258},{2,259},{3,256},{4,261},{5,262},{6,263},{7,260},{8... | collective-permute-start | bytes 393224 | tf_op jit(solution)/shard_map/ppermute | solution.py:166
  75.5 1.3 collective-permute-start.5
  76.8 1.5 %collective-permute-start.6 = (f32[32,1024]{1,0:T(8,128)S(1)}, f32[32,1024]{1,0:T(8,128)S(1)}, u32[]{:S(2)}, u32[]{:S(2)}) collective-permute-start(f32[32,1024]{1,0:T(8,128)S(1)} %fusion.16), channel_id=1, source_target_pairs={{0,259},{1,256},{2,257},{3,258},{4,263},{5,260},{6,261},{7,262},{8... | collective-permute-start | bytes 393224 | tf_op jit(solution)/shard_map/ppermute | solution.py:166
  78.4 0.9 collective-permute-done.5
  79.3 1.4 collective-permute-done.6
  81.0 0.7 copy-done.19
  86.8 0.7 copy-done.7
  87.5 12.0 %shard_map.200 = f32[4,32,1,64]{3,2,1,0:T(1,128)} custom-call(f32[32,64,64]{2,1,0:T(8,128)} %bitcast.162, f32[4,5,32,1,64]{4,3,2,1,0:T(1,128)} %copy-done.7, f32[4,32,1,64]{3,2,1,0:T(1,128)} %bitcast.173), custom_call_target="tpu_custom_call" | custom-call | tf_op jit(solution)/shard_map/pallas_call | solution.py:33
  99.5 1.0 reduce_sum.116
  101.5 3.4 %collective-permute-start.10 = (f32[32,256]{1,0:T(8,128)S(1)}, f32[32,256]{1,0:T(8,128)S(1)}, u32[]{:S(2)}, u32[]{:S(2)}) collective-permute-start(f32[32,256]{1,0:T(8,128)S(1)} %get-tuple-element.26), channel_id=1, source_target_pairs={{0,3},{1,0},{2,1},{3,2},{4,7},{5,4},{6,5},{7,6},{8,11},{9,8},{10,9... | collective-permute-start | bytes 98312 | tf_op jit(solution)/shard_map/ppermute | solution.py:158
  104.9 3.7 %collective-permute-start.8 = (f32[32,256]{1,0:T(8,128)S(1)}, f32[32,256]{1,0:T(8,128)S(1)}, u32[]{:S(2)}, u32[]{:S(2)}) collective-permute-start(f32[32,256]{1,0:T(8,128)S(1)} %get-tuple-element.25), channel_id=1, source_target_pairs={{0,1},{1,2},{2,3},{3,0},{4,5},{5,6},{6,7},{7,4},{8,9},{9,10},{10,1... | collective-permute-start | bytes 98312 | tf_op jit(solution)/shard_map/ppermute | solution.py:158
  108.6 2.2 %collective-permute-start.9 = (f32[32,256]{1,0:T(8,128)S(1)}, f32[32,256]{1,0:T(8,128)S(1)}, u32[]{:S(2)}, u32[]{:S(2)}) collective-permute-start(f32[32,256]{1,0:T(8,128)S(1)} %get-tuple-element.27), channel_id=1, source_target_pairs={{0,2},{1,3},{2,0},{3,1},{4,6},{5,7},{6,4},{7,5},{8,10},{9,11},{10,... | collective-permute-start | bytes 98312 | tf_op jit(solution)/shard_map/ppermute | solution.py:158
  110.9 1.3 collective-permute-start.7
  112.2 3.7 %collective-permute-done.9 = f32[32,256]{1,0:T(8,128)S(1)} collective-permute-done((f32[32,256]{1,0:T(8,128)S(1)}, f32[32,256]{1,0:T(8,128)S(1)}, u32[]{:S(2)}, u32[]{:S(2)}) %collective-permute-start.9) | collective-permute-done | bytes 32800 | tf_op jit(solution)/shard_map/ppermute | solution.py:158
  116.7 1.9 %scatter_fusion.1 = bf16[64,4,256]{2,1,0:T(4,128)(2,1)} fusion(bf16[64,4,256]{2,1,0:T(4,128)(2,1)} %broadcast.450, s32[8]{0:T(128)S(1)} %copy-done.50, bf16[8,4,256]{2,1,0:T(4,128)(2,1)S(1)} %fusion.88), kind=kCustom, calls=%fused_computation.4 | custom fusion | bytes 49184 | tf_op jit(solution)/shard_map/scatter | solution.py:352
  118.6 4.9 %all-to-all-start.1 = ((bf16[64,4,256]{2,1,0:T(4,128)(2,1)}), bf16[64,4,256]{2,1,0:T(4,128)(2,1)S(1)}, u32[]{:S(2)}, u32[]{:S(2)}) async-start(bf16[64,4,256]{2,1,0:T(4,128)(2,1)} %scatter_fusion.1), calls=%async_computation.1 | async-start | bytes 262144 | tf_op jit(solution)/shard_map/all_to_all | solution.py:354
  124.3 12.4 %all-to-all-done.1 = bf16[64,4,256]{2,1,0:T(4,128)(2,1)S(1)} async-done(((bf16[64,4,256]{2,1,0:T(4,128)(2,1)}), bf16[64,4,256]{2,1,0:T(4,128)(2,1)S(1)}, u32[]{:S(2)}, u32[]{:S(2)}) %all-to-all-start.1) | async-done | bytes 131104 | tf_op jit(solution)/shard_map/all_to_all | solution.py:354
  (271 shorter events, 23.5 us)
Async XLA Ops:
  0.0 70.6 %copy-start = (bf16[1,256,1024]{2,1,0:T(8,128)(2,1)S(1)}, bf16[1,256,1024]{2,1,0:T(8,128)(2,1)}, u32[]{:S(2)}) copy-start(bf16[1,256,1024]{2,1,0:T(8,128)(2,1)} %param.32) | copy-start | bytes 1572868
  4.2 29.3 %all-to-all-start = ((bf16[64,4,256]{2,1,0:T(4,128)(2,1)}), bf16[64,4,256]{2,1,0:T(4,128)(2,1)S(1)}, u32[]{:S(2)}, u32[]{:S(2)}) async-start(bf16[64,4,256]{2,1,0:T(4,128)(2,1)} %scatter_fusion), calls=%async_computation | async-start | bytes 262144 | tf_op jit(solution)/shard_map/all_to_all | solution.py:348
  22.9 0.8 copy-start.17
  24.5 23.6 %copy-start.22 = (f32[1,1,1024]{2,1,0:T(1,128)}, f32[1,1,1024]{2,1,0:T(1,128)S(1)}, u32[]{:S(2)}) copy-start(f32[1,1,1024]{2,1,0:T(1,128)S(1)} %get-tuple-element.43) | copy-start | bytes 12292
  24.5 23.6 %copy-start.24 = (f32[1,1,1024]{2,1,0:T(1,128)}, f32[1,1,1024]{2,1,0:T(1,128)S(1)}, u32[]{:S(2)}) copy-start(f32[1,1,1024]{2,1,0:T(1,128)S(1)} %get-tuple-element.45) | copy-start | bytes 12292
  24.6 23.6 %copy-start.26 = (f32[1,1,1024]{2,1,0:T(1,128)}, f32[1,1,1024]{2,1,0:T(1,128)S(1)}, u32[]{:S(2)}) copy-start(f32[1,1,1024]{2,1,0:T(1,128)S(1)} %get-tuple-element.46) | copy-start | bytes 12292
  24.6 23.9 %copy-start.31 = (f32[1,1,1024]{2,1,0:T(1,128)}, f32[1,1,1024]{2,1,0:T(1,128)S(1)}, u32[]{:S(2)}) copy-start(f32[1,1,1024]{2,1,0:T(1,128)S(1)} %get-tuple-element.44) | copy-start | bytes 12292
  24.6 27.7 %copy-start.29 = (f32[1,1,1024]{2,1,0:T(1,128)}, f32[1,1,1024]{2,1,0:T(1,128)S(1)}, u32[]{:S(2)}) copy-start(f32[1,1,1024]{2,1,0:T(1,128)S(1)} %get-tuple-element.42) | copy-start | bytes 12292
  34.3 10.6 %collective-permute-start = (bf16[59392]{0:T(1024)(128)(2,1)S(1)}, bf16[59392]{0:T(1024)(128)(2,1)S(1)}, u32[]{:S(2)}, u32[]{:S(2)}) collective-permute-start(bf16[59392]{0:T(1024)(128)(2,1)S(1)} %constant_dynamic-update-slice_fusion.23), channel_id=1, source_target_pairs={{0,3},{1,0},{2,1},{3,2},{4,7},{5,4},{6,5},{7,6},{8,11},{9,8},{10,9... | collective-permute-start | bytes 356360 | tf_op jit(solution)/shard_map/ppermute | solution.py:147
  37.0 8.2 %collective-permute-start.1 = (bf16[59392]{0:T(1024)(128)(2,1)S(1)}, bf16[59392]{0:T(1024)(128)(2,1)S(1)}, u32[]{:S(2)}, u32[]{:S(2)}) collective-permute-start(bf16[59392]{0:T(1024)(128)(2,1)S(1)} %constant_dynamic-update-slice_fusion.23), channel_id=1, source_target_pairs={{0,2},{1,3},{2,0},{3,1},{4,6},{5,7},{6,4},{7,5},{8,10},{9,11},{10,... | collective-permute-start | bytes 356360 | tf_op jit(solution)/shard_map/ppermute | solution.py:147
  40.1 6.9 %collective-permute-start.2 = (bf16[59392]{0:T(1024)(128)(2,1)S(1)}, bf16[59392]{0:T(1024)(128)(2,1)S(1)}, u32[]{:S(2)}, u32[]{:S(2)}) collective-permute-start(bf16[59392]{0:T(1024)(128)(2,1)S(1)} %constant_dynamic-update-slice_fusion.23), channel_id=1, source_target_pairs={{0,1},{1,2},{2,3},{3,0},{4,5},{5,6},{6,7},{7,4},{8,9},{9,10},{10,1... | collective-permute-start | bytes 356360 | tf_op jit(solution)/shard_map/ppermute | solution.py:147
  47.2 5.0 %copy-start.10 = (bf16[32,256]{1,0:T(8,128)(2,1)}, bf16[32,256]{1,0:T(8,128)(2,1)S(1)}, u32[]{:S(2)}) copy-start(bf16[32,256]{1,0:T(8,128)(2,1)S(1)} %slice.200) | copy-start | bytes 49156
  47.3 5.0 %copy-start.12 = (bf16[32,256]{1,0:T(8,128)(2,1)}, bf16[32,256]{1,0:T(8,128)(2,1)S(1)}, u32[]{:S(2)}) copy-start(bf16[32,256]{1,0:T(8,128)(2,1)S(1)} %slice.201) | copy-start | bytes 49156
  47.3 4.9 %copy-start.14 = (bf16[32,256]{1,0:T(8,128)(2,1)}, bf16[32,256]{1,0:T(8,128)(2,1)S(1)}, u32[]{:S(2)}) copy-start(bf16[32,256]{1,0:T(8,128)(2,1)S(1)} %slice.202) | copy-start | bytes 49156
  48.4 1.2 copy-start.2
  49.2 1.1 copy-start.1
  53.3 1.0 copy-start.3
  68.1 1.0 copy-start.5
  71.3 7.0 %copy-start.45 = (s32[8]{0:T(128)S(1)}, s32[8]{0:T(128)}, u32[]{:S(2)}) copy-start(s32[8]{0:T(128)} %copy-done.44) | copy-start | bytes 100
  71.3 9.3 %copy-start.11 = (bf16[32,256]{1,0:T(8,128)(2,1)S(1)}, bf16[32,256]{1,0:T(8,128)(2,1)}, u32[]{:S(2)}) copy-start(bf16[32,256]{1,0:T(8,128)(2,1)} %copy-done.10) | copy-start | bytes 49156
  71.3 9.3 %copy-start.13 = (bf16[32,256]{1,0:T(8,128)(2,1)S(1)}, bf16[32,256]{1,0:T(8,128)(2,1)}, u32[]{:S(2)}) copy-start(bf16[32,256]{1,0:T(8,128)(2,1)} %copy-done.12) | copy-start | bytes 49156
  71.3 9.4 %copy-start.15 = (bf16[32,256]{1,0:T(8,128)(2,1)S(1)}, bf16[32,256]{1,0:T(8,128)(2,1)}, u32[]{:S(2)}) copy-start(bf16[32,256]{1,0:T(8,128)(2,1)} %copy-done.14) | copy-start | bytes 49156
  71.5 6.9 %collective-permute-start.3 = (f32[32,1024]{1,0:T(8,128)S(1)}, f32[32,1024]{1,0:T(8,128)S(1)}, u32[]{:S(2)}, u32[]{:S(2)}) collective-permute-start(f32[32,1024]{1,0:T(8,128)S(1)} %fusion.16), channel_id=1, source_target_pairs={{0,256},{1,257},{2,258},{3,259},{4,260},{5,261},{6,262},{7,263},{8... | collective-permute-start | bytes 393224 | tf_op jit(solution)/shard_map/ppermute | solution.py:166
  72.8 5.6 %collective-permute-start.4 = (f32[32,1024]{1,0:T(8,128)S(1)}, f32[32,1024]{1,0:T(8,128)S(1)}, u32[]{:S(2)}, u32[]{:S(2)}) collective-permute-start(f32[32,1024]{1,0:T(8,128)S(1)} %fusion.16), channel_id=1, source_target_pairs={{0,257},{1,258},{2,259},{3,256},{4,261},{5,262},{6,263},{7,260},{8... | collective-permute-start | bytes 393224 | tf_op jit(solution)/shard_map/ppermute | solution.py:166
  75.5 3.8 %collective-permute-start.5 = (f32[32,1024]{1,0:T(8,128)S(1)}, f32[32,1024]{1,0:T(8,128)S(1)}, u32[]{:S(2)}, u32[]{:S(2)}) collective-permute-start(f32[32,1024]{1,0:T(8,128)S(1)} %fusion.16), channel_id=1, source_target_pairs={{0,258},{1,259},{2,256},{3,257},{4,262},{5,263},{6,260},{7,261},{8... | collective-permute-start | bytes 393224 | tf_op jit(solution)/shard_map/ppermute | solution.py:166
  76.8 3.9 %collective-permute-start.6 = (f32[32,1024]{1,0:T(8,128)S(1)}, f32[32,1024]{1,0:T(8,128)S(1)}, u32[]{:S(2)}, u32[]{:S(2)}) collective-permute-start(f32[32,1024]{1,0:T(8,128)S(1)} %fusion.16), channel_id=1, source_target_pairs={{0,259},{1,256},{2,257},{3,258},{4,263},{5,260},{6,261},{7,262},{8... | collective-permute-start | bytes 393224 | tf_op jit(solution)/shard_map/ppermute | solution.py:166
  99.5 1.0 copy-start.4
  101.5 10.6 %collective-permute-start.10 = (f32[32,256]{1,0:T(8,128)S(1)}, f32[32,256]{1,0:T(8,128)S(1)}, u32[]{:S(2)}, u32[]{:S(2)}) collective-permute-start(f32[32,256]{1,0:T(8,128)S(1)} %get-tuple-element.26), channel_id=1, source_target_pairs={{0,3},{1,0},{2,1},{3,2},{4,7},{5,4},{6,5},{7,6},{8,11},{9,8},{10,9... | collective-permute-start | bytes 98312 | tf_op jit(solution)/shard_map/ppermute | solution.py:158
  104.9 7.2 %collective-permute-start.8 = (f32[32,256]{1,0:T(8,128)S(1)}, f32[32,256]{1,0:T(8,128)S(1)}, u32[]{:S(2)}, u32[]{:S(2)}) collective-permute-start(f32[32,256]{1,0:T(8,128)S(1)} %get-tuple-element.25), channel_id=1, source_target_pairs={{0,1},{1,2},{2,3},{3,0},{4,5},{5,6},{6,7},{7,4},{8,9},{9,10},{10,1... | collective-permute-start | bytes 98312 | tf_op jit(solution)/shard_map/ppermute | solution.py:158
  108.6 7.3 %collective-permute-start.9 = (f32[32,256]{1,0:T(8,128)S(1)}, f32[32,256]{1,0:T(8,128)S(1)}, u32[]{:S(2)}, u32[]{:S(2)}) collective-permute-start(f32[32,256]{1,0:T(8,128)S(1)} %get-tuple-element.27), channel_id=1, source_target_pairs={{0,2},{1,3},{2,0},{3,1},{4,6},{5,7},{6,4},{7,5},{8,10},{9,11},{10,... | collective-permute-start | bytes 98312 | tf_op jit(solution)/shard_map/ppermute | solution.py:158
  110.9 5.1 %collective-permute-start.7 = (bf16[8,4,256]{2,1,0:T(4,128)(2,1)S(1)}, bf16[8,4,256]{2,1,0:T(4,128)(2,1)S(1)}, u32[]{:S(2)}, u32[]{:S(2)}) collective-permute-start(bf16[8,4,256]{2,1,0:T(4,128)(2,1)S(1)} %constant_dynamic-slice_fusion.2), channel_id=1, source_target_pairs={{256,0},{257,1},{258,2},{259,3},{260,4},{261,5},{262,6},{263,7},{2... | collective-permute-start | bytes 49160 | tf_op jit(solution)/shard_map/ppermute | solution.py:173
  118.6 18.1 %all-to-all-start.1 = ((bf16[64,4,256]{2,1,0:T(4,128)(2,1)}), bf16[64,4,256]{2,1,0:T(4,128)(2,1)S(1)}, u32[]{:S(2)}, u32[]{:S(2)}) async-start(bf16[64,4,256]{2,1,0:T(4,128)(2,1)} %scatter_fusion.1), calls=%async_computation.1 | async-start | bytes 262144 | tf_op jit(solution)/shard_map/all_to_all | solution.py:354
  (33 other events, 24.0 us)

commit v9 on v8

--- a/solution.py
+++ b/solution.py
@@ -19,11 +19,11 @@
         content = content_ref[position]
         pulled = jnp.sum(states * normed, axis=-1, keepdims=True)
         added = jnp.einsum(
-            "bqi,bqj->bij", content, erasing, precision=highest, preferred_element_type=jnp.float32
+            "bqi,bqj->bij", content, erasing, precision=lax.Precision.HIGH, preferred_element_type=jnp.float32
         )
         states = states * decay - pulled * normed_learn + added
         read_ref[position] = jnp.einsum(
-            "bqj,bij->bqi", acceptor, states, precision=highest, preferred_element_type=jnp.float32
+            "bqj,bij->bqi", acceptor, states, precision=lax.Precision.HIGH, preferred_element_type=jnp.float32
         )
 
 

time: 139 us -> 130 us (0.935)
  Pallas kernels: 24 us -> 14.2 us
    pallas_call x2, Pallas kernels: 24 us -> 14.2 us  [run_recurrence(): pl.pallas_call(recurrence_kernel, out_shape=jax.ShapeDtypeStruct((steps,...]
where the time goes in v9:
time: 130 us; the launch traced here: 128 us
  starting transfers between devices  48.5 us (37%)
  waiting for transfers between devices  29.8 us (23%)
  local copies, waits for them, and re-layouts  24.7 us (19%)
  Pallas kernels  14.2 us (11%)
  other arithmetic  6.03 us (5%)
  matrix products  3.34 us (3%)
  between operations  1.63 us (1%)
    all_to_all x1, starting transfers between devices, body(): lax.all_to_all(outgoing, 'req', split_axis=0, concat_axis=0, tiled=True)  16.6 us
    pallas_call x2, Pallas kernels, run_recurrence(): pl.pallas_call(recurrence_kernel, out_shape=jax.ShapeDtypeStruct((steps,...  14.2 us
    unnamed x128, local copies, waits for them, and re-layouts  12.9 us
    all_to_all x1, waiting for transfers between devices, body(): lax.all_to_all(going_back, 'req', split_axis=0, concat_axis=0, tiled=True)  12.5 us
    ppermute x3, starting transfers between devices, gather_heads(): lax.ppermute(block, 'head', [(i, (i + k) % n) for i in range(n)])  9.76 us
    ppermute x3, starting transfers between devices, scatter_heads(): lax.ppermute(chunk, 'head', [(i, (i + k) % n) for i in range(n)])  9.27 us
    all_to_all x1, waiting for transfers between devices, body(): lax.all_to_all(outgoing, 'req', split_axis=0, concat_axis=0, tiled=True)  8.96 us
    ppermute x4, starting transfers between devices, hand_over(): lax.ppermute(partial, ('section', 'head'), [(i, n + (i + k) % n) for i in...  6.74 us
  transfers between devices with their start and end apart: 13, of which 7 were waited for; matrix products, arithmetic and copies ran while one was open for 2% of the time, Pallas kernels for 0%

profile of v9, /device:TPU:6, one launch (start us, length us, event | category | flops | bytes accessed | tf_op | source)
XLA Modules:
  0.0 128.2 jit_solution(11614483346826037077)
XLA Ops:
  0.0 0.7 copy-done.34
  2.3 1.9 %scatter_fusion = bf16[64,4,256]{2,1,0:T(4,128)(2,1)} fusion(bf16[64,4,256]{2,1,0:T(4,128)(2,1)} %broadcast.450.clone, s32[8]{0:T(128)S(1)} %fusion.101, bf16[8,4,256]{2,1,0:T(4,128)(2,1)S(1)} %copy-done.33), kind=kCustom, calls=%fused_computation.3 | custom fusion | bytes 49184 | tf_op jit(solution)/shard_map/scatter | solution.py:346
  4.2 16.6 %all-to-all-start = ((bf16[64,4,256]{2,1,0:T(4,128)(2,1)}), bf16[64,4,256]{2,1,0:T(4,128)(2,1)S(1)}, u32[]{:S(2)}, u32[]{:S(2)}) async-start(bf16[64,4,256]{2,1,0:T(4,128)(2,1)} %scatter_fusion), calls=%async_computation | async-start | bytes 262144 | tf_op jit(solution)/shard_map/all_to_all | solution.py:348
  24.6 9.0 %all-to-all-done = bf16[64,4,256]{2,1,0:T(4,128)(2,1)S(1)} async-done(((bf16[64,4,256]{2,1,0:T(4,128)(2,1)}), bf16[64,4,256]{2,1,0:T(4,128)(2,1)S(1)}, u32[]{:S(2)}, u32[]{:S(2)}) %all-to-all-start) | async-done | bytes 131104 | tf_op jit(solution)/shard_map/all_to_all | solution.py:348
  34.3 2.7 %collective-permute-start = (bf16[59392]{0:T(1024)(128)(2,1)S(1)}, bf16[59392]{0:T(1024)(128)(2,1)S(1)}, u32[]{:S(2)}, u32[]{:S(2)}) collective-permute-start(bf16[59392]{0:T(1024)(128)(2,1)S(1)} %constant_dynamic-update-slice_fusion.23), channel_id=1, source_target_pairs={{0,3},{1,0},{2,1},{3,2},{4,7},{5,4},{6,5},{7,6},{8,11},{9,8},{10,9... | collective-permute-start | bytes 356360 | tf_op jit(solution)/shard_map/ppermute | solution.py:147
  37.0 3.0 %collective-permute-start.1 = (bf16[59392]{0:T(1024)(128)(2,1)S(1)}, bf16[59392]{0:T(1024)(128)(2,1)S(1)}, u32[]{:S(2)}, u32[]{:S(2)}) collective-permute-start(bf16[59392]{0:T(1024)(128)(2,1)S(1)} %constant_dynamic-update-slice_fusion.23), channel_id=1, source_target_pairs={{0,2},{1,3},{2,0},{3,1},{4,6},{5,7},{6,4},{7,5},{8,10},{9,11},{10,... | collective-permute-start | bytes 356360 | tf_op jit(solution)/shard_map/ppermute | solution.py:147
  40.1 4.0 %collective-permute-start.2 = (bf16[59392]{0:T(1024)(128)(2,1)S(1)}, bf16[59392]{0:T(1024)(128)(2,1)S(1)}, u32[]{:S(2)}, u32[]{:S(2)}) collective-permute-start(bf16[59392]{0:T(1024)(128)(2,1)S(1)} %constant_dynamic-update-slice_fusion.23), channel_id=1, source_target_pairs={{0,1},{1,2},{2,3},{3,0},{4,5},{5,6},{6,7},{7,4},{8,9},{9,10},{10,1... | collective-permute-start | bytes 356360 | tf_op jit(solution)/shard_map/ppermute | solution.py:147
  45.3 1.7 %collective-permute-done.2 = bf16[59392]{0:T(1024)(128)(2,1)S(1)} collective-permute-done((bf16[59392]{0:T(1024)(128)(2,1)S(1)}, bf16[59392]{0:T(1024)(128)(2,1)S(1)}, u32[]{:S(2)}, u32[]{:S(2)}) %collective-permute-start.2) | collective-permute-done | bytes 118816 | tf_op jit(solution)/shard_map/ppermute | solution.py:147
  48.5 0.7 copy-done.18
  50.5 0.8 multiply_multiply_fusion.1
  52.3 0.7 copy-done.20
  55.4 0.7 copy-done.6
  56.1 7.1 %shard_map.199 = f32[4,32,1,64]{3,2,1,0:T(1,128)} custom-call(f32[32,64,64]{2,1,0:T(8,128)} %bitcast.161, f32[4,5,32,1,64]{4,3,2,1,0:T(1,128)} %copy-done.6, f32[4,32,1,64]{3,2,1,0:T(1,128)} %bitcast.172), custom_call_target="tpu_custom_call" | custom-call | tf_op jit(solution)/shard_map/pallas_call | solution.py:33
  63.2 1.0 reduce_sum.112
  66.6 1.3 %collective-permute-start.3 = (f32[32,1024]{1,0:T(8,128)S(1)}, f32[32,1024]{1,0:T(8,128)S(1)}, u32[]{:S(2)}, u32[]{:S(2)}) collective-permute-start(f32[32,1024]{1,0:T(8,128)S(1)} %fusion.16), channel_id=1, source_target_pairs={{0,256},{1,257},{2,258},{3,259},{4,260},{5,261},{6,262},{7,263},{8... | collective-permute-start | bytes 393224 | tf_op jit(solution)/shard_map/ppermute | solution.py:166
  67.9 2.7 %collective-permute-start.4 = (f32[32,1024]{1,0:T(8,128)S(1)}, f32[32,1024]{1,0:T(8,128)S(1)}, u32[]{:S(2)}, u32[]{:S(2)}) collective-permute-start(f32[32,1024]{1,0:T(8,128)S(1)} %fusion.16), channel_id=1, source_target_pairs={{0,257},{1,258},{2,259},{3,256},{4,261},{5,262},{6,263},{7,260},{8... | collective-permute-start | bytes 393224 | tf_op jit(solution)/shard_map/ppermute | solution.py:166
  70.6 1.3 %collective-permute-start.5 = (f32[32,1024]{1,0:T(8,128)S(1)}, f32[32,1024]{1,0:T(8,128)S(1)}, u32[]{:S(2)}, u32[]{:S(2)}) collective-permute-start(f32[32,1024]{1,0:T(8,128)S(1)} %fusion.16), channel_id=1, source_target_pairs={{0,258},{1,259},{2,256},{3,257},{4,262},{5,263},{6,260},{7,261},{8... | collective-permute-start | bytes 393224 | tf_op jit(solution)/shard_map/ppermute | solution.py:166
  71.9 1.5 %collective-permute-start.6 = (f32[32,1024]{1,0:T(8,128)S(1)}, f32[32,1024]{1,0:T(8,128)S(1)}, u32[]{:S(2)}, u32[]{:S(2)}) collective-permute-start(f32[32,1024]{1,0:T(8,128)S(1)} %fusion.16), channel_id=1, source_target_pairs={{0,259},{1,256},{2,257},{3,258},{4,263},{5,260},{6,261},{7,262},{8... | collective-permute-start | bytes 393224 | tf_op jit(solution)/shard_map/ppermute | solution.py:166
  73.5 0.9 collective-permute-done.5
  74.4 1.4 %collective-permute-done.6 = f32[32,1024]{1,0:T(8,128)S(1)} collective-permute-done((f32[32,1024]{1,0:T(8,128)S(1)}, f32[32,1024]{1,0:T(8,128)S(1)}, u32[]{:S(2)}, u32[]{:S(2)}) %collective-permute-start.6) | collective-permute-done | bytes 131104 | tf_op jit(solution)/shard_map/ppermute | solution.py:166
  76.1 0.7 copy-done.19
  81.9 0.7 copy-done.7
  82.6 7.1 %shard_map.200 = f32[4,32,1,64]{3,2,1,0:T(1,128)} custom-call(f32[32,64,64]{2,1,0:T(8,128)} %bitcast.162, f32[4,5,32,1,64]{4,3,2,1,0:T(1,128)} %copy-done.7, f32[4,32,1,64]{3,2,1,0:T(1,128)} %bitcast.173), custom_call_target="tpu_custom_call" | custom-call | tf_op jit(solution)/shard_map/pallas_call | solution.py:33
  89.7 1.0 reduce_sum.116
  91.8 3.4 %collective-permute-start.10 = (f32[32,256]{1,0:T(8,128)S(1)}, f32[32,256]{1,0:T(8,128)S(1)}, u32[]{:S(2)}, u32[]{:S(2)}) collective-permute-start(f32[32,256]{1,0:T(8,128)S(1)} %get-tuple-element.26), channel_id=1, source_target_pairs={{0,3},{1,0},{2,1},{3,2},{4,7},{5,4},{6,5},{7,6},{8,11},{9,8},{10,9... | collective-permute-start | bytes 98312 | tf_op jit(solution)/shard_map/ppermute | solution.py:158
  95.2 3.7 %collective-permute-start.8 = (f32[32,256]{1,0:T(8,128)S(1)}, f32[32,256]{1,0:T(8,128)S(1)}, u32[]{:S(2)}, u32[]{:S(2)}) collective-permute-start(f32[32,256]{1,0:T(8,128)S(1)} %get-tuple-element.25), channel_id=1, source_target_pairs={{0,1},{1,2},{2,3},{3,0},{4,5},{5,6},{6,7},{7,4},{8,9},{9,10},{10,1... | collective-permute-start | bytes 98312 | tf_op jit(solution)/shard_map/ppermute | solution.py:158
  98.8 2.2 %collective-permute-start.9 = (f32[32,256]{1,0:T(8,128)S(1)}, f32[32,256]{1,0:T(8,128)S(1)}, u32[]{:S(2)}, u32[]{:S(2)}) collective-permute-start(f32[32,256]{1,0:T(8,128)S(1)} %get-tuple-element.27), channel_id=1, source_target_pairs={{0,2},{1,3},{2,0},{3,1},{4,6},{5,7},{6,4},{7,5},{8,10},{9,11},{10,... | collective-permute-start | bytes 98312 | tf_op jit(solution)/shard_map/ppermute | solution.py:158
  101.1 1.3 %collective-permute-start.7 = (bf16[8,4,256]{2,1,0:T(4,128)(2,1)S(1)}, bf16[8,4,256]{2,1,0:T(4,128)(2,1)S(1)}, u32[]{:S(2)}, u32[]{:S(2)}) collective-permute-start(bf16[8,4,256]{2,1,0:T(4,128)(2,1)S(1)} %constant_dynamic-slice_fusion.2), channel_id=1, source_target_pairs={{256,0},{257,1},{258,2},{259,3},{260,4},{261,5},{262,6},{263,7},{2... | collective-permute-start | bytes 49160 | tf_op jit(solution)/shard_map/ppermute | solution.py:173
  102.4 3.7 %collective-permute-done.9 = f32[32,256]{1,0:T(8,128)S(1)} collective-permute-done((f32[32,256]{1,0:T(8,128)S(1)}, f32[32,256]{1,0:T(8,128)S(1)}, u32[]{:S(2)}, u32[]{:S(2)}) %collective-permute-start.9) | collective-permute-done | bytes 32800 | tf_op jit(solution)/shard_map/ppermute | solution.py:158
  106.9 1.9 %scatter_fusion.1 = bf16[64,4,256]{2,1,0:T(4,128)(2,1)} fusion(bf16[64,4,256]{2,1,0:T(4,128)(2,1)} %broadcast.450, s32[8]{0:T(128)S(1)} %copy-done.50, bf16[8,4,256]{2,1,0:T(4,128)(2,1)S(1)} %fusion.88), kind=kCustom, calls=%fused_computation.4 | custom fusion | bytes 49184 | tf_op jit(solution)/shard_map/scatter | solution.py:352
  108.9 4.9 %all-to-all-start.1 = ((bf16[64,4,256]{2,1,0:T(4,128)(2,1)}), bf16[64,4,256]{2,1,0:T(4,128)(2,1)S(1)}, u32[]{:S(2)}, u32[]{:S(2)}) async-start(bf16[64,4,256]{2,1,0:T(4,128)(2,1)} %scatter_fusion.1), calls=%async_computation.1 | async-start | bytes 262144 | tf_op jit(solution)/shard_map/all_to_all | solution.py:354
  114.5 12.5 %all-to-all-done.1 = bf16[64,4,256]{2,1,0:T(4,128)(2,1)S(1)} async-done(((bf16[64,4,256]{2,1,0:T(4,128)(2,1)}), bf16[64,4,256]{2,1,0:T(4,128)(2,1)S(1)}, u32[]{:S(2)}, u32[]{:S(2)}) %all-to-all-start.1) | async-done | bytes 131104 | tf_op jit(solution)/shard_map/all_to_all | solution.py:354
  (271 shorter events, 23.7 us)
Async XLA Ops:
  0.0 65.7 %copy-start = (bf16[1,256,1024]{2,1,0:T(8,128)(2,1)S(1)}, bf16[1,256,1024]{2,1,0:T(8,128)(2,1)}, u32[]{:S(2)}) copy-start(bf16[1,256,1024]{2,1,0:T(8,128)(2,1)} %param.32) | copy-start | bytes 1572868
  4.2 29.3 %all-to-all-start = ((bf16[64,4,256]{2,1,0:T(4,128)(2,1)}), bf16[64,4,256]{2,1,0:T(4,128)(2,1)S(1)}, u32[]{:S(2)}, u32[]{:S(2)}) async-start(bf16[64,4,256]{2,1,0:T(4,128)(2,1)} %scatter_fusion), calls=%async_computation | async-start | bytes 262144 | tf_op jit(solution)/shard_map/all_to_all | solution.py:348
  22.9 0.8 copy-start.17
  24.5 23.6 %copy-start.22 = (f32[1,1,1024]{2,1,0:T(1,128)}, f32[1,1,1024]{2,1,0:T(1,128)S(1)}, u32[]{:S(2)}) copy-start(f32[1,1,1024]{2,1,0:T(1,128)S(1)} %get-tuple-element.43) | copy-start | bytes 12292
  24.5 23.6 %copy-start.24 = (f32[1,1,1024]{2,1,0:T(1,128)}, f32[1,1,1024]{2,1,0:T(1,128)S(1)}, u32[]{:S(2)}) copy-start(f32[1,1,1024]{2,1,0:T(1,128)S(1)} %get-tuple-element.45) | copy-start | bytes 12292
  24.6 23.6 %copy-start.26 = (f32[1,1,1024]{2,1,0:T(1,128)}, f32[1,1,1024]{2,1,0:T(1,128)S(1)}, u32[]{:S(2)}) copy-start(f32[1,1,1024]{2,1,0:T(1,128)S(1)} %get-tuple-element.46) | copy-start | bytes 12292
  24.6 23.9 %copy-start.31 = (f32[1,1,1024]{2,1,0:T(1,128)}, f32[1,1,1024]{2,1,0:T(1,128)S(1)}, u32[]{:S(2)}) copy-start(f32[1,1,1024]{2,1,0:T(1,128)S(1)} %get-tuple-element.44) | copy-start | bytes 12292
  24.6 27.7 %copy-start.29 = (f32[1,1,1024]{2,1,0:T(1,128)}, f32[1,1,1024]{2,1,0:T(1,128)S(1)}, u32[]{:S(2)}) copy-start(f32[1,1,1024]{2,1,0:T(1,128)S(1)} %get-tuple-element.42) | copy-start | bytes 12292
  34.3 10.4 %collective-permute-start = (bf16[59392]{0:T(1024)(128)(2,1)S(1)}, bf16[59392]{0:T(1024)(128)(2,1)S(1)}, u32[]{:S(2)}, u32[]{:S(2)}) collective-permute-start(bf16[59392]{0:T(1024)(128)(2,1)S(1)} %constant_dynamic-update-slice_fusion.23), channel_id=1, source_target_pairs={{0,3},{1,0},{2,1},{3,2},{4,7},{5,4},{6,5},{7,6},{8,11},{9,8},{10,9... | collective-permute-start | bytes 356360 | tf_op jit(solution)/shard_map/ppermute | solution.py:147
  37.0 8.2 %collective-permute-start.1 = (bf16[59392]{0:T(1024)(128)(2,1)S(1)}, bf16[59392]{0:T(1024)(128)(2,1)S(1)}, u32[]{:S(2)}, u32[]{:S(2)}) collective-permute-start(bf16[59392]{0:T(1024)(128)(2,1)S(1)} %constant_dynamic-update-slice_fusion.23), channel_id=1, source_target_pairs={{0,2},{1,3},{2,0},{3,1},{4,6},{5,7},{6,4},{7,5},{8,10},{9,11},{10,... | collective-permute-start | bytes 356360 | tf_op jit(solution)/shard_map/ppermute | solution.py:147
  40.1 6.9 %collective-permute-start.2 = (bf16[59392]{0:T(1024)(128)(2,1)S(1)}, bf16[59392]{0:T(1024)(128)(2,1)S(1)}, u32[]{:S(2)}, u32[]{:S(2)}) collective-permute-start(bf16[59392]{0:T(1024)(128)(2,1)S(1)} %constant_dynamic-update-slice_fusion.23), channel_id=1, source_target_pairs={{0,1},{1,2},{2,3},{3,0},{4,5},{5,6},{6,7},{7,4},{8,9},{9,10},{10,1... | collective-permute-start | bytes 356360 | tf_op jit(solution)/shard_map/ppermute | solution.py:147
  47.2 5.0 %copy-start.10 = (bf16[32,256]{1,0:T(8,128)(2,1)}, bf16[32,256]{1,0:T(8,128)(2,1)S(1)}, u32[]{:S(2)}) copy-start(bf16[32,256]{1,0:T(8,128)(2,1)S(1)} %slice.200) | copy-start | bytes 49156
  47.3 5.0 %copy-start.12 = (bf16[32,256]{1,0:T(8,128)(2,1)}, bf16[32,256]{1,0:T(8,128)(2,1)S(1)}, u32[]{:S(2)}) copy-start(bf16[32,256]{1,0:T(8,128)(2,1)S(1)} %slice.201) | copy-start | bytes 49156
  47.3 4.9 %copy-start.14 = (bf16[32,256]{1,0:T(8,128)(2,1)}, bf16[32,256]{1,0:T(8,128)(2,1)S(1)}, u32[]{:S(2)}) copy-start(bf16[32,256]{1,0:T(8,128)(2,1)S(1)} %slice.202) | copy-start | bytes 49156
  48.4 1.2 copy-start.2
  49.2 1.1 copy-start.1
  53.3 1.0 copy-start.3
  63.2 1.0 copy-start.5
  66.4 7.0 %copy-start.45 = (s32[8]{0:T(128)S(1)}, s32[8]{0:T(128)}, u32[]{:S(2)}) copy-start(s32[8]{0:T(128)} %copy-done.44) | copy-start | bytes 100
  66.4 9.3 %copy-start.11 = (bf16[32,256]{1,0:T(8,128)(2,1)S(1)}, bf16[32,256]{1,0:T(8,128)(2,1)}, u32[]{:S(2)}) copy-start(bf16[32,256]{1,0:T(8,128)(2,1)} %copy-done.10) | copy-start | bytes 49156
  66.4 9.3 %copy-start.13 = (bf16[32,256]{1,0:T(8,128)(2,1)S(1)}, bf16[32,256]{1,0:T(8,128)(2,1)}, u32[]{:S(2)}) copy-start(bf16[32,256]{1,0:T(8,128)(2,1)} %copy-done.12) | copy-start | bytes 49156
  66.4 9.3 %copy-start.15 = (bf16[32,256]{1,0:T(8,128)(2,1)S(1)}, bf16[32,256]{1,0:T(8,128)(2,1)}, u32[]{:S(2)}) copy-start(bf16[32,256]{1,0:T(8,128)(2,1)} %copy-done.14) | copy-start | bytes 49156
  66.6 6.8 %collective-permute-start.3 = (f32[32,1024]{1,0:T(8,128)S(1)}, f32[32,1024]{1,0:T(8,128)S(1)}, u32[]{:S(2)}, u32[]{:S(2)}) collective-permute-start(f32[32,1024]{1,0:T(8,128)S(1)} %fusion.16), channel_id=1, source_target_pairs={{0,256},{1,257},{2,258},{3,259},{4,260},{5,261},{6,262},{7,263},{8... | collective-permute-start | bytes 393224 | tf_op jit(solution)/shard_map/ppermute | solution.py:166
  67.9 5.5 %collective-permute-start.4 = (f32[32,1024]{1,0:T(8,128)S(1)}, f32[32,1024]{1,0:T(8,128)S(1)}, u32[]{:S(2)}, u32[]{:S(2)}) collective-permute-start(f32[32,1024]{1,0:T(8,128)S(1)} %fusion.16), channel_id=1, source_target_pairs={{0,257},{1,258},{2,259},{3,256},{4,261},{5,262},{6,263},{7,260},{8... | collective-permute-start | bytes 393224 | tf_op jit(solution)/shard_map/ppermute | solution.py:166
  70.6 3.8 %collective-permute-start.5 = (f32[32,1024]{1,0:T(8,128)S(1)}, f32[32,1024]{1,0:T(8,128)S(1)}, u32[]{:S(2)}, u32[]{:S(2)}) collective-permute-start(f32[32,1024]{1,0:T(8,128)S(1)} %fusion.16), channel_id=1, source_target_pairs={{0,258},{1,259},{2,256},{3,257},{4,262},{5,263},{6,260},{7,261},{8... | collective-permute-start | bytes 393224 | tf_op jit(solution)/shard_map/ppermute | solution.py:166
  71.9 3.9 %collective-permute-start.6 = (f32[32,1024]{1,0:T(8,128)S(1)}, f32[32,1024]{1,0:T(8,128)S(1)}, u32[]{:S(2)}, u32[]{:S(2)}) collective-permute-start(f32[32,1024]{1,0:T(8,128)S(1)} %fusion.16), channel_id=1, source_target_pairs={{0,259},{1,256},{2,257},{3,258},{4,263},{5,260},{6,261},{7,262},{8... | collective-permute-start | bytes 393224 | tf_op jit(solution)/shard_map/ppermute | solution.py:166
  89.7 1.0 copy-start.4
  91.8 10.6 %collective-permute-start.10 = (f32[32,256]{1,0:T(8,128)S(1)}, f32[32,256]{1,0:T(8,128)S(1)}, u32[]{:S(2)}, u32[]{:S(2)}) collective-permute-start(f32[32,256]{1,0:T(8,128)S(1)} %get-tuple-element.26), channel_id=1, source_target_pairs={{0,3},{1,0},{2,1},{3,2},{4,7},{5,4},{6,5},{7,6},{8,11},{9,8},{10,9... | collective-permute-start | bytes 98312 | tf_op jit(solution)/shard_map/ppermute | solution.py:158
  95.2 7.2 %collective-permute-start.8 = (f32[32,256]{1,0:T(8,128)S(1)}, f32[32,256]{1,0:T(8,128)S(1)}, u32[]{:S(2)}, u32[]{:S(2)}) collective-permute-start(f32[32,256]{1,0:T(8,128)S(1)} %get-tuple-element.25), channel_id=1, source_target_pairs={{0,1},{1,2},{2,3},{3,0},{4,5},{5,6},{6,7},{7,4},{8,9},{9,10},{10,1... | collective-permute-start | bytes 98312 | tf_op jit(solution)/shard_map/ppermute | solution.py:158
  98.8 7.3 %collective-permute-start.9 = (f32[32,256]{1,0:T(8,128)S(1)}, f32[32,256]{1,0:T(8,128)S(1)}, u32[]{:S(2)}, u32[]{:S(2)}) collective-permute-start(f32[32,256]{1,0:T(8,128)S(1)} %get-tuple-element.27), channel_id=1, source_target_pairs={{0,2},{1,3},{2,0},{3,1},{4,6},{5,7},{6,4},{7,5},{8,10},{9,11},{10,... | collective-permute-start | bytes 98312 | tf_op jit(solution)/shard_map/ppermute | solution.py:158
  101.1 5.1 %collective-permute-start.7 = (bf16[8,4,256]{2,1,0:T(4,128)(2,1)S(1)}, bf16[8,4,256]{2,1,0:T(4,128)(2,1)S(1)}, u32[]{:S(2)}, u32[]{:S(2)}) collective-permute-start(bf16[8,4,256]{2,1,0:T(4,128)(2,1)S(1)} %constant_dynamic-slice_fusion.2), channel_id=1, source_target_pairs={{256,0},{257,1},{258,2},{259,3},{260,4},{261,5},{262,6},{263,7},{2... | collective-permute-start | bytes 49160 | tf_op jit(solution)/shard_map/ppermute | solution.py:173
  108.9 18.1 %all-to-all-start.1 = ((bf16[64,4,256]{2,1,0:T(4,128)(2,1)}), bf16[64,4,256]{2,1,0:T(4,128)(2,1)S(1)}, u32[]{:S(2)}, u32[]{:S(2)}) async-start(bf16[64,4,256]{2,1,0:T(4,128)(2,1)} %scatter_fusion.1), calls=%async_computation.1 | async-start | bytes 262144 | tf_op jit(solution)/shard_map/all_to_all | solution.py:354
  (33 other events, 24.0 us)

commit v10 on v9

--- a/solution.py
+++ b/solution.py
@@ -262,7 +262,15 @@
     ).astype(jnp.bfloat16)
     me = lax.axis_index("head")
     second_in = lax.dynamic_slice_in_dim(full_second, me * shard_width, shard_width, 2)
-    first_out = hand_back(second_in)
+    first_out = lax.cond(
+        section_num == 0,
+        lambda part: (
+            inputs.astype(jnp.float32)
+            + scatter_heads(part).reshape(batch_rows, steps_count, shard_width)
+        ).astype(jnp.bfloat16),
+        lambda part: jnp.zeros_like(inputs),
+        partial_first,
+    )
     partial_second = layer_partial(full_second, full_prev, states_use, params)
     own_second = scatter_heads(partial_second).reshape(batch_rows, steps_count, shard_width)
     second_out = (second_in.astype(jnp.float32) + own_second).astype(jnp.bfloat16)

time: 130 us -> 142 us (1.092)
  starting transfers between devices: 48.5 us -> 55.2 us
  waiting for transfers between devices: 29.8 us -> 34.3 us
    ppermute x3 -> x6, starting transfers between devices: 9.27 us -> 17 us  [scatter_heads(): lax.ppermute(chunk, 'head', [(i, (i + k) % n) for i in range(n)])]
    ppermute x3 -> x6, waiting for transfers between devices: 3.75 us -> 9.76 us  [scatter_heads(): lax.ppermute(chunk, 'head', [(i, (i + k) % n) for i in range(n)])]
    unnamed x128 -> x136, local copies, waits for them, and re-layouts: 12.9 us -> 13.9 us
  transfers between devices with their start and end apart: 13 -> 15, of which waited for: 7 -> 10; matrix products, arithmetic and copies ran while one was open for 2% -> 2% of each run, Pallas kernels for 0% -> 0%
where the time goes in v10:
time: 142 us; the launch traced here: 140 us
  starting transfers between devices  55.2 us (39%)
  waiting for transfers between devices  34.3 us (24%)
  local copies, waits for them, and re-layouts  25.7 us (18%)
  Pallas kernels  14.2 us (10%)
  other arithmetic  6.17 us (4%)
  matrix products  2.73 us (2%)
  between operations  1.68 us (1%)
    ppermute x6, starting transfers between devices, scatter_heads(): lax.ppermute(chunk, 'head', [(i, (i + k) % n) for i in range(n)])  17 us
    all_to_all x1, starting transfers between devices, body(): lax.all_to_all(outgoing, 'req', split_axis=0, concat_axis=0, tiled=True)  16.6 us
    pallas_call x2, Pallas kernels, run_recurrence(): pl.pallas_call(recurrence_kernel, out_shape=jax.ShapeDtypeStruct((steps,...  14.2 us
    unnamed x136, local copies, waits for them, and re-layouts  13.9 us
    all_to_all x1, waiting for transfers between devices, body(): lax.all_to_all(going_back, 'req', split_axis=0, concat_axis=0, tiled=True)  12.2 us
    ppermute x3, starting transfers between devices, gather_heads(): lax.ppermute(block, 'head', [(i, (i + k) % n) for i in range(n)])  9.76 us
    ppermute x6, waiting for transfers between devices, scatter_heads(): lax.ppermute(chunk, 'head', [(i, (i + k) % n) for i in range(n)])  9.76 us
    all_to_all x1, waiting for transfers between devices, body(): lax.all_to_all(outgoing, 'req', split_axis=0, concat_axis=0, tiled=True)  7.87 us
  transfers between devices with their start and end apart: 15, of which 10 were waited for; matrix products, arithmetic and copies ran while one was open for 2% of the time, Pallas kernels for 0%

profile of v10, /device:TPU:6, one launch (start us, length us, event | category | flops | bytes accessed | tf_op | source)
XLA Modules:
  0.0 140.2 jit_solution(6731164440087699854)
XLA Ops:
  0.0 0.7 copy-done.33
  2.3 1.9 %scatter_fusion = bf16[64,4,256]{2,1,0:T(4,128)(2,1)} fusion(bf16[64,4,256]{2,1,0:T(4,128)(2,1)} %broadcast.459.clone, s32[8]{0:T(128)S(1)} %fusion.101, bf16[8,4,256]{2,1,0:T(4,128)(2,1)S(1)} %copy-done.32), kind=kCustom, calls=%fused_computation.3 | custom fusion | bytes 49184 | tf_op jit(solution)/shard_map/scatter | solution.py:354
  4.3 16.6 %all-to-all-start = ((bf16[64,4,256]{2,1,0:T(4,128)(2,1)}), bf16[64,4,256]{2,1,0:T(4,128)(2,1)S(1)}, u32[]{:S(2)}, u32[]{:S(2)}) async-start(bf16[64,4,256]{2,1,0:T(4,128)(2,1)} %scatter_fusion), calls=%async_computation | async-start | bytes 262144 | tf_op jit(solution)/shard_map/all_to_all | solution.py:356
  25.7 7.9 %all-to-all-done = bf16[64,4,256]{2,1,0:T(4,128)(2,1)S(1)} async-done(((bf16[64,4,256]{2,1,0:T(4,128)(2,1)}), bf16[64,4,256]{2,1,0:T(4,128)(2,1)S(1)}, u32[]{:S(2)}, u32[]{:S(2)}) %all-to-all-start) | async-done | bytes 131104 | tf_op jit(solution)/shard_map/all_to_all | solution.py:356
  34.3 2.7 %collective-permute-start.3 = (bf16[59392]{0:T(1024)(128)(2,1)S(1)}, bf16[59392]{0:T(1024)(128)(2,1)S(1)}, u32[]{:S(2)}, u32[]{:S(2)}) collective-permute-start(bf16[59392]{0:T(1024)(128)(2,1)S(1)} %constant_dynamic-update-slice_fusion.23), channel_id=1, source_target_pairs={{0,3},{1,0},{2,1},{3,2},{4,7},{5,4},{6,5},{7,6},{8,11},{9,8},{10,9... | collective-permute-start | bytes 356360 | tf_op jit(solution)/shard_map/ppermute | solution.py:147
  37.0 3.0 %collective-permute-start.4 = (bf16[59392]{0:T(1024)(128)(2,1)S(1)}, bf16[59392]{0:T(1024)(128)(2,1)S(1)}, u32[]{:S(2)}, u32[]{:S(2)}) collective-permute-start(bf16[59392]{0:T(1024)(128)(2,1)S(1)} %constant_dynamic-update-slice_fusion.23), channel_id=1, source_target_pairs={{0,2},{1,3},{2,0},{3,1},{4,6},{5,7},{6,4},{7,5},{8,10},{9,11},{10,... | collective-permute-start | bytes 356360 | tf_op jit(solution)/shard_map/ppermute | solution.py:147
  40.1 4.0 %collective-permute-start.5 = (bf16[59392]{0:T(1024)(128)(2,1)S(1)}, bf16[59392]{0:T(1024)(128)(2,1)S(1)}, u32[]{:S(2)}, u32[]{:S(2)}) collective-permute-start(bf16[59392]{0:T(1024)(128)(2,1)S(1)} %constant_dynamic-update-slice_fusion.23), channel_id=1, source_target_pairs={{0,1},{1,2},{2,3},{3,0},{4,5},{5,6},{6,7},{7,4},{8,9},{9,10},{10,1... | collective-permute-start | bytes 356360 | tf_op jit(solution)/shard_map/ppermute | solution.py:147
  45.3 1.7 %collective-permute-done.5 = bf16[59392]{0:T(1024)(128)(2,1)S(1)} collective-permute-done((bf16[59392]{0:T(1024)(128)(2,1)S(1)}, bf16[59392]{0:T(1024)(128)(2,1)S(1)}, u32[]{:S(2)}, u32[]{:S(2)}) %collective-permute-start.5) | collective-permute-done | bytes 118816 | tf_op jit(solution)/shard_map/ppermute | solution.py:147
  55.5 7.1 %shard_map.199 = f32[4,32,1,64]{3,2,1,0:T(1,128)} custom-call(f32[32,64,64]{2,1,0:T(8,128)} %bitcast.161, f32[4,5,32,1,64]{4,3,2,1,0:T(1,128)} %copy-done.6, f32[4,32,1,64]{3,2,1,0:T(1,128)} %bitcast.172), custom_call_target="tpu_custom_call" | custom-call | tf_op jit(solution)/shard_map/pallas_call | solution.py:33
  62.6 1.0 reduce_sum.112
  65.3 1.3 collective-permute-start.6
  66.6 2.7 %collective-permute-start.7 = (f32[32,1024]{1,0:T(8,128)S(1)}, f32[32,1024]{1,0:T(8,128)S(1)}, u32[]{:S(2)}, u32[]{:S(2)}) collective-permute-start(f32[32,1024]{1,0:T(8,128)S(1)} %fusion.16), channel_id=1, source_target_pairs={{0,257},{1,258},{2,259},{3,256},{4,261},{5,262},{6,263},{7,260},{8... | collective-permute-start | bytes 393224 | tf_op jit(solution)/shard_map/ppermute | solution.py:166
  69.3 13.7 %conditional.1 = (bf16[8,4,256]{2,1,0:T(4,128)(2,1)S(1)}) conditional(s32[]{:T(128)} %convert_element_type.212, () %tuple.12, (bf16[8,4,256]{2,1,0:T(4,128)(2,1)S(1)}, f32[32,1024]{1,0:T(8,128)S(1)}) %tuple.48), branch_computations={%region_8.10_spmd, %region_9.11_spmd} | conditional | flops 49206 | bytes 885447 | solution.py:265
  69.4 3.7 %collective-permute-start = (f32[32,256]{1,0:T(8,128)S(1)}, f32[32,256]{1,0:T(8,128)S(1)}, u32[]{:S(2)}, u32[]{:S(2)}) collective-permute-start(f32[32,256]{1,0:T(8,128)S(1)} %get-tuple-element.27), channel_id=1, source_target_pairs={{0,1},{1,2},{2,3},{3,0},{4,5},{5,6},{6,7},{7,4},{8,9},{9,10},{10,1... | collective-permute-start | bytes 98312 | tf_op jit(solution)/shard_map/cond/branch_1_fun/ppermute | solution.py:158
  73.2 2.8 %collective-permute-start.1 = (f32[32,256]{1,0:T(8,128)S(1)}, f32[32,256]{1,0:T(8,128)S(1)}, u32[]{:S(2)}, u32[]{:S(2)}) collective-permute-start(f32[32,256]{1,0:T(8,128)S(1)} %get-tuple-element.29), channel_id=1, source_target_pairs={{0,2},{1,3},{2,0},{3,1},{4,6},{5,7},{6,4},{7,5},{8,10},{9,11},{10,... | collective-permute-start | bytes 98312 | tf_op jit(solution)/shard_map/cond/branch_1_fun/ppermute | solution.py:158
  76.0 1.9 %collective-permute-start.2 = (f32[32,256]{1,0:T(8,128)S(1)}, f32[32,256]{1,0:T(8,128)S(1)}, u32[]{:S(2)}, u32[]{:S(2)}) collective-permute-start(f32[32,256]{1,0:T(8,128)S(1)} %get-tuple-element.28), channel_id=1, source_target_pairs={{0,3},{1,0},{2,1},{3,2},{4,7},{5,4},{6,5},{7,6},{8,11},{9,8},{10,9... | collective-permute-start | bytes 98312 | tf_op jit(solution)/shard_map/cond/branch_1_fun/ppermute | solution.py:158
  77.9 2.5 %collective-permute-done.1 = f32[32,256]{1,0:T(8,128)S(1)} collective-permute-done((f32[32,256]{1,0:T(8,128)S(1)}, f32[32,256]{1,0:T(8,128)S(1)}, u32[]{:S(2)}, u32[]{:S(2)}) %collective-permute-start.1) | collective-permute-done | bytes 32800 | tf_op jit(solution)/shard_map/cond/branch_1_fun/ppermute | solution.py:158
  80.5 2.5 %collective-permute-done.2 = f32[32,256]{1,0:T(8,128)S(1)} collective-permute-done((f32[32,256]{1,0:T(8,128)S(1)}, f32[32,256]{1,0:T(8,128)S(1)}, u32[]{:S(2)}, u32[]{:S(2)}) %collective-permute-start.2) | collective-permute-done | bytes 32800 | tf_op jit(solution)/shard_map/cond/branch_1_fun/ppermute | solution.py:158
  83.1 1.3 collective-permute-start.8
  84.4 1.5 %collective-permute-start.9 = (f32[32,1024]{1,0:T(8,128)S(1)}, f32[32,1024]{1,0:T(8,128)S(1)}, u32[]{:S(2)}, u32[]{:S(2)}) collective-permute-start(f32[32,1024]{1,0:T(8,128)S(1)} %fusion.16), channel_id=1, source_target_pairs={{0,259},{1,256},{2,257},{3,258},{4,263},{5,260},{6,261},{7,262},{8... | collective-permute-start | bytes 393224 | tf_op jit(solution)/shard_map/ppermute | solution.py:166
  85.9 1.0 collective-permute-done.8
  86.9 1.4 %collective-permute-done.9 = f32[32,1024]{1,0:T(8,128)S(1)} collective-permute-done((f32[32,1024]{1,0:T(8,128)S(1)}, f32[32,1024]{1,0:T(8,128)S(1)}, u32[]{:S(2)}, u32[]{:S(2)}) %collective-permute-start.9) | collective-permute-done | bytes 131104 | tf_op jit(solution)/shard_map/ppermute | solution.py:166
  95.1 7.1 %shard_map.200 = f32[4,32,1,64]{3,2,1,0:T(1,128)} custom-call(f32[32,64,64]{2,1,0:T(8,128)} %bitcast.162, f32[4,5,32,1,64]{4,3,2,1,0:T(1,128)} %copy-done.7, f32[4,32,1,64]{3,2,1,0:T(1,128)} %bitcast.173), custom_call_target="tpu_custom_call" | custom-call | tf_op jit(solution)/shard_map/pallas_call | solution.py:33
  102.2 1.0 reduce_sum.116
  104.9 3.3 %collective-permute-start.10 = (f32[32,256]{1,0:T(8,128)S(1)}, f32[32,256]{1,0:T(8,128)S(1)}, u32[]{:S(2)}, u32[]{:S(2)}) collective-permute-start(f32[32,256]{1,0:T(8,128)S(1)} %get-tuple-element.37), channel_id=1, source_target_pairs={{0,1},{1,2},{2,3},{3,0},{4,5},{5,6},{6,7},{7,4},{8,9},{9,10},{10,1... | collective-permute-start | bytes 98312 | tf_op jit(solution)/shard_map/ppermute | solution.py:158
  108.2 3.0 %collective-permute-start.11 = (f32[32,256]{1,0:T(8,128)S(1)}, f32[32,256]{1,0:T(8,128)S(1)}, u32[]{:S(2)}, u32[]{:S(2)}) collective-permute-start(f32[32,256]{1,0:T(8,128)S(1)} %get-tuple-element.39), channel_id=1, source_target_pairs={{0,2},{1,3},{2,0},{3,1},{4,6},{5,7},{6,4},{7,5},{8,10},{9,11},{10,... | collective-permute-start | bytes 98312 | tf_op jit(solution)/shard_map/ppermute | solution.py:158
  111.1 2.3 %collective-permute-start.12 = (f32[32,256]{1,0:T(8,128)S(1)}, f32[32,256]{1,0:T(8,128)S(1)}, u32[]{:S(2)}, u32[]{:S(2)}) collective-permute-start(f32[32,256]{1,0:T(8,128)S(1)} %get-tuple-element.38), channel_id=1, source_target_pairs={{0,3},{1,0},{2,1},{3,2},{4,7},{5,4},{6,5},{7,6},{8,11},{9,8},{10,9... | collective-permute-start | bytes 98312 | tf_op jit(solution)/shard_map/ppermute | solution.py:158
  113.5 2.0 %collective-permute-done.11 = f32[32,256]{1,0:T(8,128)S(1)} collective-permute-done((f32[32,256]{1,0:T(8,128)S(1)}, f32[32,256]{1,0:T(8,128)S(1)}, u32[]{:S(2)}, u32[]{:S(2)}) %collective-permute-start.11) | collective-permute-done | bytes 32800 | tf_op jit(solution)/shard_map/ppermute | solution.py:158
  115.5 2.7 %collective-permute-done.12 = f32[32,256]{1,0:T(8,128)S(1)} collective-permute-done((f32[32,256]{1,0:T(8,128)S(1)}, f32[32,256]{1,0:T(8,128)S(1)}, u32[]{:S(2)}, u32[]{:S(2)}) %collective-permute-start.12) | collective-permute-done | bytes 32800 | tf_op jit(solution)/shard_map/ppermute | solution.py:158
  118.9 1.9 %scatter_fusion.1 = bf16[64,4,256]{2,1,0:T(4,128)(2,1)} fusion(bf16[64,4,256]{2,1,0:T(4,128)(2,1)} %broadcast.459, s32[8]{0:T(128)S(1)} %fusion.100, bf16[8,4,256]{2,1,0:T(4,128)(2,1)S(1)} %fusion.88), kind=kCustom, calls=%fused_computation.4 | custom fusion | bytes 49184 | tf_op jit(solution)/shard_map/scatter | solution.py:360
  120.8 5.2 %all-to-all-start.1 = ((bf16[64,4,256]{2,1,0:T(4,128)(2,1)}), bf16[64,4,256]{2,1,0:T(4,128)(2,1)S(1)}, u32[]{:S(2)}, u32[]{:S(2)}) async-start(bf16[64,4,256]{2,1,0:T(4,128)(2,1)} %scatter_fusion.1), calls=%async_computation.1 | async-start | bytes 262144 | tf_op jit(solution)/shard_map/all_to_all | solution.py:362
  126.7 12.2 %all-to-all-done.1 = bf16[64,4,256]{2,1,0:T(4,128)(2,1)S(1)} async-done(((bf16[64,4,256]{2,1,0:T(4,128)(2,1)}), bf16[64,4,256]{2,1,0:T(4,128)(2,1)S(1)}, u32[]{:S(2)}, u32[]{:S(2)}) %all-to-all-start.1) | async-done | bytes 131104 | tf_op jit(solution)/shard_map/all_to_all | solution.py:362
  (288 shorter events, 28.5 us)
Async XLA Ops:
  0.0 64.5 %copy-start = (bf16[1,256,1024]{2,1,0:T(8,128)(2,1)S(1)}, bf16[1,256,1024]{2,1,0:T(8,128)(2,1)}, u32[]{:S(2)}) copy-start(bf16[1,256,1024]{2,1,0:T(8,128)(2,1)} %param.34) | copy-start | bytes 1572868
  4.3 29.3 %all-to-all-start = ((bf16[64,4,256]{2,1,0:T(4,128)(2,1)}), bf16[64,4,256]{2,1,0:T(4,128)(2,1)S(1)}, u32[]{:S(2)}, u32[]{:S(2)}) async-start(bf16[64,4,256]{2,1,0:T(4,128)(2,1)} %scatter_fusion), calls=%async_computation | async-start | bytes 262144 | tf_op jit(solution)/shard_map/all_to_all | solution.py:356
  25.6 22.5 %copy-start.21 = (f32[1,1,1024]{2,1,0:T(1,128)}, f32[1,1,1024]{2,1,0:T(1,128)S(1)}, u32[]{:S(2)}) copy-start(f32[1,1,1024]{2,1,0:T(1,128)S(1)} %get-tuple-element.55) | copy-start | bytes 12292
  25.6 22.5 %copy-start.23 = (f32[1,1,1024]{2,1,0:T(1,128)}, f32[1,1,1024]{2,1,0:T(1,128)S(1)}, u32[]{:S(2)}) copy-start(f32[1,1,1024]{2,1,0:T(1,128)S(1)} %get-tuple-element.57) | copy-start | bytes 12292
  25.7 22.5 %copy-start.25 = (f32[1,1,1024]{2,1,0:T(1,128)}, f32[1,1,1024]{2,1,0:T(1,128)S(1)}, u32[]{:S(2)}) copy-start(f32[1,1,1024]{2,1,0:T(1,128)S(1)} %get-tuple-element.58) | copy-start | bytes 12292
  25.7 22.8 %copy-start.30 = (f32[1,1,1024]{2,1,0:T(1,128)}, f32[1,1,1024]{2,1,0:T(1,128)S(1)}, u32[]{:S(2)}) copy-start(f32[1,1,1024]{2,1,0:T(1,128)S(1)} %get-tuple-element.56) | copy-start | bytes 12292
  25.7 26.0 %copy-start.28 = (f32[1,1,1024]{2,1,0:T(1,128)}, f32[1,1,1024]{2,1,0:T(1,128)S(1)}, u32[]{:S(2)}) copy-start(f32[1,1,1024]{2,1,0:T(1,128)S(1)} %get-tuple-element.54) | copy-start | bytes 12292
  34.3 10.5 %collective-permute-start.3 = (bf16[59392]{0:T(1024)(128)(2,1)S(1)}, bf16[59392]{0:T(1024)(128)(2,1)S(1)}, u32[]{:S(2)}, u32[]{:S(2)}) collective-permute-start(bf16[59392]{0:T(1024)(128)(2,1)S(1)} %constant_dynamic-update-slice_fusion.23), channel_id=1, source_target_pairs={{0,3},{1,0},{2,1},{3,2},{4,7},{5,4},{6,5},{7,6},{8,11},{9,8},{10,9... | collective-permute-start | bytes 356360 | tf_op jit(solution)/shard_map/ppermute | solution.py:147
  37.0 8.2 %collective-permute-start.4 = (bf16[59392]{0:T(1024)(128)(2,1)S(1)}, bf16[59392]{0:T(1024)(128)(2,1)S(1)}, u32[]{:S(2)}, u32[]{:S(2)}) collective-permute-start(bf16[59392]{0:T(1024)(128)(2,1)S(1)} %constant_dynamic-update-slice_fusion.23), channel_id=1, source_target_pairs={{0,2},{1,3},{2,0},{3,1},{4,6},{5,7},{6,4},{7,5},{8,10},{9,11},{10,... | collective-permute-start | bytes 356360 | tf_op jit(solution)/shard_map/ppermute | solution.py:147
  40.1 6.9 %collective-permute-start.5 = (bf16[59392]{0:T(1024)(128)(2,1)S(1)}, bf16[59392]{0:T(1024)(128)(2,1)S(1)}, u32[]{:S(2)}, u32[]{:S(2)}) collective-permute-start(bf16[59392]{0:T(1024)(128)(2,1)S(1)} %constant_dynamic-update-slice_fusion.23), channel_id=1, source_target_pairs={{0,1},{1,2},{2,3},{3,0},{4,5},{5,6},{6,7},{7,4},{8,9},{9,10},{10,1... | collective-permute-start | bytes 356360 | tf_op jit(solution)/shard_map/ppermute | solution.py:147
  47.2 4.4 %copy-start.8 = (bf16[32,256]{1,0:T(8,128)(2,1)}, bf16[32,256]{1,0:T(8,128)(2,1)S(1)}, u32[]{:S(2)}) copy-start(bf16[32,256]{1,0:T(8,128)(2,1)S(1)} %slice.194) | copy-start | bytes 49156
  47.3 4.4 %copy-start.10 = (bf16[32,256]{1,0:T(8,128)(2,1)}, bf16[32,256]{1,0:T(8,128)(2,1)S(1)}, u32[]{:S(2)}) copy-start(bf16[32,256]{1,0:T(8,128)(2,1)S(1)} %slice.196) | copy-start | bytes 49156
  47.3 4.3 %copy-start.12 = (bf16[32,256]{1,0:T(8,128)(2,1)}, bf16[32,256]{1,0:T(8,128)(2,1)S(1)}, u32[]{:S(2)}) copy-start(bf16[32,256]{1,0:T(8,128)(2,1)S(1)} %slice.198) | copy-start | bytes 49156
  48.4 1.2 copy-start.2
  65.1 4.2 %copy-start.14 = (bf16[8,4,256]{2,1,0:T(4,128)(2,1)S(1)}, bf16[8,4,256]{2,1,0:T(4,128)(2,1)}, u32[]{:S(2)}) copy-start(bf16[8,4,256]{2,1,0:T(4,128)(2,1)} %broadcast_select_fusion) | copy-start | bytes 49156
  65.3 20.6 %collective-permute-start.6 = (f32[32,1024]{1,0:T(8,128)S(1)}, f32[32,1024]{1,0:T(8,128)S(1)}, u32[]{:S(2)}, u32[]{:S(2)}) collective-permute-start(f32[32,1024]{1,0:T(8,128)S(1)} %fusion.16), channel_id=1, source_target_pairs={{0,256},{1,257},{2,258},{3,259},{4,260},{5,261},{6,262},{7,263},{8... | collective-permute-start | bytes 393224 | tf_op jit(solution)/shard_map/ppermute | solution.py:166
  66.6 19.3 %collective-permute-start.7 = (f32[32,1024]{1,0:T(8,128)S(1)}, f32[32,1024]{1,0:T(8,128)S(1)}, u32[]{:S(2)}, u32[]{:S(2)}) collective-permute-start(f32[32,1024]{1,0:T(8,128)S(1)} %fusion.16), channel_id=1, source_target_pairs={{0,257},{1,258},{2,259},{3,256},{4,261},{5,262},{6,263},{7,260},{8... | collective-permute-start | bytes 393224 | tf_op jit(solution)/shard_map/ppermute | solution.py:166
  69.3 19.0 %copy-start.9 = (bf16[32,256]{1,0:T(8,128)(2,1)S(1)}, bf16[32,256]{1,0:T(8,128)(2,1)}, u32[]{:S(2)}) copy-start(bf16[32,256]{1,0:T(8,128)(2,1)} %copy-done.8) | copy-start | bytes 49156
  69.3 19.0 %copy-start.11 = (bf16[32,256]{1,0:T(8,128)(2,1)S(1)}, bf16[32,256]{1,0:T(8,128)(2,1)}, u32[]{:S(2)}) copy-start(bf16[32,256]{1,0:T(8,128)(2,1)} %copy-done.10) | copy-start | bytes 49156
  69.3 19.0 %copy-start.13 = (bf16[32,256]{1,0:T(8,128)(2,1)S(1)}, bf16[32,256]{1,0:T(8,128)(2,1)}, u32[]{:S(2)}) copy-start(bf16[32,256]{1,0:T(8,128)(2,1)} %copy-done.12) | copy-start | bytes 49156
  69.4 8.5 %collective-permute-start = (f32[32,256]{1,0:T(8,128)S(1)}, f32[32,256]{1,0:T(8,128)S(1)}, u32[]{:S(2)}, u32[]{:S(2)}) collective-permute-start(f32[32,256]{1,0:T(8,128)S(1)} %get-tuple-element.27), channel_id=1, source_target_pairs={{0,1},{1,2},{2,3},{3,0},{4,5},{5,6},{6,7},{7,4},{8,9},{9,10},{10,1... | collective-permute-start | bytes 98312 | tf_op jit(solution)/shard_map/cond/branch_1_fun/ppermute | solution.py:158
  73.2 7.3 %collective-permute-start.1 = (f32[32,256]{1,0:T(8,128)S(1)}, f32[32,256]{1,0:T(8,128)S(1)}, u32[]{:S(2)}, u32[]{:S(2)}) collective-permute-start(f32[32,256]{1,0:T(8,128)S(1)} %get-tuple-element.29), channel_id=1, source_target_pairs={{0,2},{1,3},{2,0},{3,1},{4,6},{5,7},{6,4},{7,5},{8,10},{9,11},{10,... | collective-permute-start | bytes 98312 | tf_op jit(solution)/shard_map/cond/branch_1_fun/ppermute | solution.py:158
  76.0 7.0 %collective-permute-start.2 = (f32[32,256]{1,0:T(8,128)S(1)}, f32[32,256]{1,0:T(8,128)S(1)}, u32[]{:S(2)}, u32[]{:S(2)}) collective-permute-start(f32[32,256]{1,0:T(8,128)S(1)} %get-tuple-element.28), channel_id=1, source_target_pairs={{0,3},{1,0},{2,1},{3,2},{4,7},{5,4},{6,5},{7,6},{8,11},{9,8},{10,9... | collective-permute-start | bytes 98312 | tf_op jit(solution)/shard_map/cond/branch_1_fun/ppermute | solution.py:158
  83.1 2.8 %copy-start.48 = (s32[8]{0:T(128)S(1)}, s32[8]{0:T(128)}, u32[]{:S(2)}) copy-start(s32[8]{0:T(128)} %copy-done.47) | copy-start | bytes 100
  83.1 2.8 %copy-start.54 = (s32[8]{0:T(128)S(1)}, s32[8]{0:T(128)}, u32[]{:S(2)}) copy-start(s32[8]{0:T(128)} %copy-done.53) | copy-start | bytes 100
  83.1 3.8 %collective-permute-start.8 = (f32[32,1024]{1,0:T(8,128)S(1)}, f32[32,1024]{1,0:T(8,128)S(1)}, u32[]{:S(2)}, u32[]{:S(2)}) collective-permute-start(f32[32,1024]{1,0:T(8,128)S(1)} %fusion.16), channel_id=1, source_target_pairs={{0,258},{1,259},{2,256},{3,257},{4,262},{5,263},{6,260},{7,261},{8... | collective-permute-start | bytes 393224 | tf_op jit(solution)/shard_map/ppermute | solution.py:166
  84.4 3.9 %collective-permute-start.9 = (f32[32,1024]{1,0:T(8,128)S(1)}, f32[32,1024]{1,0:T(8,128)S(1)}, u32[]{:S(2)}, u32[]{:S(2)}) collective-permute-start(f32[32,1024]{1,0:T(8,128)S(1)} %fusion.16), channel_id=1, source_target_pairs={{0,259},{1,256},{2,257},{3,258},{4,263},{5,260},{6,261},{7,262},{8... | collective-permute-start | bytes 393224 | tf_op jit(solution)/shard_map/ppermute | solution.py:166
  104.9 8.6 %collective-permute-start.10 = (f32[32,256]{1,0:T(8,128)S(1)}, f32[32,256]{1,0:T(8,128)S(1)}, u32[]{:S(2)}, u32[]{:S(2)}) collective-permute-start(f32[32,256]{1,0:T(8,128)S(1)} %get-tuple-element.37), channel_id=1, source_target_pairs={{0,1},{1,2},{2,3},{3,0},{4,5},{5,6},{6,7},{7,4},{8,9},{9,10},{10,1... | collective-permute-start | bytes 98312 | tf_op jit(solution)/shard_map/ppermute | solution.py:158
  108.2 5.3 %copy-start.46 = (s32[8]{0:T(128)S(1)}, s32[8]{0:T(128)}, u32[]{:S(2)}) copy-start(s32[8]{0:T(128)} %copy-done.45) | copy-start | bytes 100
  108.2 7.3 %collective-permute-start.11 = (f32[32,256]{1,0:T(8,128)S(1)}, f32[32,256]{1,0:T(8,128)S(1)}, u32[]{:S(2)}, u32[]{:S(2)}) collective-permute-start(f32[32,256]{1,0:T(8,128)S(1)} %get-tuple-element.39), channel_id=1, source_target_pairs={{0,2},{1,3},{2,0},{3,1},{4,6},{5,7},{6,4},{7,5},{8,10},{9,11},{10,... | collective-permute-start | bytes 98312 | tf_op jit(solution)/shard_map/ppermute | solution.py:158
  111.1 7.0 %collective-permute-start.12 = (f32[32,256]{1,0:T(8,128)S(1)}, f32[32,256]{1,0:T(8,128)S(1)}, u32[]{:S(2)}, u32[]{:S(2)}) collective-permute-start(f32[32,256]{1,0:T(8,128)S(1)} %get-tuple-element.38), channel_id=1, source_target_pairs={{0,3},{1,0},{2,1},{3,2},{4,7},{5,4},{6,5},{7,6},{8,11},{9,8},{10,9... | collective-permute-start | bytes 98312 | tf_op jit(solution)/shard_map/ppermute | solution.py:158
  120.8 18.1 %all-to-all-start.1 = ((bf16[64,4,256]{2,1,0:T(4,128)(2,1)}), bf16[64,4,256]{2,1,0:T(4,128)(2,1)S(1)}, u32[]{:S(2)}, u32[]{:S(2)}) async-start(bf16[64,4,256]{2,1,0:T(4,128)(2,1)} %scatter_fusion.1), calls=%async_computation.1 | async-start | bytes 262144 | tf_op jit(solution)/shard_map/all_to_all | solution.py:362
  (39 other events, 29.4 us)

commit v11 on v9

--- a/solution.py
+++ b/solution.py
@@ -17,7 +17,9 @@
         erasing = vector_ref[position, 3]
         acceptor = vector_ref[position, 4]
         content = content_ref[position]
-        pulled = jnp.sum(states * normed, axis=-1, keepdims=True)
+        pulled = jnp.einsum(
+            "bij,bqj->biq", states, normed, precision=lax.Precision.HIGH, preferred_element_type=jnp.float32
+        )
         added = jnp.einsum(
             "bqi,bqj->bij", content, erasing, precision=lax.Precision.HIGH, preferred_element_type=jnp.float32
         )

time: 130 us -> 134 us (1.031)
  Pallas kernels: 14.2 us -> 18.9 us
    pallas_call x2, Pallas kernels: 14.2 us -> 18.9 us  [run_recurrence(): pl.pallas_call(recurrence_kernel, out_shape=jax.ShapeDtypeStruct((steps,...]
where the time goes in v11:
time: 134 us; the launch traced here: 133 us
  starting transfers between devices  48.6 us (36%)
  waiting for transfers between devices  29.7 us (22%)
  local copies, waits for them, and re-layouts  24.6 us (18%)
  Pallas kernels  18.9 us (14%)
  other arithmetic  6.03 us (4%)
  matrix products  3.34 us (2%)
  between operations  1.63 us (1%)
    pallas_call x2, Pallas kernels, run_recurrence(): pl.pallas_call(recurrence_kernel, out_shape=jax.ShapeDtypeStruct((steps,...  18.9 us
    all_to_all x1, starting transfers between devices, body(): lax.all_to_all(outgoing, 'req', split_axis=0, concat_axis=0, tiled=True)  16.6 us
    unnamed x128, local copies, waits for them, and re-layouts  12.9 us
    all_to_all x1, waiting for transfers between devices, body(): lax.all_to_all(going_back, 'req', split_axis=0, concat_axis=0, tiled=True)  12.4 us
    ppermute x3, starting transfers between devices, gather_heads(): lax.ppermute(block, 'head', [(i, (i + k) % n) for i in range(n)])  9.76 us
    ppermute x3, starting transfers between devices, scatter_heads(): lax.ppermute(chunk, 'head', [(i, (i + k) % n) for i in range(n)])  9.26 us
    all_to_all x1, waiting for transfers between devices, body(): lax.all_to_all(outgoing, 'req', split_axis=0, concat_axis=0, tiled=True)  8.96 us
    ppermute x4, starting transfers between devices, hand_over(): lax.ppermute(partial, ('section', 'head'), [(i, n + (i + k) % n) for i in...  6.74 us
  transfers between devices with their start and end apart: 13, of which 7 were waited for; matrix products, arithmetic and copies ran while one was open for 2% of the time, Pallas kernels for 0%

profile of v11, /device:TPU:6, one launch (start us, length us, event | category | flops | bytes accessed | tf_op | source)
XLA Modules:
  0.0 132.9 jit_solution(14912696414822454765)
XLA Ops:
  0.0 0.7 copy-done.34
  2.3 1.9 %scatter_fusion = bf16[64,4,256]{2,1,0:T(4,128)(2,1)} fusion(bf16[64,4,256]{2,1,0:T(4,128)(2,1)} %broadcast.450.clone, s32[8]{0:T(128)S(1)} %fusion.101, bf16[8,4,256]{2,1,0:T(4,128)(2,1)S(1)} %copy-done.33), kind=kCustom, calls=%fused_computation.3 | custom fusion | bytes 49184 | tf_op jit(solution)/shard_map/scatter | solution.py:348
  4.2 16.6 %all-to-all-start = ((bf16[64,4,256]{2,1,0:T(4,128)(2,1)}), bf16[64,4,256]{2,1,0:T(4,128)(2,1)S(1)}, u32[]{:S(2)}, u32[]{:S(2)}) async-start(bf16[64,4,256]{2,1,0:T(4,128)(2,1)} %scatter_fusion), calls=%async_computation | async-start | bytes 262144 | tf_op jit(solution)/shard_map/all_to_all | solution.py:350
  24.6 9.0 %all-to-all-done = bf16[64,4,256]{2,1,0:T(4,128)(2,1)S(1)} async-done(((bf16[64,4,256]{2,1,0:T(4,128)(2,1)}), bf16[64,4,256]{2,1,0:T(4,128)(2,1)S(1)}, u32[]{:S(2)}, u32[]{:S(2)}) %all-to-all-start) | async-done | bytes 131104 | tf_op jit(solution)/shard_map/all_to_all | solution.py:350
  34.3 2.7 %collective-permute-start = (bf16[59392]{0:T(1024)(128)(2,1)S(1)}, bf16[59392]{0:T(1024)(128)(2,1)S(1)}, u32[]{:S(2)}, u32[]{:S(2)}) collective-permute-start(bf16[59392]{0:T(1024)(128)(2,1)S(1)} %constant_dynamic-update-slice_fusion.23), channel_id=1, source_target_pairs={{0,3},{1,0},{2,1},{3,2},{4,7},{5,4},{6,5},{7,6},{8,11},{9,8},{10,9... | collective-permute-start | bytes 356360 | tf_op jit(solution)/shard_map/ppermute | solution.py:149
  37.0 3.0 %collective-permute-start.1 = (bf16[59392]{0:T(1024)(128)(2,1)S(1)}, bf16[59392]{0:T(1024)(128)(2,1)S(1)}, u32[]{:S(2)}, u32[]{:S(2)}) collective-permute-start(bf16[59392]{0:T(1024)(128)(2,1)S(1)} %constant_dynamic-update-slice_fusion.23), channel_id=1, source_target_pairs={{0,2},{1,3},{2,0},{3,1},{4,6},{5,7},{6,4},{7,5},{8,10},{9,11},{10,... | collective-permute-start | bytes 356360 | tf_op jit(solution)/shard_map/ppermute | solution.py:149
  40.1 4.0 %collective-permute-start.2 = (bf16[59392]{0:T(1024)(128)(2,1)S(1)}, bf16[59392]{0:T(1024)(128)(2,1)S(1)}, u32[]{:S(2)}, u32[]{:S(2)}) collective-permute-start(bf16[59392]{0:T(1024)(128)(2,1)S(1)} %constant_dynamic-update-slice_fusion.23), channel_id=1, source_target_pairs={{0,1},{1,2},{2,3},{3,0},{4,5},{5,6},{6,7},{7,4},{8,9},{9,10},{10,1... | collective-permute-start | bytes 356360 | tf_op jit(solution)/shard_map/ppermute | solution.py:149
  45.3 1.7 %collective-permute-done.2 = bf16[59392]{0:T(1024)(128)(2,1)S(1)} collective-permute-done((bf16[59392]{0:T(1024)(128)(2,1)S(1)}, bf16[59392]{0:T(1024)(128)(2,1)S(1)}, u32[]{:S(2)}, u32[]{:S(2)}) %collective-permute-start.2) | collective-permute-done | bytes 118816 | tf_op jit(solution)/shard_map/ppermute | solution.py:149
  48.5 0.7 copy-done.18
  50.5 0.8 multiply_multiply_fusion.1
  52.3 0.7 copy-done.20
  55.4 0.7 copy-done.6
  56.1 9.5 %shard_map.199 = f32[4,32,1,64]{3,2,1,0:T(1,128)} custom-call(f32[32,64,64]{2,1,0:T(8,128)} %bitcast.161, f32[4,5,32,1,64]{4,3,2,1,0:T(1,128)} %copy-done.6, f32[4,32,1,64]{3,2,1,0:T(1,128)} %bitcast.172), custom_call_target="tpu_custom_call" | custom-call | tf_op jit(solution)/shard_map/pallas_call | solution.py:35
  65.6 1.0 reduce_sum.112
  69.0 1.3 collective-permute-start.3
  70.3 2.7 %collective-permute-start.4 = (f32[32,1024]{1,0:T(8,128)S(1)}, f32[32,1024]{1,0:T(8,128)S(1)}, u32[]{:S(2)}, u32[]{:S(2)}) collective-permute-start(f32[32,1024]{1,0:T(8,128)S(1)} %fusion.16), channel_id=1, source_target_pairs={{0,257},{1,258},{2,259},{3,256},{4,261},{5,262},{6,263},{7,260},{8... | collective-permute-start | bytes 393224 | tf_op jit(solution)/shard_map/ppermute | solution.py:168
  73.0 1.3 collective-permute-start.5
  74.3 1.5 %collective-permute-start.6 = (f32[32,1024]{1,0:T(8,128)S(1)}, f32[32,1024]{1,0:T(8,128)S(1)}, u32[]{:S(2)}, u32[]{:S(2)}) collective-permute-start(f32[32,1024]{1,0:T(8,128)S(1)} %fusion.16), channel_id=1, source_target_pairs={{0,259},{1,256},{2,257},{3,258},{4,263},{5,260},{6,261},{7,262},{8... | collective-permute-start | bytes 393224 | tf_op jit(solution)/shard_map/ppermute | solution.py:168
  75.8 0.9 collective-permute-done.5
  76.8 1.4 %collective-permute-done.6 = f32[32,1024]{1,0:T(8,128)S(1)} collective-permute-done((f32[32,1024]{1,0:T(8,128)S(1)}, f32[32,1024]{1,0:T(8,128)S(1)}, u32[]{:S(2)}, u32[]{:S(2)}) %collective-permute-start.6) | collective-permute-done | bytes 131104 | tf_op jit(solution)/shard_map/ppermute | solution.py:168
  78.4 0.7 copy-done.19
  84.2 0.7 copy-done.7
  85.0 9.5 %shard_map.200 = f32[4,32,1,64]{3,2,1,0:T(1,128)} custom-call(f32[32,64,64]{2,1,0:T(8,128)} %bitcast.162, f32[4,5,32,1,64]{4,3,2,1,0:T(1,128)} %copy-done.7, f32[4,32,1,64]{3,2,1,0:T(1,128)} %bitcast.173), custom_call_target="tpu_custom_call" | custom-call | tf_op jit(solution)/shard_map/pallas_call | solution.py:35
  94.4 1.0 reduce_sum.116
  96.5 3.4 %collective-permute-start.10 = (f32[32,256]{1,0:T(8,128)S(1)}, f32[32,256]{1,0:T(8,128)S(1)}, u32[]{:S(2)}, u32[]{:S(2)}) collective-permute-start(f32[32,256]{1,0:T(8,128)S(1)} %get-tuple-element.26), channel_id=1, source_target_pairs={{0,3},{1,0},{2,1},{3,2},{4,7},{5,4},{6,5},{7,6},{8,11},{9,8},{10,9... | collective-permute-start | bytes 98312 | tf_op jit(solution)/shard_map/ppermute | solution.py:160
  99.9 3.7 %collective-permute-start.8 = (f32[32,256]{1,0:T(8,128)S(1)}, f32[32,256]{1,0:T(8,128)S(1)}, u32[]{:S(2)}, u32[]{:S(2)}) collective-permute-start(f32[32,256]{1,0:T(8,128)S(1)} %get-tuple-element.25), channel_id=1, source_target_pairs={{0,1},{1,2},{2,3},{3,0},{4,5},{5,6},{6,7},{7,4},{8,9},{9,10},{10,1... | collective-permute-start | bytes 98312 | tf_op jit(solution)/shard_map/ppermute | solution.py:160
  103.5 2.2 %collective-permute-start.9 = (f32[32,256]{1,0:T(8,128)S(1)}, f32[32,256]{1,0:T(8,128)S(1)}, u32[]{:S(2)}, u32[]{:S(2)}) collective-permute-start(f32[32,256]{1,0:T(8,128)S(1)} %get-tuple-element.27), channel_id=1, source_target_pairs={{0,2},{1,3},{2,0},{3,1},{4,6},{5,7},{6,4},{7,5},{8,10},{9,11},{10,... | collective-permute-start | bytes 98312 | tf_op jit(solution)/shard_map/ppermute | solution.py:160
  105.8 1.3 collective-permute-start.7
  107.1 3.7 %collective-permute-done.9 = f32[32,256]{1,0:T(8,128)S(1)} collective-permute-done((f32[32,256]{1,0:T(8,128)S(1)}, f32[32,256]{1,0:T(8,128)S(1)}, u32[]{:S(2)}, u32[]{:S(2)}) %collective-permute-start.9) | collective-permute-done | bytes 32800 | tf_op jit(solution)/shard_map/ppermute | solution.py:160
  111.6 1.9 %scatter_fusion.1 = bf16[64,4,256]{2,1,0:T(4,128)(2,1)} fusion(bf16[64,4,256]{2,1,0:T(4,128)(2,1)} %broadcast.450, s32[8]{0:T(128)S(1)} %copy-done.50, bf16[8,4,256]{2,1,0:T(4,128)(2,1)S(1)} %fusion.88), kind=kCustom, calls=%fused_computation.4 | custom fusion | bytes 49184 | tf_op jit(solution)/shard_map/scatter | solution.py:354
  113.5 4.9 %all-to-all-start.1 = ((bf16[64,4,256]{2,1,0:T(4,128)(2,1)}), bf16[64,4,256]{2,1,0:T(4,128)(2,1)S(1)}, u32[]{:S(2)}, u32[]{:S(2)}) async-start(bf16[64,4,256]{2,1,0:T(4,128)(2,1)} %scatter_fusion.1), calls=%async_computation.1 | async-start | bytes 262144 | tf_op jit(solution)/shard_map/all_to_all | solution.py:356
  119.2 12.4 %all-to-all-done.1 = bf16[64,4,256]{2,1,0:T(4,128)(2,1)S(1)} async-done(((bf16[64,4,256]{2,1,0:T(4,128)(2,1)}), bf16[64,4,256]{2,1,0:T(4,128)(2,1)S(1)}, u32[]{:S(2)}, u32[]{:S(2)}) %all-to-all-start.1) | async-done | bytes 131104 | tf_op jit(solution)/shard_map/all_to_all | solution.py:356
  (271 shorter events, 23.7 us)
Async XLA Ops:
  0.0 68.1 %copy-start = (bf16[1,256,1024]{2,1,0:T(8,128)(2,1)S(1)}, bf16[1,256,1024]{2,1,0:T(8,128)(2,1)}, u32[]{:S(2)}) copy-start(bf16[1,256,1024]{2,1,0:T(8,128)(2,1)} %param.32) | copy-start | bytes 1572868
  4.2 29.3 %all-to-all-start = ((bf16[64,4,256]{2,1,0:T(4,128)(2,1)}), bf16[64,4,256]{2,1,0:T(4,128)(2,1)S(1)}, u32[]{:S(2)}, u32[]{:S(2)}) async-start(bf16[64,4,256]{2,1,0:T(4,128)(2,1)} %scatter_fusion), calls=%async_computation | async-start | bytes 262144 | tf_op jit(solution)/shard_map/all_to_all | solution.py:350
  22.9 0.8 copy-start.17
  24.5 23.6 %copy-start.22 = (f32[1,1,1024]{2,1,0:T(1,128)}, f32[1,1,1024]{2,1,0:T(1,128)S(1)}, u32[]{:S(2)}) copy-start(f32[1,1,1024]{2,1,0:T(1,128)S(1)} %get-tuple-element.43) | copy-start | bytes 12292
  24.5 23.6 %copy-start.24 = (f32[1,1,1024]{2,1,0:T(1,128)}, f32[1,1,1024]{2,1,0:T(1,128)S(1)}, u32[]{:S(2)}) copy-start(f32[1,1,1024]{2,1,0:T(1,128)S(1)} %get-tuple-element.45) | copy-start | bytes 12292
  24.6 23.6 %copy-start.26 = (f32[1,1,1024]{2,1,0:T(1,128)}, f32[1,1,1024]{2,1,0:T(1,128)S(1)}, u32[]{:S(2)}) copy-start(f32[1,1,1024]{2,1,0:T(1,128)S(1)} %get-tuple-element.46) | copy-start | bytes 12292
  24.6 23.9 %copy-start.31 = (f32[1,1,1024]{2,1,0:T(1,128)}, f32[1,1,1024]{2,1,0:T(1,128)S(1)}, u32[]{:S(2)}) copy-start(f32[1,1,1024]{2,1,0:T(1,128)S(1)} %get-tuple-element.44) | copy-start | bytes 12292
  24.6 27.7 %copy-start.29 = (f32[1,1,1024]{2,1,0:T(1,128)}, f32[1,1,1024]{2,1,0:T(1,128)S(1)}, u32[]{:S(2)}) copy-start(f32[1,1,1024]{2,1,0:T(1,128)S(1)} %get-tuple-element.42) | copy-start | bytes 12292
  34.3 10.4 %collective-permute-start = (bf16[59392]{0:T(1024)(128)(2,1)S(1)}, bf16[59392]{0:T(1024)(128)(2,1)S(1)}, u32[]{:S(2)}, u32[]{:S(2)}) collective-permute-start(bf16[59392]{0:T(1024)(128)(2,1)S(1)} %constant_dynamic-update-slice_fusion.23), channel_id=1, source_target_pairs={{0,3},{1,0},{2,1},{3,2},{4,7},{5,4},{6,5},{7,6},{8,11},{9,8},{10,9... | collective-permute-start | bytes 356360 | tf_op jit(solution)/shard_map/ppermute | solution.py:149
  37.0 8.2 %collective-permute-start.1 = (bf16[59392]{0:T(1024)(128)(2,1)S(1)}, bf16[59392]{0:T(1024)(128)(2,1)S(1)}, u32[]{:S(2)}, u32[]{:S(2)}) collective-permute-start(bf16[59392]{0:T(1024)(128)(2,1)S(1)} %constant_dynamic-update-slice_fusion.23), channel_id=1, source_target_pairs={{0,2},{1,3},{2,0},{3,1},{4,6},{5,7},{6,4},{7,5},{8,10},{9,11},{10,... | collective-permute-start | bytes 356360 | tf_op jit(solution)/shard_map/ppermute | solution.py:149
  40.1 6.9 %collective-permute-start.2 = (bf16[59392]{0:T(1024)(128)(2,1)S(1)}, bf16[59392]{0:T(1024)(128)(2,1)S(1)}, u32[]{:S(2)}, u32[]{:S(2)}) collective-permute-start(bf16[59392]{0:T(1024)(128)(2,1)S(1)} %constant_dynamic-update-slice_fusion.23), channel_id=1, source_target_pairs={{0,1},{1,2},{2,3},{3,0},{4,5},{5,6},{6,7},{7,4},{8,9},{9,10},{10,1... | collective-permute-start | bytes 356360 | tf_op jit(solution)/shard_map/ppermute | solution.py:149
  47.2 5.0 %copy-start.10 = (bf16[32,256]{1,0:T(8,128)(2,1)}, bf16[32,256]{1,0:T(8,128)(2,1)S(1)}, u32[]{:S(2)}) copy-start(bf16[32,256]{1,0:T(8,128)(2,1)S(1)} %slice.200) | copy-start | bytes 49156
  47.3 5.0 %copy-start.12 = (bf16[32,256]{1,0:T(8,128)(2,1)}, bf16[32,256]{1,0:T(8,128)(2,1)S(1)}, u32[]{:S(2)}) copy-start(bf16[32,256]{1,0:T(8,128)(2,1)S(1)} %slice.201) | copy-start | bytes 49156
  47.3 4.9 %copy-start.14 = (bf16[32,256]{1,0:T(8,128)(2,1)}, bf16[32,256]{1,0:T(8,128)(2,1)S(1)}, u32[]{:S(2)}) copy-start(bf16[32,256]{1,0:T(8,128)(2,1)S(1)} %slice.202) | copy-start | bytes 49156
  48.4 1.2 copy-start.2
  49.2 1.1 copy-start.1
  53.3 1.0 copy-start.3
  65.6 1.0 copy-start.5
  68.8 7.0 %copy-start.45 = (s32[8]{0:T(128)S(1)}, s32[8]{0:T(128)}, u32[]{:S(2)}) copy-start(s32[8]{0:T(128)} %copy-done.44) | copy-start | bytes 100
  68.8 9.4 %copy-start.11 = (bf16[32,256]{1,0:T(8,128)(2,1)S(1)}, bf16[32,256]{1,0:T(8,128)(2,1)}, u32[]{:S(2)}) copy-start(bf16[32,256]{1,0:T(8,128)(2,1)} %copy-done.10) | copy-start | bytes 49156
  68.8 9.4 %copy-start.13 = (bf16[32,256]{1,0:T(8,128)(2,1)S(1)}, bf16[32,256]{1,0:T(8,128)(2,1)}, u32[]{:S(2)}) copy-start(bf16[32,256]{1,0:T(8,128)(2,1)} %copy-done.12) | copy-start | bytes 49156
  68.8 9.4 %copy-start.15 = (bf16[32,256]{1,0:T(8,128)(2,1)S(1)}, bf16[32,256]{1,0:T(8,128)(2,1)}, u32[]{:S(2)}) copy-start(bf16[32,256]{1,0:T(8,128)(2,1)} %copy-done.14) | copy-start | bytes 49156
  69.0 6.8 %collective-permute-start.3 = (f32[32,1024]{1,0:T(8,128)S(1)}, f32[32,1024]{1,0:T(8,128)S(1)}, u32[]{:S(2)}, u32[]{:S(2)}) collective-permute-start(f32[32,1024]{1,0:T(8,128)S(1)} %fusion.16), channel_id=1, source_target_pairs={{0,256},{1,257},{2,258},{3,259},{4,260},{5,261},{6,262},{7,263},{8... | collective-permute-start | bytes 393224 | tf_op jit(solution)/shard_map/ppermute | solution.py:168
  70.3 5.5 %collective-permute-start.4 = (f32[32,1024]{1,0:T(8,128)S(1)}, f32[32,1024]{1,0:T(8,128)S(1)}, u32[]{:S(2)}, u32[]{:S(2)}) collective-permute-start(f32[32,1024]{1,0:T(8,128)S(1)} %fusion.16), channel_id=1, source_target_pairs={{0,257},{1,258},{2,259},{3,256},{4,261},{5,262},{6,263},{7,260},{8... | collective-permute-start | bytes 393224 | tf_op jit(solution)/shard_map/ppermute | solution.py:168
  73.0 3.8 %collective-permute-start.5 = (f32[32,1024]{1,0:T(8,128)S(1)}, f32[32,1024]{1,0:T(8,128)S(1)}, u32[]{:S(2)}, u32[]{:S(2)}) collective-permute-start(f32[32,1024]{1,0:T(8,128)S(1)} %fusion.16), channel_id=1, source_target_pairs={{0,258},{1,259},{2,256},{3,257},{4,262},{5,263},{6,260},{7,261},{8... | collective-permute-start | bytes 393224 | tf_op jit(solution)/shard_map/ppermute | solution.py:168
  74.3 3.9 %collective-permute-start.6 = (f32[32,1024]{1,0:T(8,128)S(1)}, f32[32,1024]{1,0:T(8,128)S(1)}, u32[]{:S(2)}, u32[]{:S(2)}) collective-permute-start(f32[32,1024]{1,0:T(8,128)S(1)} %fusion.16), channel_id=1, source_target_pairs={{0,259},{1,256},{2,257},{3,258},{4,263},{5,260},{6,261},{7,262},{8... | collective-permute-start | bytes 393224 | tf_op jit(solution)/shard_map/ppermute | solution.py:168
  94.4 1.0 copy-start.4
  96.5 10.6 %collective-permute-start.10 = (f32[32,256]{1,0:T(8,128)S(1)}, f32[32,256]{1,0:T(8,128)S(1)}, u32[]{:S(2)}, u32[]{:S(2)}) collective-permute-start(f32[32,256]{1,0:T(8,128)S(1)} %get-tuple-element.26), channel_id=1, source_target_pairs={{0,3},{1,0},{2,1},{3,2},{4,7},{5,4},{6,5},{7,6},{8,11},{9,8},{10,9... | collective-permute-start | bytes 98312 | tf_op jit(solution)/shard_map/ppermute | solution.py:160
  99.9 7.2 %collective-permute-start.8 = (f32[32,256]{1,0:T(8,128)S(1)}, f32[32,256]{1,0:T(8,128)S(1)}, u32[]{:S(2)}, u32[]{:S(2)}) collective-permute-start(f32[32,256]{1,0:T(8,128)S(1)} %get-tuple-element.25), channel_id=1, source_target_pairs={{0,1},{1,2},{2,3},{3,0},{4,5},{5,6},{6,7},{7,4},{8,9},{9,10},{10,1... | collective-permute-start | bytes 98312 | tf_op jit(solution)/shard_map/ppermute | solution.py:160
  103.5 7.3 %collective-permute-start.9 = (f32[32,256]{1,0:T(8,128)S(1)}, f32[32,256]{1,0:T(8,128)S(1)}, u32[]{:S(2)}, u32[]{:S(2)}) collective-permute-start(f32[32,256]{1,0:T(8,128)S(1)} %get-tuple-element.27), channel_id=1, source_target_pairs={{0,2},{1,3},{2,0},{3,1},{4,6},{5,7},{6,4},{7,5},{8,10},{9,11},{10,... | collective-permute-start | bytes 98312 | tf_op jit(solution)/shard_map/ppermute | solution.py:160
  105.8 5.1 %collective-permute-start.7 = (bf16[8,4,256]{2,1,0:T(4,128)(2,1)S(1)}, bf16[8,4,256]{2,1,0:T(4,128)(2,1)S(1)}, u32[]{:S(2)}, u32[]{:S(2)}) collective-permute-start(bf16[8,4,256]{2,1,0:T(4,128)(2,1)S(1)} %constant_dynamic-slice_fusion.2), channel_id=1, source_target_pairs={{256,0},{257,1},{258,2},{259,3},{260,4},{261,5},{262,6},{263,7},{2... | collective-permute-start | bytes 49160 | tf_op jit(solution)/shard_map/ppermute | solution.py:175
  113.5 18.1 %all-to-all-start.1 = ((bf16[64,4,256]{2,1,0:T(4,128)(2,1)}), bf16[64,4,256]{2,1,0:T(4,128)(2,1)S(1)}, u32[]{:S(2)}, u32[]{:S(2)}) async-start(bf16[64,4,256]{2,1,0:T(4,128)(2,1)} %scatter_fusion.1), calls=%async_computation.1 | async-start | bytes 262144 | tf_op jit(solution)/shard_map/all_to_all | solution.py:356
  (33 other events, 24.0 us)

commit v12 on v9

--- a/solution.py
+++ b/solution.py
@@ -269,6 +269,16 @@
     return jnp.where(section_num == 0, first_out, second_out)
 
 
+def place_rows(rows, index, count):
+    found = index[None, :] == jnp.arange(count, dtype=jnp.int32)[:, None]
+    source = jnp.sum(
+        jnp.where(found, jnp.arange(index.shape[0], dtype=jnp.int32)[None, :], 0), axis=1
+    )
+    present = jnp.any(found, axis=1)
+    picked = jnp.take(rows, source, axis=0)
+    return jnp.where(present.reshape((count,) + (1,) * (rows.ndim - 1)), picked, jnp.zeros_like(picked))
+
+
 def body(
     embedding_per_slot,
     tally_per_slot,
@@ -340,17 +350,11 @@
     )
     states_local = memory_per_request.reshape(memory_per_request.shape[1:])
     last_local = previous_step_feature.reshape(previous_step_feature.shape[1:])
-    outgoing = (
-        jnp.zeros((buffer_rows,) + embedding_per_slot.shape[1:], jnp.bfloat16)
-        .at[arrival_slot]
-        .set(embedding_per_slot)
-    )
+    outgoing = place_rows(embedding_per_slot, arrival_slot, buffer_rows)
     arrived = lax.all_to_all(outgoing, "req", split_axis=0, concat_axis=0, tiled=True)
     inputs = jnp.take(arrived, home_slot, axis=0)
     result = run_sections(inputs, states_local, last_local, params)
-    going_back = (
-        jnp.zeros((buffer_rows,) + result.shape[1:], jnp.bfloat16).at[home_slot].set(result)
-    )
+    going_back = place_rows(result, home_slot, buffer_rows)
     returned = lax.all_to_all(going_back, "req", split_axis=0, concat_axis=0, tiled=True)
     result = jnp.take(returned, arrival_slot, axis=0)
     live_mask = (

time: 130 us -> 129 us (level)
  waiting for transfers between devices: 29.8 us -> 24.4 us
  other arithmetic: 6.03 us -> 11 us
  starting transfers between devices: 48.5 us -> 50.4 us
  local copies, waits for them, and re-layouts: 24.7 us -> 22.9 us
    scatter x2 -> x0, local copies, waits for them, and re-layouts: 3.85 us -> none  [the longest x1 1.93 us: body(): jnp.zeros((buffer_rows,) + result.shape[1:], jnp.bfloat16).at[home_slot]]
    ppermute x3, waiting for transfers between devices: 3.75 us -> 1.92 us  [scatter_heads(): lax.ppermute(chunk, 'head', [(i, (i + k) % n) for i in range(n)])]
    select_n x3 -> x5, other arithmetic: 0.61 us -> 2.22 us  [the longest x2 1.71 us: place_rows(): jnp.where(present.reshape((count,) + (1,) * (rows.ndim - 1)), picked, jnp...]
    gather x0 -> x2, local copies, waits for them, and re-layouts: none -> 1.5 us  [place_rows(): picked = jnp.take(rows, source, axis=0)]
    all_to_all x1, waiting for transfers between devices: 8.96 us -> 7.47 us  [body(): lax.all_to_all(outgoing, 'req', split_axis=0, concat_axis=0, tiled=True)]
    another operation x2 -> x0, local copies, waits for them, and re-layouts: 1.38 us -> none
    unnamed x128 -> x134, local copies, waits for them, and re-layouts: 12.9 us -> 14.1 us
  transfers between devices with their start and end apart: 13 -> 13, of which waited for: 7 -> 6; matrix products, arithmetic and copies ran while one was open for 2% -> 3% of each run, Pallas kernels for 0% -> 0%
where the time goes in v12:
time: 129 us; the launch traced here: 127 us
  starting transfers between devices  50.4 us (39%)
  waiting for transfers between devices  24.4 us (19%)
  local copies, waits for them, and re-layouts  22.9 us (18%)
  Pallas kernels  14.2 us (11%)
  other arithmetic  11 us (9%)
  matrix products  2.72 us (2%)
  between operations  1.55 us (1%)
    all_to_all x1, starting transfers between devices, body(): lax.all_to_all(outgoing, 'req', split_axis=0, concat_axis=0, tiled=True)  16.6 us
    pallas_call x2, Pallas kernels, run_recurrence(): pl.pallas_call(recurrence_kernel, out_shape=jax.ShapeDtypeStruct((steps,...  14.2 us
    unnamed x134, local copies, waits for them, and re-layouts  14.1 us
    all_to_all x1, waiting for transfers between devices, body(): lax.all_to_all(going_back, 'req', split_axis=0, concat_axis=0, tiled=True)  11.6 us
    ppermute x3, starting transfers between devices, scatter_heads(): lax.ppermute(chunk, 'head', [(i, (i + k) % n) for i in range(n)])  9.83 us
    ppermute x3, starting transfers between devices, gather_heads(): lax.ppermute(block, 'head', [(i, (i + k) % n) for i in range(n)])  9.76 us
    all_to_all x1, waiting for transfers between devices, body(): lax.all_to_all(outgoing, 'req', split_axis=0, concat_axis=0, tiled=True)  7.47 us
    ppermute x4, starting transfers between devices, hand_over(): lax.ppermute(partial, ('section', 'head'), [(i, n + (i + k) % n) for i in...  6.73 us
  transfers between devices with their start and end apart: 13, of which 6 were waited for; matrix products, arithmetic and copies ran while one was open for 3% of the time, Pallas kernels for 0%

profile of v12, /device:TPU:6, one launch (start us, length us, event | category | flops | bytes accessed | tf_op | source)
XLA Modules:
  0.0 127.1 jit_solution(6660774213864847061)
XLA Ops:
  0.0 0.8 reshape.787
  2.8 0.9 select_select_fusion.1
  3.7 16.6 %all-to-all-start = ((bf16[64,4,256]{2,1,0:T(4,128)(2,1)}), bf16[64,4,256]{2,1,0:T(4,128)(2,1)S(1)}, u32[]{:S(2)}, u32[]{:S(2)}) async-start(bf16[64,4,256]{2,1,0:T(4,128)(2,1)} %select_select_fusion.1), calls=%async_computation | async-start | bytes 262144 | tf_op jit(solution)/shard_map/all_to_all | solution.py:354
  25.5 7.5 %all-to-all-done = bf16[64,4,256]{2,1,0:T(4,128)(2,1)S(1)} async-done(((bf16[64,4,256]{2,1,0:T(4,128)(2,1)}), bf16[64,4,256]{2,1,0:T(4,128)(2,1)S(1)}, u32[]{:S(2)}, u32[]{:S(2)}) %all-to-all-start) | async-done | bytes 131104 | tf_op jit(solution)/shard_map/all_to_all | solution.py:354
  33.7 2.7 %collective-permute-start = (bf16[59392]{0:T(1024)(128)(2,1)S(1)}, bf16[59392]{0:T(1024)(128)(2,1)S(1)}, u32[]{:S(2)}, u32[]{:S(2)}) collective-permute-start(bf16[59392]{0:T(1024)(128)(2,1)S(1)} %constant_dynamic-update-slice_fusion.23), channel_id=1, source_target_pairs={{0,3},{1,0},{2,1},{3,2},{4,7},{5,4},{6,5},{7,6},{8,11},{9,8},{10,9... | collective-permute-start | bytes 356360 | tf_op jit(solution)/shard_map/ppermute | solution.py:147
  36.5 3.0 %collective-permute-start.1 = (bf16[59392]{0:T(1024)(128)(2,1)S(1)}, bf16[59392]{0:T(1024)(128)(2,1)S(1)}, u32[]{:S(2)}, u32[]{:S(2)}) collective-permute-start(bf16[59392]{0:T(1024)(128)(2,1)S(1)} %constant_dynamic-update-slice_fusion.23), channel_id=1, source_target_pairs={{0,2},{1,3},{2,0},{3,1},{4,6},{5,7},{6,4},{7,5},{8,10},{9,11},{10,... | collective-permute-start | bytes 356360 | tf_op jit(solution)/shard_map/ppermute | solution.py:147
  39.5 4.0 %collective-permute-start.2 = (bf16[59392]{0:T(1024)(128)(2,1)S(1)}, bf16[59392]{0:T(1024)(128)(2,1)S(1)}, u32[]{:S(2)}, u32[]{:S(2)}) collective-permute-start(bf16[59392]{0:T(1024)(128)(2,1)S(1)} %constant_dynamic-update-slice_fusion.23), channel_id=1, source_target_pairs={{0,1},{1,2},{2,3},{3,0},{4,5},{5,6},{6,7},{7,4},{8,9},{9,10},{10,1... | collective-permute-start | bytes 356360 | tf_op jit(solution)/shard_map/ppermute | solution.py:147
  44.7 1.7 %collective-permute-done.2 = bf16[59392]{0:T(1024)(128)(2,1)S(1)} collective-permute-done((bf16[59392]{0:T(1024)(128)(2,1)S(1)}, bf16[59392]{0:T(1024)(128)(2,1)S(1)}, u32[]{:S(2)}, u32[]{:S(2)}) %collective-permute-start.2) | collective-permute-done | bytes 118816 | tf_op jit(solution)/shard_map/ppermute | solution.py:147
  47.9 0.7 copy-done.16
  51.1 0.7 copy-done.18
  54.6 0.7 copy-done.7
  55.3 7.1 %shard_map.199 = f32[4,32,1,64]{3,2,1,0:T(1,128)} custom-call(f32[32,64,64]{2,1,0:T(8,128)} %bitcast.141, f32[4,5,32,1,64]{4,3,2,1,0:T(1,128)} %copy-done.7, f32[4,32,1,64]{3,2,1,0:T(1,128)} %bitcast.152), custom_call_target="tpu_custom_call" | custom-call | tf_op jit(solution)/shard_map/pallas_call | solution.py:33
  62.4 1.0 reduce_sum.128
  64.8 1.4 %collective-permute-start.6 = (f32[32,1024]{1,0:T(8,128)S(1)}, f32[32,1024]{1,0:T(8,128)S(1)}, u32[]{:S(2)}, u32[]{:S(2)}) collective-permute-start(f32[32,1024]{1,0:T(8,128)S(1)} %fusion.16), channel_id=1, source_target_pairs={{0,259},{1,256},{2,257},{3,258},{4,263},{5,260},{6,261},{7,262},{8... | collective-permute-start | bytes 393224 | tf_op jit(solution)/shard_map/ppermute | solution.py:166
  66.3 1.3 %collective-permute-start.5 = (f32[32,1024]{1,0:T(8,128)S(1)}, f32[32,1024]{1,0:T(8,128)S(1)}, u32[]{:S(2)}, u32[]{:S(2)}) collective-permute-start(f32[32,1024]{1,0:T(8,128)S(1)} %fusion.16), channel_id=1, source_target_pairs={{0,258},{1,259},{2,256},{3,257},{4,262},{5,263},{6,260},{7,261},{8... | collective-permute-start | bytes 393224 | tf_op jit(solution)/shard_map/ppermute | solution.py:166
  67.6 1.3 %collective-permute-start.3 = (f32[32,1024]{1,0:T(8,128)S(1)}, f32[32,1024]{1,0:T(8,128)S(1)}, u32[]{:S(2)}, u32[]{:S(2)}) collective-permute-start(f32[32,1024]{1,0:T(8,128)S(1)} %fusion.16), channel_id=1, source_target_pairs={{0,256},{1,257},{2,258},{3,259},{4,260},{5,261},{6,262},{7,263},{8... | collective-permute-start | bytes 393224 | tf_op jit(solution)/shard_map/ppermute | solution.py:166
  68.9 2.7 %collective-permute-start.4 = (f32[32,1024]{1,0:T(8,128)S(1)}, f32[32,1024]{1,0:T(8,128)S(1)}, u32[]{:S(2)}, u32[]{:S(2)}) collective-permute-start(f32[32,1024]{1,0:T(8,128)S(1)} %fusion.16), channel_id=1, source_target_pairs={{0,257},{1,258},{2,259},{3,256},{4,261},{5,262},{6,263},{7,260},{8... | collective-permute-start | bytes 393224 | tf_op jit(solution)/shard_map/ppermute | solution.py:166
  72.9 1.0 collective-permute-done.4
  73.9 0.8 fusion.32
  80.9 0.7 copy-done.8
  81.7 7.1 %shard_map.200 = f32[4,32,1,64]{3,2,1,0:T(1,128)} custom-call(f32[32,64,64]{2,1,0:T(8,128)} %bitcast.142, f32[4,5,32,1,64]{4,3,2,1,0:T(1,128)} %copy-done.8, f32[4,32,1,64]{3,2,1,0:T(1,128)} %bitcast.153), custom_call_target="tpu_custom_call" | custom-call | tf_op jit(solution)/shard_map/pallas_call | solution.py:33
  88.8 1.0 reduce_sum.132
  91.1 2.8 %collective-permute-start.10 = (f32[32,256]{1,0:T(8,128)S(1)}, f32[32,256]{1,0:T(8,128)S(1)}, u32[]{:S(2)}, u32[]{:S(2)}) collective-permute-start(f32[32,256]{1,0:T(8,128)S(1)} %get-tuple-element.27), channel_id=1, source_target_pairs={{0,3},{1,0},{2,1},{3,2},{4,7},{5,4},{6,5},{7,6},{8,11},{9,8},{10,9... | collective-permute-start | bytes 98312 | tf_op jit(solution)/shard_map/ppermute | solution.py:158
  93.9 4.3 %collective-permute-start.9 = (f32[32,256]{1,0:T(8,128)S(1)}, f32[32,256]{1,0:T(8,128)S(1)}, u32[]{:S(2)}, u32[]{:S(2)}) collective-permute-start(f32[32,256]{1,0:T(8,128)S(1)} %get-tuple-element.28), channel_id=1, source_target_pairs={{0,2},{1,3},{2,0},{3,1},{4,6},{5,7},{6,4},{7,5},{8,10},{9,11},{10,... | collective-permute-start | bytes 98312 | tf_op jit(solution)/shard_map/ppermute | solution.py:158
  98.2 2.7 %collective-permute-start.8 = (f32[32,256]{1,0:T(8,128)S(1)}, f32[32,256]{1,0:T(8,128)S(1)}, u32[]{:S(2)}, u32[]{:S(2)}) collective-permute-start(f32[32,256]{1,0:T(8,128)S(1)} %get-tuple-element.26), channel_id=1, source_target_pairs={{0,1},{1,2},{2,3},{3,0},{4,5},{5,6},{6,7},{7,4},{8,9},{9,10},{10,1... | collective-permute-start | bytes 98312 | tf_op jit(solution)/shard_map/ppermute | solution.py:158
  101.0 1.3 %collective-permute-start.7 = (bf16[8,4,256]{2,1,0:T(4,128)(2,1)S(1)}, bf16[8,4,256]{2,1,0:T(4,128)(2,1)S(1)}, u32[]{:S(2)}, u32[]{:S(2)}) collective-permute-start(bf16[8,4,256]{2,1,0:T(4,128)(2,1)S(1)} %constant_dynamic-slice_fusion.2), channel_id=1, source_target_pairs={{256,0},{257,1},{258,2},{259,3},{260,4},{261,5},{262,6},{263,7},{2... | collective-permute-start | bytes 49160 | tf_op jit(solution)/shard_map/ppermute | solution.py:173
  102.3 1.9 %collective-permute-done.8 = f32[32,256]{1,0:T(8,128)S(1)} collective-permute-done((f32[32,256]{1,0:T(8,128)S(1)}, f32[32,256]{1,0:T(8,128)S(1)}, u32[]{:S(2)}, u32[]{:S(2)}) %collective-permute-start.8) | collective-permute-done | bytes 32800 | tf_op jit(solution)/shard_map/ppermute | solution.py:158
  104.3 0.8 gather_fusion.3
  105.2 0.9 select_select_fusion
  106.0 6.2 %all-to-all-start.1 = ((bf16[64,4,256]{2,1,0:T(4,128)(2,1)}), bf16[64,4,256]{2,1,0:T(4,128)(2,1)S(1)}, u32[]{:S(2)}, u32[]{:S(2)}) async-start(bf16[64,4,256]{2,1,0:T(4,128)(2,1)} %select_select_fusion), calls=%async_computation.1 | async-start | bytes 262144 | tf_op jit(solution)/shard_map/all_to_all | solution.py:358
  113.6 11.6 %all-to-all-done.1 = bf16[64,4,256]{2,1,0:T(4,128)(2,1)S(1)} async-done(((bf16[64,4,256]{2,1,0:T(4,128)(2,1)}), bf16[64,4,256]{2,1,0:T(4,128)(2,1)S(1)}, u32[]{:S(2)}, u32[]{:S(2)}) %all-to-all-start.1) | async-done | bytes 131104 | tf_op jit(solution)/shard_map/all_to_all | solution.py:358
  126.4 0.7 fusion.89
  (288 shorter events, 27.6 us)
Async XLA Ops:
  0.0 64.0 %copy-start = (bf16[1,256,1024]{2,1,0:T(8,128)(2,1)S(1)}, bf16[1,256,1024]{2,1,0:T(8,128)(2,1)}, u32[]{:S(2)}) copy-start(bf16[1,256,1024]{2,1,0:T(8,128)(2,1)} %param.34) | copy-start | bytes 1572868
  0.8 1.3 %copy-start.6 = (bf16[8,4,256]{2,1,0:T(4,128)(2,1)S(1)}, bf16[8,4,256]{2,1,0:T(4,128)(2,1)}, u32[]{:S(2)}) copy-start(bf16[8,4,256]{2,1,0:T(4,128)(2,1)} %param.25) | copy-start | bytes 49156
  3.7 29.3 %all-to-all-start = ((bf16[64,4,256]{2,1,0:T(4,128)(2,1)}), bf16[64,4,256]{2,1,0:T(4,128)(2,1)S(1)}, u32[]{:S(2)}, u32[]{:S(2)}) async-start(bf16[64,4,256]{2,1,0:T(4,128)(2,1)} %select_select_fusion.1), calls=%async_computation | async-start | bytes 262144 | tf_op jit(solution)/shard_map/all_to_all | solution.py:354
  25.5 21.6 %copy-start.20 = (f32[1,1,1024]{2,1,0:T(1,128)}, f32[1,1,1024]{2,1,0:T(1,128)S(1)}, u32[]{:S(2)}) copy-start(f32[1,1,1024]{2,1,0:T(1,128)S(1)} %get-tuple-element.46) | copy-start | bytes 12292
  25.5 21.6 %copy-start.22 = (f32[1,1,1024]{2,1,0:T(1,128)}, f32[1,1,1024]{2,1,0:T(1,128)S(1)}, u32[]{:S(2)}) copy-start(f32[1,1,1024]{2,1,0:T(1,128)S(1)} %get-tuple-element.44) | copy-start | bytes 12292
  25.5 21.6 %copy-start.24 = (f32[1,1,1024]{2,1,0:T(1,128)}, f32[1,1,1024]{2,1,0:T(1,128)S(1)}, u32[]{:S(2)}) copy-start(f32[1,1,1024]{2,1,0:T(1,128)S(1)} %get-tuple-element.47) | copy-start | bytes 12292
  25.5 22.4 %copy-start.29 = (f32[1,1,1024]{2,1,0:T(1,128)}, f32[1,1,1024]{2,1,0:T(1,128)S(1)}, u32[]{:S(2)}) copy-start(f32[1,1,1024]{2,1,0:T(1,128)S(1)} %get-tuple-element.45) | copy-start | bytes 12292
  25.5 25.5 %copy-start.27 = (f32[1,1,1024]{2,1,0:T(1,128)}, f32[1,1,1024]{2,1,0:T(1,128)S(1)}, u32[]{:S(2)}) copy-start(f32[1,1,1024]{2,1,0:T(1,128)S(1)} %get-tuple-element.43) | copy-start | bytes 12292
  33.7 10.3 %collective-permute-start = (bf16[59392]{0:T(1024)(128)(2,1)S(1)}, bf16[59392]{0:T(1024)(128)(2,1)S(1)}, u32[]{:S(2)}, u32[]{:S(2)}) collective-permute-start(bf16[59392]{0:T(1024)(128)(2,1)S(1)} %constant_dynamic-update-slice_fusion.23), channel_id=1, source_target_pairs={{0,3},{1,0},{2,1},{3,2},{4,7},{5,4},{6,5},{7,6},{8,11},{9,8},{10,9... | collective-permute-start | bytes 356360 | tf_op jit(solution)/shard_map/ppermute | solution.py:147
  36.5 8.2 %collective-permute-start.1 = (bf16[59392]{0:T(1024)(128)(2,1)S(1)}, bf16[59392]{0:T(1024)(128)(2,1)S(1)}, u32[]{:S(2)}, u32[]{:S(2)}) collective-permute-start(bf16[59392]{0:T(1024)(128)(2,1)S(1)} %constant_dynamic-update-slice_fusion.23), channel_id=1, source_target_pairs={{0,2},{1,3},{2,0},{3,1},{4,6},{5,7},{6,4},{7,5},{8,10},{9,11},{10,... | collective-permute-start | bytes 356360 | tf_op jit(solution)/shard_map/ppermute | solution.py:147
  39.5 6.9 %collective-permute-start.2 = (bf16[59392]{0:T(1024)(128)(2,1)S(1)}, bf16[59392]{0:T(1024)(128)(2,1)S(1)}, u32[]{:S(2)}, u32[]{:S(2)}) collective-permute-start(bf16[59392]{0:T(1024)(128)(2,1)S(1)} %constant_dynamic-update-slice_fusion.23), channel_id=1, source_target_pairs={{0,1},{1,2},{2,3},{3,0},{4,5},{5,6},{6,7},{7,4},{8,9},{9,10},{10,1... | collective-permute-start | bytes 356360 | tf_op jit(solution)/shard_map/ppermute | solution.py:147
  46.5 4.5 %copy-start.9 = (bf16[32,256]{1,0:T(8,128)(2,1)}, bf16[32,256]{1,0:T(8,128)(2,1)S(1)}, u32[]{:S(2)}) copy-start(bf16[32,256]{1,0:T(8,128)(2,1)S(1)} %slice.200) | copy-start | bytes 49156
  46.6 4.5 %copy-start.11 = (bf16[32,256]{1,0:T(8,128)(2,1)}, bf16[32,256]{1,0:T(8,128)(2,1)S(1)}, u32[]{:S(2)}) copy-start(bf16[32,256]{1,0:T(8,128)(2,1)S(1)} %slice.201) | copy-start | bytes 49156
  46.7 4.4 %copy-start.13 = (bf16[32,256]{1,0:T(8,128)(2,1)}, bf16[32,256]{1,0:T(8,128)(2,1)S(1)}, u32[]{:S(2)}) copy-start(bf16[32,256]{1,0:T(8,128)(2,1)S(1)} %slice.202) | copy-start | bytes 49156
  47.9 1.2 copy-start.3
  48.6 1.1 copy-start.1
  52.5 1.1 copy-start.2
  62.4 1.0 copy-start.5
  64.6 6.9 %copy-start.51 = (s32[64]{0:T(128)S(1)}, s32[64]{0:T(128)}, u32[]{:S(2)}) copy-start(s32[64]{0:T(128)} %compare_select_fusion.3) | copy-start | bytes 772
  64.6 7.6 %copy-start.53 = (s32[8]{0:T(128)S(1)}, s32[8]{0:T(128)}, u32[]{:S(2)}) copy-start(s32[8]{0:T(128)} %copy-done.52) | copy-start | bytes 100
  64.8 8.0 %collective-permute-start.6 = (f32[32,1024]{1,0:T(8,128)S(1)}, f32[32,1024]{1,0:T(8,128)S(1)}, u32[]{:S(2)}, u32[]{:S(2)}) collective-permute-start(f32[32,1024]{1,0:T(8,128)S(1)} %fusion.16), channel_id=1, source_target_pairs={{0,259},{1,256},{2,257},{3,258},{4,263},{5,260},{6,261},{7,262},{8... | collective-permute-start | bytes 393224 | tf_op jit(solution)/shard_map/ppermute | solution.py:166
  66.3 6.6 %collective-permute-start.5 = (f32[32,1024]{1,0:T(8,128)S(1)}, f32[32,1024]{1,0:T(8,128)S(1)}, u32[]{:S(2)}, u32[]{:S(2)}) collective-permute-start(f32[32,1024]{1,0:T(8,128)S(1)} %fusion.16), channel_id=1, source_target_pairs={{0,258},{1,259},{2,256},{3,257},{4,262},{5,263},{6,260},{7,261},{8... | collective-permute-start | bytes 393224 | tf_op jit(solution)/shard_map/ppermute | solution.py:166
  67.6 5.3 %collective-permute-start.3 = (f32[32,1024]{1,0:T(8,128)S(1)}, f32[32,1024]{1,0:T(8,128)S(1)}, u32[]{:S(2)}, u32[]{:S(2)}) collective-permute-start(f32[32,1024]{1,0:T(8,128)S(1)} %fusion.16), channel_id=1, source_target_pairs={{0,256},{1,257},{2,258},{3,259},{4,260},{5,261},{6,262},{7,263},{8... | collective-permute-start | bytes 393224 | tf_op jit(solution)/shard_map/ppermute | solution.py:166
  68.9 5.0 %collective-permute-start.4 = (f32[32,1024]{1,0:T(8,128)S(1)}, f32[32,1024]{1,0:T(8,128)S(1)}, u32[]{:S(2)}, u32[]{:S(2)}) collective-permute-start(f32[32,1024]{1,0:T(8,128)S(1)} %fusion.16), channel_id=1, source_target_pairs={{0,257},{1,258},{2,259},{3,256},{4,261},{5,262},{6,263},{7,260},{8... | collective-permute-start | bytes 393224 | tf_op jit(solution)/shard_map/ppermute | solution.py:166
  72.2 1.7 %copy-start.10 = (bf16[32,256]{1,0:T(8,128)(2,1)S(1)}, bf16[32,256]{1,0:T(8,128)(2,1)}, u32[]{:S(2)}) copy-start(bf16[32,256]{1,0:T(8,128)(2,1)} %copy-done.9) | copy-start | bytes 49156
  72.2 1.7 %copy-start.12 = (bf16[32,256]{1,0:T(8,128)(2,1)S(1)}, bf16[32,256]{1,0:T(8,128)(2,1)}, u32[]{:S(2)}) copy-start(bf16[32,256]{1,0:T(8,128)(2,1)} %copy-done.11) | copy-start | bytes 49156
  88.8 1.0 copy-start.4
  91.1 11.2 %collective-permute-start.10 = (f32[32,256]{1,0:T(8,128)S(1)}, f32[32,256]{1,0:T(8,128)S(1)}, u32[]{:S(2)}, u32[]{:S(2)}) collective-permute-start(f32[32,256]{1,0:T(8,128)S(1)} %get-tuple-element.27), channel_id=1, source_target_pairs={{0,3},{1,0},{2,1},{3,2},{4,7},{5,4},{6,5},{7,6},{8,11},{9,8},{10,9... | collective-permute-start | bytes 98312 | tf_op jit(solution)/shard_map/ppermute | solution.py:158
  93.9 8.4 %collective-permute-start.9 = (f32[32,256]{1,0:T(8,128)S(1)}, f32[32,256]{1,0:T(8,128)S(1)}, u32[]{:S(2)}, u32[]{:S(2)}) collective-permute-start(f32[32,256]{1,0:T(8,128)S(1)} %get-tuple-element.28), channel_id=1, source_target_pairs={{0,2},{1,3},{2,0},{3,1},{4,6},{5,7},{6,4},{7,5},{8,10},{9,11},{10,... | collective-permute-start | bytes 98312 | tf_op jit(solution)/shard_map/ppermute | solution.py:158
  98.2 6.0 %collective-permute-start.8 = (f32[32,256]{1,0:T(8,128)S(1)}, f32[32,256]{1,0:T(8,128)S(1)}, u32[]{:S(2)}, u32[]{:S(2)}) collective-permute-start(f32[32,256]{1,0:T(8,128)S(1)} %get-tuple-element.26), channel_id=1, source_target_pairs={{0,1},{1,2},{2,3},{3,0},{4,5},{5,6},{6,7},{7,4},{8,9},{9,10},{10,1... | collective-permute-start | bytes 98312 | tf_op jit(solution)/shard_map/ppermute | solution.py:158
  101.0 3.3 %collective-permute-start.7 = (bf16[8,4,256]{2,1,0:T(4,128)(2,1)S(1)}, bf16[8,4,256]{2,1,0:T(4,128)(2,1)S(1)}, u32[]{:S(2)}, u32[]{:S(2)}) collective-permute-start(bf16[8,4,256]{2,1,0:T(4,128)(2,1)S(1)} %constant_dynamic-slice_fusion.2), channel_id=1, source_target_pairs={{256,0},{257,1},{258,2},{259,3},{260,4},{261,5},{262,6},{263,7},{2... | collective-permute-start | bytes 49160 | tf_op jit(solution)/shard_map/ppermute | solution.py:173
  106.0 19.1 %all-to-all-start.1 = ((bf16[64,4,256]{2,1,0:T(4,128)(2,1)}), bf16[64,4,256]{2,1,0:T(4,128)(2,1)S(1)}, u32[]{:S(2)}, u32[]{:S(2)}) async-start(bf16[64,4,256]{2,1,0:T(4,128)(2,1)} %select_select_fusion), calls=%async_computation.1 | async-start | bytes 262144 | tf_op jit(solution)/shard_map/all_to_all | solution.py:358
  (36 other events, 26.4 us)

commit v13 on v9

--- a/solution.py
+++ b/solution.py
@@ -263,6 +263,7 @@
     me = lax.axis_index("head")
     second_in = lax.dynamic_slice_in_dim(full_second, me * shard_width, shard_width, 2)
     first_out = hand_back(second_in)
+    full_second, first_out = lax.optimization_barrier((full_second, first_out))
     partial_second = layer_partial(full_second, full_prev, states_use, params)
     own_second = scatter_heads(partial_second).reshape(batch_rows, steps_count, shard_width)
     second_out = (second_in.astype(jnp.float32) + own_second).astype(jnp.bfloat16)

time: 130 us -> 134 us (1.031)
  waiting for transfers between devices: 29.8 us -> 33.9 us
    ppermute x1, waiting for transfers between devices: 0.01 us -> 2.25 us  [hand_back(): lax.ppermute(block, ('section', 'head'), [(n + i, i) for i in range(n)])]
    unnamed x128 -> x104, local copies, waits for them, and re-layouts: 12.9 us -> 11.8 us
  transfers between devices with their start and end apart: 13 -> 13, of which waited for: 7 -> 9; matrix products, arithmetic and copies ran while one was open for 2% -> 1% of each run, Pallas kernels for 0% -> 0%
where the time goes in v13:
time: 134 us; the launch traced here: 133 us
  starting transfers between devices  48.6 us (36%)
  waiting for transfers between devices  33.9 us (25%)
  local copies, waits for them, and re-layouts  23.7 us (18%)
  Pallas kernels  14.2 us (11%)
  other arithmetic  7.24 us (5%)
  matrix products  3.41 us (3%)
  between operations  1.56 us (1%)
    all_to_all x1, starting transfers between devices, body(): lax.all_to_all(outgoing, 'req', split_axis=0, concat_axis=0, tiled=True)  16.6 us
    pallas_call x2, Pallas kernels, run_recurrence(): pl.pallas_call(recurrence_kernel, out_shape=jax.ShapeDtypeStruct((steps,...  14.2 us
    all_to_all x1, waiting for transfers between devices, body(): lax.all_to_all(going_back, 'req', split_axis=0, concat_axis=0, tiled=True)  12 us
    unnamed x104, local copies, waits for them, and re-layouts  11.8 us
    ppermute x3, starting transfers between devices, gather_heads(): lax.ppermute(block, 'head', [(i, (i + k) % n) for i in range(n)])  9.76 us
    ppermute x3, starting transfers between devices, scatter_heads(): lax.ppermute(chunk, 'head', [(i, (i + k) % n) for i in range(n)])  9.58 us
    all_to_all x1, waiting for transfers between devices, body(): lax.all_to_all(outgoing, 'req', split_axis=0, concat_axis=0, tiled=True)  9.21 us
    ppermute x4, starting transfers between devices, hand_over(): lax.ppermute(partial, ('section', 'head'), [(i, n + (i + k) % n) for i in...  6.55 us
  transfers between devices with their start and end apart: 13, of which 9 were waited for; matrix products, arithmetic and copies ran while one was open for 1% of the time, Pallas kernels for 0%

profile of v13, /device:TPU:6, one launch (start us, length us, event | category | flops | bytes accessed | tf_op | source)
XLA Modules:
  0.0 132.6 jit_solution(6096494356562735011)
XLA Ops:
  2.3 1.9 %scatter_fusion = bf16[64,4,256]{2,1,0:T(4,128)(2,1)} fusion(bf16[64,4,256]{2,1,0:T(4,128)(2,1)} %broadcast.445.clone, s32[8]{0:T(128)S(1)} %fusion.83, bf16[8,4,256]{2,1,0:T(4,128)(2,1)S(1)} %copy-done.16), kind=kCustom, calls=%fused_computation.3 | custom fusion | bytes 49184 | tf_op jit(solution)/shard_map/scatter | solution.py:347
  4.2 16.6 %all-to-all-start = ((bf16[64,4,256]{2,1,0:T(4,128)(2,1)}), bf16[64,4,256]{2,1,0:T(4,128)(2,1)S(1)}, u32[]{:S(2)}, u32[]{:S(2)}) async-start(bf16[64,4,256]{2,1,0:T(4,128)(2,1)} %scatter_fusion), calls=%async_computation | async-start | bytes 262144 | tf_op jit(solution)/shard_map/all_to_all | solution.py:349
  24.3 9.2 %all-to-all-done = bf16[64,4,256]{2,1,0:T(4,128)(2,1)S(1)} async-done(((bf16[64,4,256]{2,1,0:T(4,128)(2,1)}), bf16[64,4,256]{2,1,0:T(4,128)(2,1)S(1)}, u32[]{:S(2)}, u32[]{:S(2)}) %all-to-all-start) | async-done | bytes 131104 | tf_op jit(solution)/shard_map/all_to_all | solution.py:349
  34.3 2.7 %collective-permute-start = (bf16[59392]{0:T(1024)(128)(2,1)S(1)}, bf16[59392]{0:T(1024)(128)(2,1)S(1)}, u32[]{:S(2)}, u32[]{:S(2)}) collective-permute-start(bf16[59392]{0:T(1024)(128)(2,1)S(1)} %constant_dynamic-update-slice_fusion.23), channel_id=1, source_target_pairs={{0,3},{1,0},{2,1},{3,2},{4,7},{5,4},{6,5},{7,6},{8,11},{9,8},{10,9... | collective-permute-start | bytes 356360 | tf_op jit(solution)/shard_map/ppermute | solution.py:147
  37.0 3.0 %collective-permute-start.1 = (bf16[59392]{0:T(1024)(128)(2,1)S(1)}, bf16[59392]{0:T(1024)(128)(2,1)S(1)}, u32[]{:S(2)}, u32[]{:S(2)}) collective-permute-start(bf16[59392]{0:T(1024)(128)(2,1)S(1)} %constant_dynamic-update-slice_fusion.23), channel_id=1, source_target_pairs={{0,2},{1,3},{2,0},{3,1},{4,6},{5,7},{6,4},{7,5},{8,10},{9,11},{10,... | collective-permute-start | bytes 356360 | tf_op jit(solution)/shard_map/ppermute | solution.py:147
  40.0 4.0 %collective-permute-start.2 = (bf16[59392]{0:T(1024)(128)(2,1)S(1)}, bf16[59392]{0:T(1024)(128)(2,1)S(1)}, u32[]{:S(2)}, u32[]{:S(2)}) collective-permute-start(bf16[59392]{0:T(1024)(128)(2,1)S(1)} %constant_dynamic-update-slice_fusion.23), channel_id=1, source_target_pairs={{0,1},{1,2},{2,3},{3,0},{4,5},{5,6},{6,7},{7,4},{8,9},{9,10},{10,1... | collective-permute-start | bytes 356360 | tf_op jit(solution)/shard_map/ppermute | solution.py:147
  44.1 1.1 collective-permute-done.1
  45.2 1.7 %collective-permute-done.2 = bf16[59392]{0:T(1024)(128)(2,1)S(1)} collective-permute-done((bf16[59392]{0:T(1024)(128)(2,1)S(1)}, bf16[59392]{0:T(1024)(128)(2,1)S(1)}, u32[]{:S(2)}, u32[]{:S(2)}) %collective-permute-start.2) | collective-permute-done | bytes 118816 | tf_op jit(solution)/shard_map/ppermute | solution.py:147
  51.5 0.8 copy-done.11
  55.4 7.1 %shard_map.199 = f32[4,32,1,64]{3,2,1,0:T(1,128)} custom-call(f32[32,64,64]{2,1,0:T(8,128)} %bitcast.166, f32[4,5,32,1,64]{4,3,2,1,0:T(1,128)} %copy-done.5, f32[4,32,1,64]{3,2,1,0:T(1,128)} %bitcast.177), custom_call_target="tpu_custom_call" | custom-call | tf_op jit(solution)/shard_map/pallas_call | solution.py:33
  62.5 1.0 reduce_sum.112
  63.5 1.0 multiply_reduce_fusion.2
  64.6 1.0 subtract_divide_fusion.1
  66.7 0.8 fusion.16
  67.5 1.3 collective-permute-start.3
  68.8 2.7 %collective-permute-start.4 = (f32[32,1024]{1,0:T(8,128)}, f32[32,1024]{1,0:T(8,128)S(1)}, u32[]{:S(2)}, u32[]{:S(2)}) collective-permute-start(f32[32,1024]{1,0:T(8,128)} %fusion.16), channel_id=1, source_target_pairs={{0,257},{1,258},{2,259},{3,256},{4,261},{5,262},{6,263},{7,260},{8... | collective-permute-start | bytes 393224 | tf_op jit(solution)/shard_map/ppermute | solution.py:166
  71.5 1.3 collective-permute-start.5
  72.8 1.3 collective-permute-start.6
  74.3 1.3 collective-permute-done.5
  75.6 1.4 %collective-permute-done.6 = f32[32,1024]{1,0:T(8,128)S(1)} collective-permute-done((f32[32,1024]{1,0:T(8,128)}, f32[32,1024]{1,0:T(8,128)S(1)}, u32[]{:S(2)}, u32[]{:S(2)}) %collective-permute-start.6) | collective-permute-done | bytes 131104 | tf_op jit(solution)/shard_map/ppermute | solution.py:166
  77.2 1.5 %collective-permute-start.7 = (bf16[8,4,256]{2,1,0:T(4,128)(2,1)S(1)}, bf16[8,4,256]{2,1,0:T(4,128)(2,1)S(1)}, u32[]{:S(2)}, u32[]{:S(2)}) collective-permute-start(bf16[8,4,256]{2,1,0:T(4,128)(2,1)S(1)} %constant_dynamic-slice_fusion.2), channel_id=1, source_target_pairs={{256,0},{257,1},{258,2},{259,3},{260,4},{261,5},{262,6},{263,7},{2... | collective-permute-start | bytes 49160 | tf_op jit(solution)/shard_map/ppermute | solution.py:173
  78.7 2.2 %collective-permute-done.7 = bf16[8,4,256]{2,1,0:T(4,128)(2,1)S(1)} collective-permute-done((bf16[8,4,256]{2,1,0:T(4,128)(2,1)S(1)}, bf16[8,4,256]{2,1,0:T(4,128)(2,1)S(1)}, u32[]{:S(2)}, u32[]{:S(2)}) %collective-permute-start.7) | collective-permute-done | bytes 16416 | tf_op jit(solution)/shard_map/ppermute | solution.py:173
  81.3 0.8 copy-done.10
  87.1 7.1 %shard_map.200 = f32[4,32,1,64]{3,2,1,0:T(1,128)} custom-call(f32[32,64,64]{2,1,0:T(8,128)} %bitcast.167, f32[4,5,32,1,64]{4,3,2,1,0:T(1,128)} %copy-done.6, f32[4,32,1,64]{3,2,1,0:T(1,128)} %bitcast.178), custom_call_target="tpu_custom_call" | custom-call | tf_op jit(solution)/shard_map/pallas_call | solution.py:33
  94.3 1.0 reduce_sum.116
  96.9 2.6 %collective-permute-start.10 = (f32[32,256]{1,0:T(8,128)S(1)}, f32[32,256]{1,0:T(8,128)S(1)}, u32[]{:S(2)}, u32[]{:S(2)}) collective-permute-start(f32[32,256]{1,0:T(8,128)S(1)} %get-tuple-element.33), channel_id=1, source_target_pairs={{0,3},{1,0},{2,1},{3,2},{4,7},{5,4},{6,5},{7,6},{8,11},{9,8},{10,9... | collective-permute-start | bytes 98312 | tf_op jit(solution)/shard_map/ppermute | solution.py:158
  99.5 4.4 %collective-permute-start.8 = (f32[32,256]{1,0:T(8,128)S(1)}, f32[32,256]{1,0:T(8,128)S(1)}, u32[]{:S(2)}, u32[]{:S(2)}) collective-permute-start(f32[32,256]{1,0:T(8,128)S(1)} %get-tuple-element.32), channel_id=1, source_target_pairs={{0,1},{1,2},{2,3},{3,0},{4,5},{5,6},{6,7},{7,4},{8,9},{9,10},{10,1... | collective-permute-start | bytes 98312 | tf_op jit(solution)/shard_map/ppermute | solution.py:158
  104.0 2.5 %collective-permute-start.9 = (f32[32,256]{1,0:T(8,128)S(1)}, f32[32,256]{1,0:T(8,128)S(1)}, u32[]{:S(2)}, u32[]{:S(2)}) collective-permute-start(f32[32,256]{1,0:T(8,128)S(1)} %get-tuple-element.34), channel_id=1, source_target_pairs={{0,2},{1,3},{2,0},{3,1},{4,6},{5,7},{6,4},{7,5},{8,10},{9,11},{10,... | collective-permute-start | bytes 98312 | tf_op jit(solution)/shard_map/ppermute | solution.py:158
  106.6 4.7 %collective-permute-done.9 = f32[32,256]{1,0:T(8,128)S(1)} collective-permute-done((f32[32,256]{1,0:T(8,128)S(1)}, f32[32,256]{1,0:T(8,128)S(1)}, u32[]{:S(2)}, u32[]{:S(2)}) %collective-permute-start.9) | collective-permute-done | bytes 32800 | tf_op jit(solution)/shard_map/ppermute | solution.py:158
  112.0 1.9 %scatter_fusion.1 = bf16[64,4,256]{2,1,0:T(4,128)(2,1)} fusion(bf16[64,4,256]{2,1,0:T(4,128)(2,1)} %broadcast.445, s32[8]{0:T(128)S(1)} %fusion.82, bf16[8,4,256]{2,1,0:T(4,128)(2,1)S(1)} %fusion.70), kind=kCustom, calls=%fused_computation.4 | custom fusion | bytes 49184 | tf_op jit(solution)/shard_map/scatter | solution.py:353
  114.0 4.6 %all-to-all-start.1 = ((bf16[64,4,256]{2,1,0:T(4,128)(2,1)}), bf16[64,4,256]{2,1,0:T(4,128)(2,1)S(1)}, u32[]{:S(2)}, u32[]{:S(2)}) async-start(bf16[64,4,256]{2,1,0:T(4,128)(2,1)} %scatter_fusion.1), calls=%async_computation.1 | async-start | bytes 262144 | tf_op jit(solution)/shard_map/all_to_all | solution.py:355
  119.3 12.0 %all-to-all-done.1 = bf16[64,4,256]{2,1,0:T(4,128)(2,1)S(1)} async-done(((bf16[64,4,256]{2,1,0:T(4,128)(2,1)}), bf16[64,4,256]{2,1,0:T(4,128)(2,1)S(1)}, u32[]{:S(2)}, u32[]{:S(2)}) %all-to-all-start.1) | async-done | bytes 131104 | tf_op jit(solution)/shard_map/all_to_all | solution.py:355
  (251 shorter events, 24.4 us)
Async XLA Ops:
  0.0 49.7 %copy-start = (bf16[1,1024,256]{2,1,0:T(8,128)(2,1)S(1)}, bf16[1,1024,256]{2,1,0:T(8,128)(2,1)}, u32[]{:S(2)}) copy-start(bf16[1,1024,256]{2,1,0:T(8,128)(2,1)} %param.29) | copy-start | bytes 1572868
  4.2 29.3 %all-to-all-start = ((bf16[64,4,256]{2,1,0:T(4,128)(2,1)}), bf16[64,4,256]{2,1,0:T(4,128)(2,1)S(1)}, u32[]{:S(2)}, u32[]{:S(2)}) async-start(bf16[64,4,256]{2,1,0:T(4,128)(2,1)} %scatter_fusion), calls=%async_computation | async-start | bytes 262144 | tf_op jit(solution)/shard_map/all_to_all | solution.py:349
  20.8 1.5 %copy-start.7 = (bf16[1,256,96]{1,2,0:T(8,128)(2,1)S(1)}, bf16[1,256,96]{1,2,0:T(8,128)(2,1)}, u32[]{:S(2)}) copy-start(bf16[1,256,96]{1,2,0:T(8,128)(2,1)} %param.33) | copy-start | bytes 147460
  22.4 0.8 copy-start.8
  34.2 9.8 %copy-start.13 = (bf16[1,5,1024]{2,1,0:T(8,128)(2,1)S(1)}, bf16[1,5,1024]{2,1,0:T(8,128)(2,1)}, u32[]{:S(2)}) copy-start(bf16[1,5,1024]{2,1,0:T(8,128)(2,1)} %param.28) | copy-start | bytes 30724
  34.3 9.8 %collective-permute-start = (bf16[59392]{0:T(1024)(128)(2,1)S(1)}, bf16[59392]{0:T(1024)(128)(2,1)S(1)}, u32[]{:S(2)}, u32[]{:S(2)}) collective-permute-start(bf16[59392]{0:T(1024)(128)(2,1)S(1)} %constant_dynamic-update-slice_fusion.23), channel_id=1, source_target_pairs={{0,3},{1,0},{2,1},{3,2},{4,7},{5,4},{6,5},{7,6},{8,11},{9,8},{10,9... | collective-permute-start | bytes 356360 | tf_op jit(solution)/shard_map/ppermute | solution.py:147
  37.0 8.2 %collective-permute-start.1 = (bf16[59392]{0:T(1024)(128)(2,1)S(1)}, bf16[59392]{0:T(1024)(128)(2,1)S(1)}, u32[]{:S(2)}, u32[]{:S(2)}) collective-permute-start(bf16[59392]{0:T(1024)(128)(2,1)S(1)} %constant_dynamic-update-slice_fusion.23), channel_id=1, source_target_pairs={{0,2},{1,3},{2,0},{3,1},{4,6},{5,7},{6,4},{7,5},{8,10},{9,11},{10,... | collective-permute-start | bytes 356360 | tf_op jit(solution)/shard_map/ppermute | solution.py:147
  40.0 6.9 %collective-permute-start.2 = (bf16[59392]{0:T(1024)(128)(2,1)S(1)}, bf16[59392]{0:T(1024)(128)(2,1)S(1)}, u32[]{:S(2)}, u32[]{:S(2)}) collective-permute-start(bf16[59392]{0:T(1024)(128)(2,1)S(1)} %constant_dynamic-update-slice_fusion.23), channel_id=1, source_target_pairs={{0,1},{1,2},{2,3},{3,0},{4,5},{5,6},{6,7},{7,4},{8,9},{9,10},{10,1... | collective-permute-start | bytes 356360 | tf_op jit(solution)/shard_map/ppermute | solution.py:147
  44.1 4.3 %copy-start.14 = (f32[1,1,1024]{2,1,0:T(1,128)}, f32[1,1,1024]{2,1,0:T(1,128)S(1)}, u32[]{:S(2)}) copy-start(f32[1,1,1024]{2,1,0:T(1,128)S(1)} %get-tuple-element.51) | copy-start | bytes 12292
  48.3 0.8 copy-start.9
  48.3 0.8 copy-start.33
  48.3 1.2 copy-start.1
  51.5 0.8 copy-start.11
  52.6 1.0 copy-start.2
  62.5 3.5 %copy-start.3 = (bf16[1,256,1024]{2,1,0:T(8,128)(2,1)S(1)}, bf16[1,256,1024]{2,1,0:T(8,128)(2,1)}, u32[]{:S(2)}) copy-start(bf16[1,256,1024]{2,1,0:T(8,128)(2,1)} %param.32) | copy-start | bytes 1572868
  67.5 6.6 %collective-permute-start.3 = (f32[32,1024]{1,0:T(8,128)}, f32[32,1024]{1,0:T(8,128)S(1)}, u32[]{:S(2)}, u32[]{:S(2)}) collective-permute-start(f32[32,1024]{1,0:T(8,128)} %fusion.16), channel_id=1, source_target_pairs={{0,256},{1,257},{2,258},{3,259},{4,260},{5,261},{6,262},{7,263},{8... | collective-permute-start | bytes 393224 | tf_op jit(solution)/shard_map/ppermute | solution.py:166
  68.8 5.5 %collective-permute-start.4 = (f32[32,1024]{1,0:T(8,128)}, f32[32,1024]{1,0:T(8,128)S(1)}, u32[]{:S(2)}, u32[]{:S(2)}) collective-permute-start(f32[32,1024]{1,0:T(8,128)} %fusion.16), channel_id=1, source_target_pairs={{0,257},{1,258},{2,259},{3,256},{4,261},{5,262},{6,263},{7,260},{8... | collective-permute-start | bytes 393224 | tf_op jit(solution)/shard_map/ppermute | solution.py:166
  71.5 4.1 %collective-permute-start.5 = (f32[32,1024]{1,0:T(8,128)}, f32[32,1024]{1,0:T(8,128)S(1)}, u32[]{:S(2)}, u32[]{:S(2)}) collective-permute-start(f32[32,1024]{1,0:T(8,128)} %fusion.16), channel_id=1, source_target_pairs={{0,258},{1,259},{2,256},{3,257},{4,262},{5,263},{6,260},{7,261},{8... | collective-permute-start | bytes 393224 | tf_op jit(solution)/shard_map/ppermute | solution.py:166
  72.8 4.2 %collective-permute-start.6 = (f32[32,1024]{1,0:T(8,128)}, f32[32,1024]{1,0:T(8,128)S(1)}, u32[]{:S(2)}, u32[]{:S(2)}) collective-permute-start(f32[32,1024]{1,0:T(8,128)} %fusion.16), channel_id=1, source_target_pairs={{0,259},{1,256},{2,257},{3,258},{4,263},{5,260},{6,261},{7,262},{8... | collective-permute-start | bytes 393224 | tf_op jit(solution)/shard_map/ppermute | solution.py:166
  77.1 1.5 %copy-start.32 = (s32[8]{0:T(128)S(1)}, s32[8]{0:T(128)}, u32[]{:S(2)}) copy-start(s32[8]{0:T(128)} %copy-done.31) | copy-start | bytes 100
  77.1 1.5 %copy-start.38 = (s32[8]{0:T(128)S(1)}, s32[8]{0:T(128)}, u32[]{:S(2)}) copy-start(s32[8]{0:T(128)} %copy-done.37) | copy-start | bytes 100
  77.2 3.8 %collective-permute-start.7 = (bf16[8,4,256]{2,1,0:T(4,128)(2,1)S(1)}, bf16[8,4,256]{2,1,0:T(4,128)(2,1)S(1)}, u32[]{:S(2)}, u32[]{:S(2)}) collective-permute-start(bf16[8,4,256]{2,1,0:T(4,128)(2,1)S(1)} %constant_dynamic-slice_fusion.2), channel_id=1, source_target_pairs={{256,0},{257,1},{258,2},{259,3},{260,4},{261,5},{262,6},{263,7},{2... | collective-permute-start | bytes 49160 | tf_op jit(solution)/shard_map/ppermute | solution.py:173
  78.7 2.3 %copy-start.15 = (f32[1,1,1024]{2,1,0:T(1,128)S(1)}, f32[1,1,1024]{2,1,0:T(1,128)}, u32[]{:S(2)}) copy-start(f32[1,1,1024]{2,1,0:T(1,128)} %copy-done.14) | copy-start | bytes 12292
  81.2 0.8 copy-start.10
  81.2 0.8 copy-start.34
  83.9 0.8 copy-start.12
  94.3 1.0 copy-start.4
  96.9 9.7 %collective-permute-start.10 = (f32[32,256]{1,0:T(8,128)S(1)}, f32[32,256]{1,0:T(8,128)S(1)}, u32[]{:S(2)}, u32[]{:S(2)}) collective-permute-start(f32[32,256]{1,0:T(8,128)S(1)} %get-tuple-element.33), channel_id=1, source_target_pairs={{0,3},{1,0},{2,1},{3,2},{4,7},{5,4},{6,5},{7,6},{8,11},{9,8},{10,9... | collective-permute-start | bytes 98312 | tf_op jit(solution)/shard_map/ppermute | solution.py:158
  99.5 7.0 %copy-start.30 = (s32[8]{0:T(128)S(1)}, s32[8]{0:T(128)}, u32[]{:S(2)}) copy-start(s32[8]{0:T(128)} %copy-done.29) | copy-start | bytes 100
  99.5 7.0 %collective-permute-start.8 = (f32[32,256]{1,0:T(8,128)S(1)}, f32[32,256]{1,0:T(8,128)S(1)}, u32[]{:S(2)}, u32[]{:S(2)}) collective-permute-start(f32[32,256]{1,0:T(8,128)S(1)} %get-tuple-element.32), channel_id=1, source_target_pairs={{0,1},{1,2},{2,3},{3,0},{4,5},{5,6},{6,7},{7,4},{8,9},{9,10},{10,1... | collective-permute-start | bytes 98312 | tf_op jit(solution)/shard_map/ppermute | solution.py:158
  104.0 7.3 %collective-permute-start.9 = (f32[32,256]{1,0:T(8,128)S(1)}, f32[32,256]{1,0:T(8,128)S(1)}, u32[]{:S(2)}, u32[]{:S(2)}) collective-permute-start(f32[32,256]{1,0:T(8,128)S(1)} %get-tuple-element.34), channel_id=1, source_target_pairs={{0,2},{1,3},{2,0},{3,1},{4,6},{5,7},{6,4},{7,5},{8,10},{9,11},{10,... | collective-permute-start | bytes 98312 | tf_op jit(solution)/shard_map/ppermute | solution.py:158
  114.0 17.4 %all-to-all-start.1 = ((bf16[64,4,256]{2,1,0:T(4,128)(2,1)}), bf16[64,4,256]{2,1,0:T(4,128)(2,1)S(1)}, u32[]{:S(2)}, u32[]{:S(2)}) async-start(bf16[64,4,256]{2,1,0:T(4,128)(2,1)} %scatter_fusion.1), calls=%async_computation.1 | async-start | bytes 262144 | tf_op jit(solution)/shard_map/all_to_all | solution.py:355
  (21 other events, 14.3 us)
